TPU v7x, 256 devices: a whole 4x4x8 slice. The times are simulated.
256 devices in a mesh: section: 4 (over x), seq: 16 (over z, y_hi), tp: 4 (over y_lo, core).
Axes of the slice: x: 4, y: 4 (y_hi: 2, y_lo: 2; y = y_hi * 2 + y_lo), z: 8, core: 2. Of those that a mesh axis runs over, the one named last changes fastest.
Arguments:
- queries: bfloat16 [4, 4096, 8192], P('section', 'seq', 'tp'), may hold values from -135 to 135
- upstream: bfloat16 [4, 4096, 8192], P('section', 'seq', 'tp'), may hold values from -48 to 48
- shared_kv: bfloat16 [2, 4096, 1024], P(None, ('seq', 'tp')), may hold values from -5 to 5
Outputs:
- d_queries: bfloat16 [4, 4096, 8192], P('section', 'seq', 'tp')
- d_shared_kv: float32 [2, 4096, 1024], P(None, ('seq', 'tp'))
All inputs are finite; a program needn't handle non-finite values.
Results may differ from a plain program's by a relative error of at most 0.0098.
Values may be sent and summed in bfloat16 or wider, within the bound.
No kernel may reach another device: no remote copies, remote signals or barrier semaphores. Data moves between devices by JAX's collectives and lax.ppermute only.
A program may use at most 128 MiB of HBM per device.

v0:
```python
import math

import jax
import jax.numpy as jnp
from jax import lax
from jax.sharding import PartitionSpec as P

QH = 64
KVH = 8
HD = 128
WINDOW = 1024


def shifted(value, axis, by):
    peers = lax.axis_size(axis)
    pairs = [(i, i + by) for i in range(peers) if 0 <= i + by < peers]
    return lax.ppermute(value, axis, pairs)


def head_grads(query_block, grad_block, keys_head, values_head, allowed, score_scale):
    scores = (
        jnp.einsum("rgd,ed->gre", query_block, keys_head, preferred_element_type=jnp.float32)
        * score_scale
    )
    masked = jnp.where(allowed[None], scores, -jnp.inf)
    highest = jnp.max(masked, axis=-1, keepdims=True)
    weights = jnp.exp(masked - highest)
    probs = weights / jnp.sum(weights, axis=-1, keepdims=True)
    probs_b = probs.astype(jnp.bfloat16)
    attn_out = jnp.einsum("gre,ed->rgd", probs_b, values_head, preferred_element_type=jnp.float32)
    delta = jnp.sum(grad_block.astype(jnp.float32) * attn_out, axis=-1)
    dprobs = jnp.einsum("rgd,ed->gre", grad_block, values_head, preferred_element_type=jnp.float32)
    dscores = probs * (dprobs - jnp.transpose(delta)[:, :, None])
    dscores_b = dscores.astype(jnp.bfloat16)
    grad_query = (
        jnp.einsum("gre,ed->rgd", dscores_b, keys_head, preferred_element_type=jnp.float32)
        * score_scale
    )
    grad_key = (
        jnp.einsum("gre,rgd->ed", dscores_b, query_block, preferred_element_type=jnp.float32)
        * score_scale
    )
    grad_value = jnp.einsum("gre,rgd->ed", probs_b, grad_block, preferred_element_type=jnp.float32)
    return (grad_query, grad_key, grad_value)


def body(queries, upstream, shared_kv):
    local_kv = lax.all_to_all(shared_kv, "tp", split_axis=2, concat_axis=1, tiled=True)
    tok_rows = local_kv.shape[1]
    kv_cols = local_kv.shape[2]
    head_size = HD
    local_kv_heads = kv_cols // head_size
    group_size = QH // KVH
    block_heads = max(1, group_size // 2)
    span_blocks = WINDOW // tok_rows
    score_scale = 1.0 / math.sqrt(head_size)
    earlier = [shifted(local_kv, "seq", span_blocks - offset) for offset in range(span_blocks)]
    extended = jnp.concatenate(earlier + [local_kv], axis=1)
    ext_rows = extended.shape[1]
    position = lax.axis_index("seq")
    row_ids = lax.broadcasted_iota(jnp.int32, (tok_rows, ext_rows), 0)
    key_ids = lax.broadcasted_iota(jnp.int32, (tok_rows, ext_rows), 1)
    allowed = (
        (key_ids >= row_ids + 1)
        & (key_ids <= row_ids + WINDOW)
        & (position * tok_rows - WINDOW + key_ids >= 0)
    )
    query_heads = queries.reshape(tok_rows, -1, head_size)
    grad_heads = upstream.reshape(tok_rows, -1, head_size)
    query_parts = []
    key_parts = []
    value_parts = []
    for kv_head in range(local_kv_heads):
        keys_head = extended[0, :, kv_head * head_size : (kv_head + 1) * head_size]
        values_head = extended[1, :, kv_head * head_size : (kv_head + 1) * head_size]
        key_total = jnp.zeros((ext_rows, head_size), jnp.float32)
        value_total = jnp.zeros((ext_rows, head_size), jnp.float32)
        for first_head in range(kv_head * group_size, (kv_head + 1) * group_size, block_heads):
            query_block = query_heads[:, first_head : first_head + block_heads]
            grad_block = grad_heads[:, first_head : first_head + block_heads]
            grad_query, grad_key, grad_value = head_grads(
                query_block, grad_block, keys_head, values_head, allowed, score_scale
            )
            query_parts.append(grad_query)
            key_total = key_total + grad_key
            value_total = value_total + grad_value
        key_parts.append(key_total)
        value_parts.append(value_total)
    d_queries = jnp.concatenate(query_parts, axis=1).reshape(1, tok_rows, -1).astype(jnp.bfloat16)
    grad_ext = jnp.stack([jnp.concatenate(key_parts, axis=1), jnp.concatenate(value_parts, axis=1)])
    own_rows = grad_ext[:, span_blocks * tok_rows :, :]
    for offset in range(span_blocks):
        own_rows = own_rows + shifted(
            grad_ext[:, offset * tok_rows : (offset + 1) * tok_rows, :].astype(jnp.bfloat16),
            "seq",
            offset - span_blocks,
        ).astype(jnp.float32)
    summed = lax.psum(own_rows, "section")
    d_shared_kv = lax.all_to_all(summed, "tp", split_axis=1, concat_axis=2, tiled=True)
    return (d_queries, d_shared_kv)


def solution(mesh):
    in_specs = (P("section", "seq", "tp"), P("section", "seq", "tp"), P(None, ("seq", "tp"), None))
    out_specs = (P("section", "seq", "tp"), P(None, ("seq", "tp"), None))
    return jax.shard_map(body, mesh=mesh, in_specs=in_specs, out_specs=out_specs, check_vma=False)
```

profile of v0, /device:TPU:80, one launch (start us, length us, event | category | flops | bytes accessed | tf_op | source)
XLA Modules:
  0.0 227.1 jit_solution(4104117547018688944)
XLA Ops:
  9.6 3.4 %all-to-all-start = ((bf16[4,2,16384]{2,1,0:T(2,128)(2,1)}), bf16[4,2,16384]{2,1,0:T(2,128)(2,1)S(1)}, u32[]{:S(2)}, u32[]{:S(2)}) async-start(bf16[4,2,16384]{2,1,0:T(2,128)(2,1)} %reshape.105), calls=%async_computation | async-start | bytes 524288 | tf_op jit(solution)/shard_map/all_to_all | solution.py:48
  13.1 5.9 %all-to-all-done = bf16[4,2,16384]{2,1,0:T(2,128)(2,1)S(1)} async-done(((bf16[4,2,16384]{2,1,0:T(2,128)(2,1)}), bf16[4,2,16384]{2,1,0:T(2,128)(2,1)S(1)}, u32[]{:S(2)}, u32[]{:S(2)}) %all-to-all-start) | async-done | bytes 262176 | tf_op jit(solution)/shard_map/all_to_all | solution.py:48
  20.4 6.4 %collective-permute-start = (bf16[2,256,256]{2,1,0:T(8,128)(2,1)}, bf16[2,256,256]{2,1,0:T(8,128)(2,1)}, u32[]{:S(2)}, u32[]{:S(2)}) collective-permute-start(bf16[2,256,256]{2,1,0:T(8,128)(2,1)} %bitcast.2), channel_id=1, source_target_pairs={{0,16},{4,20},{8,24},{12,28},{16,32},{20,36},{24,40},{28,44},{32,4... | collective-permute-start | bytes 786440 | tf_op jit(solution)/shard_map/ppermute | solution.py:17
  28.4 2.9 %collective-permute-start.2 = (bf16[2,256,256]{2,1,0:T(8,128)(2,1)}, bf16[2,256,256]{2,1,0:T(8,128)(2,1)}, u32[]{:S(2)}, u32[]{:S(2)}) collective-permute-start(bf16[2,256,256]{2,1,0:T(8,128)(2,1)} %bitcast.2), channel_id=1, source_target_pairs={{0,8},{4,12},{8,16},{12,20},{16,24},{20,28},{24,32},{28,36},{32,40... | collective-permute-start | bytes 786440 | tf_op jit(solution)/shard_map/ppermute | solution.py:17
  31.4 3.2 %collective-permute-start.1 = (bf16[2,256,256]{2,1,0:T(8,128)(2,1)}, bf16[2,256,256]{2,1,0:T(8,128)(2,1)}, u32[]{:S(2)}, u32[]{:S(2)}) collective-permute-start(bf16[2,256,256]{2,1,0:T(8,128)(2,1)} %bitcast.2), channel_id=1, source_target_pairs={{0,12},{4,16},{8,20},{12,24},{16,28},{20,32},{24,36},{28,40},{32,4... | collective-permute-start | bytes 786440 | tf_op jit(solution)/shard_map/ppermute | solution.py:17
  39.7 5.3 %collective-permute-start.3 = (bf16[2,256,256]{2,1,0:T(8,128)(2,1)}, bf16[2,256,256]{2,1,0:T(8,128)(2,1)S(1)}, u32[]{:S(2)}, u32[]{:S(2)}) collective-permute-start(bf16[2,256,256]{2,1,0:T(8,128)(2,1)} %bitcast.2), channel_id=1, source_target_pairs={{0,4},{4,8},{8,12},{12,16},{16,20},{20,24},{24,28},{28,32},{32,36}... | collective-permute-start | bytes 786440 | tf_op jit(solution)/shard_map/ppermute | solution.py:17
  46.0 10.2 %collective-permute-done.1 = bf16[2,256,256]{2,1,0:T(8,128)(2,1)} collective-permute-done((bf16[2,256,256]{2,1,0:T(8,128)(2,1)}, bf16[2,256,256]{2,1,0:T(8,128)(2,1)}, u32[]{:S(2)}, u32[]{:S(2)}) %collective-permute-start.1) | collective-permute-done | bytes 262176 | tf_op jit(solution)/shard_map/ppermute | solution.py:17
  58.2 2.3 %collective-permute-done.3 = bf16[2,256,256]{2,1,0:T(8,128)(2,1)S(1)} collective-permute-done((bf16[2,256,256]{2,1,0:T(8,128)(2,1)}, bf16[2,256,256]{2,1,0:T(8,128)(2,1)S(1)}, u32[]{:S(2)}, u32[]{:S(2)}) %collective-permute-start.3) | collective-permute-done | bytes 262176 | tf_op jit(solution)/shard_map/ppermute | solution.py:17
  61.4 5.3 %exponential_reduce_fusion.3 = (f32[4,256]{1,0:T(4,128)S(1)}, f32[4,256,1280]{1,2,0:T(8,128)}) fusion(pred[256,1280]{0,1:T(8,128)(4,1)} %fusion.28, bf16[256,16,128]{0,2,1:T(8,128)(2,1)S(1)} %bitcast.227, bf16[2,1280,256]{2,1,0:T(8,128)(2,1)S(1)} %constant_dynamic-update-slice_fusion), kind=kOutput, calls=%fused_computation.31 | convolution fusion | flops 340788480 | bytes 6164480 | tf_op jit(solution)/shard_map/sub | solution.py:27
  66.7 5.1 %exponential_reduce_fusion.1 = (f32[4,256]{1,0:T(4,128)S(1)}, f32[4,256,1280]{1,2,0:T(8,128)}) fusion(pred[256,1280]{0,1:T(8,128)(4,1)} %fusion.28, bf16[256,16,128]{0,2,1:T(8,128)(2,1)S(1)} %bitcast.228, bf16[2,1280,256]{2,1,0:T(8,128)(2,1)S(1)} %constant_dynamic-update-slice_fusion), kind=kOutput, calls=%fused_computation.27 | convolution fusion | flops 340788480 | bytes 6164480 | tf_op jit(solution)/shard_map/sub | solution.py:27
  71.8 5.1 %exponential_reduce_fusion.2 = (f32[4,256]{1,0:T(4,128)S(1)}, f32[4,256,1280]{1,2,0:T(8,128)}) fusion(pred[256,1280]{0,1:T(8,128)(4,1)} %fusion.28, bf16[256,16,128]{0,2,1:T(8,128)(2,1)S(1)} %bitcast.229, bf16[2,1280,256]{2,1,0:T(8,128)(2,1)S(1)} %constant_dynamic-update-slice_fusion), kind=kOutput, calls=%fused_computation.29 | convolution fusion | flops 340788480 | bytes 6164480 | tf_op jit(solution)/shard_map/sub | solution.py:27
  77.0 5.1 %exponential_reduce_fusion = (f32[4,256]{1,0:T(4,128)S(1)}, f32[4,256,1280]{1,2,0:T(8,128)}) fusion(pred[256,1280]{0,1:T(8,128)(4,1)} %fusion.28, bf16[256,16,128]{0,2,1:T(8,128)(2,1)S(1)} %bitcast.230, bf16[2,1280,256]{2,1,0:T(8,128)(2,1)S(1)} %constant_dynamic-update-slice_fusion), kind=kOutput, calls=%fused_computation.25 | convolution fusion | flops 340788480 | bytes 6164480 | tf_op jit(solution)/shard_map/sub | solution.py:27
  82.0 4.0 %fusion.23 = bf16[4,256,1280]{1,2,0:T(8,128)(2,1)S(1)} fusion(f32[4,256]{1,0:T(4,128)S(1)} %get-tuple-element.24, f32[4,256,1280]{1,2,0:T(8,128)} %get-tuple-element.25), kind=kLoop, calls=%fused_computation.50 | loop fusion | flops 2621440 | bytes 7868416 | tf_op jit(solution)/shard_map/convert_element_type | solution.py:29
  109.3 2.5 %fusion.9 = bf16[4,256,1280]{1,2,0:T(8,128)(2,1)S(1)} fusion(f32[4,256]{1,0:T(4,128)S(1)} %bitcast.240, f32[4,256]{1,0:T(4,128)S(1)} %get-tuple-element.18, f32[4,256,1280]{1,2,0:T(8,128)S(1)} %bitcast.220, bf16[2,1280,256]{2,1,0:T(8,128)(2,1)S(1)} %copy-done.5, bf16[256,16,128]{0,2,1:T(8,128)(2,1)} %bitcast.218), kind=kOutput, calls=%fused_computation.10 | convolution fusion | flops 340787200 | bytes 8462336 | tf_op jit(solution)/shard_map/rgd,ed->gre/dot_general | solution.py:32
  116.2 3.8 %collective-permute-start.7 = (bf16[2,256,256]{1,2,0:T(8,128)(2,1)S(1)}, bf16[2,256,256]{1,2,0:T(8,128)(2,1)S(1)}, u32[]{:S(2)}, u32[]{:S(2)}) collective-permute-start(bf16[2,256,256]{1,2,0:T(8,128)(2,1)S(1)} %get-tuple-element.11), channel_id=1, source_target_pairs={{4,0},{8,4},{12,8},{16,12},{20,16},{24,20},{28,24},{32,28},{36,32}... | collective-permute-start | bytes 786440 | tf_op jit(solution)/shard_map/ppermute | solution.py:17
  124.4 8.0 %collective-permute-done.4 = bf16[2,256,256]{1,2,0:T(8,128)(2,1)S(1)} collective-permute-done((bf16[2,256,256]{1,2,0:T(8,128)(2,1)S(1)}, bf16[2,256,256]{1,2,0:T(8,128)(2,1)S(1)}, u32[]{:S(2)}, u32[]{:S(2)}) %collective-permute-start.4) | collective-permute-done | bytes 262176 | tf_op jit(solution)/shard_map/ppermute | solution.py:17
  132.4 7.0 %collective-permute-done.7 = bf16[2,256,256]{1,2,0:T(8,128)(2,1)S(1)} collective-permute-done((bf16[2,256,256]{1,2,0:T(8,128)(2,1)S(1)}, bf16[2,256,256]{1,2,0:T(8,128)(2,1)S(1)}, u32[]{:S(2)}, u32[]{:S(2)}) %collective-permute-start.7) | collective-permute-done | bytes 262176 | tf_op jit(solution)/shard_map/ppermute | solution.py:17
  139.4 17.3 %collective-permute-done.5 = bf16[2,256,256]{1,2,0:T(8,128)(2,1)S(1)} collective-permute-done((bf16[2,256,256]{1,2,0:T(8,128)(2,1)S(1)}, bf16[2,256,256]{1,2,0:T(8,128)(2,1)S(1)}, u32[]{:S(2)}, u32[]{:S(2)}) %collective-permute-start.5) | collective-permute-done | bytes 262176 | tf_op jit(solution)/shard_map/ppermute | solution.py:17
  157.7 3.2 %fusion.42 = bf16[256,4,128]{0,2,1:T(8,128)(2,1)} fusion(bf16[4,256,1280]{1,2,0:T(8,128)(2,1)} %copy-done.2, bf16[2,1280,256]{2,1,0:T(8,128)(2,1)} %copy-done.4), kind=kOutput, calls=%fused_computation.81 | convolution fusion | flops 335806464 | bytes 3211264 | tf_op jit(solution)/shard_map/gre,ed->rgd/dot_general | solution.py:36
  160.9 2.2 fusion.43
  163.2 41.9 %all-reduce.2.cloned.1.call-done = f32[2,256,256]{1,2,0:T(8,128)} async-done(((f32[2,256,256]{1,2,0:T(8,128)}), f32[2,256,256]{1,2,0:T(8,128)}) %all-reduce.2.cloned.1.call-update) | async-done | bytes 524304 | tf_op jit(solution)/shard_map/psum | solution.py:98
  205.1 2.0 copy.191
  207.1 3.5 %all-to-all-start.1 = ((f32[2,256,256]{2,0,1:T(2,128)}), f32[2,256,256]{2,0,1:T(2,128)S(1)}, u32[]{:S(2)}, u32[]{:S(2)}) async-start(f32[2,256,256]{2,0,1:T(2,128)} %copy.191), calls=%async_computation.1 | async-start | bytes 1048576 | tf_op jit(solution)/shard_map/all_to_all | solution.py:99
  213.8 5.6 %all-to-all-done.1 = f32[2,256,256]{2,0,1:T(2,128)S(1)} async-done(((f32[2,256,256]{2,0,1:T(2,128)}), f32[2,256,256]{2,0,1:T(2,128)S(1)}, u32[]{:S(2)}, u32[]{:S(2)}) %all-to-all-start.1) | async-done | bytes 524320 | tf_op jit(solution)/shard_map/all_to_all | solution.py:99
  (106 shorter events, 51.3 us)
Async XLA Ops:
  7.2 20.7 %copy-start.12 = (bf16[1,256,2048]{2,1,0:T(8,128)(2,1)S(1)}, bf16[1,256,2048]{2,1,0:T(8,128)(2,1)}, u32[]{:S(2)}) copy-start(bf16[1,256,2048]{2,1,0:T(8,128)(2,1)} %param.4) | copy-start | bytes 3145732
  9.6 9.4 %all-to-all-start = ((bf16[4,2,16384]{2,1,0:T(2,128)(2,1)}), bf16[4,2,16384]{2,1,0:T(2,128)(2,1)S(1)}, u32[]{:S(2)}, u32[]{:S(2)}) async-start(bf16[4,2,16384]{2,1,0:T(2,128)(2,1)} %reshape.105), calls=%async_computation | async-start | bytes 524288 | tf_op jit(solution)/shard_map/all_to_all | solution.py:48
  13.0 192.0 %all-reduce.2.cloned.1.call-start = ((), (), s32[]{:S(2)}) async-start(), calls=%async_computation.2 | async-start | bytes 1048576 | tf_op jit(solution)/shard_map/psum | solution.py:98
  20.4 24.6 %collective-permute-start = (bf16[2,256,256]{2,1,0:T(8,128)(2,1)}, bf16[2,256,256]{2,1,0:T(8,128)(2,1)}, u32[]{:S(2)}, u32[]{:S(2)}) collective-permute-start(bf16[2,256,256]{2,1,0:T(8,128)(2,1)} %bitcast.2), channel_id=1, source_target_pairs={{0,16},{4,20},{8,24},{12,28},{16,32},{20,36},{24,40},{28,44},{32,4... | collective-permute-start | bytes 786440 | tf_op jit(solution)/shard_map/ppermute | solution.py:17
  28.4 79.6 %copy-start.3 = (bf16[1,256,2048]{1,2,0:T(8,128)(2,1)}, bf16[1,256,2048]{1,2,0:T(8,128)(2,1)S(1)}, u32[]{:S(2)}) copy-start(bf16[1,256,2048]{1,2,0:T(8,128)(2,1)S(1)} %copy.147) | copy-start | bytes 3145732
  28.4 28.7 %collective-permute-start.2 = (bf16[2,256,256]{2,1,0:T(8,128)(2,1)}, bf16[2,256,256]{2,1,0:T(8,128)(2,1)}, u32[]{:S(2)}, u32[]{:S(2)}) collective-permute-start(bf16[2,256,256]{2,1,0:T(8,128)(2,1)} %bitcast.2), channel_id=1, source_target_pairs={{0,8},{4,12},{8,16},{12,20},{16,24},{20,28},{24,32},{28,36},{32,40... | collective-permute-start | bytes 786440 | tf_op jit(solution)/shard_map/ppermute | solution.py:17
  31.4 24.8 %collective-permute-start.1 = (bf16[2,256,256]{2,1,0:T(8,128)(2,1)}, bf16[2,256,256]{2,1,0:T(8,128)(2,1)}, u32[]{:S(2)}, u32[]{:S(2)}) collective-permute-start(bf16[2,256,256]{2,1,0:T(8,128)(2,1)} %bitcast.2), channel_id=1, source_target_pairs={{0,12},{4,16},{8,20},{12,24},{16,28},{20,32},{24,36},{28,40},{32,4... | collective-permute-start | bytes 786440 | tf_op jit(solution)/shard_map/ppermute | solution.py:17
  36.1 59.8 %copy-start.6 = (bf16[1,256,2048]{1,2,0:T(8,128)(2,1)}, bf16[1,256,2048]{1,2,0:T(8,128)(2,1)S(1)}, u32[]{:S(2)}) copy-start(bf16[1,256,2048]{1,2,0:T(8,128)(2,1)S(1)} %copy.145) | copy-start | bytes 3145732
  39.7 20.7 %collective-permute-start.3 = (bf16[2,256,256]{2,1,0:T(8,128)(2,1)}, bf16[2,256,256]{2,1,0:T(8,128)(2,1)S(1)}, u32[]{:S(2)}, u32[]{:S(2)}) collective-permute-start(bf16[2,256,256]{2,1,0:T(8,128)(2,1)} %bitcast.2), channel_id=1, source_target_pairs={{0,4},{4,8},{8,12},{12,16},{16,20},{20,24},{24,28},{28,32},{32,36}... | collective-permute-start | bytes 786440 | tf_op jit(solution)/shard_map/ppermute | solution.py:17
  61.4 45.3 %copy-start.4 = (bf16[2,1280,256]{2,1,0:T(8,128)(2,1)}, bf16[2,1280,256]{2,1,0:T(8,128)(2,1)S(1)}, u32[]{:S(2)}) copy-start(bf16[2,1280,256]{2,1,0:T(8,128)(2,1)S(1)} %constant_dynamic-update-slice_fusion) | copy-start | bytes 3932164
  82.0 6.3 %slice-start.6 = ((s8[5242880]{0:T(1024)(128)(4,1)}), s8[4194304]{0:T(1024)(128)(4,1)S(1)}, s32[]{:S(2)}) async-start(s8[5242880]{0:T(1024)(128)(4,1)} %bitcast.225), calls=%async_computation.9 | async-start | bytes 8388608
  88.3 2.5 %slice-start.5 = ((s8[5242880]{0:T(1024)(128)(4,1)}), s8[1048576]{0:T(1024)(128)(4,1)S(1)}, s32[]{:S(2)}) async-start(s8[5242880]{0:T(1024)(128)(4,1)} %bitcast.223), calls=%async_computation.8 | async-start | bytes 2097152
  94.7 2.7 %slice-start.2 = ((s8[5242880]{0:T(1024)(128)(4,1)}), s8[4194304]{0:T(1024)(128)(4,1)S(1)}, s32[]{:S(2)}) async-start(s8[5242880]{0:T(1024)(128)(4,1)} %bitcast.221), calls=%async_computation.5 | async-start | bytes 8388608
  94.7 3.4 %slice-start.3 = ((s8[5242880]{0:T(1024)(128)(4,1)}), s8[1048576]{0:T(1024)(128)(4,1)S(1)}, s32[]{:S(2)}) async-start(s8[5242880]{0:T(1024)(128)(4,1)} %bitcast.221), calls=%async_computation.6 | async-start | bytes 2097152
  101.9 2.4 %slice-start = ((s8[5242880]{0:T(1024)(128)(4,1)}), s8[4194304]{0:T(1024)(128)(4,1)S(1)}, s32[]{:S(2)}) async-start(s8[5242880]{0:T(1024)(128)(4,1)} %bitcast.219), calls=%async_computation.3 | async-start | bytes 8388608
  101.9 3.4 %slice-start.1 = ((s8[5242880]{0:T(1024)(128)(4,1)}), s8[1048576]{0:T(1024)(128)(4,1)S(1)}, s32[]{:S(2)}) async-start(s8[5242880]{0:T(1024)(128)(4,1)} %bitcast.219), calls=%async_computation.4 | async-start | bytes 2097152
  103.0 8.8 %copy-start = (bf16[4,256,1280]{1,2,0:T(8,128)(2,1)}, bf16[4,256,1280]{1,2,0:T(8,128)(2,1)S(1)}, u32[]{:S(2)}) copy-start(bf16[4,256,1280]{1,2,0:T(8,128)(2,1)S(1)} %fusion.13) | copy-start | bytes 7864324
  109.3 2.5 %copy-start.7 = (bf16[1,256,2048]{1,2,0:T(8,128)(2,1)S(1)}, bf16[1,256,2048]{1,2,0:T(8,128)(2,1)}, u32[]{:S(2)}) copy-start(bf16[1,256,2048]{1,2,0:T(8,128)(2,1)} %copy-done.6) | copy-start | bytes 3145732
  114.3 18.1 %collective-permute-start.4 = (bf16[2,256,256]{1,2,0:T(8,128)(2,1)S(1)}, bf16[2,256,256]{1,2,0:T(8,128)(2,1)S(1)}, u32[]{:S(2)}, u32[]{:S(2)}) collective-permute-start(bf16[2,256,256]{1,2,0:T(8,128)(2,1)S(1)} %get-tuple-element.10), channel_id=1, source_target_pairs={{16,0},{20,4},{24,8},{28,12},{32,16},{36,20},{40,24},{44,28},{48,3... | collective-permute-start | bytes 786440 | tf_op jit(solution)/shard_map/ppermute | solution.py:17
  116.2 23.2 %collective-permute-start.7 = (bf16[2,256,256]{1,2,0:T(8,128)(2,1)S(1)}, bf16[2,256,256]{1,2,0:T(8,128)(2,1)S(1)}, u32[]{:S(2)}, u32[]{:S(2)}) collective-permute-start(bf16[2,256,256]{1,2,0:T(8,128)(2,1)S(1)} %get-tuple-element.11), channel_id=1, source_target_pairs={{4,0},{8,4},{12,8},{16,12},{20,16},{24,20},{28,24},{32,28},{36,32}... | collective-permute-start | bytes 786440 | tf_op jit(solution)/shard_map/ppermute | solution.py:17
  120.0 19.4 %collective-permute-start.6 = (bf16[2,256,256]{1,2,0:T(8,128)(2,1)S(1)}, bf16[2,256,256]{1,2,0:T(8,128)(2,1)S(1)}, u32[]{:S(2)}, u32[]{:S(2)}) collective-permute-start(bf16[2,256,256]{1,2,0:T(8,128)(2,1)S(1)} %get-tuple-element.12), channel_id=1, source_target_pairs={{8,0},{12,4},{16,8},{20,12},{24,16},{28,20},{32,24},{36,28},{40,32... | collective-permute-start | bytes 786440 | tf_op jit(solution)/shard_map/ppermute | solution.py:17
  121.9 34.8 %collective-permute-start.5 = (bf16[2,256,256]{1,2,0:T(8,128)(2,1)S(1)}, bf16[2,256,256]{1,2,0:T(8,128)(2,1)S(1)}, u32[]{:S(2)}, u32[]{:S(2)}) collective-permute-start(bf16[2,256,256]{1,2,0:T(8,128)(2,1)S(1)} %get-tuple-element.13), channel_id=1, source_target_pairs={{12,0},{16,4},{20,8},{24,12},{28,16},{32,20},{36,24},{40,28},{44,3... | collective-permute-start | bytes 786440 | tf_op jit(solution)/shard_map/ppermute | solution.py:17
  157.7 3.2 %copy-start.1 = (bf16[4,256,1280]{1,2,0:T(8,128)(2,1)S(1)}, bf16[4,256,1280]{1,2,0:T(8,128)(2,1)}, u32[]{:S(2)}) copy-start(bf16[4,256,1280]{1,2,0:T(8,128)(2,1)} %copy-done) | copy-start | bytes 7864324
  207.1 12.3 %all-to-all-start.1 = ((f32[2,256,256]{2,0,1:T(2,128)}), f32[2,256,256]{2,0,1:T(2,128)S(1)}, u32[]{:S(2)}, u32[]{:S(2)}) async-start(f32[2,256,256]{2,0,1:T(2,128)} %copy.191), calls=%async_computation.1 | async-start | bytes 1048576 | tf_op jit(solution)/shard_map/all_to_all | solution.py:99
  (10 other events, 15.4 us)
Sparse Core Ops, SparseCore 0:
  157.8 47.2 all-reduce.1
where the time goes:
time: 229 us; the launch traced here: 227 us
  waiting for transfers between devices  98.2 us (43%)
  matrix products  47 us (21%)
  starting transfers between devices  34.2 us (15%)
  local copies, waits for them, and re-layouts  22.1 us (10%)
  between operations  14.6 us (6%)
  other arithmetic  11 us (5%)
    ppermute x8, waiting for transfers between devices, shifted(): return lax.ppermute(value, axis, pairs)  44.8 us
    psum x1, waiting for transfers between devices, body(): summed = lax.psum(own_rows, 'section')  41.9 us
    ppermute x8, starting transfers between devices, shifted(): return lax.ppermute(value, axis, pairs)  27.3 us
    sub x4, matrix products, head_grads(): weights = jnp.exp(masked - highest)  20.6 us
    unnamed x61, local copies, waits for them, and re-layouts  17.1 us
    convert_element_type x4, other arithmetic, head_grads(): probs_b = probs.astype(jnp.bfloat16)  8.43 us
    dot_general x4, matrix products, head_grads(): jnp.einsum('gre,ed->rgd', dscores_b, keys_head, preferred_element_type=jn...  7.58 us
    all_to_all x1, waiting for transfers between devices, body(): lax.all_to_all(shared_kv, 'tp', split_axis=2, concat_axis=1, tiled=True)  5.89 us
  transfers between devices with their start and end apart: 11, of which 8 were waited for; matrix products, arithmetic and copies ran while one was open for 8% of the time, Pallas kernels for 0%

commit v1 on v0

--- a/solution.py
+++ b/solution.py
@@ -95,8 +95,15 @@
             "seq",
             offset - span_blocks,
         ).astype(jnp.float32)
-    summed = lax.psum(own_rows, "section")
-    d_shared_kv = lax.all_to_all(summed, "tp", split_axis=1, concat_axis=2, tiled=True)
+    by_token = lax.all_to_all(own_rows, "tp", split_axis=1, concat_axis=2, tiled=True)
+    sections = lax.axis_size("section")
+    kinds, rows, cols = by_token.shape
+    pieces = by_token.reshape(kinds, sections, rows // sections, cols)
+    pieces = lax.all_to_all(pieces, "section", split_axis=1, concat_axis=1)
+    chunk = pieces[:, 0]
+    for other in range(1, sections):
+        chunk = chunk + pieces[:, other]
+    d_shared_kv = lax.all_gather(chunk, "section", axis=1, tiled=True)
     return (d_queries, d_shared_kv)
 
 

time: 229 us -> 195 us (0.85)
  waiting for transfers between devices: 98.2 us -> 60.1 us
  between operations: 14.6 us -> 1.24 us
  blocking collectives: 0 us -> 12.8 us
  starting transfers between devices: 34.2 us -> 38.4 us
    psum x1 -> x0, waiting for transfers between devices: 41.9 us -> none  [body(): summed = lax.psum(own_rows, 'section')]
    all_gather x0 -> x1, blocking collectives: none -> 12.8 us  [body(): d_shared_kv = lax.all_gather(chunk, 'section', axis=1, tiled=True)]
    all_to_all x1 -> x2, starting transfers between devices: 3.47 us -> 7.77 us  [the longest x1 4.3 us: body(): pieces = lax.all_to_all(pieces, 'section', split_axis=1, concat_axis=1)]
    all_to_all x1 -> x2, waiting for transfers between devices: 5.59 us -> 9.32 us  [the longest x1 6.01 us: body(): pieces = lax.all_to_all(pieces, 'section', split_axis=1, concat_axis=1)]
    reshape x0 -> x2, local copies, waits for them, and re-layouts: none -> 2.95 us  [body(): pieces = by_token.reshape(kinds, sections, rows // sections, cols)]
    unnamed x61 -> x62, local copies, waits for them, and re-layouts: 17.1 us -> 17.8 us
  transfers between devices with their start and end apart: 11 -> 11, of which waited for: 8 -> 8; matrix products, arithmetic and copies ran while one was open for 8% -> 10% of each run, Pallas kernels for 0% -> 0%
where the time goes in v1:
time: 195 us; the launch traced here: 194 us
  waiting for transfers between devices  60.1 us (31%)
  matrix products  46.9 us (24%)
  starting transfers between devices  38.4 us (20%)
  local copies, waits for them, and re-layouts  24.2 us (12%)
  blocking collectives  12.8 us (7%)
  other arithmetic  10.2 us (5%)
    ppermute x8, waiting for transfers between devices, shifted(): return lax.ppermute(value, axis, pairs)  44.8 us
    ppermute x8, starting transfers between devices, shifted(): return lax.ppermute(value, axis, pairs)  27.3 us
    sub x4, matrix products, head_grads(): weights = jnp.exp(masked - highest)  20.6 us
    unnamed x62, local copies, waits for them, and re-layouts  17.8 us
    all_gather x1, blocking collectives, body(): d_shared_kv = lax.all_gather(chunk, 'section', axis=1, tiled=True)  12.8 us
    convert_element_type x4, other arithmetic, head_grads(): probs_b = probs.astype(jnp.bfloat16)  8.43 us
    dot_general x4, matrix products, head_grads(): jnp.einsum('gre,ed->rgd', dscores_b, keys_head, preferred_element_type=jn...  7.58 us
    all_to_all x1, waiting for transfers between devices, body(): pieces = lax.all_to_all(pieces, 'section', split_axis=1, concat_axis=1)  6.01 us
  transfers between devices with their start and end apart: 11, of which 8 were waited for; matrix products, arithmetic and copies ran while one was open for 10% of the time, Pallas kernels for 0%

profile of v1, /device:TPU:80, one launch (start us, length us, event | category | flops | bytes accessed | tf_op | source)
XLA Modules:
  0.0 194.0 jit_solution(16692141543035240085)
XLA Ops:
  3.1 3.4 %all-to-all-start = ((bf16[4,2,16384]{2,1,0:T(2,128)(2,1)}), bf16[4,2,16384]{2,1,0:T(2,128)(2,1)S(1)}, u32[]{:S(2)}, u32[]{:S(2)}) async-start(bf16[4,2,16384]{2,1,0:T(2,128)(2,1)} %reshape.114), calls=%async_computation | async-start | bytes 524288 | tf_op jit(solution)/shard_map/all_to_all | solution.py:48
  6.5 5.9 %all-to-all-done = bf16[4,2,16384]{2,1,0:T(2,128)(2,1)S(1)} async-done(((bf16[4,2,16384]{2,1,0:T(2,128)(2,1)}), bf16[4,2,16384]{2,1,0:T(2,128)(2,1)S(1)}, u32[]{:S(2)}, u32[]{:S(2)}) %all-to-all-start) | async-done | bytes 262176 | tf_op jit(solution)/shard_map/all_to_all | solution.py:48
  13.8 6.4 %collective-permute-start = (bf16[2,256,256]{2,1,0:T(8,128)(2,1)}, bf16[2,256,256]{2,1,0:T(8,128)(2,1)}, u32[]{:S(2)}, u32[]{:S(2)}) collective-permute-start(bf16[2,256,256]{2,1,0:T(8,128)(2,1)} %bitcast.2), channel_id=1, source_target_pairs={{0,16},{4,20},{8,24},{12,28},{16,32},{20,36},{24,40},{28,44},{32,4... | collective-permute-start | bytes 786440 | tf_op jit(solution)/shard_map/ppermute | solution.py:17
  21.9 2.9 %collective-permute-start.2 = (bf16[2,256,256]{2,1,0:T(8,128)(2,1)}, bf16[2,256,256]{2,1,0:T(8,128)(2,1)}, u32[]{:S(2)}, u32[]{:S(2)}) collective-permute-start(bf16[2,256,256]{2,1,0:T(8,128)(2,1)} %bitcast.2), channel_id=1, source_target_pairs={{0,8},{4,12},{8,16},{12,20},{16,24},{20,28},{24,32},{28,36},{32,40... | collective-permute-start | bytes 786440 | tf_op jit(solution)/shard_map/ppermute | solution.py:17
  24.8 3.2 %collective-permute-start.1 = (bf16[2,256,256]{2,1,0:T(8,128)(2,1)}, bf16[2,256,256]{2,1,0:T(8,128)(2,1)}, u32[]{:S(2)}, u32[]{:S(2)}) collective-permute-start(bf16[2,256,256]{2,1,0:T(8,128)(2,1)} %bitcast.2), channel_id=1, source_target_pairs={{0,12},{4,16},{8,20},{12,24},{16,28},{20,32},{24,36},{28,40},{32,4... | collective-permute-start | bytes 786440 | tf_op jit(solution)/shard_map/ppermute | solution.py:17
  33.1 5.3 %collective-permute-start.3 = (bf16[2,256,256]{2,1,0:T(8,128)(2,1)}, bf16[2,256,256]{2,1,0:T(8,128)(2,1)S(1)}, u32[]{:S(2)}, u32[]{:S(2)}) collective-permute-start(bf16[2,256,256]{2,1,0:T(8,128)(2,1)} %bitcast.2), channel_id=1, source_target_pairs={{0,4},{4,8},{8,12},{12,16},{16,20},{20,24},{24,28},{28,32},{32,36}... | collective-permute-start | bytes 786440 | tf_op jit(solution)/shard_map/ppermute | solution.py:17
  39.4 10.3 %collective-permute-done.1 = bf16[2,256,256]{2,1,0:T(8,128)(2,1)} collective-permute-done((bf16[2,256,256]{2,1,0:T(8,128)(2,1)}, bf16[2,256,256]{2,1,0:T(8,128)(2,1)}, u32[]{:S(2)}, u32[]{:S(2)}) %collective-permute-start.1) | collective-permute-done | bytes 262176 | tf_op jit(solution)/shard_map/ppermute | solution.py:17
  51.6 2.3 %collective-permute-done.3 = bf16[2,256,256]{2,1,0:T(8,128)(2,1)S(1)} collective-permute-done((bf16[2,256,256]{2,1,0:T(8,128)(2,1)}, bf16[2,256,256]{2,1,0:T(8,128)(2,1)S(1)}, u32[]{:S(2)}, u32[]{:S(2)}) %collective-permute-start.3) | collective-permute-done | bytes 262176 | tf_op jit(solution)/shard_map/ppermute | solution.py:17
  54.9 5.3 %exponential_reduce_fusion.3 = (f32[4,256]{1,0:T(4,128)S(1)}, f32[4,256,1280]{1,2,0:T(8,128)}) fusion(pred[256,1280]{0,1:T(8,128)(4,1)} %fusion.28, bf16[256,16,128]{0,2,1:T(8,128)(2,1)S(1)} %bitcast.226, bf16[2,1280,256]{2,1,0:T(8,128)(2,1)S(1)} %constant_dynamic-update-slice_fusion), kind=kOutput, calls=%fused_computation.31 | convolution fusion | flops 340788480 | bytes 6164480 | tf_op jit(solution)/shard_map/sub | solution.py:27
  60.2 5.1 %exponential_reduce_fusion.1 = (f32[4,256]{1,0:T(4,128)S(1)}, f32[4,256,1280]{1,2,0:T(8,128)}) fusion(pred[256,1280]{0,1:T(8,128)(4,1)} %fusion.28, bf16[256,16,128]{0,2,1:T(8,128)(2,1)S(1)} %bitcast.227, bf16[2,1280,256]{2,1,0:T(8,128)(2,1)S(1)} %constant_dynamic-update-slice_fusion), kind=kOutput, calls=%fused_computation.27 | convolution fusion | flops 340788480 | bytes 6164480 | tf_op jit(solution)/shard_map/sub | solution.py:27
  65.3 5.1 %exponential_reduce_fusion.2 = (f32[4,256]{1,0:T(4,128)S(1)}, f32[4,256,1280]{1,2,0:T(8,128)}) fusion(pred[256,1280]{0,1:T(8,128)(4,1)} %fusion.28, bf16[256,16,128]{0,2,1:T(8,128)(2,1)S(1)} %bitcast.228, bf16[2,1280,256]{2,1,0:T(8,128)(2,1)S(1)} %constant_dynamic-update-slice_fusion), kind=kOutput, calls=%fused_computation.29 | convolution fusion | flops 340788480 | bytes 6164480 | tf_op jit(solution)/shard_map/sub | solution.py:27
  70.4 5.1 %exponential_reduce_fusion = (f32[4,256]{1,0:T(4,128)S(1)}, f32[4,256,1280]{1,2,0:T(8,128)}) fusion(pred[256,1280]{0,1:T(8,128)(4,1)} %fusion.28, bf16[256,16,128]{0,2,1:T(8,128)(2,1)S(1)} %bitcast.229, bf16[2,1280,256]{2,1,0:T(8,128)(2,1)S(1)} %constant_dynamic-update-slice_fusion), kind=kOutput, calls=%fused_computation.25 | convolution fusion | flops 340788480 | bytes 6164480 | tf_op jit(solution)/shard_map/sub | solution.py:27
  75.5 4.0 %fusion.23 = bf16[4,256,1280]{1,2,0:T(8,128)(2,1)S(1)} fusion(f32[4,256]{1,0:T(4,128)S(1)} %get-tuple-element.22, f32[4,256,1280]{1,2,0:T(8,128)} %get-tuple-element.23), kind=kLoop, calls=%fused_computation.50 | loop fusion | flops 2621440 | bytes 7868416 | tf_op jit(solution)/shard_map/convert_element_type | solution.py:29
  102.8 2.5 %fusion.9 = bf16[4,256,1280]{1,2,0:T(8,128)(2,1)S(1)} fusion(f32[4,256]{1,0:T(4,128)S(1)} %bitcast.239, f32[4,256]{1,0:T(4,128)S(1)} %get-tuple-element.16, f32[4,256,1280]{1,2,0:T(8,128)S(1)} %bitcast.219, bf16[2,1280,256]{2,1,0:T(8,128)(2,1)S(1)} %copy-done.5, bf16[256,16,128]{0,2,1:T(8,128)(2,1)} %bitcast.217), kind=kOutput, calls=%fused_computation.10 | convolution fusion | flops 340787200 | bytes 8462336 | tf_op jit(solution)/shard_map/rgd,ed->gre/dot_general | solution.py:32
  109.6 3.8 %collective-permute-start.7 = (bf16[2,256,256]{1,2,0:T(8,128)(2,1)S(1)}, bf16[2,256,256]{1,2,0:T(8,128)(2,1)S(1)}, u32[]{:S(2)}, u32[]{:S(2)}) collective-permute-start(bf16[2,256,256]{1,2,0:T(8,128)(2,1)S(1)} %get-tuple-element.9), channel_id=1, source_target_pairs={{4,0},{8,4},{12,8},{16,12},{20,16},{24,20},{28,24},{32,28},{36,32}... | collective-permute-start | bytes 786440 | tf_op jit(solution)/shard_map/ppermute | solution.py:17
  117.8 8.0 %collective-permute-done.4 = bf16[2,256,256]{1,2,0:T(8,128)(2,1)S(1)} collective-permute-done((bf16[2,256,256]{1,2,0:T(8,128)(2,1)S(1)}, bf16[2,256,256]{1,2,0:T(8,128)(2,1)S(1)}, u32[]{:S(2)}, u32[]{:S(2)}) %collective-permute-start.4) | collective-permute-done | bytes 262176 | tf_op jit(solution)/shard_map/ppermute | solution.py:17
  125.8 7.0 %collective-permute-done.7 = bf16[2,256,256]{1,2,0:T(8,128)(2,1)S(1)} collective-permute-done((bf16[2,256,256]{1,2,0:T(8,128)(2,1)S(1)}, bf16[2,256,256]{1,2,0:T(8,128)(2,1)S(1)}, u32[]{:S(2)}, u32[]{:S(2)}) %collective-permute-start.7) | collective-permute-done | bytes 262176 | tf_op jit(solution)/shard_map/ppermute | solution.py:17
  132.8 17.3 %collective-permute-done.5 = bf16[2,256,256]{1,2,0:T(8,128)(2,1)S(1)} collective-permute-done((bf16[2,256,256]{1,2,0:T(8,128)(2,1)S(1)}, bf16[2,256,256]{1,2,0:T(8,128)(2,1)S(1)}, u32[]{:S(2)}, u32[]{:S(2)}) %collective-permute-start.5) | collective-permute-done | bytes 262176 | tf_op jit(solution)/shard_map/ppermute | solution.py:17
  151.3 3.5 %all-to-all-start.1 = ((f32[2,256,256]{2,0,1:T(2,128)}), f32[2,256,256]{2,0,1:T(2,128)S(1)}, u32[]{:S(2)}, u32[]{:S(2)}) async-start(f32[2,256,256]{2,0,1:T(2,128)} %copy.141), calls=%async_computation.1 | async-start | bytes 1048576 | tf_op jit(solution)/shard_map/all_to_all | solution.py:98
  154.8 3.2 %fusion.42 = bf16[256,4,128]{0,2,1:T(8,128)(2,1)} fusion(bf16[4,256,1280]{1,2,0:T(8,128)(2,1)} %copy-done.2, bf16[2,1280,256]{2,1,0:T(8,128)(2,1)} %copy-done.4), kind=kOutput, calls=%fused_computation.81 | convolution fusion | flops 335806464 | bytes 3211264 | tf_op jit(solution)/shard_map/gre,ed->rgd/dot_general | solution.py:36
  160.2 3.3 %all-to-all-done.1 = f32[2,256,256]{2,0,1:T(2,128)S(1)} async-done(((f32[2,256,256]{2,0,1:T(2,128)}), f32[2,256,256]{2,0,1:T(2,128)S(1)}, u32[]{:S(2)}, u32[]{:S(2)}) %all-to-all-start.1) | async-done | bytes 524320 | tf_op jit(solution)/shard_map/all_to_all | solution.py:98
  166.9 4.3 %all-to-all-start.2 = ((f32[2,4,16,1024]{3,2,0,1:T(8,128)}), f32[2,4,16,1024]{3,2,0,1:T(8,128)S(1)}, u32[]{:S(2)}, u32[]{:S(2)}) async-start(f32[2,4,16,1024]{3,2,0,1:T(8,128)} %copy.144), calls=%async_computation.2 | async-start | bytes 1048576 | tf_op jit(solution)/shard_map/all_to_all | solution.py:102
  174.3 6.0 %all-to-all-done.2 = f32[2,4,16,1024]{3,2,0,1:T(8,128)S(1)} async-done(((f32[2,4,16,1024]{3,2,0,1:T(8,128)}), f32[2,4,16,1024]{3,2,0,1:T(8,128)S(1)}, u32[]{:S(2)}, u32[]{:S(2)}) %all-to-all-start.2) | async-done | bytes 524320 | tf_op jit(solution)/shard_map/all_to_all | solution.py:102
  180.4 12.8 %all-gather = f32[2,1,64,1024]{3,2,0,1:T(8,128)S(1)} all-gather(f32[2,1,16,1024]{3,2,0,1:T(8,128)S(1)} %slice_add_fusion), channel_id=2, replica_groups=mesh['section'=4,'seq'=16,'tp'=4] {'section'}, dimensions={2}, use_global_device_ids=true | all-gather | bytes 655360 | tf_op jit(solution)/shard_map/all_gather | solution.py:106
  (110 shorter events, 56.9 us)
Async XLA Ops:
  0.6 20.7 %copy-start.12 = (bf16[1,256,2048]{2,1,0:T(8,128)(2,1)S(1)}, bf16[1,256,2048]{2,1,0:T(8,128)(2,1)}, u32[]{:S(2)}) copy-start(bf16[1,256,2048]{2,1,0:T(8,128)(2,1)} %param.4) | copy-start | bytes 3145732
  3.1 9.4 %all-to-all-start = ((bf16[4,2,16384]{2,1,0:T(2,128)(2,1)}), bf16[4,2,16384]{2,1,0:T(2,128)(2,1)S(1)}, u32[]{:S(2)}, u32[]{:S(2)}) async-start(bf16[4,2,16384]{2,1,0:T(2,128)(2,1)} %reshape.114), calls=%async_computation | async-start | bytes 524288 | tf_op jit(solution)/shard_map/all_to_all | solution.py:48
  13.8 24.6 %collective-permute-start = (bf16[2,256,256]{2,1,0:T(8,128)(2,1)}, bf16[2,256,256]{2,1,0:T(8,128)(2,1)}, u32[]{:S(2)}, u32[]{:S(2)}) collective-permute-start(bf16[2,256,256]{2,1,0:T(8,128)(2,1)} %bitcast.2), channel_id=1, source_target_pairs={{0,16},{4,20},{8,24},{12,28},{16,32},{20,36},{24,40},{28,44},{32,4... | collective-permute-start | bytes 786440 | tf_op jit(solution)/shard_map/ppermute | solution.py:17
  21.9 79.6 %copy-start.3 = (bf16[1,256,2048]{1,2,0:T(8,128)(2,1)}, bf16[1,256,2048]{1,2,0:T(8,128)(2,1)S(1)}, u32[]{:S(2)}) copy-start(bf16[1,256,2048]{1,2,0:T(8,128)(2,1)S(1)} %copy.97) | copy-start | bytes 3145732
  21.9 28.7 %collective-permute-start.2 = (bf16[2,256,256]{2,1,0:T(8,128)(2,1)}, bf16[2,256,256]{2,1,0:T(8,128)(2,1)}, u32[]{:S(2)}, u32[]{:S(2)}) collective-permute-start(bf16[2,256,256]{2,1,0:T(8,128)(2,1)} %bitcast.2), channel_id=1, source_target_pairs={{0,8},{4,12},{8,16},{12,20},{16,24},{20,28},{24,32},{28,36},{32,40... | collective-permute-start | bytes 786440 | tf_op jit(solution)/shard_map/ppermute | solution.py:17
  24.8 24.8 %collective-permute-start.1 = (bf16[2,256,256]{2,1,0:T(8,128)(2,1)}, bf16[2,256,256]{2,1,0:T(8,128)(2,1)}, u32[]{:S(2)}, u32[]{:S(2)}) collective-permute-start(bf16[2,256,256]{2,1,0:T(8,128)(2,1)} %bitcast.2), channel_id=1, source_target_pairs={{0,12},{4,16},{8,20},{12,24},{16,28},{20,32},{24,36},{28,40},{32,4... | collective-permute-start | bytes 786440 | tf_op jit(solution)/shard_map/ppermute | solution.py:17
  29.6 59.7 %copy-start.6 = (bf16[1,256,2048]{1,2,0:T(8,128)(2,1)}, bf16[1,256,2048]{1,2,0:T(8,128)(2,1)S(1)}, u32[]{:S(2)}) copy-start(bf16[1,256,2048]{1,2,0:T(8,128)(2,1)S(1)} %copy.95) | copy-start | bytes 3145732
  33.1 20.8 %collective-permute-start.3 = (bf16[2,256,256]{2,1,0:T(8,128)(2,1)}, bf16[2,256,256]{2,1,0:T(8,128)(2,1)S(1)}, u32[]{:S(2)}, u32[]{:S(2)}) collective-permute-start(bf16[2,256,256]{2,1,0:T(8,128)(2,1)} %bitcast.2), channel_id=1, source_target_pairs={{0,4},{4,8},{8,12},{12,16},{16,20},{20,24},{24,28},{28,32},{32,36}... | collective-permute-start | bytes 786440 | tf_op jit(solution)/shard_map/ppermute | solution.py:17
  54.9 45.3 %copy-start.4 = (bf16[2,1280,256]{2,1,0:T(8,128)(2,1)}, bf16[2,1280,256]{2,1,0:T(8,128)(2,1)S(1)}, u32[]{:S(2)}) copy-start(bf16[2,1280,256]{2,1,0:T(8,128)(2,1)S(1)} %constant_dynamic-update-slice_fusion) | copy-start | bytes 3932164
  75.5 6.3 %slice-start.6 = ((s8[5242880]{0:T(1024)(128)(4,1)}), s8[4194304]{0:T(1024)(128)(4,1)S(1)}, s32[]{:S(2)}) async-start(s8[5242880]{0:T(1024)(128)(4,1)} %bitcast.224), calls=%async_computation.9 | async-start | bytes 8388608
  81.8 2.5 %slice-start.5 = ((s8[5242880]{0:T(1024)(128)(4,1)}), s8[1048576]{0:T(1024)(128)(4,1)S(1)}, s32[]{:S(2)}) async-start(s8[5242880]{0:T(1024)(128)(4,1)} %bitcast.222), calls=%async_computation.8 | async-start | bytes 2097152
  88.1 2.7 %slice-start.2 = ((s8[5242880]{0:T(1024)(128)(4,1)}), s8[4194304]{0:T(1024)(128)(4,1)S(1)}, s32[]{:S(2)}) async-start(s8[5242880]{0:T(1024)(128)(4,1)} %bitcast.220), calls=%async_computation.5 | async-start | bytes 8388608
  88.1 3.4 %slice-start.3 = ((s8[5242880]{0:T(1024)(128)(4,1)}), s8[1048576]{0:T(1024)(128)(4,1)S(1)}, s32[]{:S(2)}) async-start(s8[5242880]{0:T(1024)(128)(4,1)} %bitcast.220), calls=%async_computation.6 | async-start | bytes 2097152
  95.3 2.4 %slice-start = ((s8[5242880]{0:T(1024)(128)(4,1)}), s8[4194304]{0:T(1024)(128)(4,1)S(1)}, s32[]{:S(2)}) async-start(s8[5242880]{0:T(1024)(128)(4,1)} %bitcast.218), calls=%async_computation.3 | async-start | bytes 8388608
  95.3 3.4 %slice-start.1 = ((s8[5242880]{0:T(1024)(128)(4,1)}), s8[1048576]{0:T(1024)(128)(4,1)S(1)}, s32[]{:S(2)}) async-start(s8[5242880]{0:T(1024)(128)(4,1)} %bitcast.218), calls=%async_computation.4 | async-start | bytes 2097152
  96.4 8.8 %copy-start = (bf16[4,256,1280]{1,2,0:T(8,128)(2,1)}, bf16[4,256,1280]{1,2,0:T(8,128)(2,1)S(1)}, u32[]{:S(2)}) copy-start(bf16[4,256,1280]{1,2,0:T(8,128)(2,1)S(1)} %fusion.13) | copy-start | bytes 7864324
  102.8 2.5 %copy-start.7 = (bf16[1,256,2048]{1,2,0:T(8,128)(2,1)S(1)}, bf16[1,256,2048]{1,2,0:T(8,128)(2,1)}, u32[]{:S(2)}) copy-start(bf16[1,256,2048]{1,2,0:T(8,128)(2,1)} %copy-done.6) | copy-start | bytes 3145732
  107.7 18.1 %collective-permute-start.4 = (bf16[2,256,256]{1,2,0:T(8,128)(2,1)S(1)}, bf16[2,256,256]{1,2,0:T(8,128)(2,1)S(1)}, u32[]{:S(2)}, u32[]{:S(2)}) collective-permute-start(bf16[2,256,256]{1,2,0:T(8,128)(2,1)S(1)} %get-tuple-element.8), channel_id=1, source_target_pairs={{16,0},{20,4},{24,8},{28,12},{32,16},{36,20},{40,24},{44,28},{48,3... | collective-permute-start | bytes 786440 | tf_op jit(solution)/shard_map/ppermute | solution.py:17
  109.6 23.2 %collective-permute-start.7 = (bf16[2,256,256]{1,2,0:T(8,128)(2,1)S(1)}, bf16[2,256,256]{1,2,0:T(8,128)(2,1)S(1)}, u32[]{:S(2)}, u32[]{:S(2)}) collective-permute-start(bf16[2,256,256]{1,2,0:T(8,128)(2,1)S(1)} %get-tuple-element.9), channel_id=1, source_target_pairs={{4,0},{8,4},{12,8},{16,12},{20,16},{24,20},{28,24},{32,28},{36,32}... | collective-permute-start | bytes 786440 | tf_op jit(solution)/shard_map/ppermute | solution.py:17
  113.4 19.4 %collective-permute-start.6 = (bf16[2,256,256]{1,2,0:T(8,128)(2,1)S(1)}, bf16[2,256,256]{1,2,0:T(8,128)(2,1)S(1)}, u32[]{:S(2)}, u32[]{:S(2)}) collective-permute-start(bf16[2,256,256]{1,2,0:T(8,128)(2,1)S(1)} %get-tuple-element.10), channel_id=1, source_target_pairs={{8,0},{12,4},{16,8},{20,12},{24,16},{28,20},{32,24},{36,28},{40,32... | collective-permute-start | bytes 786440 | tf_op jit(solution)/shard_map/ppermute | solution.py:17
  115.3 34.8 %collective-permute-start.5 = (bf16[2,256,256]{1,2,0:T(8,128)(2,1)S(1)}, bf16[2,256,256]{1,2,0:T(8,128)(2,1)S(1)}, u32[]{:S(2)}, u32[]{:S(2)}) collective-permute-start(bf16[2,256,256]{1,2,0:T(8,128)(2,1)S(1)} %get-tuple-element.11), channel_id=1, source_target_pairs={{12,0},{16,4},{20,8},{24,12},{28,16},{32,20},{36,24},{40,28},{44,3... | collective-permute-start | bytes 786440 | tf_op jit(solution)/shard_map/ppermute | solution.py:17
  151.3 12.3 %all-to-all-start.1 = ((f32[2,256,256]{2,0,1:T(2,128)}), f32[2,256,256]{2,0,1:T(2,128)S(1)}, u32[]{:S(2)}, u32[]{:S(2)}) async-start(f32[2,256,256]{2,0,1:T(2,128)} %copy.141), calls=%async_computation.1 | async-start | bytes 1048576 | tf_op jit(solution)/shard_map/all_to_all | solution.py:98
  154.8 3.2 %copy-start.1 = (bf16[4,256,1280]{1,2,0:T(8,128)(2,1)S(1)}, bf16[4,256,1280]{1,2,0:T(8,128)(2,1)}, u32[]{:S(2)}) copy-start(bf16[4,256,1280]{1,2,0:T(8,128)(2,1)} %copy-done) | copy-start | bytes 7864324
  166.9 13.5 %all-to-all-start.2 = ((f32[2,4,16,1024]{3,2,0,1:T(8,128)}), f32[2,4,16,1024]{3,2,0,1:T(8,128)S(1)}, u32[]{:S(2)}, u32[]{:S(2)}) async-start(f32[2,4,16,1024]{3,2,0,1:T(8,128)} %copy.144), calls=%async_computation.2 | async-start | bytes 1048576 | tf_op jit(solution)/shard_map/all_to_all | solution.py:102
  (10 other events, 15.4 us)

commit v2 on v0

--- a/solution.py
+++ b/solution.py
@@ -44,6 +44,31 @@
     return (grad_query, grad_key, grad_value)
 
 
+def send_back(grad_ext, span_blocks, tok_rows):
+    own_rows = grad_ext[:, span_blocks * tok_rows :, :]
+    for offset in range(span_blocks):
+        own_rows = own_rows + shifted(
+            grad_ext[:, offset * tok_rows : (offset + 1) * tok_rows, :].astype(jnp.bfloat16),
+            "seq",
+            offset - span_blocks,
+        ).astype(jnp.float32)
+    return own_rows
+
+
+def scatter_layers(own_rows):
+    sections = lax.axis_size("section")
+    peers = lax.axis_size("tp")
+    kinds, rows, cols = own_rows.shape
+    pieces = own_rows.reshape(kinds, peers, sections, rows // (peers * sections), cols)
+    pieces = jnp.swapaxes(pieces, 1, 2).reshape(kinds, sections * peers, rows // (peers * sections), cols)
+    pieces = lax.all_to_all(pieces, ("section", "tp"), split_axis=1, concat_axis=1)
+    pieces = pieces.reshape(kinds, sections, peers, rows // (peers * sections), cols)
+    chunk = pieces[:, 0]
+    for other in range(1, sections):
+        chunk = chunk + pieces[:, other]
+    return jnp.swapaxes(chunk, 1, 2)
+
+
 def body(queries, upstream, shared_kv):
     local_kv = lax.all_to_all(shared_kv, "tp", split_axis=2, concat_axis=1, tiled=True)
     tok_rows = local_kv.shape[1]
@@ -54,10 +79,8 @@
     block_heads = max(1, group_size // 2)
     span_blocks = WINDOW // tok_rows
     score_scale = 1.0 / math.sqrt(head_size)
-    earlier = [shifted(local_kv, "seq", span_blocks - offset) for offset in range(span_blocks)]
-    extended = jnp.concatenate(earlier + [local_kv], axis=1)
-    ext_rows = extended.shape[1]
     position = lax.axis_index("seq")
+    ext_rows = (span_blocks + 1) * tok_rows
     row_ids = lax.broadcasted_iota(jnp.int32, (tok_rows, ext_rows), 0)
     key_ids = lax.broadcasted_iota(jnp.int32, (tok_rows, ext_rows), 1)
     allowed = (
@@ -67,12 +90,21 @@
     )
     query_heads = queries.reshape(tok_rows, -1, head_size)
     grad_heads = upstream.reshape(tok_rows, -1, head_size)
+    arrived = []
+    for kv_head in range(local_kv_heads):
+        head_kv = local_kv[:, :, kv_head * head_size : (kv_head + 1) * head_size]
+        earlier = [shifted(head_kv, "seq", span_blocks - offset) for offset in range(span_blocks)]
+        arrived.append(jnp.concatenate(earlier + [head_kv], axis=1))
     query_parts = []
-    key_parts = []
-    value_parts = []
+    chunks = []
+    previous = None
     for kv_head in range(local_kv_heads):
-        keys_head = extended[0, :, kv_head * head_size : (kv_head + 1) * head_size]
-        values_head = extended[1, :, kv_head * head_size : (kv_head + 1) * head_size]
+        extended = arrived[kv_head]
+        if previous is not None:
+            extended, previous = lax.optimization_barrier((extended, previous))
+            chunks.append(scatter_layers(send_back(previous, span_blocks, tok_rows)))
+        keys_head = extended[0]
+        values_head = extended[1]
         key_total = jnp.zeros((ext_rows, head_size), jnp.float32)
         value_total = jnp.zeros((ext_rows, head_size), jnp.float32)
         for first_head in range(kv_head * group_size, (kv_head + 1) * group_size, block_heads):
@@ -84,19 +116,12 @@
             query_parts.append(grad_query)
             key_total = key_total + grad_key
             value_total = value_total + grad_value
-        key_parts.append(key_total)
-        value_parts.append(value_total)
+        previous = jnp.stack([key_total, value_total])
+    chunks.append(scatter_layers(send_back(previous, span_blocks, tok_rows)))
     d_queries = jnp.concatenate(query_parts, axis=1).reshape(1, tok_rows, -1).astype(jnp.bfloat16)
-    grad_ext = jnp.stack([jnp.concatenate(key_parts, axis=1), jnp.concatenate(value_parts, axis=1)])
-    own_rows = grad_ext[:, span_blocks * tok_rows :, :]
-    for offset in range(span_blocks):
-        own_rows = own_rows + shifted(
-            grad_ext[:, offset * tok_rows : (offset + 1) * tok_rows, :].astype(jnp.bfloat16),
-            "seq",
-            offset - span_blocks,
-        ).astype(jnp.float32)
-    summed = lax.psum(own_rows, "section")
-    d_shared_kv = lax.all_to_all(summed, "tp", split_axis=1, concat_axis=2, tiled=True)
+    kinds, rows, tp_peers, _ = chunks[0].shape
+    joined = jnp.stack(chunks, axis=3).reshape(kinds, rows, -1)
+    d_shared_kv = lax.all_gather(joined, "section", axis=1, tiled=True)
     return (d_queries, d_shared_kv)
 
 

time: 229 us -> 187 us (0.82)
  the two profiles are of different devices: /device:TPU:80 before, /device:TPU:224 now
where the time goes in v2:
time: 187 us; the launch traced here: 186 us
  starting transfers between devices  54.3 us (29%)
  matrix products  46 us (25%)
  waiting for transfers between devices  36.4 us (19%)
  local copies, waits for them, and re-layouts  17.4 us (9%)
  other arithmetic  16.9 us (9%)
  blocking collectives  13.3 us (7%)
    ppermute x16, starting transfers between devices, shifted(): return lax.ppermute(value, axis, pairs)  43 us
    ppermute x16, waiting for transfers between devices, shifted(): return lax.ppermute(value, axis, pairs)  24.8 us
    sub x4, matrix products, head_grads(): weights = jnp.exp(masked - highest)  21.4 us
    all_gather x1, blocking collectives, body(): d_shared_kv = lax.all_gather(joined, 'section', axis=1, tiled=True)  13.3 us
    unnamed x58, local copies, waits for them, and re-layouts  12.6 us
    convert_element_type x4, other arithmetic, head_grads(): probs_b = probs.astype(jnp.bfloat16)  10.7 us
    all_to_all x2, waiting for transfers between devices, scatter_layers(): lax.all_to_all(pieces, ('section', 'tp'), split_axis=1, concat_axis=1)  8.25 us
    all_to_all x2, starting transfers between devices, scatter_layers(): lax.all_to_all(pieces, ('section', 'tp'), split_axis=1, concat_axis=1)  7.94 us
  transfers between devices with their start and end apart: 19, of which 6 were waited for; matrix products, arithmetic and copies ran while one was open for 19% of the time, Pallas kernels for 0%

profile of v2, /device:TPU:224, one launch (start us, length us, event | category | flops | bytes accessed | tf_op | source)
XLA Modules:
  0.0 185.7 jit_solution(15777052728586761453)
XLA Ops:
  3.0 3.4 %all-to-all-start = ((bf16[4,2,16384]{2,1,0:T(2,128)(2,1)}), bf16[4,2,16384]{2,1,0:T(2,128)(2,1)S(1)}, u32[]{:S(2)}, u32[]{:S(2)}) async-start(bf16[4,2,16384]{2,1,0:T(2,128)(2,1)} %reshape.139), calls=%async_computation | async-start | bytes 524288 | tf_op jit(solution)/shard_map/all_to_all | solution.py:73
  9.1 3.3 %all-to-all-done = bf16[4,2,16384]{2,1,0:T(2,128)(2,1)S(1)} async-done(((bf16[4,2,16384]{2,1,0:T(2,128)(2,1)}), bf16[4,2,16384]{2,1,0:T(2,128)(2,1)S(1)}, u32[]{:S(2)}, u32[]{:S(2)}) %all-to-all-start) | async-done | bytes 262176 | tf_op jit(solution)/shard_map/all_to_all | solution.py:73
  21.6 5.1 %collective-permute-start.3 = (bf16[2,256,128]{2,1,0:T(8,128)(2,1)}, bf16[2,256,128]{2,1,0:T(8,128)(2,1)S(1)}, u32[]{:S(2)}, u32[]{:S(2)}) collective-permute-start(bf16[2,256,128]{2,1,0:T(8,128)(2,1)} %get-tuple-element.32), channel_id=1, source_target_pairs={{0,4},{4,8},{8,12},{12,16},{16,20},{20,24},{24,28},{28,32},{32,36}... | collective-permute-start | bytes 393224 | tf_op jit(solution)/shard_map/ppermute | solution.py:17
  33.7 16.7 %collective-permute-done.5 = bf16[2,256,128]{2,1,0:T(8,128)(2,1)S(1)} collective-permute-done((bf16[2,256,128]{2,1,0:T(8,128)(2,1)}, bf16[2,256,128]{2,1,0:T(8,128)(2,1)S(1)}, u32[]{:S(2)}, u32[]{:S(2)}) %collective-permute-start.5) | collective-permute-done | bytes 131104 | tf_op jit(solution)/shard_map/ppermute | solution.py:17
  52.5 7.3 %collective-permute-done.7 = bf16[2,256,128]{2,1,0:T(8,128)(2,1)S(1)} collective-permute-done((bf16[2,256,128]{2,1,0:T(8,128)(2,1)}, bf16[2,256,128]{2,1,0:T(8,128)(2,1)S(1)}, u32[]{:S(2)}, u32[]{:S(2)}) %collective-permute-start.7) | collective-permute-done | bytes 131104 | tf_op jit(solution)/shard_map/ppermute | solution.py:17
  61.0 5.4 %exponential_reduce_fusion.2 = (f32[4,256]{1,0:T(4,128)S(1)}, f32[4,256,1280]{1,2,0:T(8,128)}) fusion(pred[256,1280]{0,1:T(8,128)(4,1)} %fusion.32, bf16[256,16,128]{0,2,1:T(8,128)(2,1)S(1)} %bitcast.273, bf16[2,1280,128]{2,1,0:T(8,128)(2,1)S(1)} %get-tuple-element.30), kind=kOutput, calls=%fused_computation.29 | convolution fusion | flops 340788480 | bytes 6164480 | tf_op jit(solution)/shard_map/sub | solution.py:27
  66.3 5.1 %exponential_reduce_fusion.3 = (f32[4,256]{1,0:T(4,128)S(1)}, f32[4,256,1280]{1,2,0:T(8,128)}) fusion(pred[256,1280]{0,1:T(8,128)(4,1)} %fusion.32, bf16[256,16,128]{0,2,1:T(8,128)(2,1)S(1)} %bitcast.274, bf16[2,1280,128]{2,1,0:T(8,128)(2,1)S(1)} %get-tuple-element.30), kind=kOutput, calls=%fused_computation.31 | convolution fusion | flops 340788480 | bytes 6164480 | tf_op jit(solution)/shard_map/sub | solution.py:27
  71.5 4.0 %fusion.26 = bf16[4,256,1280]{1,2,0:T(8,128)(2,1)S(1)} fusion(f32[4,256]{1,0:T(4,128)S(1)} %get-tuple-element.34, f32[4,256,1280]{1,2,0:T(8,128)} %get-tuple-element.35), kind=kLoop, calls=%fused_computation.50 | loop fusion | flops 2621440 | bytes 7868416 | tf_op jit(solution)/shard_map/convert_element_type | solution.py:29
  88.1 5.7 %exponential_reduce_fusion = (f32[4,256]{1,0:T(4,128)S(1)}, f32[4,256,1280]{1,2,0:T(8,128)}) fusion(pred[256,1280]{0,1:T(8,128)(4,1)} %fusion.32, bf16[256,16,128]{0,2,1:T(8,128)(2,1)S(1)} %bitcast.277, bf16[2,1280,128]{2,1,0:T(8,128)(2,1)} %copy-done.4), kind=kOutput, calls=%fused_computation.25 | convolution fusion | flops 340788480 | bytes 6164480 | tf_op jit(solution)/shard_map/sub | solution.py:27
  93.8 5.2 %exponential_reduce_fusion.1 = (f32[4,256]{1,0:T(4,128)S(1)}, f32[4,256,1280]{1,2,0:T(8,128)}) fusion(pred[256,1280]{0,1:T(8,128)(4,1)} %fusion.32, bf16[256,16,128]{0,2,1:T(8,128)(2,1)S(1)} %bitcast.278, bf16[2,1280,128]{2,1,0:T(8,128)(2,1)} %copy-done.4), kind=kOutput, calls=%fused_computation.27 | convolution fusion | flops 340788480 | bytes 6164480 | tf_op jit(solution)/shard_map/sub | solution.py:27
  99.2 5.4 %collective-permute-start.8 = (bf16[2,256,128]{2,1,0:T(8,128)(2,1)S(1)}, bf16[2,256,128]{2,1,0:T(8,128)(2,1)S(1)}, u32[]{:S(2)}, u32[]{:S(2)}) collective-permute-start(bf16[2,256,128]{2,1,0:T(8,128)(2,1)S(1)} %get-tuple-element.18), channel_id=1, source_target_pairs={{16,0},{20,4},{24,8},{28,12},{32,16},{36,20},{40,24},{44,28},{48,3... | collective-permute-start | bytes 393224 | tf_op jit(solution)/shard_map/ppermute | solution.py:17
  106.5 3.7 %collective-permute-start.10 = (bf16[2,256,128]{2,1,0:T(8,128)(2,1)S(1)}, bf16[2,256,128]{2,1,0:T(8,128)(2,1)S(1)}, u32[]{:S(2)}, u32[]{:S(2)}) collective-permute-start(bf16[2,256,128]{2,1,0:T(8,128)(2,1)S(1)} %get-tuple-element.20), channel_id=1, source_target_pairs={{8,0},{12,4},{16,8},{20,12},{24,16},{28,20},{32,24},{36,28},{40,32... | collective-permute-start | bytes 393224 | tf_op jit(solution)/shard_map/ppermute | solution.py:17
  110.2 5.8 %collective-permute-start.9 = (bf16[2,256,128]{2,1,0:T(8,128)(2,1)S(1)}, bf16[2,256,128]{2,1,0:T(8,128)(2,1)S(1)}, u32[]{:S(2)}, u32[]{:S(2)}) collective-permute-start(bf16[2,256,128]{2,1,0:T(8,128)(2,1)S(1)} %get-tuple-element.21), channel_id=1, source_target_pairs={{12,0},{16,4},{20,8},{24,12},{28,16},{32,20},{36,24},{40,28},{44,3... | collective-permute-start | bytes 393224 | tf_op jit(solution)/shard_map/ppermute | solution.py:17
  116.0 3.9 %fusion.29 = bf16[4,256,1280]{1,2,0:T(8,128)(2,1)S(1)} fusion(f32[4,256]{1,0:T(4,128)S(1)} %get-tuple-element.38, f32[4,256,1280]{1,2,0:T(8,128)} %get-tuple-element.39), kind=kLoop, calls=%fused_computation.53 | loop fusion | flops 2621440 | bytes 7868416 | tf_op jit(solution)/shard_map/convert_element_type | solution.py:29
  128.1 2.2 %fusion.11 = bf16[4,256,1280]{1,2,0:T(8,128)(2,1)S(1)} fusion(f32[4,256]{1,0:T(4,128)S(1)} %bitcast.291, f32[4,256]{1,0:T(4,128)S(1)} %get-tuple-element.40, f32[4,256,1280]{1,2,0:T(8,128)S(1)} %bitcast.265, bf16[2,1280,128]{2,1,0:T(8,128)(2,1)S(1)} %copy-done.5, bf16[256,16,128]{0,2,1:T(8,128)(2,1)} %bitcast.263), kind=kOutput, calls=%fused_computation.14 | convolution fusion | flops 340787200 | bytes 8462336 | tf_op jit(solution)/shard_map/rgd,ed->gre/dot_general | solution.py:32
  134.9 2.6 %collective-permute-start.12 = (bf16[2,256,128]{2,1,0:T(8,128)(2,1)}, bf16[2,256,128]{2,1,0:T(8,128)(2,1)}, u32[]{:S(2)}, u32[]{:S(2)}) collective-permute-start(bf16[2,256,128]{2,1,0:T(8,128)(2,1)} %get-tuple-element.22), channel_id=1, source_target_pairs={{16,0},{20,4},{24,8},{28,12},{32,16},{36,20},{40,24},{44,28},{48,3... | collective-permute-start | bytes 393224 | tf_op jit(solution)/shard_map/ppermute | solution.py:17
  137.4 2.5 %collective-permute-start.15 = (bf16[2,256,128]{2,1,0:T(8,128)(2,1)}, bf16[2,256,128]{2,1,0:T(8,128)(2,1)}, u32[]{:S(2)}, u32[]{:S(2)}) collective-permute-start(bf16[2,256,128]{2,1,0:T(8,128)(2,1)} %get-tuple-element.23), channel_id=1, source_target_pairs={{4,0},{8,4},{12,8},{16,12},{20,16},{24,20},{28,24},{32,28},{36,32}... | collective-permute-start | bytes 393224 | tf_op jit(solution)/shard_map/ppermute | solution.py:17
  141.9 4.3 %collective-permute-start.13 = (bf16[2,256,128]{2,1,0:T(8,128)(2,1)}, bf16[2,256,128]{2,1,0:T(8,128)(2,1)}, u32[]{:S(2)}, u32[]{:S(2)}) collective-permute-start(bf16[2,256,128]{2,1,0:T(8,128)(2,1)} %get-tuple-element.25), channel_id=1, source_target_pairs={{12,0},{16,4},{20,8},{24,12},{28,16},{32,20},{36,24},{40,28},{44,3... | collective-permute-start | bytes 393224 | tf_op jit(solution)/shard_map/ppermute | solution.py:17
  148.0 4.4 %all-to-all-start.1 = ((f32[2,16,16,128]{3,2,0,1:T(8,128)}), f32[2,16,16,128]{3,2,0,1:T(8,128)S(1)}, u32[]{:S(2)}, u32[]{:S(2)}) async-start(f32[2,16,16,128]{3,2,0,1:T(8,128)} %copy.137), calls=%async_computation.1 | async-start | bytes 524288 | tf_op jit(solution)/shard_map/all_to_all | solution.py:64
  152.4 2.2 %fusion.46 = bf16[256,4,128]{0,2,1:T(8,128)(2,1)} fusion(bf16[4,256,1280]{1,2,0:T(8,128)(2,1)S(1)} %fusion.11, bf16[2,1280,128]{2,1,0:T(8,128)(2,1)} %copy-done.4), kind=kOutput, calls=%fused_computation.84 | convolution fusion | flops 335806464 | bytes 3211264 | tf_op jit(solution)/shard_map/gre,ed->rgd/dot_general | solution.py:36
  156.7 3.4 %all-to-all-done.1 = f32[2,16,16,128]{3,2,0,1:T(8,128)S(1)} async-done(((f32[2,16,16,128]{3,2,0,1:T(8,128)}), f32[2,16,16,128]{3,2,0,1:T(8,128)S(1)}, u32[]{:S(2)}, u32[]{:S(2)}) %all-to-all-start.1) | async-done | bytes 262176 | tf_op jit(solution)/shard_map/all_to_all | solution.py:64
  160.1 3.5 %all-to-all-start.2 = ((f32[2,16,16,128]{3,2,0,1:T(8,128)}), f32[2,16,16,128]{3,2,0,1:T(8,128)S(1)}, u32[]{:S(2)}, u32[]{:S(2)}) async-start(f32[2,16,16,128]{3,2,0,1:T(8,128)} %copy.140), calls=%async_computation.2 | async-start | bytes 524288 | tf_op jit(solution)/shard_map/all_to_all | solution.py:64
  166.4 4.8 %all-to-all-done.2 = f32[2,16,16,128]{3,2,0,1:T(8,128)S(1)} async-done(((f32[2,16,16,128]{3,2,0,1:T(8,128)}), f32[2,16,16,128]{3,2,0,1:T(8,128)S(1)}, u32[]{:S(2)}, u32[]{:S(2)}) %all-to-all-start.2) | async-done | bytes 262176 | tf_op jit(solution)/shard_map/all_to_all | solution.py:64
  171.6 13.3 %all_gather.3 = f32[2,64,1024]{2,1,0:T(8,128)S(1)} all-gather(f32[2,16,1024]{2,1,0:T(8,128)S(1)} %reshape.118), channel_id=1, replica_groups=mesh['section'=4,'seq'=16,'tp'=4] {'section'}, dimensions={1}, use_global_device_ids=true | all-gather | bytes 655360 | tf_op jit(solution)/shard_map/all_gather | solution.py:124
  (130 shorter events, 61.1 us)
Async XLA Ops:
  3.0 9.4 %all-to-all-start = ((bf16[4,2,16384]{2,1,0:T(2,128)(2,1)}), bf16[4,2,16384]{2,1,0:T(2,128)(2,1)S(1)}, u32[]{:S(2)}, u32[]{:S(2)}) async-start(bf16[4,2,16384]{2,1,0:T(2,128)(2,1)} %reshape.139), calls=%async_computation | async-start | bytes 524288 | tf_op jit(solution)/shard_map/all_to_all | solution.py:73
  9.0 118.2 %copy-start = (bf16[1,256,2048]{1,2,0:T(8,128)(2,1)}, bf16[1,256,2048]{1,2,0:T(8,128)(2,1)S(1)}, u32[]{:S(2)}) copy-start(bf16[1,256,2048]{1,2,0:T(8,128)(2,1)S(1)} %copy.108) | copy-start | bytes 3145732
  14.0 18.4 %collective-permute-start = (bf16[2,256,128]{2,1,0:T(8,128)(2,1)}, bf16[2,256,128]{2,1,0:T(8,128)(2,1)S(1)}, u32[]{:S(2)}, u32[]{:S(2)}) collective-permute-start(bf16[2,256,128]{2,1,0:T(8,128)(2,1)} %get-tuple-element.32), channel_id=1, source_target_pairs={{0,16},{4,20},{8,24},{12,28},{16,32},{20,36},{24,40},{28,44},{32,4... | collective-permute-start | bytes 393224 | tf_op jit(solution)/shard_map/ppermute | solution.py:17
  15.2 14.9 %collective-permute-start.4 = (bf16[2,256,128]{2,1,0:T(8,128)(2,1)}, bf16[2,256,128]{2,1,0:T(8,128)(2,1)}, u32[]{:S(2)}, u32[]{:S(2)}) collective-permute-start(bf16[2,256,128]{2,1,0:T(8,128)(2,1)} %get-tuple-element.33), channel_id=1, source_target_pairs={{0,16},{4,20},{8,24},{12,28},{16,32},{20,36},{24,40},{28,44},{32,4... | collective-permute-start | bytes 393224 | tf_op jit(solution)/shard_map/ppermute | solution.py:17
  18.1 75.7 %copy-start.2 = (bf16[1,256,2048]{1,2,0:T(8,128)(2,1)}, bf16[1,256,2048]{1,2,0:T(8,128)(2,1)S(1)}, u32[]{:S(2)}) copy-start(bf16[1,256,2048]{1,2,0:T(8,128)(2,1)S(1)} %copy.106) | copy-start | bytes 3145732
  21.6 38.3 %collective-permute-start.3 = (bf16[2,256,128]{2,1,0:T(8,128)(2,1)}, bf16[2,256,128]{2,1,0:T(8,128)(2,1)S(1)}, u32[]{:S(2)}, u32[]{:S(2)}) collective-permute-start(bf16[2,256,128]{2,1,0:T(8,128)(2,1)} %get-tuple-element.32), channel_id=1, source_target_pairs={{0,4},{4,8},{8,12},{12,16},{16,20},{20,24},{24,28},{28,32},{32,36}... | collective-permute-start | bytes 393224 | tf_op jit(solution)/shard_map/ppermute | solution.py:17
  26.7 33.1 %collective-permute-start.2 = (bf16[2,256,128]{2,1,0:T(8,128)(2,1)}, bf16[2,256,128]{2,1,0:T(8,128)(2,1)S(1)}, u32[]{:S(2)}, u32[]{:S(2)}) collective-permute-start(bf16[2,256,128]{2,1,0:T(8,128)(2,1)} %get-tuple-element.32), channel_id=1, source_target_pairs={{0,8},{4,12},{8,16},{12,20},{16,24},{20,28},{24,32},{28,36},{32,40... | collective-permute-start | bytes 393224 | tf_op jit(solution)/shard_map/ppermute | solution.py:17
  28.0 31.8 %collective-permute-start.1 = (bf16[2,256,128]{2,1,0:T(8,128)(2,1)}, bf16[2,256,128]{2,1,0:T(8,128)(2,1)S(1)}, u32[]{:S(2)}, u32[]{:S(2)}) collective-permute-start(bf16[2,256,128]{2,1,0:T(8,128)(2,1)} %get-tuple-element.32), channel_id=1, source_target_pairs={{0,12},{4,16},{8,20},{12,24},{16,28},{20,32},{24,36},{28,40},{32,4... | collective-permute-start | bytes 393224 | tf_op jit(solution)/shard_map/ppermute | solution.py:17
  30.1 20.2 %collective-permute-start.5 = (bf16[2,256,128]{2,1,0:T(8,128)(2,1)}, bf16[2,256,128]{2,1,0:T(8,128)(2,1)S(1)}, u32[]{:S(2)}, u32[]{:S(2)}) collective-permute-start(bf16[2,256,128]{2,1,0:T(8,128)(2,1)} %get-tuple-element.33), channel_id=1, source_target_pairs={{0,12},{4,16},{8,20},{12,24},{16,28},{20,32},{24,36},{28,40},{32,4... | collective-permute-start | bytes 393224 | tf_op jit(solution)/shard_map/ppermute | solution.py:17
  32.4 20.1 %collective-permute-start.6 = (bf16[2,256,128]{2,1,0:T(8,128)(2,1)}, bf16[2,256,128]{2,1,0:T(8,128)(2,1)S(1)}, u32[]{:S(2)}, u32[]{:S(2)}) collective-permute-start(bf16[2,256,128]{2,1,0:T(8,128)(2,1)} %get-tuple-element.33), channel_id=1, source_target_pairs={{0,8},{4,12},{8,16},{12,20},{16,24},{20,28},{24,32},{28,36},{32,40... | collective-permute-start | bytes 393224 | tf_op jit(solution)/shard_map/ppermute | solution.py:17
  50.3 9.5 %collective-permute-start.7 = (bf16[2,256,128]{2,1,0:T(8,128)(2,1)}, bf16[2,256,128]{2,1,0:T(8,128)(2,1)S(1)}, u32[]{:S(2)}, u32[]{:S(2)}) collective-permute-start(bf16[2,256,128]{2,1,0:T(8,128)(2,1)} %get-tuple-element.33), channel_id=1, source_target_pairs={{0,4},{4,8},{8,12},{12,16},{16,20},{20,24},{24,28},{28,32},{32,36}... | collective-permute-start | bytes 393224 | tf_op jit(solution)/shard_map/ppermute | solution.py:17
  99.1 20.9 %copy-start.5 = (bf16[2,1280,128]{2,1,0:T(8,128)(2,1)S(1)}, bf16[2,1280,128]{2,1,0:T(8,128)(2,1)}, u32[]{:S(2)}) copy-start(bf16[2,1280,128]{2,1,0:T(8,128)(2,1)} %copy-done.4) | copy-start | bytes 1966084
  99.1 20.9 %copy-start.8 = (bf16[256,4,128]{2,0,1:T(8,128)(2,1)S(1)}, bf16[256,4,128]{2,0,1:T(8,128)(2,1)}, u32[]{:S(2)}) copy-start(bf16[256,4,128]{2,0,1:T(8,128)(2,1)} %copy.187) | copy-start | bytes 786436
  99.2 22.1 %slice-start.2 = ((s8[5242880]{0:T(1024)(128)(4,1)}), s8[4194304]{0:T(1024)(128)(4,1)S(1)}, s32[]{:S(2)}) async-start(s8[5242880]{0:T(1024)(128)(4,1)} %bitcast.266), calls=%async_computation.5 | async-start | bytes 8388608
  99.2 38.2 %collective-permute-start.8 = (bf16[2,256,128]{2,1,0:T(8,128)(2,1)S(1)}, bf16[2,256,128]{2,1,0:T(8,128)(2,1)S(1)}, u32[]{:S(2)}, u32[]{:S(2)}) collective-permute-start(bf16[2,256,128]{2,1,0:T(8,128)(2,1)S(1)} %get-tuple-element.18), channel_id=1, source_target_pairs={{16,0},{20,4},{24,8},{28,12},{32,16},{36,20},{40,24},{44,28},{48,3... | collective-permute-start | bytes 393224 | tf_op jit(solution)/shard_map/ppermute | solution.py:17
  104.6 35.3 %collective-permute-start.11 = (bf16[2,256,128]{2,1,0:T(8,128)(2,1)S(1)}, bf16[2,256,128]{2,1,0:T(8,128)(2,1)S(1)}, u32[]{:S(2)}, u32[]{:S(2)}) collective-permute-start(bf16[2,256,128]{2,1,0:T(8,128)(2,1)S(1)} %get-tuple-element.19), channel_id=1, source_target_pairs={{4,0},{8,4},{12,8},{16,12},{20,16},{24,20},{28,24},{32,28},{36,32}... | collective-permute-start | bytes 393224 | tf_op jit(solution)/shard_map/ppermute | solution.py:17
  106.5 35.3 %collective-permute-start.10 = (bf16[2,256,128]{2,1,0:T(8,128)(2,1)S(1)}, bf16[2,256,128]{2,1,0:T(8,128)(2,1)S(1)}, u32[]{:S(2)}, u32[]{:S(2)}) collective-permute-start(bf16[2,256,128]{2,1,0:T(8,128)(2,1)S(1)} %get-tuple-element.20), channel_id=1, source_target_pairs={{8,0},{12,4},{16,8},{20,12},{24,16},{28,20},{32,24},{36,28},{40,32... | collective-permute-start | bytes 393224 | tf_op jit(solution)/shard_map/ppermute | solution.py:17
  110.2 36.0 %collective-permute-start.9 = (bf16[2,256,128]{2,1,0:T(8,128)(2,1)S(1)}, bf16[2,256,128]{2,1,0:T(8,128)(2,1)S(1)}, u32[]{:S(2)}, u32[]{:S(2)}) collective-permute-start(bf16[2,256,128]{2,1,0:T(8,128)(2,1)S(1)} %get-tuple-element.21), channel_id=1, source_target_pairs={{12,0},{16,4},{20,8},{24,12},{28,16},{32,20},{36,24},{40,28},{44,3... | collective-permute-start | bytes 393224 | tf_op jit(solution)/shard_map/ppermute | solution.py:17
  134.9 19.8 %collective-permute-start.12 = (bf16[2,256,128]{2,1,0:T(8,128)(2,1)}, bf16[2,256,128]{2,1,0:T(8,128)(2,1)}, u32[]{:S(2)}, u32[]{:S(2)}) collective-permute-start(bf16[2,256,128]{2,1,0:T(8,128)(2,1)} %get-tuple-element.22), channel_id=1, source_target_pairs={{16,0},{20,4},{24,8},{28,12},{32,16},{36,20},{40,24},{44,28},{48,3... | collective-permute-start | bytes 393224 | tf_op jit(solution)/shard_map/ppermute | solution.py:17
  137.4 17.2 %collective-permute-start.15 = (bf16[2,256,128]{2,1,0:T(8,128)(2,1)}, bf16[2,256,128]{2,1,0:T(8,128)(2,1)}, u32[]{:S(2)}, u32[]{:S(2)}) collective-permute-start(bf16[2,256,128]{2,1,0:T(8,128)(2,1)} %get-tuple-element.23), channel_id=1, source_target_pairs={{4,0},{8,4},{12,8},{16,12},{20,16},{24,20},{28,24},{32,28},{36,32}... | collective-permute-start | bytes 393224 | tf_op jit(solution)/shard_map/ppermute | solution.py:17
  139.9 14.8 %collective-permute-start.14 = (bf16[2,256,128]{2,1,0:T(8,128)(2,1)}, bf16[2,256,128]{2,1,0:T(8,128)(2,1)}, u32[]{:S(2)}, u32[]{:S(2)}) collective-permute-start(bf16[2,256,128]{2,1,0:T(8,128)(2,1)} %get-tuple-element.24), channel_id=1, source_target_pairs={{8,0},{12,4},{16,8},{20,12},{24,16},{28,20},{32,24},{36,28},{40,32... | collective-permute-start | bytes 393224 | tf_op jit(solution)/shard_map/ppermute | solution.py:17
  141.9 12.8 %collective-permute-start.13 = (bf16[2,256,128]{2,1,0:T(8,128)(2,1)}, bf16[2,256,128]{2,1,0:T(8,128)(2,1)}, u32[]{:S(2)}, u32[]{:S(2)}) collective-permute-start(bf16[2,256,128]{2,1,0:T(8,128)(2,1)} %get-tuple-element.25), channel_id=1, source_target_pairs={{12,0},{16,4},{20,8},{24,12},{28,16},{32,20},{36,24},{40,28},{44,3... | collective-permute-start | bytes 393224 | tf_op jit(solution)/shard_map/ppermute | solution.py:17
  148.0 12.1 %all-to-all-start.1 = ((f32[2,16,16,128]{3,2,0,1:T(8,128)}), f32[2,16,16,128]{3,2,0,1:T(8,128)S(1)}, u32[]{:S(2)}, u32[]{:S(2)}) async-start(f32[2,16,16,128]{3,2,0,1:T(8,128)} %copy.137), calls=%async_computation.1 | async-start | bytes 524288 | tf_op jit(solution)/shard_map/all_to_all | solution.py:64
  160.1 11.2 %all-to-all-start.2 = ((f32[2,16,16,128]{3,2,0,1:T(8,128)}), f32[2,16,16,128]{3,2,0,1:T(8,128)S(1)}, u32[]{:S(2)}, u32[]{:S(2)}) async-start(f32[2,16,16,128]{3,2,0,1:T(8,128)} %copy.140), calls=%async_computation.2 | async-start | bytes 524288 | tf_op jit(solution)/shard_map/all_to_all | solution.py:64
  (14 other events, 79.8 us)

commit v3 on v0

v3 whole, which is shorter than its diff:
```python
import functools
import math

import jax
import jax.numpy as jnp
from jax import lax
from jax.experimental import pallas as pl
from jax.experimental.pallas import tpu as pltpu
from jax.sharding import PartitionSpec as P

QH = 64
KVH = 8
HD = 128
WINDOW = 1024


def shifted(value, axis, by):
    peers = lax.axis_size(axis)
    pairs = [(i, i + by) for i in range(peers) if 0 <= i + by < peers]
    return lax.ppermute(value, axis, pairs)


def attn_kernel(mask_ref, q_ref, g_ref, k_ref, v_ref, dq_ref, dkv_ref, *, scale):
    gi = pl.program_id(1)
    q = q_ref[...]
    do = g_ref[...]
    k = k_ref[...]
    v = v_ref[...]
    nt = (((1,), (1,)), ((), ()))
    tn = (((0,), (0,)), ((), ()))
    s = lax.dot_general(q, k, nt, preferred_element_type=jnp.float32) * scale
    s = jnp.where(mask_ref[...] != 0, s, -jnp.inf)
    m = jnp.max(s, axis=1, keepdims=True)
    w = jnp.exp(s - m)
    p = w / jnp.sum(w, axis=1, keepdims=True)
    pb = p.astype(jnp.bfloat16)
    o = jnp.dot(pb, v, preferred_element_type=jnp.float32)
    delta = jnp.sum(do.astype(jnp.float32) * o, axis=1, keepdims=True)
    dp = lax.dot_general(do, v, nt, preferred_element_type=jnp.float32)
    dsb = (p * (dp - delta)).astype(jnp.bfloat16)
    dq = jnp.dot(dsb, k, preferred_element_type=jnp.float32) * scale
    dq_ref[...] = dq.astype(dq_ref.dtype)
    dk = lax.dot_general(dsb, q, tn, preferred_element_type=jnp.float32) * scale
    dv = lax.dot_general(pb, do, tn, preferred_element_type=jnp.float32)

    @pl.when(gi == 0)
    def _():
        dkv_ref[0] = dk
        dkv_ref[1] = dv

    @pl.when(gi > 0)
    def _():
        dkv_ref[0] += dk
        dkv_ref[1] += dv

def attention_grads(mask, q, g, ext, group, hd, scale):
    rows, qcols = q.shape
    _, ext_rows, kcols = ext.shape
    heads = kcols // hd
    flops = 6 * 2 * rows * ext_rows * hd * heads * group
    return pl.pallas_call(
        functools.partial(attn_kernel, scale=scale),
        grid=(heads, group),
        in_specs=[
            pl.BlockSpec((rows, ext_rows), lambda h, i: (0, 0)),
            pl.BlockSpec((rows, hd), lambda h, i: (0, h * group + i)),
            pl.BlockSpec((rows, hd), lambda h, i: (0, h * group + i)),
            pl.BlockSpec((None, ext_rows, hd), lambda h, i: (0, 0, h)),
            pl.BlockSpec((None, ext_rows, hd), lambda h, i: (1, 0, h)),
        ],
        out_specs=[
            pl.BlockSpec((rows, hd), lambda h, i: (0, h * group + i)),
            pl.BlockSpec((2, ext_rows, hd), lambda h, i: (0, 0, h)),
        ],
        out_shape=[
            jax.ShapeDtypeStruct((rows, qcols), jnp.bfloat16),
            jax.ShapeDtypeStruct((2, ext_rows, kcols), jnp.float32),
        ],
        compiler_params=pltpu.CompilerParams(dimension_semantics=("arbitrary", "arbitrary")),
        cost_estimate=pl.CostEstimate(flops=flops, transcendentals=rows * ext_rows * heads * group,
                                      bytes_accessed=2 * q.size * 2 + q.size * 2 + ext.size * 2 + ext.size * 4 + mask.size * 4),
    )(mask, q, g, ext, ext)


def scatter_layers(own_rows):
    sections = lax.axis_size("section")
    peers = lax.axis_size("tp")
    kinds, rows, cols = own_rows.shape
    pieces = own_rows.reshape(kinds, peers, sections, rows // (peers * sections), cols)
    pieces = jnp.swapaxes(pieces, 1, 2).reshape(kinds, sections * peers, rows // (peers * sections), cols)
    pieces = lax.all_to_all(pieces, ("section", "tp"), split_axis=1, concat_axis=1)
    pieces = pieces.reshape(kinds, sections, peers, rows // (peers * sections), cols)
    chunk = pieces[:, 0]
    for other in range(1, sections):
        chunk = chunk + pieces[:, other]
    return jnp.swapaxes(chunk, 1, 2)


def body(queries, upstream, shared_kv):
    local_kv = lax.all_to_all(shared_kv, "tp", split_axis=2, concat_axis=1, tiled=True)
    tok_rows = local_kv.shape[1]
    head_size = HD
    group_size = QH // KVH
    span_blocks = WINDOW // tok_rows
    score_scale = 1.0 / math.sqrt(head_size)
    earlier = [shifted(local_kv, "seq", span_blocks - offset) for offset in range(span_blocks)]
    extended = jnp.concatenate(earlier + [local_kv], axis=1)
    ext_rows = extended.shape[1]
    position = lax.axis_index("seq")
    row_ids = lax.broadcasted_iota(jnp.int32, (tok_rows, ext_rows), 0)
    key_ids = lax.broadcasted_iota(jnp.int32, (tok_rows, ext_rows), 1)
    allowed = (
        (key_ids >= row_ids + 1)
        & (key_ids <= row_ids + WINDOW)
        & (position * tok_rows - WINDOW + key_ids >= 0)
    )
    d_query_rows, grad_ext = attention_grads(
        allowed.astype(jnp.int32),
        queries.reshape(tok_rows, -1),
        upstream.reshape(tok_rows, -1),
        extended,
        group_size,
        head_size,
        score_scale,
    )
    d_queries = d_query_rows.reshape(queries.shape)
    own_rows = grad_ext[:, span_blocks * tok_rows :, :]
    for offset in range(span_blocks):
        own_rows = own_rows + shifted(
            grad_ext[:, offset * tok_rows : (offset + 1) * tok_rows, :].astype(jnp.bfloat16),
            "seq",
            offset - span_blocks,
        ).astype(jnp.float32)
    chunk = scatter_layers(own_rows)
    kinds, rows, tp_peers, cols = chunk.shape
    d_shared_kv = lax.all_gather(chunk.reshape(kinds, rows, -1), "section", axis=1, tiled=True)
    return (d_queries, d_shared_kv)


def solution(mesh):
    in_specs = (P("section", "seq", "tp"), P("section", "seq", "tp"), P(None, ("seq", "tp"), None))
    out_specs = (P("section", "seq", "tp"), P(None, ("seq", "tp"), None))
    return jax.shard_map(body, mesh=mesh, in_specs=in_specs, out_specs=out_specs, check_vma=False)
```

time: 229 us -> 162 us (0.71)
  matrix products: 47 us -> 0 us
  waiting for transfers between devices: 98.2 us -> 56.5 us
  Pallas kernels: 0 us -> 33.3 us
  blocking collectives: 0 us -> 28.5 us
  local copies, waits for them, and re-layouts: 22.1 us -> 5.21 us
  between operations: 14.6 us -> 0.85 us
  other arithmetic: 11 us -> 4.62 us
    psum x1 -> x0, waiting for transfers between devices: 41.9 us -> none  [body(): summed = lax.psum(own_rows, 'section')]
    pallas_call x0 -> x1, Pallas kernels: none -> 33.3 us  [attention_grads(): pl.pallas_call(functools.partial(attn_kernel, scale=scale), grid=(heads,...]
    dot_general x20 -> x0, matrix products: 26.4 us -> none  [the longest x4 7.58 us: head_grads(): jnp.einsum('gre,ed->rgd', dscores_b, keys_head, preferred_element_type=jn...]
    sub x4 -> x0, matrix products: 20.6 us -> none  [head_grads(): weights = jnp.exp(masked - highest)]
    all_to_all x0 -> x1, blocking collectives: none -> 15 us  [scatter_layers(): lax.all_to_all(pieces, ('section', 'tp'), split_axis=1, concat_axis=1)]
    all_gather x0 -> x1, blocking collectives: none -> 13.5 us  [body(): lax.all_gather(chunk.reshape(kinds, rows, -1), 'section', axis=1, tiled=T...]
    unnamed x61 -> x10, local copies, waits for them, and re-layouts: 17.1 us -> 4.62 us
    convert_element_type x4 -> x1, other arithmetic: 8.43 us -> 1.52 us  [body(): allowed.astype(jnp.int32)]
  transfers between devices with their start and end apart: 11 -> 9, of which waited for: 8 -> 6; matrix products, arithmetic and copies ran while one was open for 8% -> 1% of each run, Pallas kernels for 0% -> 0%
where the time goes in v3:
time: 162 us; the launch traced here: 161 us
  waiting for transfers between devices  56.5 us (35%)
  Pallas kernels  33.3 us (21%)
  starting transfers between devices  32.2 us (20%)
  blocking collectives  28.5 us (18%)
  local copies, waits for them, and re-layouts  5.21 us (3%)
  other arithmetic  4.62 us (3%)
    ppermute x8, waiting for transfers between devices, shifted(): return lax.ppermute(value, axis, pairs)  50.5 us
    pallas_call x1, Pallas kernels, attention_grads(): pl.pallas_call(functools.partial(attn_kernel, scale=scale), grid=(heads,...  33.3 us
    ppermute x8, starting transfers between devices, shifted(): return lax.ppermute(value, axis, pairs)  28.8 us
    all_to_all x1, blocking collectives, scatter_layers(): lax.all_to_all(pieces, ('section', 'tp'), split_axis=1, concat_axis=1)  15 us
    all_gather x1, blocking collectives, body(): lax.all_gather(chunk.reshape(kinds, rows, -1), 'section', axis=1, tiled=T...  13.5 us
    all_to_all x1, waiting for transfers between devices, body(): lax.all_to_all(shared_kv, 'tp', split_axis=2, concat_axis=1, tiled=True)  5.94 us
    unnamed x10, local copies, waits for them, and re-layouts  4.62 us
    all_to_all x1, starting transfers between devices, body(): lax.all_to_all(shared_kv, 'tp', split_axis=2, concat_axis=1, tiled=True)  3.41 us
  transfers between devices with their start and end apart: 9, of which 6 were waited for; matrix products, arithmetic and copies ran while one was open for 1% of the time, Pallas kernels for 0%

profile of v3, /device:TPU:80, one launch (start us, length us, event | category | flops | bytes accessed | tf_op | source)
XLA Modules:
  0.0 161.1 jit_solution(3224613634093863289)
XLA Ops:
  0.6 1.3 copy.11
  1.9 1.1 reshape.35
  3.0 3.4 %all-to-all-start = ((bf16[4,2,16384]{2,1,0:T(2,128)(2,1)}), bf16[4,2,16384]{2,1,0:T(2,128)(2,1)S(1)}, u32[]{:S(2)}, u32[]{:S(2)}) async-start(bf16[4,2,16384]{2,1,0:T(2,128)(2,1)} %reshape.35), calls=%async_computation | async-start | bytes 524288 | tf_op jit(solution)/shard_map/all_to_all | solution.py:100
  6.4 5.9 %all-to-all-done = bf16[4,2,16384]{2,1,0:T(2,128)(2,1)S(1)} async-done(((bf16[4,2,16384]{2,1,0:T(2,128)(2,1)}), bf16[4,2,16384]{2,1,0:T(2,128)(2,1)S(1)}, u32[]{:S(2)}, u32[]{:S(2)}) %all-to-all-start) | async-done | bytes 262176 | tf_op jit(solution)/shard_map/all_to_all | solution.py:100
  13.1 3.8 %collective-permute-start.2 = (bf16[2,256,256]{2,1,0:T(8,128)(2,1)S(1)}, bf16[2,256,256]{2,1,0:T(8,128)(2,1)S(1)}, u32[]{:S(2)}, u32[]{:S(2)}) collective-permute-start(bf16[2,256,256]{2,1,0:T(8,128)(2,1)S(1)} %bitcast.25), channel_id=1, source_target_pairs={{0,8},{4,12},{8,16},{12,20},{16,24},{20,28},{24,32},{28,36},{32,40... | collective-permute-start | bytes 786440 | tf_op jit(solution)/shard_map/ppermute | solution.py:20
  17.0 5.3 %collective-permute-start.1 = (bf16[2,256,256]{2,1,0:T(8,128)(2,1)S(1)}, bf16[2,256,256]{2,1,0:T(8,128)(2,1)S(1)}, u32[]{:S(2)}, u32[]{:S(2)}) collective-permute-start(bf16[2,256,256]{2,1,0:T(8,128)(2,1)S(1)} %bitcast.26), channel_id=1, source_target_pairs={{0,12},{4,16},{8,20},{12,24},{16,28},{20,32},{24,36},{28,40},{32,4... | collective-permute-start | bytes 786440 | tf_op jit(solution)/shard_map/ppermute | solution.py:20
  22.2 3.4 %collective-permute-start = (bf16[2,256,256]{2,1,0:T(8,128)(2,1)S(1)}, bf16[2,256,256]{2,1,0:T(8,128)(2,1)S(1)}, u32[]{:S(2)}, u32[]{:S(2)}) collective-permute-start(bf16[2,256,256]{2,1,0:T(8,128)(2,1)S(1)} %bitcast.27), channel_id=1, source_target_pairs={{0,16},{4,20},{8,24},{12,28},{16,32},{20,36},{24,40},{28,44},{32,4... | collective-permute-start | bytes 786440 | tf_op jit(solution)/shard_map/ppermute | solution.py:20
  25.6 1.5 fusion.2.mask_ref
  27.1 5.1 %collective-permute-start.3 = (bf16[2,256,256]{2,1,0:T(8,128)(2,1)S(1)}, bf16[2,256,256]{2,1,0:T(8,128)(2,1)S(1)}, u32[]{:S(2)}, u32[]{:S(2)}) collective-permute-start(bf16[2,256,256]{2,1,0:T(8,128)(2,1)S(1)} %bitcast.28), channel_id=1, source_target_pairs={{0,4},{4,8},{8,12},{12,16},{16,20},{20,24},{24,28},{28,32},{32,36}... | collective-permute-start | bytes 786440 | tf_op jit(solution)/shard_map/ppermute | solution.py:20
  32.2 13.5 %collective-permute-done = bf16[2,256,256]{2,1,0:T(8,128)(2,1)S(1)} collective-permute-done((bf16[2,256,256]{2,1,0:T(8,128)(2,1)S(1)}, bf16[2,256,256]{2,1,0:T(8,128)(2,1)S(1)}, u32[]{:S(2)}, u32[]{:S(2)}) %collective-permute-start) | collective-permute-done | bytes 262176 | tf_op jit(solution)/shard_map/ppermute | solution.py:20
  45.8 4.5 %collective-permute-done.3 = bf16[2,256,256]{2,1,0:T(8,128)(2,1)S(1)} collective-permute-done((bf16[2,256,256]{2,1,0:T(8,128)(2,1)S(1)}, bf16[2,256,256]{2,1,0:T(8,128)(2,1)S(1)}, u32[]{:S(2)}, u32[]{:S(2)}) %collective-permute-start.3) | collective-permute-done | bytes 262176 | tf_op jit(solution)/shard_map/ppermute | solution.py:20
  50.4 1.0 copy-done
  51.4 33.3 %shard_map.50 = (bf16[256,2048]{1,0:T(8,128)(2,1)}, f32[2,1280,256]{2,1,0:T(8,128)}) custom-call(s32[256,1280]{1,0:T(8,128)} %fusion.2.mask_ref, bf16[256,2048]{1,0:T(8,128)(2,1)} %bitcast.31, bf16[256,2048]{1,0:T(8,128)(2,1)} %bitcast.32, bf16[2,1280,256]{2,1,0:T(8,128)(2,1)} %copy-done, bf16[2,1280,256]{2,1,0:T(8,128)(2,1)} %copy-done), custom_call_target="tpu_custom_call" | custom-call | flops 8053063680 | bytes 8388608 | tf_op jit(solution)/shard_map/pallas_call | solution.py:61
  84.7 1.9 %convert.6 = bf16[2,1280,256]{2,1,0:T(8,128)(2,1)S(1)} convert(f32[2,1280,256]{2,1,0:T(8,128)} %get-tuple-element.5) | non-fusion elementwise | flops 655360 | bytes 3932160 | tf_op jit(solution)/shard_map/convert.3
  86.7 1.9 %collective-permute-start.4 = (bf16[2,256,256]{2,1,0:T(8,128)(2,1)S(1)}, bf16[2,256,256]{2,1,0:T(8,128)(2,1)S(1)}, u32[]{:S(2)}, u32[]{:S(2)}) collective-permute-start(bf16[2,256,256]{2,1,0:T(8,128)(2,1)S(1)} %get-tuple-element.6), channel_id=1, source_target_pairs={{16,0},{20,4},{24,8},{28,12},{32,16},{36,20},{40,24},{44,28},{48,3... | collective-permute-start | bytes 786440 | tf_op jit(solution)/shard_map/ppermute | solution.py:20
  88.6 5.4 %collective-permute-start.7 = (bf16[2,256,256]{2,1,0:T(8,128)(2,1)S(1)}, bf16[2,256,256]{2,1,0:T(8,128)(2,1)S(1)}, u32[]{:S(2)}, u32[]{:S(2)}) collective-permute-start(bf16[2,256,256]{2,1,0:T(8,128)(2,1)S(1)} %get-tuple-element.7), channel_id=1, source_target_pairs={{4,0},{8,4},{12,8},{16,12},{20,16},{24,20},{28,24},{32,28},{36,32}... | collective-permute-start | bytes 786440 | tf_op jit(solution)/shard_map/ppermute | solution.py:20
  94.1 1.9 %collective-permute-start.6 = (bf16[2,256,256]{2,1,0:T(8,128)(2,1)S(1)}, bf16[2,256,256]{2,1,0:T(8,128)(2,1)S(1)}, u32[]{:S(2)}, u32[]{:S(2)}) collective-permute-start(bf16[2,256,256]{2,1,0:T(8,128)(2,1)S(1)} %get-tuple-element.8), channel_id=1, source_target_pairs={{8,0},{12,4},{16,8},{20,12},{24,16},{28,20},{32,24},{36,28},{40,32... | collective-permute-start | bytes 786440 | tf_op jit(solution)/shard_map/ppermute | solution.py:20
  96.0 1.9 %collective-permute-start.5 = (bf16[2,256,256]{2,1,0:T(8,128)(2,1)S(1)}, bf16[2,256,256]{2,1,0:T(8,128)(2,1)S(1)}, u32[]{:S(2)}, u32[]{:S(2)}) collective-permute-start(bf16[2,256,256]{2,1,0:T(8,128)(2,1)S(1)} %get-tuple-element.9), channel_id=1, source_target_pairs={{12,0},{16,4},{20,8},{24,12},{28,16},{32,20},{36,24},{40,28},{44,3... | collective-permute-start | bytes 786440 | tf_op jit(solution)/shard_map/ppermute | solution.py:20
  97.9 7.6 %collective-permute-done.4 = bf16[2,256,256]{2,1,0:T(8,128)(2,1)S(1)} collective-permute-done((bf16[2,256,256]{2,1,0:T(8,128)(2,1)S(1)}, bf16[2,256,256]{2,1,0:T(8,128)(2,1)S(1)}, u32[]{:S(2)}, u32[]{:S(2)}) %collective-permute-start.4) | collective-permute-done | bytes 262176 | tf_op jit(solution)/shard_map/ppermute | solution.py:20
  105.5 6.4 %collective-permute-done.7 = bf16[2,256,256]{2,1,0:T(8,128)(2,1)S(1)} collective-permute-done((bf16[2,256,256]{2,1,0:T(8,128)(2,1)S(1)}, bf16[2,256,256]{2,1,0:T(8,128)(2,1)S(1)}, u32[]{:S(2)}, u32[]{:S(2)}) %collective-permute-start.7) | collective-permute-done | bytes 262176 | tf_op jit(solution)/shard_map/ppermute | solution.py:20
  111.9 18.6 %collective-permute-done.5 = bf16[2,256,256]{2,1,0:T(8,128)(2,1)S(1)} collective-permute-done((bf16[2,256,256]{2,1,0:T(8,128)(2,1)S(1)}, bf16[2,256,256]{2,1,0:T(8,128)(2,1)S(1)}, u32[]{:S(2)}, u32[]{:S(2)}) %collective-permute-start.5) | collective-permute-done | bytes 262176 | tf_op jit(solution)/shard_map/ppermute | solution.py:20
  130.4 1.2 convert_add_fusion
  131.7 15.0 %all_to_all.23 = f32[2,16,16,256]{3,2,0,1:T(8,128)S(1)} all-to-all(f32[2,16,16,256]{3,2,0,1:T(8,128)S(1)} %copy.14), channel_id=1, replica_groups=mesh['section'=4,'seq'=16,'tp'=4] {'section','tp'}, dimensions={1} | all-to-all | bytes 1048576 | tf_op jit(solution)/shard_map/all_to_all | solution.py:91
  146.8 13.5 %all_gather.3 = f32[2,64,1024]{2,1,0:T(8,128)S(1)} all-gather(f32[2,16,1024]{2,1,0:T(8,128)S(1)} %bitcast.30), channel_id=1, replica_groups=mesh['section'=4,'seq'=16,'tp'=4] {'section'}, dimensions={1}, use_global_device_ids=true | all-gather | bytes 655360 | tf_op jit(solution)/shard_map/all_gather | solution.py:136
  (20 shorter events, 1.9 us)
Async XLA Ops:
  3.0 9.4 %all-to-all-start = ((bf16[4,2,16384]{2,1,0:T(2,128)(2,1)}), bf16[4,2,16384]{2,1,0:T(2,128)(2,1)S(1)}, u32[]{:S(2)}, u32[]{:S(2)}) async-start(bf16[4,2,16384]{2,1,0:T(2,128)(2,1)} %reshape.35), calls=%async_computation | async-start | bytes 524288 | tf_op jit(solution)/shard_map/all_to_all | solution.py:100
  13.1 32.6 %collective-permute-start.2 = (bf16[2,256,256]{2,1,0:T(8,128)(2,1)S(1)}, bf16[2,256,256]{2,1,0:T(8,128)(2,1)S(1)}, u32[]{:S(2)}, u32[]{:S(2)}) collective-permute-start(bf16[2,256,256]{2,1,0:T(8,128)(2,1)S(1)} %bitcast.25), channel_id=1, source_target_pairs={{0,8},{4,12},{8,16},{12,20},{16,24},{20,28},{24,32},{28,36},{32,40... | collective-permute-start | bytes 786440 | tf_op jit(solution)/shard_map/ppermute | solution.py:20
  17.0 28.8 %collective-permute-start.1 = (bf16[2,256,256]{2,1,0:T(8,128)(2,1)S(1)}, bf16[2,256,256]{2,1,0:T(8,128)(2,1)S(1)}, u32[]{:S(2)}, u32[]{:S(2)}) collective-permute-start(bf16[2,256,256]{2,1,0:T(8,128)(2,1)S(1)} %bitcast.26), channel_id=1, source_target_pairs={{0,12},{4,16},{8,20},{12,24},{16,28},{20,32},{24,36},{28,40},{32,4... | collective-permute-start | bytes 786440 | tf_op jit(solution)/shard_map/ppermute | solution.py:20
  22.2 23.5 %collective-permute-start = (bf16[2,256,256]{2,1,0:T(8,128)(2,1)S(1)}, bf16[2,256,256]{2,1,0:T(8,128)(2,1)S(1)}, u32[]{:S(2)}, u32[]{:S(2)}) collective-permute-start(bf16[2,256,256]{2,1,0:T(8,128)(2,1)S(1)} %bitcast.27), channel_id=1, source_target_pairs={{0,16},{4,20},{8,24},{12,28},{16,32},{20,36},{24,40},{28,44},{32,4... | collective-permute-start | bytes 786440 | tf_op jit(solution)/shard_map/ppermute | solution.py:20
  27.1 23.2 %collective-permute-start.3 = (bf16[2,256,256]{2,1,0:T(8,128)(2,1)S(1)}, bf16[2,256,256]{2,1,0:T(8,128)(2,1)S(1)}, u32[]{:S(2)}, u32[]{:S(2)}) collective-permute-start(bf16[2,256,256]{2,1,0:T(8,128)(2,1)S(1)} %bitcast.28), channel_id=1, source_target_pairs={{0,4},{4,8},{8,12},{12,16},{16,20},{20,24},{24,28},{28,32},{32,36}... | collective-permute-start | bytes 786440 | tf_op jit(solution)/shard_map/ppermute | solution.py:20
  50.4 1.1 copy-start
  86.7 18.8 %collective-permute-start.4 = (bf16[2,256,256]{2,1,0:T(8,128)(2,1)S(1)}, bf16[2,256,256]{2,1,0:T(8,128)(2,1)S(1)}, u32[]{:S(2)}, u32[]{:S(2)}) collective-permute-start(bf16[2,256,256]{2,1,0:T(8,128)(2,1)S(1)} %get-tuple-element.6), channel_id=1, source_target_pairs={{16,0},{20,4},{24,8},{28,12},{32,16},{36,20},{40,24},{44,28},{48,3... | collective-permute-start | bytes 786440 | tf_op jit(solution)/shard_map/ppermute | solution.py:20
  88.6 23.3 %collective-permute-start.7 = (bf16[2,256,256]{2,1,0:T(8,128)(2,1)S(1)}, bf16[2,256,256]{2,1,0:T(8,128)(2,1)S(1)}, u32[]{:S(2)}, u32[]{:S(2)}) collective-permute-start(bf16[2,256,256]{2,1,0:T(8,128)(2,1)S(1)} %get-tuple-element.7), channel_id=1, source_target_pairs={{4,0},{8,4},{12,8},{16,12},{20,16},{24,20},{28,24},{32,28},{36,32}... | collective-permute-start | bytes 786440 | tf_op jit(solution)/shard_map/ppermute | solution.py:20
  94.1 17.8 %collective-permute-start.6 = (bf16[2,256,256]{2,1,0:T(8,128)(2,1)S(1)}, bf16[2,256,256]{2,1,0:T(8,128)(2,1)S(1)}, u32[]{:S(2)}, u32[]{:S(2)}) collective-permute-start(bf16[2,256,256]{2,1,0:T(8,128)(2,1)S(1)} %get-tuple-element.8), channel_id=1, source_target_pairs={{8,0},{12,4},{16,8},{20,12},{24,16},{28,20},{32,24},{36,28},{40,32... | collective-permute-start | bytes 786440 | tf_op jit(solution)/shard_map/ppermute | solution.py:20
  96.0 34.5 %collective-permute-start.5 = (bf16[2,256,256]{2,1,0:T(8,128)(2,1)S(1)}, bf16[2,256,256]{2,1,0:T(8,128)(2,1)S(1)}, u32[]{:S(2)}, u32[]{:S(2)}) collective-permute-start(bf16[2,256,256]{2,1,0:T(8,128)(2,1)S(1)} %get-tuple-element.9), channel_id=1, source_target_pairs={{12,0},{16,4},{20,8},{24,12},{28,16},{32,20},{36,24},{40,28},{44,3... | collective-permute-start | bytes 786440 | tf_op jit(solution)/shard_map/ppermute | solution.py:20

commit v4 on v3

--- a/solution.py
+++ b/solution.py
@@ -20,28 +20,34 @@
     return lax.ppermute(value, axis, pairs)
 
 
-def attn_kernel(mask_ref, q_ref, g_ref, k_ref, v_ref, dq_ref, dkv_ref, *, scale):
+def attn_kernel(bias_ref, q_ref, g_ref, k_ref, v_ref, dq_ref, dkv_ref, *, scale, hd, per_step):
     gi = pl.program_id(1)
-    q = q_ref[...]
-    do = g_ref[...]
     k = k_ref[...]
     v = v_ref[...]
+    bias = bias_ref[...]
     nt = (((1,), (1,)), ((), ()))
     tn = (((0,), (0,)), ((), ()))
-    s = lax.dot_general(q, k, nt, preferred_element_type=jnp.float32) * scale
-    s = jnp.where(mask_ref[...] != 0, s, -jnp.inf)
-    m = jnp.max(s, axis=1, keepdims=True)
-    w = jnp.exp(s - m)
-    p = w / jnp.sum(w, axis=1, keepdims=True)
-    pb = p.astype(jnp.bfloat16)
-    o = jnp.dot(pb, v, preferred_element_type=jnp.float32)
-    delta = jnp.sum(do.astype(jnp.float32) * o, axis=1, keepdims=True)
-    dp = lax.dot_general(do, v, nt, preferred_element_type=jnp.float32)
-    dsb = (p * (dp - delta)).astype(jnp.bfloat16)
-    dq = jnp.dot(dsb, k, preferred_element_type=jnp.float32) * scale
-    dq_ref[...] = dq.astype(dq_ref.dtype)
-    dk = lax.dot_general(dsb, q, tn, preferred_element_type=jnp.float32) * scale
-    dv = lax.dot_general(pb, do, tn, preferred_element_type=jnp.float32)
+    dk = None
+    dv = None
+    for part in range(per_step):
+        cols = slice(part * hd, (part + 1) * hd)
+        q = q_ref[:, cols]
+        do = g_ref[:, cols]
+        s = lax.dot_general(q, k, nt, preferred_element_type=jnp.float32) * scale + bias
+        m = jnp.max(s, axis=1, keepdims=True)
+        w = jnp.exp(s - m)
+        p = w * (1.0 / jnp.sum(w, axis=1, keepdims=True))
+        pb = p.astype(jnp.bfloat16)
+        o = jnp.dot(pb, v, preferred_element_type=jnp.float32)
+        delta = jnp.sum(do.astype(jnp.float32) * o, axis=1, keepdims=True)
+        dp = lax.dot_general(do, v, nt, preferred_element_type=jnp.float32)
+        dsb = (p * (dp - delta)).astype(jnp.bfloat16)
+        dq = jnp.dot(dsb, k, preferred_element_type=jnp.float32) * scale
+        dq_ref[:, cols] = dq.astype(dq_ref.dtype)
+        dk_part = lax.dot_general(dsb, q, tn, preferred_element_type=jnp.float32) * scale
+        dv_part = lax.dot_general(pb, do, tn, preferred_element_type=jnp.float32)
+        dk = dk_part if dk is None else dk + dk_part
+        dv = dv_part if dv is None else dv + dv_part
 
     @pl.when(gi == 0)
     def _():
@@ -53,23 +59,26 @@
         dkv_ref[0] += dk
         dkv_ref[1] += dv
 
-def attention_grads(mask, q, g, ext, group, hd, scale):
+
+def attention_grads(bias, q, g, ext, group, hd, scale, per_step):
     rows, qcols = q.shape
     _, ext_rows, kcols = ext.shape
     heads = kcols // hd
+    steps = group // per_step
+    width = per_step * hd
     flops = 6 * 2 * rows * ext_rows * hd * heads * group
     return pl.pallas_call(
-        functools.partial(attn_kernel, scale=scale),
-        grid=(heads, group),
+        functools.partial(attn_kernel, scale=scale, hd=hd, per_step=per_step),
+        grid=(heads, steps),
         in_specs=[
             pl.BlockSpec((rows, ext_rows), lambda h, i: (0, 0)),
-            pl.BlockSpec((rows, hd), lambda h, i: (0, h * group + i)),
-            pl.BlockSpec((rows, hd), lambda h, i: (0, h * group + i)),
+            pl.BlockSpec((rows, width), lambda h, i: (0, h * steps + i)),
+            pl.BlockSpec((rows, width), lambda h, i: (0, h * steps + i)),
             pl.BlockSpec((None, ext_rows, hd), lambda h, i: (0, 0, h)),
             pl.BlockSpec((None, ext_rows, hd), lambda h, i: (1, 0, h)),
         ],
         out_specs=[
-            pl.BlockSpec((rows, hd), lambda h, i: (0, h * group + i)),
+            pl.BlockSpec((rows, width), lambda h, i: (0, h * steps + i)),
             pl.BlockSpec((2, ext_rows, hd), lambda h, i: (0, 0, h)),
         ],
         out_shape=[
@@ -77,9 +86,12 @@
             jax.ShapeDtypeStruct((2, ext_rows, kcols), jnp.float32),
         ],
         compiler_params=pltpu.CompilerParams(dimension_semantics=("arbitrary", "arbitrary")),
-        cost_estimate=pl.CostEstimate(flops=flops, transcendentals=rows * ext_rows * heads * group,
-                                      bytes_accessed=2 * q.size * 2 + q.size * 2 + ext.size * 2 + ext.size * 4 + mask.size * 4),
-    )(mask, q, g, ext, ext)
+        cost_estimate=pl.CostEstimate(
+            flops=flops,
+            transcendentals=rows * ext_rows * heads * group,
+            bytes_accessed=3 * q.size * 2 + ext.size * 2 + ext.size * 4 + bias.size * 4,
+        ),
+    )(bias, q, g, ext, ext)
 
 
 def scatter_layers(own_rows):
@@ -114,14 +126,16 @@
         & (key_ids <= row_ids + WINDOW)
         & (position * tok_rows - WINDOW + key_ids >= 0)
     )
+    bias = jnp.where(allowed, 0.0, -jnp.inf).astype(jnp.float32)
     d_query_rows, grad_ext = attention_grads(
-        allowed.astype(jnp.int32),
+        bias,
         queries.reshape(tok_rows, -1),
         upstream.reshape(tok_rows, -1),
         extended,
         group_size,
         head_size,
         score_scale,
+        2,
     )
     d_queries = d_query_rows.reshape(queries.shape)
     own_rows = grad_ext[:, span_blocks * tok_rows :, :]

time: 162 us -> 161 us (level)
  no operation moved by 1% of the time
where the time goes in v4:
time: 161 us
  waiting for transfers between devices  56.4 us (35%)
  Pallas kernels  32.7 us (20%)
  starting transfers between devices  32.2 us (20%)
  blocking collectives  28.5 us (18%)
  local copies, waits for them, and re-layouts  5.21 us (3%)
  other arithmetic  4.72 us (3%)
    ppermute x8, waiting for transfers between devices, shifted(): return lax.ppermute(value, axis, pairs)  50.4 us
    pallas_call x1, Pallas kernels, attention_grads(): pl.pallas_call(functools.partial(attn_kernel, scale=scale, hd=hd, per_ste...  32.7 us
    ppermute x8, starting transfers between devices, shifted(): return lax.ppermute(value, axis, pairs)  28.7 us
    all_to_all x1, blocking collectives, scatter_layers(): lax.all_to_all(pieces, ('section', 'tp'), split_axis=1, concat_axis=1)  15 us
    all_gather x1, blocking collectives, body(): lax.all_gather(chunk.reshape(kinds, rows, -1), 'section', axis=1, tiled=T...  13.5 us
    all_to_all x1, waiting for transfers between devices, body(): lax.all_to_all(shared_kv, 'tp', split_axis=2, concat_axis=1, tiled=True)  5.94 us
    unnamed x10, local copies, waits for them, and re-layouts  4.62 us
    all_to_all x1, starting transfers between devices, body(): lax.all_to_all(shared_kv, 'tp', split_axis=2, concat_axis=1, tiled=True)  3.41 us
  transfers between devices with their start and end apart: 9, of which 6 were waited for; matrix products, arithmetic and copies ran while one was open for 1% of the time, Pallas kernels for 0%

profile of v4, /device:TPU:80, one launch (start us, length us, event | category | flops | bytes accessed | tf_op | source)
XLA Modules:
  0.0 160.5 jit_solution(15316358774802794774)
XLA Ops:
  0.6 1.3 copy.11
  1.9 1.1 reshape.35
  3.0 3.4 %all-to-all-start = ((bf16[4,2,16384]{2,1,0:T(2,128)(2,1)}), bf16[4,2,16384]{2,1,0:T(2,128)(2,1)S(1)}, u32[]{:S(2)}, u32[]{:S(2)}) async-start(bf16[4,2,16384]{2,1,0:T(2,128)(2,1)} %reshape.35), calls=%async_computation | async-start | bytes 524288 | tf_op jit(solution)/shard_map/all_to_all | solution.py:112
  6.4 5.9 %all-to-all-done = bf16[4,2,16384]{2,1,0:T(2,128)(2,1)S(1)} async-done(((bf16[4,2,16384]{2,1,0:T(2,128)(2,1)}), bf16[4,2,16384]{2,1,0:T(2,128)(2,1)S(1)}, u32[]{:S(2)}, u32[]{:S(2)}) %all-to-all-start) | async-done | bytes 262176 | tf_op jit(solution)/shard_map/all_to_all | solution.py:112
  13.1 3.8 %collective-permute-start.2 = (bf16[2,256,256]{2,1,0:T(8,128)(2,1)S(1)}, bf16[2,256,256]{2,1,0:T(8,128)(2,1)S(1)}, u32[]{:S(2)}, u32[]{:S(2)}) collective-permute-start(bf16[2,256,256]{2,1,0:T(8,128)(2,1)S(1)} %bitcast.25), channel_id=1, source_target_pairs={{0,8},{4,12},{8,16},{12,20},{16,24},{20,28},{24,32},{28,36},{32,40... | collective-permute-start | bytes 786440 | tf_op jit(solution)/shard_map/ppermute | solution.py:20
  17.0 5.3 %collective-permute-start.1 = (bf16[2,256,256]{2,1,0:T(8,128)(2,1)S(1)}, bf16[2,256,256]{2,1,0:T(8,128)(2,1)S(1)}, u32[]{:S(2)}, u32[]{:S(2)}) collective-permute-start(bf16[2,256,256]{2,1,0:T(8,128)(2,1)S(1)} %bitcast.26), channel_id=1, source_target_pairs={{0,12},{4,16},{8,20},{12,24},{16,28},{20,32},{24,36},{28,40},{32,4... | collective-permute-start | bytes 786440 | tf_op jit(solution)/shard_map/ppermute | solution.py:20
  22.2 3.4 %collective-permute-start = (bf16[2,256,256]{2,1,0:T(8,128)(2,1)S(1)}, bf16[2,256,256]{2,1,0:T(8,128)(2,1)S(1)}, u32[]{:S(2)}, u32[]{:S(2)}) collective-permute-start(bf16[2,256,256]{2,1,0:T(8,128)(2,1)S(1)} %bitcast.27), channel_id=1, source_target_pairs={{0,16},{4,20},{8,24},{12,28},{16,32},{20,36},{24,40},{28,44},{32,4... | collective-permute-start | bytes 786440 | tf_op jit(solution)/shard_map/ppermute | solution.py:20
  25.6 1.6 %fusion.2.bias_ref = f32[256,1280]{1,0:T(8,128)} fusion(s32[256]{0:T(256)S(1)} %get-tuple-element.10, s32[256]{0:T(256)S(1)} %get-tuple-element.11, pred[1280]{0:T(1024)(128)(4,1)S(1)} %add_compare_fusion), kind=kLoop, calls=%fused_computation.4 | loop fusion | flops 1638400 | bytes 1314048 | tf_op jit(solution)/shard_map/jit(_where)/select_n | solution.py:129
  27.2 5.1 %collective-permute-start.3 = (bf16[2,256,256]{2,1,0:T(8,128)(2,1)S(1)}, bf16[2,256,256]{2,1,0:T(8,128)(2,1)S(1)}, u32[]{:S(2)}, u32[]{:S(2)}) collective-permute-start(bf16[2,256,256]{2,1,0:T(8,128)(2,1)S(1)} %bitcast.28), channel_id=1, source_target_pairs={{0,4},{4,8},{8,12},{12,16},{16,20},{20,24},{24,28},{28,32},{32,36}... | collective-permute-start | bytes 786440 | tf_op jit(solution)/shard_map/ppermute | solution.py:20
  32.3 13.4 %collective-permute-done = bf16[2,256,256]{2,1,0:T(8,128)(2,1)S(1)} collective-permute-done((bf16[2,256,256]{2,1,0:T(8,128)(2,1)S(1)}, bf16[2,256,256]{2,1,0:T(8,128)(2,1)S(1)}, u32[]{:S(2)}, u32[]{:S(2)}) %collective-permute-start) | collective-permute-done | bytes 262176 | tf_op jit(solution)/shard_map/ppermute | solution.py:20
  45.8 4.5 %collective-permute-done.3 = bf16[2,256,256]{2,1,0:T(8,128)(2,1)S(1)} collective-permute-done((bf16[2,256,256]{2,1,0:T(8,128)(2,1)S(1)}, bf16[2,256,256]{2,1,0:T(8,128)(2,1)S(1)}, u32[]{:S(2)}, u32[]{:S(2)}) %collective-permute-start.3) | collective-permute-done | bytes 262176 | tf_op jit(solution)/shard_map/ppermute | solution.py:20
  50.4 1.0 copy-done
  51.4 32.7 %shard_map.50 = (bf16[256,2048]{1,0:T(8,128)(2,1)}, f32[2,1280,256]{2,1,0:T(8,128)}) custom-call(f32[256,1280]{1,0:T(8,128)} %fusion.2.bias_ref, bf16[256,2048]{1,0:T(8,128)(2,1)} %bitcast.31, bf16[256,2048]{1,0:T(8,128)(2,1)} %bitcast.32, bf16[2,1280,256]{2,1,0:T(8,128)(2,1)} %copy-done, bf16[2,1280,256]{2,1,0:T(8,128)(2,1)} %copy-done), custom_call_target="tpu_custom_call" | custom-call | flops 8053063680 | bytes 8388608 | tf_op jit(solution)/shard_map/pallas_call | solution.py:70
  84.1 1.9 %convert.6 = bf16[2,1280,256]{2,1,0:T(8,128)(2,1)S(1)} convert(f32[2,1280,256]{2,1,0:T(8,128)} %get-tuple-element.5) | non-fusion elementwise | flops 655360 | bytes 3932160 | tf_op jit(solution)/shard_map/convert.3
  86.1 1.9 %collective-permute-start.4 = (bf16[2,256,256]{2,1,0:T(8,128)(2,1)S(1)}, bf16[2,256,256]{2,1,0:T(8,128)(2,1)S(1)}, u32[]{:S(2)}, u32[]{:S(2)}) collective-permute-start(bf16[2,256,256]{2,1,0:T(8,128)(2,1)S(1)} %get-tuple-element.6), channel_id=1, source_target_pairs={{16,0},{20,4},{24,8},{28,12},{32,16},{36,20},{40,24},{44,28},{48,3... | collective-permute-start | bytes 786440 | tf_op jit(solution)/shard_map/ppermute | solution.py:20
  88.0 5.4 %collective-permute-start.7 = (bf16[2,256,256]{2,1,0:T(8,128)(2,1)S(1)}, bf16[2,256,256]{2,1,0:T(8,128)(2,1)S(1)}, u32[]{:S(2)}, u32[]{:S(2)}) collective-permute-start(bf16[2,256,256]{2,1,0:T(8,128)(2,1)S(1)} %get-tuple-element.7), channel_id=1, source_target_pairs={{4,0},{8,4},{12,8},{16,12},{20,16},{24,20},{28,24},{32,28},{36,32}... | collective-permute-start | bytes 786440 | tf_op jit(solution)/shard_map/ppermute | solution.py:20
  93.5 1.9 %collective-permute-start.6 = (bf16[2,256,256]{2,1,0:T(8,128)(2,1)S(1)}, bf16[2,256,256]{2,1,0:T(8,128)(2,1)S(1)}, u32[]{:S(2)}, u32[]{:S(2)}) collective-permute-start(bf16[2,256,256]{2,1,0:T(8,128)(2,1)S(1)} %get-tuple-element.8), channel_id=1, source_target_pairs={{8,0},{12,4},{16,8},{20,12},{24,16},{28,20},{32,24},{36,28},{40,32... | collective-permute-start | bytes 786440 | tf_op jit(solution)/shard_map/ppermute | solution.py:20
  95.4 1.9 %collective-permute-start.5 = (bf16[2,256,256]{2,1,0:T(8,128)(2,1)S(1)}, bf16[2,256,256]{2,1,0:T(8,128)(2,1)S(1)}, u32[]{:S(2)}, u32[]{:S(2)}) collective-permute-start(bf16[2,256,256]{2,1,0:T(8,128)(2,1)S(1)} %get-tuple-element.9), channel_id=1, source_target_pairs={{12,0},{16,4},{20,8},{24,12},{28,16},{32,20},{36,24},{40,28},{44,3... | collective-permute-start | bytes 786440 | tf_op jit(solution)/shard_map/ppermute | solution.py:20
  97.3 7.6 %collective-permute-done.4 = bf16[2,256,256]{2,1,0:T(8,128)(2,1)S(1)} collective-permute-done((bf16[2,256,256]{2,1,0:T(8,128)(2,1)S(1)}, bf16[2,256,256]{2,1,0:T(8,128)(2,1)S(1)}, u32[]{:S(2)}, u32[]{:S(2)}) %collective-permute-start.4) | collective-permute-done | bytes 262176 | tf_op jit(solution)/shard_map/ppermute | solution.py:20
  104.9 6.4 %collective-permute-done.7 = bf16[2,256,256]{2,1,0:T(8,128)(2,1)S(1)} collective-permute-done((bf16[2,256,256]{2,1,0:T(8,128)(2,1)S(1)}, bf16[2,256,256]{2,1,0:T(8,128)(2,1)S(1)}, u32[]{:S(2)}, u32[]{:S(2)}) %collective-permute-start.7) | collective-permute-done | bytes 262176 | tf_op jit(solution)/shard_map/ppermute | solution.py:20
  111.3 18.6 %collective-permute-done.5 = bf16[2,256,256]{2,1,0:T(8,128)(2,1)S(1)} collective-permute-done((bf16[2,256,256]{2,1,0:T(8,128)(2,1)S(1)}, bf16[2,256,256]{2,1,0:T(8,128)(2,1)S(1)}, u32[]{:S(2)}, u32[]{:S(2)}) %collective-permute-start.5) | collective-permute-done | bytes 262176 | tf_op jit(solution)/shard_map/ppermute | solution.py:20
  129.8 1.2 convert_add_fusion
  131.1 15.0 %all_to_all.23 = f32[2,16,16,256]{3,2,0,1:T(8,128)S(1)} all-to-all(f32[2,16,16,256]{3,2,0,1:T(8,128)S(1)} %copy.14), channel_id=1, replica_groups=mesh['section'=4,'seq'=16,'tp'=4] {'section','tp'}, dimensions={1} | all-to-all | bytes 1048576 | tf_op jit(solution)/shard_map/all_to_all | solution.py:103
  146.3 13.5 %all_gather.3 = f32[2,64,1024]{2,1,0:T(8,128)S(1)} all-gather(f32[2,16,1024]{2,1,0:T(8,128)S(1)} %bitcast.30), channel_id=1, replica_groups=mesh['section'=4,'seq'=16,'tp'=4] {'section'}, dimensions={1}, use_global_device_ids=true | all-gather | bytes 655360 | tf_op jit(solution)/shard_map/all_gather | solution.py:150
  (20 shorter events, 1.9 us)
Async XLA Ops:
  3.0 9.4 %all-to-all-start = ((bf16[4,2,16384]{2,1,0:T(2,128)(2,1)}), bf16[4,2,16384]{2,1,0:T(2,128)(2,1)S(1)}, u32[]{:S(2)}, u32[]{:S(2)}) async-start(bf16[4,2,16384]{2,1,0:T(2,128)(2,1)} %reshape.35), calls=%async_computation | async-start | bytes 524288 | tf_op jit(solution)/shard_map/all_to_all | solution.py:112
  13.1 32.6 %collective-permute-start.2 = (bf16[2,256,256]{2,1,0:T(8,128)(2,1)S(1)}, bf16[2,256,256]{2,1,0:T(8,128)(2,1)S(1)}, u32[]{:S(2)}, u32[]{:S(2)}) collective-permute-start(bf16[2,256,256]{2,1,0:T(8,128)(2,1)S(1)} %bitcast.25), channel_id=1, source_target_pairs={{0,8},{4,12},{8,16},{12,20},{16,24},{20,28},{24,32},{28,36},{32,40... | collective-permute-start | bytes 786440 | tf_op jit(solution)/shard_map/ppermute | solution.py:20
  17.0 28.8 %collective-permute-start.1 = (bf16[2,256,256]{2,1,0:T(8,128)(2,1)S(1)}, bf16[2,256,256]{2,1,0:T(8,128)(2,1)S(1)}, u32[]{:S(2)}, u32[]{:S(2)}) collective-permute-start(bf16[2,256,256]{2,1,0:T(8,128)(2,1)S(1)} %bitcast.26), channel_id=1, source_target_pairs={{0,12},{4,16},{8,20},{12,24},{16,28},{20,32},{24,36},{28,40},{32,4... | collective-permute-start | bytes 786440 | tf_op jit(solution)/shard_map/ppermute | solution.py:20
  22.2 23.5 %collective-permute-start = (bf16[2,256,256]{2,1,0:T(8,128)(2,1)S(1)}, bf16[2,256,256]{2,1,0:T(8,128)(2,1)S(1)}, u32[]{:S(2)}, u32[]{:S(2)}) collective-permute-start(bf16[2,256,256]{2,1,0:T(8,128)(2,1)S(1)} %bitcast.27), channel_id=1, source_target_pairs={{0,16},{4,20},{8,24},{12,28},{16,32},{20,36},{24,40},{28,44},{32,4... | collective-permute-start | bytes 786440 | tf_op jit(solution)/shard_map/ppermute | solution.py:20
  27.2 23.1 %collective-permute-start.3 = (bf16[2,256,256]{2,1,0:T(8,128)(2,1)S(1)}, bf16[2,256,256]{2,1,0:T(8,128)(2,1)S(1)}, u32[]{:S(2)}, u32[]{:S(2)}) collective-permute-start(bf16[2,256,256]{2,1,0:T(8,128)(2,1)S(1)} %bitcast.28), channel_id=1, source_target_pairs={{0,4},{4,8},{8,12},{12,16},{16,20},{20,24},{24,28},{28,32},{32,36}... | collective-permute-start | bytes 786440 | tf_op jit(solution)/shard_map/ppermute | solution.py:20
  50.4 1.1 copy-start
  86.1 18.8 %collective-permute-start.4 = (bf16[2,256,256]{2,1,0:T(8,128)(2,1)S(1)}, bf16[2,256,256]{2,1,0:T(8,128)(2,1)S(1)}, u32[]{:S(2)}, u32[]{:S(2)}) collective-permute-start(bf16[2,256,256]{2,1,0:T(8,128)(2,1)S(1)} %get-tuple-element.6), channel_id=1, source_target_pairs={{16,0},{20,4},{24,8},{28,12},{32,16},{36,20},{40,24},{44,28},{48,3... | collective-permute-start | bytes 786440 | tf_op jit(solution)/shard_map/ppermute | solution.py:20
  88.0 23.2 %collective-permute-start.7 = (bf16[2,256,256]{2,1,0:T(8,128)(2,1)S(1)}, bf16[2,256,256]{2,1,0:T(8,128)(2,1)S(1)}, u32[]{:S(2)}, u32[]{:S(2)}) collective-permute-start(bf16[2,256,256]{2,1,0:T(8,128)(2,1)S(1)} %get-tuple-element.7), channel_id=1, source_target_pairs={{4,0},{8,4},{12,8},{16,12},{20,16},{24,20},{28,24},{32,28},{36,32}... | collective-permute-start | bytes 786440 | tf_op jit(solution)/shard_map/ppermute | solution.py:20
  93.5 17.8 %collective-permute-start.6 = (bf16[2,256,256]{2,1,0:T(8,128)(2,1)S(1)}, bf16[2,256,256]{2,1,0:T(8,128)(2,1)S(1)}, u32[]{:S(2)}, u32[]{:S(2)}) collective-permute-start(bf16[2,256,256]{2,1,0:T(8,128)(2,1)S(1)} %get-tuple-element.8), channel_id=1, source_target_pairs={{8,0},{12,4},{16,8},{20,12},{24,16},{28,20},{32,24},{36,28},{40,32... | collective-permute-start | bytes 786440 | tf_op jit(solution)/shard_map/ppermute | solution.py:20
  95.4 34.5 %collective-permute-start.5 = (bf16[2,256,256]{2,1,0:T(8,128)(2,1)S(1)}, bf16[2,256,256]{2,1,0:T(8,128)(2,1)S(1)}, u32[]{:S(2)}, u32[]{:S(2)}) collective-permute-start(bf16[2,256,256]{2,1,0:T(8,128)(2,1)S(1)} %get-tuple-element.9), channel_id=1, source_target_pairs={{12,0},{16,4},{20,8},{24,12},{28,16},{32,20},{36,24},{40,28},{44,3... | collective-permute-start | bytes 786440 | tf_op jit(solution)/shard_map/ppermute | solution.py:20

commit v5 on v3

--- a/solution.py
+++ b/solution.py
@@ -20,46 +20,63 @@
     return lax.ppermute(value, axis, pairs)
 
 
-def attn_kernel(mask_ref, q_ref, g_ref, k_ref, v_ref, dq_ref, dkv_ref, *, scale):
+def attn_kernel(bias_ref, q_ref, g_ref, k_ref, v_ref, dq_ref, dkv_ref, held, *, scale, hd, row_chunk, key_chunk):
     gi = pl.program_id(1)
-    q = q_ref[...]
-    do = g_ref[...]
-    k = k_ref[...]
-    v = v_ref[...]
+    rows = q_ref.shape[0]
+    ext_rows = k_ref.shape[0]
+    key_parts = ext_rows // key_chunk
     nt = (((1,), (1,)), ((), ()))
     tn = (((0,), (0,)), ((), ()))
-    s = lax.dot_general(q, k, nt, preferred_element_type=jnp.float32) * scale
-    s = jnp.where(mask_ref[...] != 0, s, -jnp.inf)
-    m = jnp.max(s, axis=1, keepdims=True)
-    w = jnp.exp(s - m)
-    p = w / jnp.sum(w, axis=1, keepdims=True)
-    pb = p.astype(jnp.bfloat16)
-    o = jnp.dot(pb, v, preferred_element_type=jnp.float32)
-    delta = jnp.sum(do.astype(jnp.float32) * o, axis=1, keepdims=True)
-    dp = lax.dot_general(do, v, nt, preferred_element_type=jnp.float32)
-    dsb = (p * (dp - delta)).astype(jnp.bfloat16)
-    dq = jnp.dot(dsb, k, preferred_element_type=jnp.float32) * scale
-    dq_ref[...] = dq.astype(dq_ref.dtype)
-    dk = lax.dot_general(dsb, q, tn, preferred_element_type=jnp.float32) * scale
-    dv = lax.dot_general(pb, do, tn, preferred_element_type=jnp.float32)
 
     @pl.when(gi == 0)
     def _():
-        dkv_ref[0] = dk
-        dkv_ref[1] = dv
+        dkv_ref[...] = jnp.zeros_like(dkv_ref)
 
-    @pl.when(gi > 0)
-    def _():
-        dkv_ref[0] += dk
-        dkv_ref[1] += dv
+    for part in range(rows // row_chunk):
+        lines = pl.ds(part * row_chunk, row_chunk)
+        q = q_ref[lines, :]
+        do = g_ref[lines, :]
+        highest = jnp.full((row_chunk, 1), -jnp.inf, jnp.float32)
+        for c in range(key_parts):
+            keys = pl.ds(c * key_chunk, key_chunk)
+            s = lax.dot_general(q, k_ref[keys, :], nt, preferred_element_type=jnp.float32) * scale
+            s = s + bias_ref[lines, keys]
+            held[c] = s
+            highest = jnp.maximum(highest, jnp.max(s, axis=1, keepdims=True))
+        total = jnp.zeros((row_chunk, 1), jnp.float32)
+        for c in range(key_parts):
+            w = jnp.exp(held[c] - highest)
+            held[c] = w
+            total = total + jnp.sum(w, axis=1, keepdims=True)
+        inverse = 1.0 / total
+        out = jnp.zeros((row_chunk, hd), jnp.float32)
+        for c in range(key_parts):
+            keys = pl.ds(c * key_chunk, key_chunk)
+            p = held[c] * inverse
+            held[c] = p
+            out = out + jnp.dot(p.astype(jnp.bfloat16), v_ref[keys, :], preferred_element_type=jnp.float32)
+        delta = jnp.sum(do.astype(jnp.float32) * out, axis=1, keepdims=True)
+        dq = jnp.zeros((row_chunk, hd), jnp.float32)
+        for c in range(key_parts):
+            keys = pl.ds(c * key_chunk, key_chunk)
+            v = v_ref[keys, :]
+            k = k_ref[keys, :]
+            p = held[c]
+            dp = lax.dot_general(do, v, nt, preferred_element_type=jnp.float32)
+            dsb = (p * (dp - delta)).astype(jnp.bfloat16)
+            dq = dq + jnp.dot(dsb, k, preferred_element_type=jnp.float32)
+            dkv_ref[0, keys, :] += lax.dot_general(dsb, q, tn, preferred_element_type=jnp.float32) * scale
+            dkv_ref[1, keys, :] += lax.dot_general(p.astype(jnp.bfloat16), do, tn, preferred_element_type=jnp.float32)
+        dq_ref[lines, :] = (dq * scale).astype(dq_ref.dtype)
 
-def attention_grads(mask, q, g, ext, group, hd, scale):
+
+def attention_grads(bias, q, g, ext, group, hd, scale, row_chunk, key_chunk):
     rows, qcols = q.shape
     _, ext_rows, kcols = ext.shape
     heads = kcols // hd
     flops = 6 * 2 * rows * ext_rows * hd * heads * group
     return pl.pallas_call(
-        functools.partial(attn_kernel, scale=scale),
+        functools.partial(attn_kernel, scale=scale, hd=hd, row_chunk=row_chunk, key_chunk=key_chunk),
         grid=(heads, group),
         in_specs=[
             pl.BlockSpec((rows, ext_rows), lambda h, i: (0, 0)),
@@ -76,10 +93,14 @@
             jax.ShapeDtypeStruct((rows, qcols), jnp.bfloat16),
             jax.ShapeDtypeStruct((2, ext_rows, kcols), jnp.float32),
         ],
+        scratch_shapes=[pltpu.VMEM((ext_rows // key_chunk, row_chunk, key_chunk), jnp.float32)],
         compiler_params=pltpu.CompilerParams(dimension_semantics=("arbitrary", "arbitrary")),
-        cost_estimate=pl.CostEstimate(flops=flops, transcendentals=rows * ext_rows * heads * group,
-                                      bytes_accessed=2 * q.size * 2 + q.size * 2 + ext.size * 2 + ext.size * 4 + mask.size * 4),
-    )(mask, q, g, ext, ext)
+        cost_estimate=pl.CostEstimate(
+            flops=flops,
+            transcendentals=rows * ext_rows * heads * group,
+            bytes_accessed=3 * q.size * 2 + ext.size * 2 + ext.size * 4 + bias.size * 4,
+        ),
+    )(bias, q, g, ext, ext)
 
 
 def scatter_layers(own_rows):
@@ -114,14 +135,17 @@
         & (key_ids <= row_ids + WINDOW)
         & (position * tok_rows - WINDOW + key_ids >= 0)
     )
+    bias = jnp.where(allowed, 0.0, -jnp.inf).astype(jnp.float32)
     d_query_rows, grad_ext = attention_grads(
-        allowed.astype(jnp.int32),
+        bias,
         queries.reshape(tok_rows, -1),
         upstream.reshape(tok_rows, -1),
         extended,
         group_size,
         head_size,
         score_scale,
+        128,
+        256,
     )
     d_queries = d_query_rows.reshape(queries.shape)
     own_rows = grad_ext[:, span_blocks * tok_rows :, :]

time: 162 us -> 191 us (1.18)
  Pallas kernels: 33.3 us -> 62.1 us
    pallas_call x1, Pallas kernels: 33.3 us -> 62.1 us  [attention_grads(): pl.pallas_call(functools.partial(attn_kernel, scale=scale, hd=hd, row_chu...]
where the time goes in v5:
time: 191 us; the launch traced here: 190 us
  Pallas kernels  62.1 us (33%)
  waiting for transfers between devices  56.4 us (30%)
  starting transfers between devices  32.2 us (17%)
  blocking collectives  28.5 us (15%)
  local copies, waits for them, and re-layouts  5.21 us (3%)
  other arithmetic  4.72 us (2%)
    pallas_call x1, Pallas kernels, attention_grads(): pl.pallas_call(functools.partial(attn_kernel, scale=scale, hd=hd, row_chu...  62.1 us
    ppermute x8, waiting for transfers between devices, shifted(): return lax.ppermute(value, axis, pairs)  50.4 us
    ppermute x8, starting transfers between devices, shifted(): return lax.ppermute(value, axis, pairs)  28.8 us
    all_to_all x1, blocking collectives, scatter_layers(): lax.all_to_all(pieces, ('section', 'tp'), split_axis=1, concat_axis=1)  15 us
    all_gather x1, blocking collectives, body(): lax.all_gather(chunk.reshape(kinds, rows, -1), 'section', axis=1, tiled=T...  13.5 us
    all_to_all x1, waiting for transfers between devices, body(): lax.all_to_all(shared_kv, 'tp', split_axis=2, concat_axis=1, tiled=True)  5.94 us
    unnamed x10, local copies, waits for them, and re-layouts  4.62 us
  transfers between devices with their start and end apart: 9, of which 6 were waited for; matrix products, arithmetic and copies ran while one was open for 1% of the time, Pallas kernels for 0%

profile of v5, /device:TPU:80, one launch (start us, length us, event | category | flops | bytes accessed | tf_op | source)
XLA Modules:
  0.0 190.0 jit_solution(942068518774682513)
XLA Ops:
  0.6 1.3 copy.11
  1.9 1.1 reshape.35
  3.0 3.4 %all-to-all-start = ((bf16[4,2,16384]{2,1,0:T(2,128)(2,1)}), bf16[4,2,16384]{2,1,0:T(2,128)(2,1)S(1)}, u32[]{:S(2)}, u32[]{:S(2)}) async-start(bf16[4,2,16384]{2,1,0:T(2,128)(2,1)} %reshape.35), calls=%async_computation | async-start | bytes 524288 | tf_op jit(solution)/shard_map/all_to_all | solution.py:121
  6.4 5.9 %all-to-all-done = bf16[4,2,16384]{2,1,0:T(2,128)(2,1)S(1)} async-done(((bf16[4,2,16384]{2,1,0:T(2,128)(2,1)}), bf16[4,2,16384]{2,1,0:T(2,128)(2,1)S(1)}, u32[]{:S(2)}, u32[]{:S(2)}) %all-to-all-start) | async-done | bytes 262176 | tf_op jit(solution)/shard_map/all_to_all | solution.py:121
  13.1 3.8 %collective-permute-start.2 = (bf16[2,256,256]{2,1,0:T(8,128)(2,1)S(1)}, bf16[2,256,256]{2,1,0:T(8,128)(2,1)S(1)}, u32[]{:S(2)}, u32[]{:S(2)}) collective-permute-start(bf16[2,256,256]{2,1,0:T(8,128)(2,1)S(1)} %bitcast.25), channel_id=1, source_target_pairs={{0,8},{4,12},{8,16},{12,20},{16,24},{20,28},{24,32},{28,36},{32,40... | collective-permute-start | bytes 786440 | tf_op jit(solution)/shard_map/ppermute | solution.py:20
  17.0 5.3 %collective-permute-start.1 = (bf16[2,256,256]{2,1,0:T(8,128)(2,1)S(1)}, bf16[2,256,256]{2,1,0:T(8,128)(2,1)S(1)}, u32[]{:S(2)}, u32[]{:S(2)}) collective-permute-start(bf16[2,256,256]{2,1,0:T(8,128)(2,1)S(1)} %bitcast.26), channel_id=1, source_target_pairs={{0,12},{4,16},{8,20},{12,24},{16,28},{20,32},{24,36},{28,40},{32,4... | collective-permute-start | bytes 786440 | tf_op jit(solution)/shard_map/ppermute | solution.py:20
  22.2 3.4 %collective-permute-start = (bf16[2,256,256]{2,1,0:T(8,128)(2,1)S(1)}, bf16[2,256,256]{2,1,0:T(8,128)(2,1)S(1)}, u32[]{:S(2)}, u32[]{:S(2)}) collective-permute-start(bf16[2,256,256]{2,1,0:T(8,128)(2,1)S(1)} %bitcast.27), channel_id=1, source_target_pairs={{0,16},{4,20},{8,24},{12,28},{16,32},{20,36},{24,40},{28,44},{32,4... | collective-permute-start | bytes 786440 | tf_op jit(solution)/shard_map/ppermute | solution.py:20
  25.6 1.6 fusion.2.bias_ref
  27.2 5.1 %collective-permute-start.3 = (bf16[2,256,256]{2,1,0:T(8,128)(2,1)S(1)}, bf16[2,256,256]{2,1,0:T(8,128)(2,1)S(1)}, u32[]{:S(2)}, u32[]{:S(2)}) collective-permute-start(bf16[2,256,256]{2,1,0:T(8,128)(2,1)S(1)} %bitcast.28), channel_id=1, source_target_pairs={{0,4},{4,8},{8,12},{12,16},{16,20},{20,24},{24,28},{28,32},{32,36}... | collective-permute-start | bytes 786440 | tf_op jit(solution)/shard_map/ppermute | solution.py:20
  32.3 13.4 %collective-permute-done = bf16[2,256,256]{2,1,0:T(8,128)(2,1)S(1)} collective-permute-done((bf16[2,256,256]{2,1,0:T(8,128)(2,1)S(1)}, bf16[2,256,256]{2,1,0:T(8,128)(2,1)S(1)}, u32[]{:S(2)}, u32[]{:S(2)}) %collective-permute-start) | collective-permute-done | bytes 262176 | tf_op jit(solution)/shard_map/ppermute | solution.py:20
  45.8 4.5 %collective-permute-done.3 = bf16[2,256,256]{2,1,0:T(8,128)(2,1)S(1)} collective-permute-done((bf16[2,256,256]{2,1,0:T(8,128)(2,1)S(1)}, bf16[2,256,256]{2,1,0:T(8,128)(2,1)S(1)}, u32[]{:S(2)}, u32[]{:S(2)}) %collective-permute-start.3) | collective-permute-done | bytes 262176 | tf_op jit(solution)/shard_map/ppermute | solution.py:20
  50.4 1.0 copy-done
  51.4 62.1 %shard_map.50 = (bf16[256,2048]{1,0:T(8,128)(2,1)}, f32[2,1280,256]{2,1,0:T(8,128)}) custom-call(f32[256,1280]{1,0:T(8,128)} %fusion.2.bias_ref, bf16[256,2048]{1,0:T(8,128)(2,1)} %bitcast.31, bf16[256,2048]{1,0:T(8,128)(2,1)} %bitcast.32, bf16[2,1280,256]{2,1,0:T(8,128)(2,1)} %copy-done, bf16[2,1280,256]{2,1,0:T(8,128)(2,1)} %copy-done), custom_call_target="tpu_custom_call" | custom-call | flops 8053063680 | bytes 8388608 | tf_op jit(solution)/shard_map/pallas_call | solution.py:78
  113.6 1.9 convert.6
  115.5 1.9 %collective-permute-start.4 = (bf16[2,256,256]{2,1,0:T(8,128)(2,1)S(1)}, bf16[2,256,256]{2,1,0:T(8,128)(2,1)S(1)}, u32[]{:S(2)}, u32[]{:S(2)}) collective-permute-start(bf16[2,256,256]{2,1,0:T(8,128)(2,1)S(1)} %get-tuple-element.6), channel_id=1, source_target_pairs={{16,0},{20,4},{24,8},{28,12},{32,16},{36,20},{40,24},{44,28},{48,3... | collective-permute-start | bytes 786440 | tf_op jit(solution)/shard_map/ppermute | solution.py:20
  117.5 5.4 %collective-permute-start.7 = (bf16[2,256,256]{2,1,0:T(8,128)(2,1)S(1)}, bf16[2,256,256]{2,1,0:T(8,128)(2,1)S(1)}, u32[]{:S(2)}, u32[]{:S(2)}) collective-permute-start(bf16[2,256,256]{2,1,0:T(8,128)(2,1)S(1)} %get-tuple-element.7), channel_id=1, source_target_pairs={{4,0},{8,4},{12,8},{16,12},{20,16},{24,20},{28,24},{32,28},{36,32}... | collective-permute-start | bytes 786440 | tf_op jit(solution)/shard_map/ppermute | solution.py:20
  122.9 1.9 %collective-permute-start.6 = (bf16[2,256,256]{2,1,0:T(8,128)(2,1)S(1)}, bf16[2,256,256]{2,1,0:T(8,128)(2,1)S(1)}, u32[]{:S(2)}, u32[]{:S(2)}) collective-permute-start(bf16[2,256,256]{2,1,0:T(8,128)(2,1)S(1)} %get-tuple-element.8), channel_id=1, source_target_pairs={{8,0},{12,4},{16,8},{20,12},{24,16},{28,20},{32,24},{36,28},{40,32... | collective-permute-start | bytes 786440 | tf_op jit(solution)/shard_map/ppermute | solution.py:20
  124.8 1.9 %collective-permute-start.5 = (bf16[2,256,256]{2,1,0:T(8,128)(2,1)S(1)}, bf16[2,256,256]{2,1,0:T(8,128)(2,1)S(1)}, u32[]{:S(2)}, u32[]{:S(2)}) collective-permute-start(bf16[2,256,256]{2,1,0:T(8,128)(2,1)S(1)} %get-tuple-element.9), channel_id=1, source_target_pairs={{12,0},{16,4},{20,8},{24,12},{28,16},{32,20},{36,24},{40,28},{44,3... | collective-permute-start | bytes 786440 | tf_op jit(solution)/shard_map/ppermute | solution.py:20
  126.8 7.6 %collective-permute-done.4 = bf16[2,256,256]{2,1,0:T(8,128)(2,1)S(1)} collective-permute-done((bf16[2,256,256]{2,1,0:T(8,128)(2,1)S(1)}, bf16[2,256,256]{2,1,0:T(8,128)(2,1)S(1)}, u32[]{:S(2)}, u32[]{:S(2)}) %collective-permute-start.4) | collective-permute-done | bytes 262176 | tf_op jit(solution)/shard_map/ppermute | solution.py:20
  134.3 6.4 %collective-permute-done.7 = bf16[2,256,256]{2,1,0:T(8,128)(2,1)S(1)} collective-permute-done((bf16[2,256,256]{2,1,0:T(8,128)(2,1)S(1)}, bf16[2,256,256]{2,1,0:T(8,128)(2,1)S(1)}, u32[]{:S(2)}, u32[]{:S(2)}) %collective-permute-start.7) | collective-permute-done | bytes 262176 | tf_op jit(solution)/shard_map/ppermute | solution.py:20
  140.7 18.6 %collective-permute-done.5 = bf16[2,256,256]{2,1,0:T(8,128)(2,1)S(1)} collective-permute-done((bf16[2,256,256]{2,1,0:T(8,128)(2,1)S(1)}, bf16[2,256,256]{2,1,0:T(8,128)(2,1)S(1)}, u32[]{:S(2)}, u32[]{:S(2)}) %collective-permute-start.5) | collective-permute-done | bytes 262176 | tf_op jit(solution)/shard_map/ppermute | solution.py:20
  159.3 1.2 convert_add_fusion
  160.6 15.0 %all_to_all.23 = f32[2,16,16,256]{3,2,0,1:T(8,128)S(1)} all-to-all(f32[2,16,16,256]{3,2,0,1:T(8,128)S(1)} %copy.14), channel_id=1, replica_groups=mesh['section'=4,'seq'=16,'tp'=4] {'section','tp'}, dimensions={1} | all-to-all | bytes 1048576 | tf_op jit(solution)/shard_map/all_to_all | solution.py:112
  175.7 13.5 %all_gather.3 = f32[2,64,1024]{2,1,0:T(8,128)S(1)} all-gather(f32[2,16,1024]{2,1,0:T(8,128)S(1)} %bitcast.30), channel_id=1, replica_groups=mesh['section'=4,'seq'=16,'tp'=4] {'section'}, dimensions={1}, use_global_device_ids=true | all-gather | bytes 655360 | tf_op jit(solution)/shard_map/all_gather | solution.py:160
  (20 shorter events, 1.9 us)
Async XLA Ops:
  3.0 9.4 %all-to-all-start = ((bf16[4,2,16384]{2,1,0:T(2,128)(2,1)}), bf16[4,2,16384]{2,1,0:T(2,128)(2,1)S(1)}, u32[]{:S(2)}, u32[]{:S(2)}) async-start(bf16[4,2,16384]{2,1,0:T(2,128)(2,1)} %reshape.35), calls=%async_computation | async-start | bytes 524288 | tf_op jit(solution)/shard_map/all_to_all | solution.py:121
  13.1 32.6 %collective-permute-start.2 = (bf16[2,256,256]{2,1,0:T(8,128)(2,1)S(1)}, bf16[2,256,256]{2,1,0:T(8,128)(2,1)S(1)}, u32[]{:S(2)}, u32[]{:S(2)}) collective-permute-start(bf16[2,256,256]{2,1,0:T(8,128)(2,1)S(1)} %bitcast.25), channel_id=1, source_target_pairs={{0,8},{4,12},{8,16},{12,20},{16,24},{20,28},{24,32},{28,36},{32,40... | collective-permute-start | bytes 786440 | tf_op jit(solution)/shard_map/ppermute | solution.py:20
  17.0 28.8 %collective-permute-start.1 = (bf16[2,256,256]{2,1,0:T(8,128)(2,1)S(1)}, bf16[2,256,256]{2,1,0:T(8,128)(2,1)S(1)}, u32[]{:S(2)}, u32[]{:S(2)}) collective-permute-start(bf16[2,256,256]{2,1,0:T(8,128)(2,1)S(1)} %bitcast.26), channel_id=1, source_target_pairs={{0,12},{4,16},{8,20},{12,24},{16,28},{20,32},{24,36},{28,40},{32,4... | collective-permute-start | bytes 786440 | tf_op jit(solution)/shard_map/ppermute | solution.py:20
  22.2 23.5 %collective-permute-start = (bf16[2,256,256]{2,1,0:T(8,128)(2,1)S(1)}, bf16[2,256,256]{2,1,0:T(8,128)(2,1)S(1)}, u32[]{:S(2)}, u32[]{:S(2)}) collective-permute-start(bf16[2,256,256]{2,1,0:T(8,128)(2,1)S(1)} %bitcast.27), channel_id=1, source_target_pairs={{0,16},{4,20},{8,24},{12,28},{16,32},{20,36},{24,40},{28,44},{32,4... | collective-permute-start | bytes 786440 | tf_op jit(solution)/shard_map/ppermute | solution.py:20
  27.2 23.1 %collective-permute-start.3 = (bf16[2,256,256]{2,1,0:T(8,128)(2,1)S(1)}, bf16[2,256,256]{2,1,0:T(8,128)(2,1)S(1)}, u32[]{:S(2)}, u32[]{:S(2)}) collective-permute-start(bf16[2,256,256]{2,1,0:T(8,128)(2,1)S(1)} %bitcast.28), channel_id=1, source_target_pairs={{0,4},{4,8},{8,12},{12,16},{16,20},{20,24},{24,28},{28,32},{32,36}... | collective-permute-start | bytes 786440 | tf_op jit(solution)/shard_map/ppermute | solution.py:20
  50.4 1.1 copy-start
  115.5 18.8 %collective-permute-start.4 = (bf16[2,256,256]{2,1,0:T(8,128)(2,1)S(1)}, bf16[2,256,256]{2,1,0:T(8,128)(2,1)S(1)}, u32[]{:S(2)}, u32[]{:S(2)}) collective-permute-start(bf16[2,256,256]{2,1,0:T(8,128)(2,1)S(1)} %get-tuple-element.6), channel_id=1, source_target_pairs={{16,0},{20,4},{24,8},{28,12},{32,16},{36,20},{40,24},{44,28},{48,3... | collective-permute-start | bytes 786440 | tf_op jit(solution)/shard_map/ppermute | solution.py:20
  117.5 23.3 %collective-permute-start.7 = (bf16[2,256,256]{2,1,0:T(8,128)(2,1)S(1)}, bf16[2,256,256]{2,1,0:T(8,128)(2,1)S(1)}, u32[]{:S(2)}, u32[]{:S(2)}) collective-permute-start(bf16[2,256,256]{2,1,0:T(8,128)(2,1)S(1)} %get-tuple-element.7), channel_id=1, source_target_pairs={{4,0},{8,4},{12,8},{16,12},{20,16},{24,20},{28,24},{32,28},{36,32}... | collective-permute-start | bytes 786440 | tf_op jit(solution)/shard_map/ppermute | solution.py:20
  122.9 17.8 %collective-permute-start.6 = (bf16[2,256,256]{2,1,0:T(8,128)(2,1)S(1)}, bf16[2,256,256]{2,1,0:T(8,128)(2,1)S(1)}, u32[]{:S(2)}, u32[]{:S(2)}) collective-permute-start(bf16[2,256,256]{2,1,0:T(8,128)(2,1)S(1)} %get-tuple-element.8), channel_id=1, source_target_pairs={{8,0},{12,4},{16,8},{20,12},{24,16},{28,20},{32,24},{36,28},{40,32... | collective-permute-start | bytes 786440 | tf_op jit(solution)/shard_map/ppermute | solution.py:20
  124.8 34.5 %collective-permute-start.5 = (bf16[2,256,256]{2,1,0:T(8,128)(2,1)S(1)}, bf16[2,256,256]{2,1,0:T(8,128)(2,1)S(1)}, u32[]{:S(2)}, u32[]{:S(2)}) collective-permute-start(bf16[2,256,256]{2,1,0:T(8,128)(2,1)S(1)} %get-tuple-element.9), channel_id=1, source_target_pairs={{12,0},{16,4},{20,8},{24,12},{28,16},{32,20},{36,24},{40,28},{44,3... | collective-permute-start | bytes 786440 | tf_op jit(solution)/shard_map/ppermute | solution.py:20

commit v6 on v4

--- a/solution.py
+++ b/solution.py
@@ -20,7 +20,8 @@
     return lax.ppermute(value, axis, pairs)
 
 
-def attn_kernel(bias_ref, q_ref, g_ref, k_ref, v_ref, dq_ref, dkv_ref, *, scale, hd, per_step):
+def attn_kernel(bias_ref, q_ref, g_ref, k_ref, v_ref, *rest, scale, hd, per_step):
+    dq_ref, dkv_ref = rest[-2:]
     gi = pl.program_id(1)
     k = k_ref[...]
     v = v_ref[...]
@@ -60,10 +61,9 @@
         dkv_ref[1] += dv
 
 
-def attention_grads(bias, q, g, ext, group, hd, scale, per_step):
-    rows, qcols = q.shape
-    _, ext_rows, kcols = ext.shape
-    heads = kcols // hd
+def attention_grads(bias, q, g, ext, group, hd, scale, per_step, head0, heads, after=()):
+    rows, _ = q.shape
+    _, ext_rows, _ = ext.shape
     steps = group // per_step
     width = per_step * hd
     flops = 6 * 2 * rows * ext_rows * hd * heads * group
@@ -72,26 +72,27 @@
         grid=(heads, steps),
         in_specs=[
             pl.BlockSpec((rows, ext_rows), lambda h, i: (0, 0)),
-            pl.BlockSpec((rows, width), lambda h, i: (0, h * steps + i)),
-            pl.BlockSpec((rows, width), lambda h, i: (0, h * steps + i)),
-            pl.BlockSpec((None, ext_rows, hd), lambda h, i: (0, 0, h)),
-            pl.BlockSpec((None, ext_rows, hd), lambda h, i: (1, 0, h)),
-        ],
+            pl.BlockSpec((rows, width), lambda h, i: (0, (head0 + h) * steps + i)),
+            pl.BlockSpec((rows, width), lambda h, i: (0, (head0 + h) * steps + i)),
+            pl.BlockSpec((None, ext_rows, hd), lambda h, i: (0, 0, head0 + h)),
+            pl.BlockSpec((None, ext_rows, hd), lambda h, i: (1, 0, head0 + h)),
+        ]
+        + [pl.BlockSpec(memory_space=pl.ANY) for _ in after],
         out_specs=[
             pl.BlockSpec((rows, width), lambda h, i: (0, h * steps + i)),
             pl.BlockSpec((2, ext_rows, hd), lambda h, i: (0, 0, h)),
         ],
         out_shape=[
-            jax.ShapeDtypeStruct((rows, qcols), jnp.bfloat16),
-            jax.ShapeDtypeStruct((2, ext_rows, kcols), jnp.float32),
+            jax.ShapeDtypeStruct((rows, heads * group * hd), jnp.bfloat16),
+            jax.ShapeDtypeStruct((2, ext_rows, heads * hd), jnp.float32),
         ],
         compiler_params=pltpu.CompilerParams(dimension_semantics=("arbitrary", "arbitrary")),
         cost_estimate=pl.CostEstimate(
             flops=flops,
             transcendentals=rows * ext_rows * heads * group,
-            bytes_accessed=3 * q.size * 2 + ext.size * 2 + ext.size * 4 + bias.size * 4,
+            bytes_accessed=(3 * rows * group * 2 + ext_rows * 2 * 6) * hd * heads + bias.size * 4,
         ),
-    )(bias, q, g, ext, ext)
+    )(bias, q, g, ext, ext, *after)
 
 
 def scatter_layers(own_rows):
@@ -127,24 +128,27 @@
         & (position * tok_rows - WINDOW + key_ids >= 0)
     )
     bias = jnp.where(allowed, 0.0, -jnp.inf).astype(jnp.float32)
-    d_query_rows, grad_ext = attention_grads(
-        bias,
-        queries.reshape(tok_rows, -1),
-        upstream.reshape(tok_rows, -1),
-        extended,
-        group_size,
-        head_size,
-        score_scale,
-        2,
-    )
-    d_queries = d_query_rows.reshape(queries.shape)
-    own_rows = grad_ext[:, span_blocks * tok_rows :, :]
-    for offset in range(span_blocks):
-        own_rows = own_rows + shifted(
-            grad_ext[:, offset * tok_rows : (offset + 1) * tok_rows, :].astype(jnp.bfloat16),
-            "seq",
-            offset - span_blocks,
-        ).astype(jnp.float32)
+    query_rows = queries.reshape(tok_rows, -1)
+    grad_rows = upstream.reshape(tok_rows, -1)
+    local_heads = extended.shape[2] // head_size
+    d_query_parts = []
+    own_parts = []
+    sent = []
+    for kv_head in range(local_heads):
+        d_query_part, grad_ext = attention_grads(
+            bias, query_rows, grad_rows, extended, group_size, head_size, score_scale, 2, kv_head, 1, sent
+        )
+        d_query_parts.append(d_query_part)
+        sent = [
+            grad_ext[:, offset * tok_rows : (offset + 1) * tok_rows, :].astype(jnp.bfloat16)
+            for offset in range(span_blocks)
+        ]
+        own_rows = grad_ext[:, span_blocks * tok_rows :, :]
+        for offset in range(span_blocks):
+            own_rows = own_rows + shifted(sent[offset], "seq", offset - span_blocks).astype(jnp.float32)
+        own_parts.append(own_rows)
+    d_queries = jnp.concatenate(d_query_parts, axis=1).reshape(queries.shape)
+    own_rows = jnp.concatenate(own_parts, axis=2)
     chunk = scatter_layers(own_rows)
     kinds, rows, tp_peers, cols = chunk.shape
     d_shared_kv = lax.all_gather(chunk.reshape(kinds, rows, -1), "section", axis=1, tiled=True)

time: 161 us -> 160 us (level)
  blocking collectives: 28.5 us -> 13.5 us
  starting transfers between devices: 32.2 us -> 43.3 us
  waiting for transfers between devices: 56.4 us -> 53.3 us
  other arithmetic: 4.72 us -> 7.63 us
  Pallas kernels: 32.7 us -> 35 us
    all_to_all x1 -> x0, blocking collectives: 15 us -> none  [scatter_layers(): lax.all_to_all(pieces, ('section', 'tp'), split_axis=1, concat_axis=1)]
    ppermute x8 -> x12, waiting for transfers between devices: 50.4 us -> 37.6 us  [shifted(): return lax.ppermute(value, axis, pairs)]
    all_to_all x0 -> x1, waiting for transfers between devices: none -> 9.75 us  [scatter_layers(): lax.all_to_all(pieces, ('section', 'tp'), split_axis=1, concat_axis=1)]
    ppermute x8 -> x12, starting transfers between devices: 28.7 us -> 34.9 us  [shifted(): return lax.ppermute(value, axis, pairs)]
    all_to_all x0 -> x1, starting transfers between devices: none -> 4.97 us  [scatter_layers(): lax.all_to_all(pieces, ('section', 'tp'), split_axis=1, concat_axis=1)]
    pallas_call x1 -> x2, Pallas kernels: 32.7 us -> 35 us  [attention_grads(): pl.pallas_call(functools.partial(attn_kernel, scale=scale, hd=hd, per_ste...]
    unnamed x10 -> x22, local copies, waits for them, and re-layouts: 4.62 us -> 4.68 us
  transfers between devices with their start and end apart: 9 -> 14, of which waited for: 6 -> 8; matrix products, arithmetic and copies ran while one was open for 1% -> 3% of each run, Pallas kernels for 0% -> 11%
where the time goes in v6:
time: 160 us
  waiting for transfers between devices  53.3 us (33%)
  starting transfers between devices  43.3 us (27%)
  Pallas kernels  35 us (22%)
  blocking collectives  13.5 us (8%)
  other arithmetic  7.63 us (5%)
  local copies, waits for them, and re-layouts  6.09 us (4%)
    ppermute x12, waiting for transfers between devices, shifted(): return lax.ppermute(value, axis, pairs)  37.6 us
    pallas_call x2, Pallas kernels, attention_grads(): pl.pallas_call(functools.partial(attn_kernel, scale=scale, hd=hd, per_ste...  35 us
    ppermute x12, starting transfers between devices, shifted(): return lax.ppermute(value, axis, pairs)  34.9 us
    all_gather x1, blocking collectives, body(): lax.all_gather(chunk.reshape(kinds, rows, -1), 'section', axis=1, tiled=T...  13.5 us
    all_to_all x1, waiting for transfers between devices, scatter_layers(): lax.all_to_all(pieces, ('section', 'tp'), split_axis=1, concat_axis=1)  9.75 us
    all_to_all x1, waiting for transfers between devices, body(): lax.all_to_all(shared_kv, 'tp', split_axis=2, concat_axis=1, tiled=True)  5.94 us
    all_to_all x1, starting transfers between devices, scatter_layers(): lax.all_to_all(pieces, ('section', 'tp'), split_axis=1, concat_axis=1)  4.97 us
    unnamed x22, local copies, waits for them, and re-layouts  4.68 us
  transfers between devices with their start and end apart: 14, of which 8 were waited for; matrix products, arithmetic and copies ran while one was open for 3% of the time, Pallas kernels for 11%

profile of v6, /device:TPU:80, one launch (start us, length us, event | category | flops | bytes accessed | tf_op | source)
XLA Modules:
  0.0 159.7 jit_solution(18320040848741715065)
XLA Ops:
  3.0 3.4 %all-to-all-start = ((bf16[4,2,16384]{2,1,0:T(2,128)(2,1)}), bf16[4,2,16384]{2,1,0:T(2,128)(2,1)S(1)}, u32[]{:S(2)}, u32[]{:S(2)}) async-start(bf16[4,2,16384]{2,1,0:T(2,128)(2,1)} %reshape.35), calls=%async_computation | async-start | bytes 524288 | tf_op jit(solution)/shard_map/all_to_all | solution.py:113
  6.4 5.9 %all-to-all-done = bf16[4,2,16384]{2,1,0:T(2,128)(2,1)S(1)} async-done(((bf16[4,2,16384]{2,1,0:T(2,128)(2,1)}), bf16[4,2,16384]{2,1,0:T(2,128)(2,1)S(1)}, u32[]{:S(2)}, u32[]{:S(2)}) %all-to-all-start) | async-done | bytes 262176 | tf_op jit(solution)/shard_map/all_to_all | solution.py:113
  13.1 6.4 %collective-permute-start = (bf16[2,256,256]{2,1,0:T(8,128)(2,1)S(1)}, bf16[2,256,256]{2,1,0:T(8,128)(2,1)S(1)}, u32[]{:S(2)}, u32[]{:S(2)}) collective-permute-start(bf16[2,256,256]{2,1,0:T(8,128)(2,1)S(1)} %bitcast.26), channel_id=1, source_target_pairs={{0,16},{4,20},{8,24},{12,28},{16,32},{20,36},{24,40},{28,44},{32,4... | collective-permute-start | bytes 786440 | tf_op jit(solution)/shard_map/ppermute | solution.py:20
  19.5 3.2 %collective-permute-start.1 = (bf16[2,256,256]{2,1,0:T(8,128)(2,1)S(1)}, bf16[2,256,256]{2,1,0:T(8,128)(2,1)S(1)}, u32[]{:S(2)}, u32[]{:S(2)}) collective-permute-start(bf16[2,256,256]{2,1,0:T(8,128)(2,1)S(1)} %bitcast.27), channel_id=1, source_target_pairs={{0,12},{4,16},{8,20},{12,24},{16,28},{20,32},{24,36},{28,40},{32,4... | collective-permute-start | bytes 786440 | tf_op jit(solution)/shard_map/ppermute | solution.py:20
  22.7 2.9 %collective-permute-start.2 = (bf16[2,256,256]{2,1,0:T(8,128)(2,1)S(1)}, bf16[2,256,256]{2,1,0:T(8,128)(2,1)S(1)}, u32[]{:S(2)}, u32[]{:S(2)}) collective-permute-start(bf16[2,256,256]{2,1,0:T(8,128)(2,1)S(1)} %bitcast.28), channel_id=1, source_target_pairs={{0,8},{4,12},{8,16},{12,20},{16,24},{20,28},{24,32},{28,36},{32,40... | collective-permute-start | bytes 786440 | tf_op jit(solution)/shard_map/ppermute | solution.py:20
  27.3 5.1 %collective-permute-start.3 = (bf16[2,256,256]{2,1,0:T(8,128)(2,1)S(1)}, bf16[2,256,256]{2,1,0:T(8,128)(2,1)S(1)}, u32[]{:S(2)}, u32[]{:S(2)}) collective-permute-start(bf16[2,256,256]{2,1,0:T(8,128)(2,1)S(1)} %bitcast.29), channel_id=1, source_target_pairs={{0,4},{4,8},{8,12},{12,16},{16,20},{20,24},{24,28},{28,32},{32,36}... | collective-permute-start | bytes 786440 | tf_op jit(solution)/shard_map/ppermute | solution.py:20
  32.4 10.6 %collective-permute-done.1 = bf16[2,256,256]{2,1,0:T(8,128)(2,1)S(1)} collective-permute-done((bf16[2,256,256]{2,1,0:T(8,128)(2,1)S(1)}, bf16[2,256,256]{2,1,0:T(8,128)(2,1)S(1)}, u32[]{:S(2)}, u32[]{:S(2)}) %collective-permute-start.1) | collective-permute-done | bytes 262176 | tf_op jit(solution)/shard_map/ppermute | solution.py:20
  43.0 5.6 %collective-permute-done.2 = bf16[2,256,256]{2,1,0:T(8,128)(2,1)S(1)} collective-permute-done((bf16[2,256,256]{2,1,0:T(8,128)(2,1)S(1)}, bf16[2,256,256]{2,1,0:T(8,128)(2,1)S(1)}, u32[]{:S(2)}, u32[]{:S(2)}) %collective-permute-start.2) | collective-permute-done | bytes 262176 | tf_op jit(solution)/shard_map/ppermute | solution.py:20
  48.6 4.2 %collective-permute-done.3 = bf16[2,256,256]{2,1,0:T(8,128)(2,1)S(1)} collective-permute-done((bf16[2,256,256]{2,1,0:T(8,128)(2,1)S(1)}, bf16[2,256,256]{2,1,0:T(8,128)(2,1)S(1)}, u32[]{:S(2)}, u32[]{:S(2)}) %collective-permute-start.3) | collective-permute-done | bytes 262176 | tf_op jit(solution)/shard_map/ppermute | solution.py:20
  53.9 17.5 %shard_map.50 = (bf16[256,1024]{1,0:T(8,128)(2,1)}, f32[2,1280,128]{2,1,0:T(8,128)}) custom-call(f32[256,1280]{1,0:T(8,128)} %fusion.2.bias_ref, bf16[256,2048]{1,0:T(8,128)(2,1)} %bitcast.32, bf16[256,2048]{1,0:T(8,128)(2,1)} %bitcast.34, bf16[2,1280,256]{2,1,0:T(8,128)(2,1)} %copy-done.6, bf16[2,1280,256]{2,1,0:T(8,128)(2,1)} %copy-done.6), custom_call_target="tpu_custom_call" | custom-call | flops 4026531840 | bytes 4849664 | tf_op jit(solution)/shard_map/pallas_call | solution.py:70
  72.9 1.9 %collective-permute-start.4 = (bf16[2,256,128]{2,1,0:T(8,128)(2,1)S(1)}, bf16[2,256,128]{2,1,0:T(8,128)(2,1)S(1)}, u32[]{:S(2)}, u32[]{:S(2)}) collective-permute-start(bf16[2,256,128]{2,1,0:T(8,128)(2,1)S(1)} %get-tuple-element.17.rest_0_), channel_id=1, source_target_pairs={{16,0},{20,4},{24,8},{28,12},{32,16},{36,20},{40,24},{44,28},{48,3... | collective-permute-start | bytes 393224 | tf_op jit(solution)/shard_map/ppermute | solution.py:20
  74.8 1.9 %collective-permute-start.5 = (bf16[2,256,128]{2,1,0:T(8,128)(2,1)S(1)}, bf16[2,256,128]{2,1,0:T(8,128)(2,1)S(1)}, u32[]{:S(2)}, u32[]{:S(2)}) collective-permute-start(bf16[2,256,128]{2,1,0:T(8,128)(2,1)S(1)} %get-tuple-element.16.rest_1_), channel_id=1, source_target_pairs={{12,0},{16,4},{20,8},{24,12},{28,16},{32,20},{36,24},{40,28},{44,3... | collective-permute-start | bytes 393224 | tf_op jit(solution)/shard_map/ppermute | solution.py:20
  76.7 1.9 %collective-permute-start.6 = (bf16[2,256,128]{2,1,0:T(8,128)(2,1)S(1)}, bf16[2,256,128]{2,1,0:T(8,128)(2,1)S(1)}, u32[]{:S(2)}, u32[]{:S(2)}) collective-permute-start(bf16[2,256,128]{2,1,0:T(8,128)(2,1)S(1)} %get-tuple-element.15.rest_2_), channel_id=1, source_target_pairs={{8,0},{12,4},{16,8},{20,12},{24,16},{28,20},{32,24},{36,28},{40,32... | collective-permute-start | bytes 393224 | tf_op jit(solution)/shard_map/ppermute | solution.py:20
  78.7 3.9 %collective-permute-start.7 = (bf16[2,256,128]{2,1,0:T(8,128)(2,1)S(1)}, bf16[2,256,128]{2,1,0:T(8,128)(2,1)S(1)}, u32[]{:S(2)}, u32[]{:S(2)}) collective-permute-start(bf16[2,256,128]{2,1,0:T(8,128)(2,1)S(1)} %get-tuple-element.14.rest_3_), channel_id=1, source_target_pairs={{4,0},{8,4},{12,8},{16,12},{20,16},{24,20},{28,24},{32,28},{36,32}... | collective-permute-start | bytes 393224 | tf_op jit(solution)/shard_map/ppermute | solution.py:20
  82.6 17.5 %shard_map.51 = (bf16[256,1024]{1,0:T(8,128)(2,1)}, f32[2,1280,128]{2,1,0:T(8,128)}) custom-call(f32[256,1280]{1,0:T(8,128)} %fusion.2.bias_ref, bf16[256,2048]{1,0:T(8,128)(2,1)} %bitcast.33, bf16[256,2048]{1,0:T(8,128)(2,1)} %bitcast.35, bf16[2,1280,256]{2,1,0:T(8,128)(2,1)} %copy-done.6, bf16[2,1280,256]{2,1,0:T(8,128)(2,1)} %copy-done.6, ...), custom_call_target="tpu_custom_call" | custom-call | flops 4026531840 | bytes 4849664 | tf_op jit(solution)/shard_map/pallas_call | solution.py:70
  101.5 1.9 %collective-permute-start.10 = (bf16[2,256,128]{2,1,0:T(8,128)(2,1)S(1)}, bf16[2,256,128]{2,1,0:T(8,128)(2,1)S(1)}, u32[]{:S(2)}, u32[]{:S(2)}) collective-permute-start(bf16[2,256,128]{2,1,0:T(8,128)(2,1)S(1)} %get-tuple-element.12), channel_id=1, source_target_pairs={{8,0},{12,4},{16,8},{20,12},{24,16},{28,20},{32,24},{36,28},{40,32... | collective-permute-start | bytes 393224 | tf_op jit(solution)/shard_map/ppermute | solution.py:20
  103.5 1.9 %collective-permute-start.11 = (bf16[2,256,128]{2,1,0:T(8,128)(2,1)S(1)}, bf16[2,256,128]{2,1,0:T(8,128)(2,1)S(1)}, u32[]{:S(2)}, u32[]{:S(2)}) collective-permute-start(bf16[2,256,128]{2,1,0:T(8,128)(2,1)S(1)} %get-tuple-element.11), channel_id=1, source_target_pairs={{4,0},{8,4},{12,8},{16,12},{20,16},{24,20},{28,24},{32,28},{36,32}... | collective-permute-start | bytes 393224 | tf_op jit(solution)/shard_map/ppermute | solution.py:20
  105.4 1.9 %collective-permute-start.8 = (bf16[2,256,128]{2,1,0:T(8,128)(2,1)S(1)}, bf16[2,256,128]{2,1,0:T(8,128)(2,1)S(1)}, u32[]{:S(2)}, u32[]{:S(2)}) collective-permute-start(bf16[2,256,128]{2,1,0:T(8,128)(2,1)S(1)} %get-tuple-element.10), channel_id=1, source_target_pairs={{16,0},{20,4},{24,8},{28,12},{32,16},{36,20},{40,24},{44,28},{48,3... | collective-permute-start | bytes 393224 | tf_op jit(solution)/shard_map/ppermute | solution.py:20
  110.3 3.4 %collective-permute-done.11 = bf16[2,256,128]{2,1,0:T(8,128)(2,1)S(1)} collective-permute-done((bf16[2,256,128]{2,1,0:T(8,128)(2,1)S(1)}, bf16[2,256,128]{2,1,0:T(8,128)(2,1)S(1)}, u32[]{:S(2)}, u32[]{:S(2)}) %collective-permute-start.11) | collective-permute-done | bytes 131104 | tf_op jit(solution)/shard_map/ppermute | solution.py:20
  113.8 6.7 %collective-permute-done.8 = bf16[2,256,128]{2,1,0:T(8,128)(2,1)S(1)} collective-permute-done((bf16[2,256,128]{2,1,0:T(8,128)(2,1)S(1)}, bf16[2,256,128]{2,1,0:T(8,128)(2,1)S(1)}, u32[]{:S(2)}, u32[]{:S(2)}) %collective-permute-start.8) | collective-permute-done | bytes 131104 | tf_op jit(solution)/shard_map/ppermute | solution.py:20
  120.5 7.0 %collective-permute-done.9 = bf16[2,256,128]{2,1,0:T(8,128)(2,1)S(1)} collective-permute-done((bf16[2,256,128]{2,1,0:T(8,128)(2,1)S(1)}, bf16[2,256,128]{2,1,0:T(8,128)(2,1)S(1)}, u32[]{:S(2)}, u32[]{:S(2)}) %collective-permute-start.9) | collective-permute-done | bytes 131104 | tf_op jit(solution)/shard_map/ppermute | solution.py:20
  129.5 5.0 %all-to-all-start.1 = ((f32[2,16,16,256]{3,2,0,1:T(8,128)}), f32[2,16,16,256]{3,2,0,1:T(8,128)S(1)}, u32[]{:S(2)}, u32[]{:S(2)}) async-start(f32[2,16,16,256]{3,2,0,1:T(8,128)} %copy.14), calls=%async_computation.1 | async-start | bytes 1048576 | tf_op jit(solution)/shard_map/all_to_all | solution.py:104
  135.6 9.7 %all-to-all-done.1 = f32[2,16,16,256]{3,2,0,1:T(8,128)S(1)} async-done(((f32[2,16,16,256]{3,2,0,1:T(8,128)}), f32[2,16,16,256]{3,2,0,1:T(8,128)S(1)}, u32[]{:S(2)}, u32[]{:S(2)}) %all-to-all-start.1) | async-done | bytes 524320 | tf_op jit(solution)/shard_map/all_to_all | solution.py:104
  145.4 13.5 %all_gather.3 = f32[2,64,1024]{2,1,0:T(8,128)S(1)} all-gather(f32[2,16,1024]{2,1,0:T(8,128)S(1)} %bitcast.31), channel_id=1, replica_groups=mesh['section'=4,'seq'=16,'tp'=4] {'section'}, dimensions={1}, use_global_device_ids=true | all-gather | bytes 655360 | tf_op jit(solution)/shard_map/all_gather | solution.py:154
  (47 shorter events, 15.7 us)
Async XLA Ops:
  3.0 9.4 %all-to-all-start = ((bf16[4,2,16384]{2,1,0:T(2,128)(2,1)}), bf16[4,2,16384]{2,1,0:T(2,128)(2,1)S(1)}, u32[]{:S(2)}, u32[]{:S(2)}) async-start(bf16[4,2,16384]{2,1,0:T(2,128)(2,1)} %reshape.35), calls=%async_computation | async-start | bytes 524288 | tf_op jit(solution)/shard_map/all_to_all | solution.py:113
  13.1 19.2 %collective-permute-start = (bf16[2,256,256]{2,1,0:T(8,128)(2,1)S(1)}, bf16[2,256,256]{2,1,0:T(8,128)(2,1)S(1)}, u32[]{:S(2)}, u32[]{:S(2)}) collective-permute-start(bf16[2,256,256]{2,1,0:T(8,128)(2,1)S(1)} %bitcast.26), channel_id=1, source_target_pairs={{0,16},{4,20},{8,24},{12,28},{16,32},{20,36},{24,40},{28,44},{32,4... | collective-permute-start | bytes 786440 | tf_op jit(solution)/shard_map/ppermute | solution.py:20
  19.5 23.4 %collective-permute-start.1 = (bf16[2,256,256]{2,1,0:T(8,128)(2,1)S(1)}, bf16[2,256,256]{2,1,0:T(8,128)(2,1)S(1)}, u32[]{:S(2)}, u32[]{:S(2)}) collective-permute-start(bf16[2,256,256]{2,1,0:T(8,128)(2,1)S(1)} %bitcast.27), channel_id=1, source_target_pairs={{0,12},{4,16},{8,20},{12,24},{16,28},{20,32},{24,36},{28,40},{32,4... | collective-permute-start | bytes 786440 | tf_op jit(solution)/shard_map/ppermute | solution.py:20
  22.7 25.9 %collective-permute-start.2 = (bf16[2,256,256]{2,1,0:T(8,128)(2,1)S(1)}, bf16[2,256,256]{2,1,0:T(8,128)(2,1)S(1)}, u32[]{:S(2)}, u32[]{:S(2)}) collective-permute-start(bf16[2,256,256]{2,1,0:T(8,128)(2,1)S(1)} %bitcast.28), channel_id=1, source_target_pairs={{0,8},{4,12},{8,16},{12,20},{16,24},{20,28},{24,32},{28,36},{32,40... | collective-permute-start | bytes 786440 | tf_op jit(solution)/shard_map/ppermute | solution.py:20
  27.3 25.6 %collective-permute-start.3 = (bf16[2,256,256]{2,1,0:T(8,128)(2,1)S(1)}, bf16[2,256,256]{2,1,0:T(8,128)(2,1)S(1)}, u32[]{:S(2)}, u32[]{:S(2)}) collective-permute-start(bf16[2,256,256]{2,1,0:T(8,128)(2,1)S(1)} %bitcast.29), channel_id=1, source_target_pairs={{0,4},{4,8},{8,12},{12,16},{16,20},{20,24},{24,28},{28,32},{32,36}... | collective-permute-start | bytes 786440 | tf_op jit(solution)/shard_map/ppermute | solution.py:20
  52.9 1.1 copy-start.6
  72.8 9.7 %copy-start.2 = (bf16[2,256,128]{2,1,0:T(8,128)(2,1)}, bf16[2,256,128]{2,1,0:T(8,128)(2,1)S(1)}, u32[]{:S(2)}) copy-start(bf16[2,256,128]{2,1,0:T(8,128)(2,1)S(1)} %get-tuple-element.14.rest_3_) | copy-start | bytes 393220
  72.9 9.7 %copy-start.3 = (bf16[2,256,128]{2,1,0:T(8,128)(2,1)}, bf16[2,256,128]{2,1,0:T(8,128)(2,1)S(1)}, u32[]{:S(2)}) copy-start(bf16[2,256,128]{2,1,0:T(8,128)(2,1)S(1)} %get-tuple-element.15.rest_2_) | copy-start | bytes 393220
  72.9 9.7 %copy-start.4 = (bf16[2,256,128]{2,1,0:T(8,128)(2,1)}, bf16[2,256,128]{2,1,0:T(8,128)(2,1)S(1)}, u32[]{:S(2)}) copy-start(bf16[2,256,128]{2,1,0:T(8,128)(2,1)S(1)} %get-tuple-element.16.rest_1_) | copy-start | bytes 393220
  72.9 9.7 %copy-start.5 = (bf16[2,256,128]{2,1,0:T(8,128)(2,1)}, bf16[2,256,128]{2,1,0:T(8,128)(2,1)S(1)}, u32[]{:S(2)}) copy-start(bf16[2,256,128]{2,1,0:T(8,128)(2,1)S(1)} %get-tuple-element.17.rest_0_) | copy-start | bytes 393220
  72.9 30.6 %collective-permute-start.4 = (bf16[2,256,128]{2,1,0:T(8,128)(2,1)S(1)}, bf16[2,256,128]{2,1,0:T(8,128)(2,1)S(1)}, u32[]{:S(2)}, u32[]{:S(2)}) collective-permute-start(bf16[2,256,128]{2,1,0:T(8,128)(2,1)S(1)} %get-tuple-element.17.rest_0_), channel_id=1, source_target_pairs={{16,0},{20,4},{24,8},{28,12},{32,16},{36,20},{40,24},{44,28},{48,3... | collective-permute-start | bytes 393224 | tf_op jit(solution)/shard_map/ppermute | solution.py:20
  74.8 30.6 %collective-permute-start.5 = (bf16[2,256,128]{2,1,0:T(8,128)(2,1)S(1)}, bf16[2,256,128]{2,1,0:T(8,128)(2,1)S(1)}, u32[]{:S(2)}, u32[]{:S(2)}) collective-permute-start(bf16[2,256,128]{2,1,0:T(8,128)(2,1)S(1)} %get-tuple-element.16.rest_1_), channel_id=1, source_target_pairs={{12,0},{16,4},{20,8},{24,12},{28,16},{32,20},{36,24},{40,28},{44,3... | collective-permute-start | bytes 393224 | tf_op jit(solution)/shard_map/ppermute | solution.py:20
  76.7 30.6 %collective-permute-start.6 = (bf16[2,256,128]{2,1,0:T(8,128)(2,1)S(1)}, bf16[2,256,128]{2,1,0:T(8,128)(2,1)S(1)}, u32[]{:S(2)}, u32[]{:S(2)}) collective-permute-start(bf16[2,256,128]{2,1,0:T(8,128)(2,1)S(1)} %get-tuple-element.15.rest_2_), channel_id=1, source_target_pairs={{8,0},{12,4},{16,8},{20,12},{24,16},{28,20},{32,24},{36,28},{40,32... | collective-permute-start | bytes 393224 | tf_op jit(solution)/shard_map/ppermute | solution.py:20
  78.7 30.6 %collective-permute-start.7 = (bf16[2,256,128]{2,1,0:T(8,128)(2,1)S(1)}, bf16[2,256,128]{2,1,0:T(8,128)(2,1)S(1)}, u32[]{:S(2)}, u32[]{:S(2)}) collective-permute-start(bf16[2,256,128]{2,1,0:T(8,128)(2,1)S(1)} %get-tuple-element.14.rest_3_), channel_id=1, source_target_pairs={{4,0},{8,4},{12,8},{16,12},{20,16},{24,20},{28,24},{32,28},{36,32}... | collective-permute-start | bytes 393224 | tf_op jit(solution)/shard_map/ppermute | solution.py:20
  101.5 8.8 %collective-permute-start.10 = (bf16[2,256,128]{2,1,0:T(8,128)(2,1)S(1)}, bf16[2,256,128]{2,1,0:T(8,128)(2,1)S(1)}, u32[]{:S(2)}, u32[]{:S(2)}) collective-permute-start(bf16[2,256,128]{2,1,0:T(8,128)(2,1)S(1)} %get-tuple-element.12), channel_id=1, source_target_pairs={{8,0},{12,4},{16,8},{20,12},{24,16},{28,20},{32,24},{36,28},{40,32... | collective-permute-start | bytes 393224 | tf_op jit(solution)/shard_map/ppermute | solution.py:20
  103.5 10.3 %collective-permute-start.11 = (bf16[2,256,128]{2,1,0:T(8,128)(2,1)S(1)}, bf16[2,256,128]{2,1,0:T(8,128)(2,1)S(1)}, u32[]{:S(2)}, u32[]{:S(2)}) collective-permute-start(bf16[2,256,128]{2,1,0:T(8,128)(2,1)S(1)} %get-tuple-element.11), channel_id=1, source_target_pairs={{4,0},{8,4},{12,8},{16,12},{20,16},{24,20},{28,24},{32,28},{36,32}... | collective-permute-start | bytes 393224 | tf_op jit(solution)/shard_map/ppermute | solution.py:20
  105.4 15.1 %collective-permute-start.8 = (bf16[2,256,128]{2,1,0:T(8,128)(2,1)S(1)}, bf16[2,256,128]{2,1,0:T(8,128)(2,1)S(1)}, u32[]{:S(2)}, u32[]{:S(2)}) collective-permute-start(bf16[2,256,128]{2,1,0:T(8,128)(2,1)S(1)} %get-tuple-element.10), channel_id=1, source_target_pairs={{16,0},{20,4},{24,8},{28,12},{32,16},{36,20},{40,24},{44,28},{48,3... | collective-permute-start | bytes 393224 | tf_op jit(solution)/shard_map/ppermute | solution.py:20
  107.4 20.2 %collective-permute-start.9 = (bf16[2,256,128]{2,1,0:T(8,128)(2,1)S(1)}, bf16[2,256,128]{2,1,0:T(8,128)(2,1)S(1)}, u32[]{:S(2)}, u32[]{:S(2)}) collective-permute-start(bf16[2,256,128]{2,1,0:T(8,128)(2,1)S(1)} %get-tuple-element.13), channel_id=1, source_target_pairs={{12,0},{16,4},{20,8},{24,12},{28,16},{32,20},{36,24},{40,28},{44,3... | collective-permute-start | bytes 393224 | tf_op jit(solution)/shard_map/ppermute | solution.py:20
  128.6 5.9 %copy-start = (bf16[256,1024]{1,0:T(8,128)(2,1)S(1)}, bf16[256,1024]{1,0:T(8,128)(2,1)}, u32[]{:S(2)}) copy-start(bf16[256,1024]{1,0:T(8,128)(2,1)} %get-tuple-element.6) | copy-start | bytes 1572868
  128.7 5.8 %copy-start.1 = (bf16[256,1024]{1,0:T(8,128)(2,1)S(1)}, bf16[256,1024]{1,0:T(8,128)(2,1)}, u32[]{:S(2)}) copy-start(bf16[256,1024]{1,0:T(8,128)(2,1)} %get-tuple-element.8) | copy-start | bytes 1572868
  129.5 15.8 %all-to-all-start.1 = ((f32[2,16,16,256]{3,2,0,1:T(8,128)}), f32[2,16,16,256]{3,2,0,1:T(8,128)S(1)}, u32[]{:S(2)}, u32[]{:S(2)}) async-start(f32[2,16,16,256]{3,2,0,1:T(8,128)} %copy.14), calls=%async_computation.1 | async-start | bytes 1048576 | tf_op jit(solution)/shard_map/all_to_all | solution.py:104

commit v7 on v6

--- a/solution.py
+++ b/solution.py
@@ -116,8 +116,13 @@
     group_size = QH // KVH
     span_blocks = WINDOW // tok_rows
     score_scale = 1.0 / math.sqrt(head_size)
-    earlier = [shifted(local_kv, "seq", span_blocks - offset) for offset in range(span_blocks)]
-    extended = jnp.concatenate(earlier + [local_kv], axis=1)
+    sections = lax.axis_size("section")
+    quarter = tok_rows // sections
+    mine = lax.dynamic_slice_in_dim(local_kv, lax.axis_index("section") * quarter, quarter, axis=1)
+    earlier = jnp.stack([shifted(mine, "seq", span_blocks - offset) for offset in range(span_blocks)], axis=1)
+    gathered = lax.all_gather(earlier, "section", axis=2)
+    kinds, _, _, _, cols = gathered.shape
+    extended = jnp.concatenate([gathered.reshape(kinds, span_blocks * tok_rows, cols), local_kv], axis=1)
     ext_rows = extended.shape[1]
     position = lax.axis_index("seq")
     row_ids = lax.broadcasted_iota(jnp.int32, (tok_rows, ext_rows), 0)

time: 160 us -> 182 us (1.14)
  between operations: 1.03 us -> 14.4 us
  waiting for transfers between devices: 53.3 us -> 57.6 us
  other arithmetic: 7.63 us -> 9.56 us
    all_gather x0 -> x1, waiting for transfers between devices: none -> 25 us  [body(): gathered = lax.all_gather(earlier, 'section', axis=2)]
    ppermute x12, waiting for transfers between devices: 37.6 us -> 16.9 us  [shifted(): return lax.ppermute(value, axis, pairs)]
    unnamed x22 -> x16, local copies, waits for them, and re-layouts: 4.68 us -> 3.53 us
  transfers between devices with their start and end apart: 14 -> 15, of which waited for: 8 -> 7; matrix products, arithmetic and copies ran while one was open for 3% -> 3% of each run, Pallas kernels for 11% -> 10%
where the time goes in v7:
time: 182 us; the launch traced here: 181 us
  waiting for transfers between devices  57.6 us (32%)
  starting transfers between devices  44.4 us (24%)
  Pallas kernels  34.9 us (19%)
  between operations  14.4 us (8%)
  blocking collectives  13.5 us (7%)
  other arithmetic  9.56 us (5%)
  local copies, waits for them, and re-layouts  6.22 us (3%)
    ppermute x12, starting transfers between devices, shifted(): return lax.ppermute(value, axis, pairs)  36.2 us
    pallas_call x2, Pallas kernels, attention_grads(): pl.pallas_call(functools.partial(attn_kernel, scale=scale, hd=hd, per_ste...  34.9 us
    all_gather x1, waiting for transfers between devices, body(): gathered = lax.all_gather(earlier, 'section', axis=2)  25 us
    ppermute x12, waiting for transfers between devices, shifted(): return lax.ppermute(value, axis, pairs)  16.9 us
    all_gather x1, blocking collectives, body(): lax.all_gather(chunk.reshape(kinds, rows, -1), 'section', axis=1, tiled=T...  13.5 us
    all_to_all x1, waiting for transfers between devices, scatter_layers(): lax.all_to_all(pieces, ('section', 'tp'), split_axis=1, concat_axis=1)  9.75 us
    all_to_all x1, waiting for transfers between devices, body(): lax.all_to_all(shared_kv, 'tp', split_axis=2, concat_axis=1, tiled=True)  5.92 us
    all_to_all x1, starting transfers between devices, scatter_layers(): lax.all_to_all(pieces, ('section', 'tp'), split_axis=1, concat_axis=1)  4.82 us
  transfers between devices with their start and end apart: 15, of which 7 were waited for; matrix products, arithmetic and copies ran while one was open for 3% of the time, Pallas kernels for 10%

profile of v7, /device:TPU:80, one launch (start us, length us, event | category | flops | bytes accessed | tf_op | source)
XLA Modules:
  0.0 180.7 jit_solution(4881701133993131361)
XLA Ops:
  9.5 3.4 %all-to-all-start = ((bf16[4,2,16384]{2,1,0:T(2,128)(2,1)}), bf16[4,2,16384]{2,1,0:T(2,128)(2,1)S(1)}, u32[]{:S(2)}, u32[]{:S(2)}) async-start(bf16[4,2,16384]{2,1,0:T(2,128)(2,1)} %reshape.41), calls=%async_computation | async-start | bytes 524288 | tf_op jit(solution)/shard_map/all_to_all | solution.py:113
  13.0 5.9 %all-to-all-done = bf16[4,2,16384]{2,1,0:T(2,128)(2,1)S(1)} async-done(((bf16[4,2,16384]{2,1,0:T(2,128)(2,1)}), bf16[4,2,16384]{2,1,0:T(2,128)(2,1)S(1)}, u32[]{:S(2)}, u32[]{:S(2)}) %all-to-all-start) | async-done | bytes 262176 | tf_op jit(solution)/shard_map/all_to_all | solution.py:113
  19.7 6.4 %collective-permute-start = (bf16[2,64,256]{2,1,0:T(8,128)(2,1)S(1)}, bf16[2,64,256]{2,1,0:T(8,128)(2,1)S(1)}, u32[]{:S(2)}, u32[]{:S(2)}) collective-permute-start(bf16[2,64,256]{2,1,0:T(8,128)(2,1)S(1)} %constant_dynamic-slice_fusion), channel_id=1, source_target_pairs={{0,16},{4,20},{8,24},{12,28},{16,32},{20,36},{24,40},{28,44},{32,4... | collective-permute-start | bytes 196616 | tf_op jit(solution)/shard_map/ppermute | solution.py:20
  26.1 3.2 %collective-permute-start.1 = (bf16[2,64,256]{2,1,0:T(8,128)(2,1)S(1)}, bf16[2,64,256]{2,1,0:T(8,128)(2,1)S(1)}, u32[]{:S(2)}, u32[]{:S(2)}) collective-permute-start(bf16[2,64,256]{2,1,0:T(8,128)(2,1)S(1)} %constant_dynamic-slice_fusion), channel_id=1, source_target_pairs={{0,12},{4,16},{8,20},{12,24},{16,28},{20,32},{24,36},{28,40},{32,4... | collective-permute-start | bytes 196616 | tf_op jit(solution)/shard_map/ppermute | solution.py:20
  29.3 2.9 %collective-permute-start.2 = (bf16[2,64,256]{2,1,0:T(8,128)(2,1)S(1)}, bf16[2,64,256]{2,1,0:T(8,128)(2,1)S(1)}, u32[]{:S(2)}, u32[]{:S(2)}) collective-permute-start(bf16[2,64,256]{2,1,0:T(8,128)(2,1)S(1)} %constant_dynamic-slice_fusion), channel_id=1, source_target_pairs={{0,8},{4,12},{8,16},{12,20},{16,24},{20,28},{24,32},{28,36},{32,40... | collective-permute-start | bytes 196616 | tf_op jit(solution)/shard_map/ppermute | solution.py:20
  32.2 5.1 %collective-permute-start.3 = (bf16[2,64,256]{2,1,0:T(8,128)(2,1)S(1)}, bf16[2,64,256]{2,1,0:T(8,128)(2,1)S(1)}, u32[]{:S(2)}, u32[]{:S(2)}) collective-permute-start(bf16[2,64,256]{2,1,0:T(8,128)(2,1)S(1)} %constant_dynamic-slice_fusion), channel_id=1, source_target_pairs={{0,4},{4,8},{8,12},{12,16},{16,20},{20,24},{24,28},{28,32},{32,36}... | collective-permute-start | bytes 196616 | tf_op jit(solution)/shard_map/ppermute | solution.py:20
  37.3 2.5 %collective-permute-done.3 = bf16[2,64,256]{2,1,0:T(8,128)(2,1)S(1)} collective-permute-done((bf16[2,64,256]{2,1,0:T(8,128)(2,1)S(1)}, bf16[2,64,256]{2,1,0:T(8,128)(2,1)S(1)}, u32[]{:S(2)}, u32[]{:S(2)}) %collective-permute-start.3) | collective-permute-done | bytes 65568 | tf_op jit(solution)/shard_map/ppermute | solution.py:20
  42.3 25.0 %all-gather.3.cloned.1.call-done = bf16[2,4,256,256]{3,2,0,1:T(8,128)(2,1)} async-done(((bf16[2,4,64,256]{3,2,0,1:T(8,128)(2,1)}), bf16[2,4,256,256]{3,2,0,1:T(8,128)(2,1)}) %all-gather.3.cloned.1.call-update) | async-done | bytes 1048592 | tf_op jit(solution)/shard_map/all_gather | solution.py:123
  69.8 17.4 %shard_map.50 = (bf16[256,1024]{1,0:T(8,128)(2,1)}, f32[2,1280,128]{2,1,0:T(8,128)}) custom-call(f32[256,1280]{1,0:T(8,128)} %fusion.2.bias_ref, bf16[256,2048]{1,0:T(8,128)(2,1)} %bitcast.39, bf16[256,2048]{1,0:T(8,128)(2,1)} %bitcast.41, bf16[2,1280,256]{2,1,0:T(8,128)(2,1)} %pad_maximum_fusion.k_ref.v_ref, bf16[2,1280,256]{2,1,0:T(8,128)(2,1)} %pad_maximum_fusion.k_ref.v_ref), custom_call_target="tpu_custom_call" | custom-call | flops 4026531840 | bytes 4849664 | tf_op jit(solution)/shard_map/pallas_call | solution.py:70
  88.7 2.3 %collective-permute-start.4 = (bf16[2,256,128]{2,1,0:T(8,128)(2,1)S(1)}, bf16[2,256,128]{2,1,0:T(8,128)(2,1)S(1)}, u32[]{:S(2)}, u32[]{:S(2)}) collective-permute-start(bf16[2,256,128]{2,1,0:T(8,128)(2,1)S(1)} %get-tuple-element.17.rest_0_), channel_id=1, source_target_pairs={{16,0},{20,4},{24,8},{28,12},{32,16},{36,20},{40,24},{44,28},{48,3... | collective-permute-start | bytes 393224 | tf_op jit(solution)/shard_map/ppermute | solution.py:20
  91.0 1.9 %collective-permute-start.5 = (bf16[2,256,128]{2,1,0:T(8,128)(2,1)S(1)}, bf16[2,256,128]{2,1,0:T(8,128)(2,1)S(1)}, u32[]{:S(2)}, u32[]{:S(2)}) collective-permute-start(bf16[2,256,128]{2,1,0:T(8,128)(2,1)S(1)} %get-tuple-element.16.rest_1_), channel_id=1, source_target_pairs={{12,0},{16,4},{20,8},{24,12},{28,16},{32,20},{36,24},{40,28},{44,3... | collective-permute-start | bytes 393224 | tf_op jit(solution)/shard_map/ppermute | solution.py:20
  92.9 1.9 %collective-permute-start.6 = (bf16[2,256,128]{2,1,0:T(8,128)(2,1)S(1)}, bf16[2,256,128]{2,1,0:T(8,128)(2,1)S(1)}, u32[]{:S(2)}, u32[]{:S(2)}) collective-permute-start(bf16[2,256,128]{2,1,0:T(8,128)(2,1)S(1)} %get-tuple-element.15.rest_2_), channel_id=1, source_target_pairs={{8,0},{12,4},{16,8},{20,12},{24,16},{28,20},{32,24},{36,28},{40,32... | collective-permute-start | bytes 393224 | tf_op jit(solution)/shard_map/ppermute | solution.py:20
  94.9 4.2 %collective-permute-start.7 = (bf16[2,256,128]{2,1,0:T(8,128)(2,1)S(1)}, bf16[2,256,128]{2,1,0:T(8,128)(2,1)S(1)}, u32[]{:S(2)}, u32[]{:S(2)}) collective-permute-start(bf16[2,256,128]{2,1,0:T(8,128)(2,1)S(1)} %get-tuple-element.14.rest_3_), channel_id=1, source_target_pairs={{4,0},{8,4},{12,8},{16,12},{20,16},{24,20},{28,24},{32,28},{36,32}... | collective-permute-start | bytes 393224 | tf_op jit(solution)/shard_map/ppermute | solution.py:20
  99.2 17.5 %shard_map.51 = (bf16[256,1024]{1,0:T(8,128)(2,1)}, f32[2,1280,128]{2,1,0:T(8,128)}) custom-call(f32[256,1280]{1,0:T(8,128)} %fusion.2.bias_ref, bf16[256,2048]{1,0:T(8,128)(2,1)} %bitcast.40, bf16[256,2048]{1,0:T(8,128)(2,1)} %bitcast.42, bf16[2,1280,256]{2,1,0:T(8,128)(2,1)} %pad_maximum_fusion.k_ref.v_ref, ...), custom_call_target="tpu_custom_call" | custom-call | flops 4026531840 | bytes 4849664 | tf_op jit(solution)/shard_map/pallas_call | solution.py:70
  118.1 1.9 %collective-permute-start.10 = (bf16[2,256,128]{2,1,0:T(8,128)(2,1)S(1)}, bf16[2,256,128]{2,1,0:T(8,128)(2,1)S(1)}, u32[]{:S(2)}, u32[]{:S(2)}) collective-permute-start(bf16[2,256,128]{2,1,0:T(8,128)(2,1)S(1)} %get-tuple-element.12), channel_id=1, source_target_pairs={{8,0},{12,4},{16,8},{20,12},{24,16},{28,20},{32,24},{36,28},{40,32... | collective-permute-start | bytes 393224 | tf_op jit(solution)/shard_map/ppermute | solution.py:20
  120.1 2.4 %collective-permute-start.11 = (bf16[2,256,128]{2,1,0:T(8,128)(2,1)S(1)}, bf16[2,256,128]{2,1,0:T(8,128)(2,1)S(1)}, u32[]{:S(2)}, u32[]{:S(2)}) collective-permute-start(bf16[2,256,128]{2,1,0:T(8,128)(2,1)S(1)} %get-tuple-element.11), channel_id=1, source_target_pairs={{4,0},{8,4},{12,8},{16,12},{20,16},{24,20},{28,24},{32,28},{36,32}... | collective-permute-start | bytes 393224 | tf_op jit(solution)/shard_map/ppermute | solution.py:20
  122.5 1.9 %collective-permute-start.8 = (bf16[2,256,128]{2,1,0:T(8,128)(2,1)S(1)}, bf16[2,256,128]{2,1,0:T(8,128)(2,1)S(1)}, u32[]{:S(2)}, u32[]{:S(2)}) collective-permute-start(bf16[2,256,128]{2,1,0:T(8,128)(2,1)S(1)} %get-tuple-element.10), channel_id=1, source_target_pairs={{16,0},{20,4},{24,8},{28,12},{32,16},{36,20},{40,24},{44,28},{48,3... | collective-permute-start | bytes 393224 | tf_op jit(solution)/shard_map/ppermute | solution.py:20
  124.5 1.9 %collective-permute-start.9 = (bf16[2,256,128]{2,1,0:T(8,128)(2,1)S(1)}, bf16[2,256,128]{2,1,0:T(8,128)(2,1)S(1)}, u32[]{:S(2)}, u32[]{:S(2)}) collective-permute-start(bf16[2,256,128]{2,1,0:T(8,128)(2,1)S(1)} %get-tuple-element.13), channel_id=1, source_target_pairs={{12,0},{16,4},{20,8},{24,12},{28,16},{32,20},{36,24},{40,28},{44,3... | collective-permute-start | bytes 393224 | tf_op jit(solution)/shard_map/ppermute | solution.py:20
  127.4 4.7 %collective-permute-done.11 = bf16[2,256,128]{2,1,0:T(8,128)(2,1)S(1)} collective-permute-done((bf16[2,256,128]{2,1,0:T(8,128)(2,1)S(1)}, bf16[2,256,128]{2,1,0:T(8,128)(2,1)S(1)}, u32[]{:S(2)}, u32[]{:S(2)}) %collective-permute-start.11) | collective-permute-done | bytes 131104 | tf_op jit(solution)/shard_map/ppermute | solution.py:20
  132.1 2.4 %collective-permute-done.8 = bf16[2,256,128]{2,1,0:T(8,128)(2,1)S(1)} collective-permute-done((bf16[2,256,128]{2,1,0:T(8,128)(2,1)S(1)}, bf16[2,256,128]{2,1,0:T(8,128)(2,1)S(1)}, u32[]{:S(2)}, u32[]{:S(2)}) %collective-permute-start.8) | collective-permute-done | bytes 131104 | tf_op jit(solution)/shard_map/ppermute | solution.py:20
  134.6 7.2 %collective-permute-done.9 = bf16[2,256,128]{2,1,0:T(8,128)(2,1)S(1)} collective-permute-done((bf16[2,256,128]{2,1,0:T(8,128)(2,1)S(1)}, bf16[2,256,128]{2,1,0:T(8,128)(2,1)S(1)}, u32[]{:S(2)}, u32[]{:S(2)}) %collective-permute-start.9) | collective-permute-done | bytes 131104 | tf_op jit(solution)/shard_map/ppermute | solution.py:20
  143.8 4.8 %all-to-all-start.1 = ((f32[2,16,16,256]{3,2,0,1:T(8,128)}), f32[2,16,16,256]{3,2,0,1:T(8,128)S(1)}, u32[]{:S(2)}, u32[]{:S(2)}) async-start(f32[2,16,16,256]{3,2,0,1:T(8,128)} %copy.17), calls=%async_computation.1 | async-start | bytes 1048576 | tf_op jit(solution)/shard_map/all_to_all | solution.py:104
  149.7 9.7 %all-to-all-done.1 = f32[2,16,16,256]{3,2,0,1:T(8,128)S(1)} async-done(((f32[2,16,16,256]{3,2,0,1:T(8,128)}), f32[2,16,16,256]{3,2,0,1:T(8,128)S(1)}, u32[]{:S(2)}, u32[]{:S(2)}) %all-to-all-start.1) | async-done | bytes 524320 | tf_op jit(solution)/shard_map/all_to_all | solution.py:104
  159.6 13.5 %all_gather.11 = f32[2,64,1024]{2,1,0:T(8,128)S(1)} all-gather(f32[2,16,1024]{2,1,0:T(8,128)S(1)} %bitcast.34), channel_id=1, replica_groups=mesh['section'=4,'seq'=16,'tp'=4] {'section'}, dimensions={1}, use_global_device_ids=true | all-gather | bytes 655360 | tf_op jit(solution)/shard_map/all_gather | solution.py:159
  (47 shorter events, 15.9 us)
Async XLA Ops:
  9.5 9.4 %all-to-all-start = ((bf16[4,2,16384]{2,1,0:T(2,128)(2,1)}), bf16[4,2,16384]{2,1,0:T(2,128)(2,1)S(1)}, u32[]{:S(2)}, u32[]{:S(2)}) async-start(bf16[4,2,16384]{2,1,0:T(2,128)(2,1)} %reshape.41), calls=%async_computation | async-start | bytes 524288 | tf_op jit(solution)/shard_map/all_to_all | solution.py:113
  12.9 54.4 %all-gather.3.cloned.1.call-start = ((), (), s32[]{:S(2)}) async-start(), calls=%async_computation.2 | async-start | bytes 1310720 | tf_op jit(solution)/shard_map/all_gather | solution.py:123
  19.7 17.6 %collective-permute-start = (bf16[2,64,256]{2,1,0:T(8,128)(2,1)S(1)}, bf16[2,64,256]{2,1,0:T(8,128)(2,1)S(1)}, u32[]{:S(2)}, u32[]{:S(2)}) collective-permute-start(bf16[2,64,256]{2,1,0:T(8,128)(2,1)S(1)} %constant_dynamic-slice_fusion), channel_id=1, source_target_pairs={{0,16},{4,20},{8,24},{12,28},{16,32},{20,36},{24,40},{28,44},{32,4... | collective-permute-start | bytes 196616 | tf_op jit(solution)/shard_map/ppermute | solution.py:20
  26.1 11.2 %collective-permute-start.1 = (bf16[2,64,256]{2,1,0:T(8,128)(2,1)S(1)}, bf16[2,64,256]{2,1,0:T(8,128)(2,1)S(1)}, u32[]{:S(2)}, u32[]{:S(2)}) collective-permute-start(bf16[2,64,256]{2,1,0:T(8,128)(2,1)S(1)} %constant_dynamic-slice_fusion), channel_id=1, source_target_pairs={{0,12},{4,16},{8,20},{12,24},{16,28},{20,32},{24,36},{28,40},{32,4... | collective-permute-start | bytes 196616 | tf_op jit(solution)/shard_map/ppermute | solution.py:20
  29.3 8.1 %collective-permute-start.2 = (bf16[2,64,256]{2,1,0:T(8,128)(2,1)S(1)}, bf16[2,64,256]{2,1,0:T(8,128)(2,1)S(1)}, u32[]{:S(2)}, u32[]{:S(2)}) collective-permute-start(bf16[2,64,256]{2,1,0:T(8,128)(2,1)S(1)} %constant_dynamic-slice_fusion), channel_id=1, source_target_pairs={{0,8},{4,12},{8,16},{12,20},{16,24},{20,28},{24,32},{28,36},{32,40... | collective-permute-start | bytes 196616 | tf_op jit(solution)/shard_map/ppermute | solution.py:20
  32.2 7.7 %collective-permute-start.3 = (bf16[2,64,256]{2,1,0:T(8,128)(2,1)S(1)}, bf16[2,64,256]{2,1,0:T(8,128)(2,1)S(1)}, u32[]{:S(2)}, u32[]{:S(2)}) collective-permute-start(bf16[2,64,256]{2,1,0:T(8,128)(2,1)S(1)} %constant_dynamic-slice_fusion), channel_id=1, source_target_pairs={{0,4},{4,8},{8,12},{12,16},{16,20},{20,24},{24,28},{28,32},{32,36}... | collective-permute-start | bytes 196616 | tf_op jit(solution)/shard_map/ppermute | solution.py:20
  88.7 10.5 %copy-start.2 = (bf16[2,256,128]{2,1,0:T(8,128)(2,1)}, bf16[2,256,128]{2,1,0:T(8,128)(2,1)S(1)}, u32[]{:S(2)}) copy-start(bf16[2,256,128]{2,1,0:T(8,128)(2,1)S(1)} %get-tuple-element.14.rest_3_) | copy-start | bytes 393220
  88.7 10.5 %copy-start.3 = (bf16[2,256,128]{2,1,0:T(8,128)(2,1)}, bf16[2,256,128]{2,1,0:T(8,128)(2,1)S(1)}, u32[]{:S(2)}) copy-start(bf16[2,256,128]{2,1,0:T(8,128)(2,1)S(1)} %get-tuple-element.15.rest_2_) | copy-start | bytes 393220
  88.7 10.5 %copy-start.4 = (bf16[2,256,128]{2,1,0:T(8,128)(2,1)}, bf16[2,256,128]{2,1,0:T(8,128)(2,1)S(1)}, u32[]{:S(2)}) copy-start(bf16[2,256,128]{2,1,0:T(8,128)(2,1)S(1)} %get-tuple-element.16.rest_1_) | copy-start | bytes 393220
  88.7 10.5 %copy-start.5 = (bf16[2,256,128]{2,1,0:T(8,128)(2,1)}, bf16[2,256,128]{2,1,0:T(8,128)(2,1)S(1)}, u32[]{:S(2)}) copy-start(bf16[2,256,128]{2,1,0:T(8,128)(2,1)S(1)} %get-tuple-element.17.rest_0_) | copy-start | bytes 393220
  88.7 31.4 %collective-permute-start.4 = (bf16[2,256,128]{2,1,0:T(8,128)(2,1)S(1)}, bf16[2,256,128]{2,1,0:T(8,128)(2,1)S(1)}, u32[]{:S(2)}, u32[]{:S(2)}) collective-permute-start(bf16[2,256,128]{2,1,0:T(8,128)(2,1)S(1)} %get-tuple-element.17.rest_0_), channel_id=1, source_target_pairs={{16,0},{20,4},{24,8},{28,12},{32,16},{36,20},{40,24},{44,28},{48,3... | collective-permute-start | bytes 393224 | tf_op jit(solution)/shard_map/ppermute | solution.py:20
  91.0 31.5 %collective-permute-start.5 = (bf16[2,256,128]{2,1,0:T(8,128)(2,1)S(1)}, bf16[2,256,128]{2,1,0:T(8,128)(2,1)S(1)}, u32[]{:S(2)}, u32[]{:S(2)}) collective-permute-start(bf16[2,256,128]{2,1,0:T(8,128)(2,1)S(1)} %get-tuple-element.16.rest_1_), channel_id=1, source_target_pairs={{12,0},{16,4},{20,8},{24,12},{28,16},{32,20},{36,24},{40,28},{44,3... | collective-permute-start | bytes 393224 | tf_op jit(solution)/shard_map/ppermute | solution.py:20
  92.9 31.5 %collective-permute-start.6 = (bf16[2,256,128]{2,1,0:T(8,128)(2,1)S(1)}, bf16[2,256,128]{2,1,0:T(8,128)(2,1)S(1)}, u32[]{:S(2)}, u32[]{:S(2)}) collective-permute-start(bf16[2,256,128]{2,1,0:T(8,128)(2,1)S(1)} %get-tuple-element.15.rest_2_), channel_id=1, source_target_pairs={{8,0},{12,4},{16,8},{20,12},{24,16},{28,20},{32,24},{36,28},{40,32... | collective-permute-start | bytes 393224 | tf_op jit(solution)/shard_map/ppermute | solution.py:20
  94.9 31.5 %collective-permute-start.7 = (bf16[2,256,128]{2,1,0:T(8,128)(2,1)S(1)}, bf16[2,256,128]{2,1,0:T(8,128)(2,1)S(1)}, u32[]{:S(2)}, u32[]{:S(2)}) collective-permute-start(bf16[2,256,128]{2,1,0:T(8,128)(2,1)S(1)} %get-tuple-element.14.rest_3_), channel_id=1, source_target_pairs={{4,0},{8,4},{12,8},{16,12},{20,16},{24,20},{28,24},{32,28},{36,32}... | collective-permute-start | bytes 393224 | tf_op jit(solution)/shard_map/ppermute | solution.py:20
  118.1 9.3 %collective-permute-start.10 = (bf16[2,256,128]{2,1,0:T(8,128)(2,1)S(1)}, bf16[2,256,128]{2,1,0:T(8,128)(2,1)S(1)}, u32[]{:S(2)}, u32[]{:S(2)}) collective-permute-start(bf16[2,256,128]{2,1,0:T(8,128)(2,1)S(1)} %get-tuple-element.12), channel_id=1, source_target_pairs={{8,0},{12,4},{16,8},{20,12},{24,16},{28,20},{32,24},{36,28},{40,32... | collective-permute-start | bytes 393224 | tf_op jit(solution)/shard_map/ppermute | solution.py:20
  120.1 12.1 %collective-permute-start.11 = (bf16[2,256,128]{2,1,0:T(8,128)(2,1)S(1)}, bf16[2,256,128]{2,1,0:T(8,128)(2,1)S(1)}, u32[]{:S(2)}, u32[]{:S(2)}) collective-permute-start(bf16[2,256,128]{2,1,0:T(8,128)(2,1)S(1)} %get-tuple-element.11), channel_id=1, source_target_pairs={{4,0},{8,4},{12,8},{16,12},{20,16},{24,20},{28,24},{32,28},{36,32}... | collective-permute-start | bytes 393224 | tf_op jit(solution)/shard_map/ppermute | solution.py:20
  122.5 12.1 %collective-permute-start.8 = (bf16[2,256,128]{2,1,0:T(8,128)(2,1)S(1)}, bf16[2,256,128]{2,1,0:T(8,128)(2,1)S(1)}, u32[]{:S(2)}, u32[]{:S(2)}) collective-permute-start(bf16[2,256,128]{2,1,0:T(8,128)(2,1)S(1)} %get-tuple-element.10), channel_id=1, source_target_pairs={{16,0},{20,4},{24,8},{28,12},{32,16},{36,20},{40,24},{44,28},{48,3... | collective-permute-start | bytes 393224 | tf_op jit(solution)/shard_map/ppermute | solution.py:20
  124.5 17.3 %collective-permute-start.9 = (bf16[2,256,128]{2,1,0:T(8,128)(2,1)S(1)}, bf16[2,256,128]{2,1,0:T(8,128)(2,1)S(1)}, u32[]{:S(2)}, u32[]{:S(2)}) collective-permute-start(bf16[2,256,128]{2,1,0:T(8,128)(2,1)S(1)} %get-tuple-element.13), channel_id=1, source_target_pairs={{12,0},{16,4},{20,8},{24,12},{28,16},{32,20},{36,24},{40,28},{44,3... | collective-permute-start | bytes 393224 | tf_op jit(solution)/shard_map/ppermute | solution.py:20
  142.9 5.7 %copy-start = (bf16[256,1024]{1,0:T(8,128)(2,1)S(1)}, bf16[256,1024]{1,0:T(8,128)(2,1)}, u32[]{:S(2)}) copy-start(bf16[256,1024]{1,0:T(8,128)(2,1)} %get-tuple-element.6) | copy-start | bytes 1572868
  142.9 5.7 %copy-start.1 = (bf16[256,1024]{1,0:T(8,128)(2,1)S(1)}, bf16[256,1024]{1,0:T(8,128)(2,1)}, u32[]{:S(2)}) copy-start(bf16[256,1024]{1,0:T(8,128)(2,1)} %get-tuple-element.8) | copy-start | bytes 1572868
  143.8 15.7 %all-to-all-start.1 = ((f32[2,16,16,256]{3,2,0,1:T(8,128)}), f32[2,16,16,256]{3,2,0,1:T(8,128)S(1)}, u32[]{:S(2)}, u32[]{:S(2)}) async-start(f32[2,16,16,256]{3,2,0,1:T(8,128)} %copy.17), calls=%async_computation.1 | async-start | bytes 1048576 | tf_op jit(solution)/shard_map/all_to_all | solution.py:104
Sparse Core Ops, SparseCore 0:
  40.7 26.5 all-gather.2

commit v8 on v6

--- a/solution.py
+++ b/solution.py
@@ -101,8 +101,8 @@
     kinds, rows, cols = own_rows.shape
     pieces = own_rows.reshape(kinds, peers, sections, rows // (peers * sections), cols)
     pieces = jnp.swapaxes(pieces, 1, 2).reshape(kinds, sections * peers, rows // (peers * sections), cols)
-    pieces = lax.all_to_all(pieces, ("section", "tp"), split_axis=1, concat_axis=1)
-    pieces = pieces.reshape(kinds, sections, peers, rows // (peers * sections), cols)
+    pieces = lax.all_to_all(pieces.astype(jnp.bfloat16), ("section", "tp"), split_axis=1, concat_axis=1)
+    pieces = pieces.astype(jnp.float32).reshape(kinds, sections, peers, rows // (peers * sections), cols)
     chunk = pieces[:, 0]
     for other in range(1, sections):
         chunk = chunk + pieces[:, other]
@@ -151,7 +151,9 @@
     own_rows = jnp.concatenate(own_parts, axis=2)
     chunk = scatter_layers(own_rows)
     kinds, rows, tp_peers, cols = chunk.shape
-    d_shared_kv = lax.all_gather(chunk.reshape(kinds, rows, -1), "section", axis=1, tiled=True)
+    d_shared_kv = lax.all_gather(
+        chunk.reshape(kinds, rows, -1).astype(jnp.bfloat16), "section", axis=1, tiled=True
+    ).astype(jnp.float32)
     return (d_queries, d_shared_kv)
 
 

time: 160 us -> 156 us (0.975)
  waiting for transfers between devices: 53.3 us -> 50.1 us
    all_to_all x1, waiting for transfers between devices: 9.75 us -> 6.59 us  [scatter_layers(): lax.all_to_all(pieces.astype(jnp.bfloat16), ('section', 'tp'), split_axis...]
    another operation x2 -> x4, other arithmetic: 2.81 us -> 4.88 us
    add x2 -> x0, other arithmetic: 2.06 us -> none  [body(): own_rows + shifted(sent[offset], 'seq', offset - span_blocks).astype(jnp....]
    unnamed x22 -> x21, local copies, waits for them, and re-layouts: 4.68 us -> 3.89 us
where the time goes in v8:
time: 156 us; the launch traced here: 155 us
  waiting for transfers between devices  50.1 us (32%)
  starting transfers between devices  43.3 us (28%)
  Pallas kernels  35 us (22%)
  blocking collectives  12.5 us (8%)
  other arithmetic  8.54 us (5%)
  local copies, waits for them, and re-layouts  5.13 us (3%)
    ppermute x12, waiting for transfers between devices, shifted(): return lax.ppermute(value, axis, pairs)  37.5 us
    pallas_call x2, Pallas kernels, attention_grads(): pl.pallas_call(functools.partial(attn_kernel, scale=scale, hd=hd, per_ste...  35 us
    ppermute x12, starting transfers between devices, shifted(): return lax.ppermute(value, axis, pairs)  34.9 us
    all_gather x1, blocking collectives, body(): lax.all_gather(chunk.reshape(kinds, rows, -1).astype(jnp.bfloat16), 'sect...  12.5 us
    all_to_all x1, waiting for transfers between devices, scatter_layers(): lax.all_to_all(pieces.astype(jnp.bfloat16), ('section', 'tp'), split_axis...  6.59 us
    all_to_all x1, waiting for transfers between devices, body(): lax.all_to_all(shared_kv, 'tp', split_axis=2, concat_axis=1, tiled=True)  5.94 us
    all_to_all x1, starting transfers between devices, scatter_layers(): lax.all_to_all(pieces.astype(jnp.bfloat16), ('section', 'tp'), split_axis...  4.97 us
    another operation x4, other arithmetic  4.88 us
  transfers between devices with their start and end apart: 14, of which 8 were waited for; matrix products, arithmetic and copies ran while one was open for 3% of the time, Pallas kernels for 11%

profile of v8, /device:TPU:80, one launch (start us, length us, event | category | flops | bytes accessed | tf_op | source)
XLA Modules:
  0.0 155.5 jit_solution(2557371576171022291)
XLA Ops:
  3.0 3.4 %all-to-all-start = ((bf16[4,2,16384]{2,1,0:T(2,128)(2,1)}), bf16[4,2,16384]{2,1,0:T(2,128)(2,1)S(1)}, u32[]{:S(2)}, u32[]{:S(2)}) async-start(bf16[4,2,16384]{2,1,0:T(2,128)(2,1)} %reshape.36), calls=%async_computation | async-start | bytes 524288 | tf_op jit(solution)/shard_map/all_to_all | solution.py:113
  6.4 5.9 %all-to-all-done = bf16[4,2,16384]{2,1,0:T(2,128)(2,1)S(1)} async-done(((bf16[4,2,16384]{2,1,0:T(2,128)(2,1)}), bf16[4,2,16384]{2,1,0:T(2,128)(2,1)S(1)}, u32[]{:S(2)}, u32[]{:S(2)}) %all-to-all-start) | async-done | bytes 262176 | tf_op jit(solution)/shard_map/all_to_all | solution.py:113
  13.1 6.4 %collective-permute-start = (bf16[2,256,256]{2,1,0:T(8,128)(2,1)S(1)}, bf16[2,256,256]{2,1,0:T(8,128)(2,1)S(1)}, u32[]{:S(2)}, u32[]{:S(2)}) collective-permute-start(bf16[2,256,256]{2,1,0:T(8,128)(2,1)S(1)} %bitcast.24), channel_id=1, source_target_pairs={{0,16},{4,20},{8,24},{12,28},{16,32},{20,36},{24,40},{28,44},{32,4... | collective-permute-start | bytes 786440 | tf_op jit(solution)/shard_map/ppermute | solution.py:20
  19.5 3.2 %collective-permute-start.1 = (bf16[2,256,256]{2,1,0:T(8,128)(2,1)S(1)}, bf16[2,256,256]{2,1,0:T(8,128)(2,1)S(1)}, u32[]{:S(2)}, u32[]{:S(2)}) collective-permute-start(bf16[2,256,256]{2,1,0:T(8,128)(2,1)S(1)} %bitcast.25), channel_id=1, source_target_pairs={{0,12},{4,16},{8,20},{12,24},{16,28},{20,32},{24,36},{28,40},{32,4... | collective-permute-start | bytes 786440 | tf_op jit(solution)/shard_map/ppermute | solution.py:20
  22.7 2.9 %collective-permute-start.2 = (bf16[2,256,256]{2,1,0:T(8,128)(2,1)S(1)}, bf16[2,256,256]{2,1,0:T(8,128)(2,1)S(1)}, u32[]{:S(2)}, u32[]{:S(2)}) collective-permute-start(bf16[2,256,256]{2,1,0:T(8,128)(2,1)S(1)} %bitcast.26), channel_id=1, source_target_pairs={{0,8},{4,12},{8,16},{12,20},{16,24},{20,28},{24,32},{28,36},{32,40... | collective-permute-start | bytes 786440 | tf_op jit(solution)/shard_map/ppermute | solution.py:20
  27.3 5.1 %collective-permute-start.3 = (bf16[2,256,256]{2,1,0:T(8,128)(2,1)S(1)}, bf16[2,256,256]{2,1,0:T(8,128)(2,1)S(1)}, u32[]{:S(2)}, u32[]{:S(2)}) collective-permute-start(bf16[2,256,256]{2,1,0:T(8,128)(2,1)S(1)} %bitcast.27), channel_id=1, source_target_pairs={{0,4},{4,8},{8,12},{12,16},{16,20},{20,24},{24,28},{28,32},{32,36}... | collective-permute-start | bytes 786440 | tf_op jit(solution)/shard_map/ppermute | solution.py:20
  32.4 10.6 %collective-permute-done.1 = bf16[2,256,256]{2,1,0:T(8,128)(2,1)S(1)} collective-permute-done((bf16[2,256,256]{2,1,0:T(8,128)(2,1)S(1)}, bf16[2,256,256]{2,1,0:T(8,128)(2,1)S(1)}, u32[]{:S(2)}, u32[]{:S(2)}) %collective-permute-start.1) | collective-permute-done | bytes 262176 | tf_op jit(solution)/shard_map/ppermute | solution.py:20
  43.0 5.6 %collective-permute-done.2 = bf16[2,256,256]{2,1,0:T(8,128)(2,1)S(1)} collective-permute-done((bf16[2,256,256]{2,1,0:T(8,128)(2,1)S(1)}, bf16[2,256,256]{2,1,0:T(8,128)(2,1)S(1)}, u32[]{:S(2)}, u32[]{:S(2)}) %collective-permute-start.2) | collective-permute-done | bytes 262176 | tf_op jit(solution)/shard_map/ppermute | solution.py:20
  48.6 4.2 %collective-permute-done.3 = bf16[2,256,256]{2,1,0:T(8,128)(2,1)S(1)} collective-permute-done((bf16[2,256,256]{2,1,0:T(8,128)(2,1)S(1)}, bf16[2,256,256]{2,1,0:T(8,128)(2,1)S(1)}, u32[]{:S(2)}, u32[]{:S(2)}) %collective-permute-start.3) | collective-permute-done | bytes 262176 | tf_op jit(solution)/shard_map/ppermute | solution.py:20
  53.9 17.5 %shard_map.50 = (bf16[256,1024]{1,0:T(8,128)(2,1)}, f32[2,1280,128]{2,1,0:T(8,128)}) custom-call(f32[256,1280]{1,0:T(8,128)} %fusion.2.bias_ref, bf16[256,2048]{1,0:T(8,128)(2,1)} %bitcast.33, bf16[256,2048]{1,0:T(8,128)(2,1)} %bitcast.35, bf16[2,1280,256]{2,1,0:T(8,128)(2,1)} %copy-done.6, bf16[2,1280,256]{2,1,0:T(8,128)(2,1)} %copy-done.6), custom_call_target="tpu_custom_call" | custom-call | flops 4026531840 | bytes 4849664 | tf_op jit(solution)/shard_map/pallas_call | solution.py:70
  72.9 1.9 %collective-permute-start.4 = (bf16[2,256,128]{2,1,0:T(8,128)(2,1)S(1)}, bf16[2,256,128]{2,1,0:T(8,128)(2,1)S(1)}, u32[]{:S(2)}, u32[]{:S(2)}) collective-permute-start(bf16[2,256,128]{2,1,0:T(8,128)(2,1)S(1)} %get-tuple-element.17.rest_0_), channel_id=1, source_target_pairs={{16,0},{20,4},{24,8},{28,12},{32,16},{36,20},{40,24},{44,28},{48,3... | collective-permute-start | bytes 393224 | tf_op jit(solution)/shard_map/ppermute | solution.py:20
  74.8 1.9 %collective-permute-start.5 = (bf16[2,256,128]{2,1,0:T(8,128)(2,1)S(1)}, bf16[2,256,128]{2,1,0:T(8,128)(2,1)S(1)}, u32[]{:S(2)}, u32[]{:S(2)}) collective-permute-start(bf16[2,256,128]{2,1,0:T(8,128)(2,1)S(1)} %get-tuple-element.16.rest_1_), channel_id=1, source_target_pairs={{12,0},{16,4},{20,8},{24,12},{28,16},{32,20},{36,24},{40,28},{44,3... | collective-permute-start | bytes 393224 | tf_op jit(solution)/shard_map/ppermute | solution.py:20
  76.7 1.9 %collective-permute-start.6 = (bf16[2,256,128]{2,1,0:T(8,128)(2,1)S(1)}, bf16[2,256,128]{2,1,0:T(8,128)(2,1)S(1)}, u32[]{:S(2)}, u32[]{:S(2)}) collective-permute-start(bf16[2,256,128]{2,1,0:T(8,128)(2,1)S(1)} %get-tuple-element.15.rest_2_), channel_id=1, source_target_pairs={{8,0},{12,4},{16,8},{20,12},{24,16},{28,20},{32,24},{36,28},{40,32... | collective-permute-start | bytes 393224 | tf_op jit(solution)/shard_map/ppermute | solution.py:20
  78.7 3.9 %collective-permute-start.7 = (bf16[2,256,128]{2,1,0:T(8,128)(2,1)S(1)}, bf16[2,256,128]{2,1,0:T(8,128)(2,1)S(1)}, u32[]{:S(2)}, u32[]{:S(2)}) collective-permute-start(bf16[2,256,128]{2,1,0:T(8,128)(2,1)S(1)} %get-tuple-element.14.rest_3_), channel_id=1, source_target_pairs={{4,0},{8,4},{12,8},{16,12},{20,16},{24,20},{28,24},{32,28},{36,32}... | collective-permute-start | bytes 393224 | tf_op jit(solution)/shard_map/ppermute | solution.py:20
  82.6 17.5 %shard_map.51 = (bf16[256,1024]{1,0:T(8,128)(2,1)}, f32[2,1280,128]{2,1,0:T(8,128)}) custom-call(f32[256,1280]{1,0:T(8,128)} %fusion.2.bias_ref, bf16[256,2048]{1,0:T(8,128)(2,1)} %bitcast.34, bf16[256,2048]{1,0:T(8,128)(2,1)} %bitcast.36, bf16[2,1280,256]{2,1,0:T(8,128)(2,1)} %copy-done.6, bf16[2,1280,256]{2,1,0:T(8,128)(2,1)} %copy-done.6, ...), custom_call_target="tpu_custom_call" | custom-call | flops 4026531840 | bytes 4849664 | tf_op jit(solution)/shard_map/pallas_call | solution.py:70
  101.5 1.9 %collective-permute-start.10 = (bf16[2,256,128]{2,1,0:T(8,128)(2,1)S(1)}, bf16[2,256,128]{2,1,0:T(8,128)(2,1)S(1)}, u32[]{:S(2)}, u32[]{:S(2)}) collective-permute-start(bf16[2,256,128]{2,1,0:T(8,128)(2,1)S(1)} %get-tuple-element.12), channel_id=1, source_target_pairs={{8,0},{12,4},{16,8},{20,12},{24,16},{28,20},{32,24},{36,28},{40,32... | collective-permute-start | bytes 393224 | tf_op jit(solution)/shard_map/ppermute | solution.py:20
  103.5 1.9 %collective-permute-start.11 = (bf16[2,256,128]{2,1,0:T(8,128)(2,1)S(1)}, bf16[2,256,128]{2,1,0:T(8,128)(2,1)S(1)}, u32[]{:S(2)}, u32[]{:S(2)}) collective-permute-start(bf16[2,256,128]{2,1,0:T(8,128)(2,1)S(1)} %get-tuple-element.11), channel_id=1, source_target_pairs={{4,0},{8,4},{12,8},{16,12},{20,16},{24,20},{28,24},{32,28},{36,32}... | collective-permute-start | bytes 393224 | tf_op jit(solution)/shard_map/ppermute | solution.py:20
  105.4 1.9 %collective-permute-start.8 = (bf16[2,256,128]{2,1,0:T(8,128)(2,1)S(1)}, bf16[2,256,128]{2,1,0:T(8,128)(2,1)S(1)}, u32[]{:S(2)}, u32[]{:S(2)}) collective-permute-start(bf16[2,256,128]{2,1,0:T(8,128)(2,1)S(1)} %get-tuple-element.10), channel_id=1, source_target_pairs={{16,0},{20,4},{24,8},{28,12},{32,16},{36,20},{40,24},{44,28},{48,3... | collective-permute-start | bytes 393224 | tf_op jit(solution)/shard_map/ppermute | solution.py:20
  110.4 3.4 %collective-permute-done.11 = bf16[2,256,128]{2,1,0:T(8,128)(2,1)S(1)} collective-permute-done((bf16[2,256,128]{2,1,0:T(8,128)(2,1)S(1)}, bf16[2,256,128]{2,1,0:T(8,128)(2,1)S(1)}, u32[]{:S(2)}, u32[]{:S(2)}) %collective-permute-start.11) | collective-permute-done | bytes 131104 | tf_op jit(solution)/shard_map/ppermute | solution.py:20
  113.8 6.7 %collective-permute-done.8 = bf16[2,256,128]{2,1,0:T(8,128)(2,1)S(1)} collective-permute-done((bf16[2,256,128]{2,1,0:T(8,128)(2,1)S(1)}, bf16[2,256,128]{2,1,0:T(8,128)(2,1)S(1)}, u32[]{:S(2)}, u32[]{:S(2)}) %collective-permute-start.8) | collective-permute-done | bytes 131104 | tf_op jit(solution)/shard_map/ppermute | solution.py:20
  120.5 7.0 %collective-permute-done.9 = bf16[2,256,128]{2,1,0:T(8,128)(2,1)S(1)} collective-permute-done((bf16[2,256,128]{2,1,0:T(8,128)(2,1)S(1)}, bf16[2,256,128]{2,1,0:T(8,128)(2,1)S(1)}, u32[]{:S(2)}, u32[]{:S(2)}) %collective-permute-start.9) | collective-permute-done | bytes 131104 | tf_op jit(solution)/shard_map/ppermute | solution.py:20
  129.4 5.0 %all-to-all-start.1 = ((bf16[2,16,16,256]{3,2,0,1:T(8,128)(2,1)}), bf16[2,16,16,256]{3,2,0,1:T(8,128)(2,1)S(1)}, u32[]{:S(2)}, u32[]{:S(2)}) async-start(bf16[2,16,16,256]{3,2,0,1:T(8,128)(2,1)} %copy.14), calls=%async_computation.1 | async-start | bytes 524288 | tf_op jit(solution)/shard_map/all_to_all | solution.py:104
  135.4 6.6 %all-to-all-done.1 = bf16[2,16,16,256]{3,2,0,1:T(8,128)(2,1)S(1)} async-done(((bf16[2,16,16,256]{3,2,0,1:T(8,128)(2,1)}), bf16[2,16,16,256]{3,2,0,1:T(8,128)(2,1)S(1)}, u32[]{:S(2)}, u32[]{:S(2)}) %all-to-all-start.1) | async-done | bytes 262176 | tf_op jit(solution)/shard_map/all_to_all | solution.py:104
  142.1 12.5 %all_gather.3 = bf16[2,64,1024]{2,1,0:T(8,128)(2,1)S(1)} all-gather(bf16[2,16,1024]{2,1,0:T(8,128)(2,1)S(1)} %bitcast.32), channel_id=1, replica_groups=mesh['section'=4,'seq'=16,'tp'=4] {'section'}, dimensions={1}, use_global_device_ids=true | all-gather | bytes 327680 | tf_op jit(solution)/shard_map/all_gather | solution.py:154
  (48 shorter events, 15.6 us)
Async XLA Ops:
  3.0 9.4 %all-to-all-start = ((bf16[4,2,16384]{2,1,0:T(2,128)(2,1)}), bf16[4,2,16384]{2,1,0:T(2,128)(2,1)S(1)}, u32[]{:S(2)}, u32[]{:S(2)}) async-start(bf16[4,2,16384]{2,1,0:T(2,128)(2,1)} %reshape.36), calls=%async_computation | async-start | bytes 524288 | tf_op jit(solution)/shard_map/all_to_all | solution.py:113
  13.1 19.2 %collective-permute-start = (bf16[2,256,256]{2,1,0:T(8,128)(2,1)S(1)}, bf16[2,256,256]{2,1,0:T(8,128)(2,1)S(1)}, u32[]{:S(2)}, u32[]{:S(2)}) collective-permute-start(bf16[2,256,256]{2,1,0:T(8,128)(2,1)S(1)} %bitcast.24), channel_id=1, source_target_pairs={{0,16},{4,20},{8,24},{12,28},{16,32},{20,36},{24,40},{28,44},{32,4... | collective-permute-start | bytes 786440 | tf_op jit(solution)/shard_map/ppermute | solution.py:20
  19.5 23.4 %collective-permute-start.1 = (bf16[2,256,256]{2,1,0:T(8,128)(2,1)S(1)}, bf16[2,256,256]{2,1,0:T(8,128)(2,1)S(1)}, u32[]{:S(2)}, u32[]{:S(2)}) collective-permute-start(bf16[2,256,256]{2,1,0:T(8,128)(2,1)S(1)} %bitcast.25), channel_id=1, source_target_pairs={{0,12},{4,16},{8,20},{12,24},{16,28},{20,32},{24,36},{28,40},{32,4... | collective-permute-start | bytes 786440 | tf_op jit(solution)/shard_map/ppermute | solution.py:20
  22.7 25.9 %collective-permute-start.2 = (bf16[2,256,256]{2,1,0:T(8,128)(2,1)S(1)}, bf16[2,256,256]{2,1,0:T(8,128)(2,1)S(1)}, u32[]{:S(2)}, u32[]{:S(2)}) collective-permute-start(bf16[2,256,256]{2,1,0:T(8,128)(2,1)S(1)} %bitcast.26), channel_id=1, source_target_pairs={{0,8},{4,12},{8,16},{12,20},{16,24},{20,28},{24,32},{28,36},{32,40... | collective-permute-start | bytes 786440 | tf_op jit(solution)/shard_map/ppermute | solution.py:20
  27.3 25.6 %collective-permute-start.3 = (bf16[2,256,256]{2,1,0:T(8,128)(2,1)S(1)}, bf16[2,256,256]{2,1,0:T(8,128)(2,1)S(1)}, u32[]{:S(2)}, u32[]{:S(2)}) collective-permute-start(bf16[2,256,256]{2,1,0:T(8,128)(2,1)S(1)} %bitcast.27), channel_id=1, source_target_pairs={{0,4},{4,8},{8,12},{12,16},{16,20},{20,24},{24,28},{28,32},{32,36}... | collective-permute-start | bytes 786440 | tf_op jit(solution)/shard_map/ppermute | solution.py:20
  52.9 1.1 copy-start.6
  72.8 9.7 %copy-start.2 = (bf16[2,256,128]{2,1,0:T(8,128)(2,1)}, bf16[2,256,128]{2,1,0:T(8,128)(2,1)S(1)}, u32[]{:S(2)}) copy-start(bf16[2,256,128]{2,1,0:T(8,128)(2,1)S(1)} %get-tuple-element.14.rest_3_) | copy-start | bytes 393220
  72.9 9.7 %copy-start.3 = (bf16[2,256,128]{2,1,0:T(8,128)(2,1)}, bf16[2,256,128]{2,1,0:T(8,128)(2,1)S(1)}, u32[]{:S(2)}) copy-start(bf16[2,256,128]{2,1,0:T(8,128)(2,1)S(1)} %get-tuple-element.15.rest_2_) | copy-start | bytes 393220
  72.9 9.7 %copy-start.4 = (bf16[2,256,128]{2,1,0:T(8,128)(2,1)}, bf16[2,256,128]{2,1,0:T(8,128)(2,1)S(1)}, u32[]{:S(2)}) copy-start(bf16[2,256,128]{2,1,0:T(8,128)(2,1)S(1)} %get-tuple-element.16.rest_1_) | copy-start | bytes 393220
  72.9 9.7 %copy-start.5 = (bf16[2,256,128]{2,1,0:T(8,128)(2,1)}, bf16[2,256,128]{2,1,0:T(8,128)(2,1)S(1)}, u32[]{:S(2)}) copy-start(bf16[2,256,128]{2,1,0:T(8,128)(2,1)S(1)} %get-tuple-element.17.rest_0_) | copy-start | bytes 393220
  72.9 30.6 %collective-permute-start.4 = (bf16[2,256,128]{2,1,0:T(8,128)(2,1)S(1)}, bf16[2,256,128]{2,1,0:T(8,128)(2,1)S(1)}, u32[]{:S(2)}, u32[]{:S(2)}) collective-permute-start(bf16[2,256,128]{2,1,0:T(8,128)(2,1)S(1)} %get-tuple-element.17.rest_0_), channel_id=1, source_target_pairs={{16,0},{20,4},{24,8},{28,12},{32,16},{36,20},{40,24},{44,28},{48,3... | collective-permute-start | bytes 393224 | tf_op jit(solution)/shard_map/ppermute | solution.py:20
  74.8 30.6 %collective-permute-start.5 = (bf16[2,256,128]{2,1,0:T(8,128)(2,1)S(1)}, bf16[2,256,128]{2,1,0:T(8,128)(2,1)S(1)}, u32[]{:S(2)}, u32[]{:S(2)}) collective-permute-start(bf16[2,256,128]{2,1,0:T(8,128)(2,1)S(1)} %get-tuple-element.16.rest_1_), channel_id=1, source_target_pairs={{12,0},{16,4},{20,8},{24,12},{28,16},{32,20},{36,24},{40,28},{44,3... | collective-permute-start | bytes 393224 | tf_op jit(solution)/shard_map/ppermute | solution.py:20
  76.7 30.6 %collective-permute-start.6 = (bf16[2,256,128]{2,1,0:T(8,128)(2,1)S(1)}, bf16[2,256,128]{2,1,0:T(8,128)(2,1)S(1)}, u32[]{:S(2)}, u32[]{:S(2)}) collective-permute-start(bf16[2,256,128]{2,1,0:T(8,128)(2,1)S(1)} %get-tuple-element.15.rest_2_), channel_id=1, source_target_pairs={{8,0},{12,4},{16,8},{20,12},{24,16},{28,20},{32,24},{36,28},{40,32... | collective-permute-start | bytes 393224 | tf_op jit(solution)/shard_map/ppermute | solution.py:20
  78.7 30.6 %collective-permute-start.7 = (bf16[2,256,128]{2,1,0:T(8,128)(2,1)S(1)}, bf16[2,256,128]{2,1,0:T(8,128)(2,1)S(1)}, u32[]{:S(2)}, u32[]{:S(2)}) collective-permute-start(bf16[2,256,128]{2,1,0:T(8,128)(2,1)S(1)} %get-tuple-element.14.rest_3_), channel_id=1, source_target_pairs={{4,0},{8,4},{12,8},{16,12},{20,16},{24,20},{28,24},{32,28},{36,32}... | collective-permute-start | bytes 393224 | tf_op jit(solution)/shard_map/ppermute | solution.py:20
  101.5 8.8 %collective-permute-start.10 = (bf16[2,256,128]{2,1,0:T(8,128)(2,1)S(1)}, bf16[2,256,128]{2,1,0:T(8,128)(2,1)S(1)}, u32[]{:S(2)}, u32[]{:S(2)}) collective-permute-start(bf16[2,256,128]{2,1,0:T(8,128)(2,1)S(1)} %get-tuple-element.12), channel_id=1, source_target_pairs={{8,0},{12,4},{16,8},{20,12},{24,16},{28,20},{32,24},{36,28},{40,32... | collective-permute-start | bytes 393224 | tf_op jit(solution)/shard_map/ppermute | solution.py:20
  103.5 10.3 %collective-permute-start.11 = (bf16[2,256,128]{2,1,0:T(8,128)(2,1)S(1)}, bf16[2,256,128]{2,1,0:T(8,128)(2,1)S(1)}, u32[]{:S(2)}, u32[]{:S(2)}) collective-permute-start(bf16[2,256,128]{2,1,0:T(8,128)(2,1)S(1)} %get-tuple-element.11), channel_id=1, source_target_pairs={{4,0},{8,4},{12,8},{16,12},{20,16},{24,20},{28,24},{32,28},{36,32}... | collective-permute-start | bytes 393224 | tf_op jit(solution)/shard_map/ppermute | solution.py:20
  105.4 15.1 %collective-permute-start.8 = (bf16[2,256,128]{2,1,0:T(8,128)(2,1)S(1)}, bf16[2,256,128]{2,1,0:T(8,128)(2,1)S(1)}, u32[]{:S(2)}, u32[]{:S(2)}) collective-permute-start(bf16[2,256,128]{2,1,0:T(8,128)(2,1)S(1)} %get-tuple-element.10), channel_id=1, source_target_pairs={{16,0},{20,4},{24,8},{28,12},{32,16},{36,20},{40,24},{44,28},{48,3... | collective-permute-start | bytes 393224 | tf_op jit(solution)/shard_map/ppermute | solution.py:20
  107.4 20.2 %collective-permute-start.9 = (bf16[2,256,128]{2,1,0:T(8,128)(2,1)S(1)}, bf16[2,256,128]{2,1,0:T(8,128)(2,1)S(1)}, u32[]{:S(2)}, u32[]{:S(2)}) collective-permute-start(bf16[2,256,128]{2,1,0:T(8,128)(2,1)S(1)} %get-tuple-element.13), channel_id=1, source_target_pairs={{12,0},{16,4},{20,8},{24,12},{28,16},{32,20},{36,24},{40,28},{44,3... | collective-permute-start | bytes 393224 | tf_op jit(solution)/shard_map/ppermute | solution.py:20
  110.3 24.0 %copy-start = (bf16[256,1024]{1,0:T(8,128)(2,1)S(1)}, bf16[256,1024]{1,0:T(8,128)(2,1)}, u32[]{:S(2)}) copy-start(bf16[256,1024]{1,0:T(8,128)(2,1)} %get-tuple-element.6) | copy-start | bytes 1572868
  110.4 24.0 %copy-start.1 = (bf16[256,1024]{1,0:T(8,128)(2,1)S(1)}, bf16[256,1024]{1,0:T(8,128)(2,1)}, u32[]{:S(2)}) copy-start(bf16[256,1024]{1,0:T(8,128)(2,1)} %get-tuple-element.8) | copy-start | bytes 1572868
  129.4 12.6 %all-to-all-start.1 = ((bf16[2,16,16,256]{3,2,0,1:T(8,128)(2,1)}), bf16[2,16,16,256]{3,2,0,1:T(8,128)(2,1)S(1)}, u32[]{:S(2)}, u32[]{:S(2)}) async-start(bf16[2,16,16,256]{3,2,0,1:T(8,128)(2,1)} %copy.14), calls=%async_computation.1 | async-start | bytes 524288 | tf_op jit(solution)/shard_map/all_to_all | solution.py:104

commit v9 on v8

--- a/solution.py
+++ b/solution.py
@@ -45,8 +45,8 @@
         dsb = (p * (dp - delta)).astype(jnp.bfloat16)
         dq = jnp.dot(dsb, k, preferred_element_type=jnp.float32) * scale
         dq_ref[:, cols] = dq.astype(dq_ref.dtype)
-        dk_part = lax.dot_general(dsb, q, tn, preferred_element_type=jnp.float32) * scale
-        dv_part = lax.dot_general(pb, do, tn, preferred_element_type=jnp.float32)
+        dk_part = lax.dot_general(q, dsb, tn, preferred_element_type=jnp.float32) * scale
+        dv_part = lax.dot_general(do, pb, tn, preferred_element_type=jnp.float32)
         dk = dk_part if dk is None else dk + dk_part
         dv = dv_part if dv is None else dv + dv_part
 
@@ -80,11 +80,11 @@
         + [pl.BlockSpec(memory_space=pl.ANY) for _ in after],
         out_specs=[
             pl.BlockSpec((rows, width), lambda h, i: (0, h * steps + i)),
-            pl.BlockSpec((2, ext_rows, hd), lambda h, i: (0, 0, h)),
+            pl.BlockSpec((2, hd, ext_rows), lambda h, i: (0, h, 0)),
         ],
         out_shape=[
             jax.ShapeDtypeStruct((rows, heads * group * hd), jnp.bfloat16),
-            jax.ShapeDtypeStruct((2, ext_rows, heads * hd), jnp.float32),
+            jax.ShapeDtypeStruct((2, heads * hd, ext_rows), jnp.float32),
         ],
         compiler_params=pltpu.CompilerParams(dimension_semantics=("arbitrary", "arbitrary")),
         cost_estimate=pl.CostEstimate(
@@ -138,6 +138,7 @@
         d_query_part, grad_ext = attention_grads(
             bias, query_rows, grad_rows, extended, group_size, head_size, score_scale, 2, kv_head, 1, sent
         )
+        grad_ext = jnp.swapaxes(grad_ext, 1, 2)
         d_query_parts.append(d_query_part)
         sent = [
             grad_ext[:, offset * tok_rows : (offset + 1) * tok_rows, :].astype(jnp.bfloat16)

time: 156 us -> 151 us (0.968)
  Pallas kernels: 35 us -> 29.2 us
  other arithmetic: 8.54 us -> 4.01 us
  local copies, waits for them, and re-layouts: 5.13 us -> 9.15 us
    pallas_call x2, Pallas kernels: 35 us -> 29.2 us  [attention_grads(): pl.pallas_call(functools.partial(attn_kernel, scale=scale, hd=hd, per_ste...]
    another operation x4, other arithmetic: 4.88 us -> 0.35 us
    pallas_call x0 -> x2, local copies, waits for them, and re-layouts: none -> 3.41 us  [attention_grads(): pl.pallas_call(functools.partial(attn_kernel, scale=scale, hd=hd, per_ste...]
    unnamed x21 -> x19, local copies, waits for them, and re-layouts: 3.89 us -> 3.84 us
  transfers between devices with their start and end apart: 14 -> 14, of which waited for: 8 -> 9; matrix products, arithmetic and copies ran while one was open for 3% -> 3% of each run, Pallas kernels for 11% -> 10%
where the time goes in v9:
time: 151 us; the launch traced here: 150 us
  waiting for transfers between devices  51 us (34%)
  starting transfers between devices  43.2 us (29%)
  Pallas kernels  29.2 us (19%)
  blocking collectives  12.5 us (8%)
  local copies, waits for them, and re-layouts  9.15 us (6%)
  other arithmetic  4.01 us (3%)
    ppermute x12, waiting for transfers between devices, shifted(): return lax.ppermute(value, axis, pairs)  38.5 us
    ppermute x12, starting transfers between devices, shifted(): return lax.ppermute(value, axis, pairs)  34.9 us
    pallas_call x2, Pallas kernels, attention_grads(): pl.pallas_call(functools.partial(attn_kernel, scale=scale, hd=hd, per_ste...  29.2 us
    all_gather x1, blocking collectives, body(): lax.all_gather(chunk.reshape(kinds, rows, -1).astype(jnp.bfloat16), 'sect...  12.5 us
    all_to_all x1, waiting for transfers between devices, scatter_layers(): lax.all_to_all(pieces.astype(jnp.bfloat16), ('section', 'tp'), split_axis...  6.59 us
    all_to_all x1, waiting for transfers between devices, body(): lax.all_to_all(shared_kv, 'tp', split_axis=2, concat_axis=1, tiled=True)  5.94 us
    all_to_all x1, starting transfers between devices, scatter_layers(): lax.all_to_all(pieces.astype(jnp.bfloat16), ('section', 'tp'), split_axis...  4.96 us
    unnamed x19, local copies, waits for them, and re-layouts  3.84 us
  transfers between devices with their start and end apart: 14, of which 9 were waited for; matrix products, arithmetic and copies ran while one was open for 3% of the time, Pallas kernels for 10%

profile of v9, /device:TPU:80, one launch (start us, length us, event | category | flops | bytes accessed | tf_op | source)
XLA Modules:
  0.0 150.1 jit_solution(1563736224514190825)
XLA Ops:
  3.0 3.4 %all-to-all-start = ((bf16[4,2,16384]{2,1,0:T(2,128)(2,1)}), bf16[4,2,16384]{2,1,0:T(2,128)(2,1)S(1)}, u32[]{:S(2)}, u32[]{:S(2)}) async-start(bf16[4,2,16384]{2,1,0:T(2,128)(2,1)} %reshape.36), calls=%async_computation | async-start | bytes 524288 | tf_op jit(solution)/shard_map/all_to_all | solution.py:113
  6.4 5.9 %all-to-all-done = bf16[4,2,16384]{2,1,0:T(2,128)(2,1)S(1)} async-done(((bf16[4,2,16384]{2,1,0:T(2,128)(2,1)}), bf16[4,2,16384]{2,1,0:T(2,128)(2,1)S(1)}, u32[]{:S(2)}, u32[]{:S(2)}) %all-to-all-start) | async-done | bytes 262176 | tf_op jit(solution)/shard_map/all_to_all | solution.py:113
  13.1 6.4 %collective-permute-start = (bf16[2,256,256]{2,1,0:T(8,128)(2,1)S(1)}, bf16[2,256,256]{2,1,0:T(8,128)(2,1)S(1)}, u32[]{:S(2)}, u32[]{:S(2)}) collective-permute-start(bf16[2,256,256]{2,1,0:T(8,128)(2,1)S(1)} %bitcast.30), channel_id=1, source_target_pairs={{0,16},{4,20},{8,24},{12,28},{16,32},{20,36},{24,40},{28,44},{32,4... | collective-permute-start | bytes 786440 | tf_op jit(solution)/shard_map/ppermute | solution.py:20
  19.5 3.2 %collective-permute-start.1 = (bf16[2,256,256]{2,1,0:T(8,128)(2,1)S(1)}, bf16[2,256,256]{2,1,0:T(8,128)(2,1)S(1)}, u32[]{:S(2)}, u32[]{:S(2)}) collective-permute-start(bf16[2,256,256]{2,1,0:T(8,128)(2,1)S(1)} %bitcast.31), channel_id=1, source_target_pairs={{0,12},{4,16},{8,20},{12,24},{16,28},{20,32},{24,36},{28,40},{32,4... | collective-permute-start | bytes 786440 | tf_op jit(solution)/shard_map/ppermute | solution.py:20
  22.7 2.9 %collective-permute-start.2 = (bf16[2,256,256]{2,1,0:T(8,128)(2,1)S(1)}, bf16[2,256,256]{2,1,0:T(8,128)(2,1)S(1)}, u32[]{:S(2)}, u32[]{:S(2)}) collective-permute-start(bf16[2,256,256]{2,1,0:T(8,128)(2,1)S(1)} %bitcast.32), channel_id=1, source_target_pairs={{0,8},{4,12},{8,16},{12,20},{16,24},{20,28},{24,32},{28,36},{32,40... | collective-permute-start | bytes 786440 | tf_op jit(solution)/shard_map/ppermute | solution.py:20
  27.3 5.1 %collective-permute-start.3 = (bf16[2,256,256]{2,1,0:T(8,128)(2,1)S(1)}, bf16[2,256,256]{2,1,0:T(8,128)(2,1)S(1)}, u32[]{:S(2)}, u32[]{:S(2)}) collective-permute-start(bf16[2,256,256]{2,1,0:T(8,128)(2,1)S(1)} %bitcast.33), channel_id=1, source_target_pairs={{0,4},{4,8},{8,12},{12,16},{16,20},{20,24},{24,28},{28,32},{32,36}... | collective-permute-start | bytes 786440 | tf_op jit(solution)/shard_map/ppermute | solution.py:20
  32.4 10.6 %collective-permute-done.1 = bf16[2,256,256]{2,1,0:T(8,128)(2,1)S(1)} collective-permute-done((bf16[2,256,256]{2,1,0:T(8,128)(2,1)S(1)}, bf16[2,256,256]{2,1,0:T(8,128)(2,1)S(1)}, u32[]{:S(2)}, u32[]{:S(2)}) %collective-permute-start.1) | collective-permute-done | bytes 262176 | tf_op jit(solution)/shard_map/ppermute | solution.py:20
  43.0 5.6 %collective-permute-done.2 = bf16[2,256,256]{2,1,0:T(8,128)(2,1)S(1)} collective-permute-done((bf16[2,256,256]{2,1,0:T(8,128)(2,1)S(1)}, bf16[2,256,256]{2,1,0:T(8,128)(2,1)S(1)}, u32[]{:S(2)}, u32[]{:S(2)}) %collective-permute-start.2) | collective-permute-done | bytes 262176 | tf_op jit(solution)/shard_map/ppermute | solution.py:20
  48.6 4.2 %collective-permute-done.3 = bf16[2,256,256]{2,1,0:T(8,128)(2,1)S(1)} collective-permute-done((bf16[2,256,256]{2,1,0:T(8,128)(2,1)S(1)}, bf16[2,256,256]{2,1,0:T(8,128)(2,1)S(1)}, u32[]{:S(2)}, u32[]{:S(2)}) %collective-permute-start.3) | collective-permute-done | bytes 262176 | tf_op jit(solution)/shard_map/ppermute | solution.py:20
  53.9 14.6 %shard_map.50 = (bf16[256,1024]{1,0:T(8,128)(2,1)}, f32[2,128,1280]{2,1,0:T(8,128)}) custom-call(f32[256,1280]{1,0:T(8,128)} %fusion.2.bias_ref, bf16[256,2048]{1,0:T(8,128)(2,1)} %bitcast.39, bf16[256,2048]{1,0:T(8,128)(2,1)} %bitcast.41, bf16[2,1280,256]{2,1,0:T(8,128)(2,1)} %copy-done.5, bf16[2,1280,256]{2,1,0:T(8,128)(2,1)} %copy-done.5), custom_call_target="tpu_custom_call" | custom-call | flops 4026531840 | bytes 4849664 | tf_op jit(solution)/shard_map/pallas_call | solution.py:70
  72.9 1.9 %collective-permute-start.5 = (bf16[2,256,128]{2,1,0:T(8,128)(2,1)S(1)}, bf16[2,256,128]{2,1,0:T(8,128)(2,1)S(1)}, u32[]{:S(2)}, u32[]{:S(2)}) collective-permute-start(bf16[2,256,128]{2,1,0:T(8,128)(2,1)S(1)} %get-tuple-element.16.rest_1_), channel_id=1, source_target_pairs={{12,0},{16,4},{20,8},{24,12},{28,16},{32,20},{36,24},{40,28},{44,3... | collective-permute-start | bytes 393224 | tf_op jit(solution)/shard_map/ppermute | solution.py:20
  74.8 1.9 %collective-permute-start.6 = (bf16[2,256,128]{2,1,0:T(8,128)(2,1)S(1)}, bf16[2,256,128]{2,1,0:T(8,128)(2,1)S(1)}, u32[]{:S(2)}, u32[]{:S(2)}) collective-permute-start(bf16[2,256,128]{2,1,0:T(8,128)(2,1)S(1)} %get-tuple-element.15.rest_2_), channel_id=1, source_target_pairs={{8,0},{12,4},{16,8},{20,12},{24,16},{28,20},{32,24},{36,28},{40,32... | collective-permute-start | bytes 393224 | tf_op jit(solution)/shard_map/ppermute | solution.py:20
  76.8 3.9 %collective-permute-start.7 = (bf16[2,256,128]{2,1,0:T(8,128)(2,1)S(1)}, bf16[2,256,128]{2,1,0:T(8,128)(2,1)S(1)}, u32[]{:S(2)}, u32[]{:S(2)}) collective-permute-start(bf16[2,256,128]{2,1,0:T(8,128)(2,1)S(1)} %get-tuple-element.14.rest_3_), channel_id=1, source_target_pairs={{4,0},{8,4},{12,8},{16,12},{20,16},{24,20},{28,24},{32,28},{36,32}... | collective-permute-start | bytes 393224 | tf_op jit(solution)/shard_map/ppermute | solution.py:20
  80.7 14.6 %shard_map.51 = (bf16[256,1024]{1,0:T(8,128)(2,1)}, f32[2,128,1280]{2,1,0:T(8,128)}) custom-call(f32[256,1280]{1,0:T(8,128)} %fusion.2.bias_ref, bf16[256,2048]{1,0:T(8,128)(2,1)} %bitcast.40, bf16[256,2048]{1,0:T(8,128)(2,1)} %bitcast.42, bf16[2,1280,256]{2,1,0:T(8,128)(2,1)} %copy-done.5, bf16[2,1280,256]{2,1,0:T(8,128)(2,1)} %copy-done.5, ...), custom_call_target="tpu_custom_call" | custom-call | flops 4026531840 | bytes 4849664 | tf_op jit(solution)/shard_map/pallas_call | solution.py:70
  97.2 1.9 %collective-permute-start.10 = (bf16[2,256,128]{2,1,0:T(8,128)(2,1)S(1)}, bf16[2,256,128]{2,1,0:T(8,128)(2,1)S(1)}, u32[]{:S(2)}, u32[]{:S(2)}) collective-permute-start(bf16[2,256,128]{2,1,0:T(8,128)(2,1)S(1)} %get-tuple-element.12), channel_id=1, source_target_pairs={{8,0},{12,4},{16,8},{20,12},{24,16},{28,20},{32,24},{36,28},{40,32... | collective-permute-start | bytes 393224 | tf_op jit(solution)/shard_map/ppermute | solution.py:20
  99.1 1.9 %collective-permute-start.11 = (bf16[2,256,128]{2,1,0:T(8,128)(2,1)S(1)}, bf16[2,256,128]{2,1,0:T(8,128)(2,1)S(1)}, u32[]{:S(2)}, u32[]{:S(2)}) collective-permute-start(bf16[2,256,128]{2,1,0:T(8,128)(2,1)S(1)} %get-tuple-element.11), channel_id=1, source_target_pairs={{4,0},{8,4},{12,8},{16,12},{20,16},{24,20},{28,24},{32,28},{36,32}... | collective-permute-start | bytes 393224 | tf_op jit(solution)/shard_map/ppermute | solution.py:20
  101.0 1.9 %collective-permute-start.8 = (bf16[2,256,128]{2,1,0:T(8,128)(2,1)S(1)}, bf16[2,256,128]{2,1,0:T(8,128)(2,1)S(1)}, u32[]{:S(2)}, u32[]{:S(2)}) collective-permute-start(bf16[2,256,128]{2,1,0:T(8,128)(2,1)S(1)} %get-tuple-element.10), channel_id=1, source_target_pairs={{16,0},{20,4},{24,8},{28,12},{32,16},{36,20},{40,24},{44,28},{48,3... | collective-permute-start | bytes 393224 | tf_op jit(solution)/shard_map/ppermute | solution.py:20
  103.0 1.9 %collective-permute-start.9 = (bf16[2,256,128]{2,1,0:T(8,128)(2,1)S(1)}, bf16[2,256,128]{2,1,0:T(8,128)(2,1)S(1)}, u32[]{:S(2)}, u32[]{:S(2)}) collective-permute-start(bf16[2,256,128]{2,1,0:T(8,128)(2,1)S(1)} %get-tuple-element.13), channel_id=1, source_target_pairs={{12,0},{16,4},{20,8},{24,12},{28,16},{32,20},{36,24},{40,28},{44,3... | collective-permute-start | bytes 393224 | tf_op jit(solution)/shard_map/ppermute | solution.py:20
  105.5 3.9 %collective-permute-done.11 = bf16[2,256,128]{2,1,0:T(8,128)(2,1)S(1)} collective-permute-done((bf16[2,256,128]{2,1,0:T(8,128)(2,1)S(1)}, bf16[2,256,128]{2,1,0:T(8,128)(2,1)S(1)}, u32[]{:S(2)}, u32[]{:S(2)}) %collective-permute-start.11) | collective-permute-done | bytes 131104 | tf_op jit(solution)/shard_map/ppermute | solution.py:20
  109.4 6.8 %collective-permute-done.8 = bf16[2,256,128]{2,1,0:T(8,128)(2,1)S(1)} collective-permute-done((bf16[2,256,128]{2,1,0:T(8,128)(2,1)S(1)}, bf16[2,256,128]{2,1,0:T(8,128)(2,1)S(1)}, u32[]{:S(2)}, u32[]{:S(2)}) %collective-permute-start.8) | collective-permute-done | bytes 131104 | tf_op jit(solution)/shard_map/ppermute | solution.py:20
  116.2 7.0 %collective-permute-done.9 = bf16[2,256,128]{2,1,0:T(8,128)(2,1)S(1)} collective-permute-done((bf16[2,256,128]{2,1,0:T(8,128)(2,1)S(1)}, bf16[2,256,128]{2,1,0:T(8,128)(2,1)S(1)}, u32[]{:S(2)}, u32[]{:S(2)}) %collective-permute-start.9) | collective-permute-done | bytes 131104 | tf_op jit(solution)/shard_map/ppermute | solution.py:20
  124.0 5.0 %all-to-all-start.1 = ((bf16[2,16,16,256]{3,2,0,1:T(8,128)(2,1)}), bf16[2,16,16,256]{3,2,0,1:T(8,128)(2,1)S(1)}, u32[]{:S(2)}, u32[]{:S(2)}) async-start(bf16[2,16,16,256]{3,2,0,1:T(8,128)(2,1)} %copy.22), calls=%async_computation.1 | async-start | bytes 524288 | tf_op jit(solution)/shard_map/all_to_all | solution.py:104
  130.1 6.6 %all-to-all-done.1 = bf16[2,16,16,256]{3,2,0,1:T(8,128)(2,1)S(1)} async-done(((bf16[2,16,16,256]{3,2,0,1:T(8,128)(2,1)}), bf16[2,16,16,256]{3,2,0,1:T(8,128)(2,1)S(1)}, u32[]{:S(2)}, u32[]{:S(2)}) %all-to-all-start.1) | async-done | bytes 262176 | tf_op jit(solution)/shard_map/all_to_all | solution.py:104
  136.8 12.5 %all_gather.3 = bf16[2,64,1024]{2,1,0:T(8,128)(2,1)S(1)} all-gather(bf16[2,16,1024]{2,1,0:T(8,128)(2,1)S(1)} %bitcast.38), channel_id=1, replica_groups=mesh['section'=4,'seq'=16,'tp'=4] {'section'}, dimensions={1}, use_global_device_ids=true | all-gather | bytes 327680 | tf_op jit(solution)/shard_map/all_gather | solution.py:155
  (48 shorter events, 15.6 us)
Async XLA Ops:
  3.0 9.4 %all-to-all-start = ((bf16[4,2,16384]{2,1,0:T(2,128)(2,1)}), bf16[4,2,16384]{2,1,0:T(2,128)(2,1)S(1)}, u32[]{:S(2)}, u32[]{:S(2)}) async-start(bf16[4,2,16384]{2,1,0:T(2,128)(2,1)} %reshape.36), calls=%async_computation | async-start | bytes 524288 | tf_op jit(solution)/shard_map/all_to_all | solution.py:113
  13.1 19.2 %collective-permute-start = (bf16[2,256,256]{2,1,0:T(8,128)(2,1)S(1)}, bf16[2,256,256]{2,1,0:T(8,128)(2,1)S(1)}, u32[]{:S(2)}, u32[]{:S(2)}) collective-permute-start(bf16[2,256,256]{2,1,0:T(8,128)(2,1)S(1)} %bitcast.30), channel_id=1, source_target_pairs={{0,16},{4,20},{8,24},{12,28},{16,32},{20,36},{24,40},{28,44},{32,4... | collective-permute-start | bytes 786440 | tf_op jit(solution)/shard_map/ppermute | solution.py:20
  19.5 23.4 %collective-permute-start.1 = (bf16[2,256,256]{2,1,0:T(8,128)(2,1)S(1)}, bf16[2,256,256]{2,1,0:T(8,128)(2,1)S(1)}, u32[]{:S(2)}, u32[]{:S(2)}) collective-permute-start(bf16[2,256,256]{2,1,0:T(8,128)(2,1)S(1)} %bitcast.31), channel_id=1, source_target_pairs={{0,12},{4,16},{8,20},{12,24},{16,28},{20,32},{24,36},{28,40},{32,4... | collective-permute-start | bytes 786440 | tf_op jit(solution)/shard_map/ppermute | solution.py:20
  22.7 25.9 %collective-permute-start.2 = (bf16[2,256,256]{2,1,0:T(8,128)(2,1)S(1)}, bf16[2,256,256]{2,1,0:T(8,128)(2,1)S(1)}, u32[]{:S(2)}, u32[]{:S(2)}) collective-permute-start(bf16[2,256,256]{2,1,0:T(8,128)(2,1)S(1)} %bitcast.32), channel_id=1, source_target_pairs={{0,8},{4,12},{8,16},{12,20},{16,24},{20,28},{24,32},{28,36},{32,40... | collective-permute-start | bytes 786440 | tf_op jit(solution)/shard_map/ppermute | solution.py:20
  27.3 25.6 %collective-permute-start.3 = (bf16[2,256,256]{2,1,0:T(8,128)(2,1)S(1)}, bf16[2,256,256]{2,1,0:T(8,128)(2,1)S(1)}, u32[]{:S(2)}, u32[]{:S(2)}) collective-permute-start(bf16[2,256,256]{2,1,0:T(8,128)(2,1)S(1)} %bitcast.33), channel_id=1, source_target_pairs={{0,4},{4,8},{8,12},{12,16},{16,20},{20,24},{24,28},{28,32},{32,36}... | collective-permute-start | bytes 786440 | tf_op jit(solution)/shard_map/ppermute | solution.py:20
  52.9 1.1 copy-start.5
  71.0 9.7 %copy-start.2 = (bf16[2,256,128]{2,1,0:T(8,128)(2,1)}, bf16[2,256,128]{2,1,0:T(8,128)(2,1)S(1)}, u32[]{:S(2)}) copy-start(bf16[2,256,128]{2,1,0:T(8,128)(2,1)S(1)} %get-tuple-element.14.rest_3_) | copy-start | bytes 393220
  71.0 9.7 %copy-start.3 = (bf16[2,256,128]{2,1,0:T(8,128)(2,1)}, bf16[2,256,128]{2,1,0:T(8,128)(2,1)S(1)}, u32[]{:S(2)}) copy-start(bf16[2,256,128]{2,1,0:T(8,128)(2,1)S(1)} %get-tuple-element.15.rest_2_) | copy-start | bytes 393220
  71.0 9.7 %copy-start.4 = (bf16[2,256,128]{2,1,0:T(8,128)(2,1)}, bf16[2,256,128]{2,1,0:T(8,128)(2,1)S(1)}, u32[]{:S(2)}) copy-start(bf16[2,256,128]{2,1,0:T(8,128)(2,1)S(1)} %get-tuple-element.16.rest_1_) | copy-start | bytes 393220
  71.0 28.1 %collective-permute-start.4 = (bf16[2,256,128]{2,1,0:T(8,128)(2,1)}, bf16[2,256,128]{2,1,0:T(8,128)(2,1)S(1)}, u32[]{:S(2)}, u32[]{:S(2)}) collective-permute-start(bf16[2,256,128]{2,1,0:T(8,128)(2,1)} %get-tuple-element.17.rest_0_), channel_id=1, source_target_pairs={{16,0},{20,4},{24,8},{28,12},{32,16},{36,20},{40,24},{44,28},{48,3... | collective-permute-start | bytes 393224 | tf_op jit(solution)/shard_map/ppermute | solution.py:20
  72.9 28.1 %collective-permute-start.5 = (bf16[2,256,128]{2,1,0:T(8,128)(2,1)S(1)}, bf16[2,256,128]{2,1,0:T(8,128)(2,1)S(1)}, u32[]{:S(2)}, u32[]{:S(2)}) collective-permute-start(bf16[2,256,128]{2,1,0:T(8,128)(2,1)S(1)} %get-tuple-element.16.rest_1_), channel_id=1, source_target_pairs={{12,0},{16,4},{20,8},{24,12},{28,16},{32,20},{36,24},{40,28},{44,3... | collective-permute-start | bytes 393224 | tf_op jit(solution)/shard_map/ppermute | solution.py:20
  74.8 28.1 %collective-permute-start.6 = (bf16[2,256,128]{2,1,0:T(8,128)(2,1)S(1)}, bf16[2,256,128]{2,1,0:T(8,128)(2,1)S(1)}, u32[]{:S(2)}, u32[]{:S(2)}) collective-permute-start(bf16[2,256,128]{2,1,0:T(8,128)(2,1)S(1)} %get-tuple-element.15.rest_2_), channel_id=1, source_target_pairs={{8,0},{12,4},{16,8},{20,12},{24,16},{28,20},{32,24},{36,28},{40,32... | collective-permute-start | bytes 393224 | tf_op jit(solution)/shard_map/ppermute | solution.py:20
  76.8 28.1 %collective-permute-start.7 = (bf16[2,256,128]{2,1,0:T(8,128)(2,1)S(1)}, bf16[2,256,128]{2,1,0:T(8,128)(2,1)S(1)}, u32[]{:S(2)}, u32[]{:S(2)}) collective-permute-start(bf16[2,256,128]{2,1,0:T(8,128)(2,1)S(1)} %get-tuple-element.14.rest_3_), channel_id=1, source_target_pairs={{4,0},{8,4},{12,8},{16,12},{20,16},{24,20},{28,24},{32,28},{36,32}... | collective-permute-start | bytes 393224 | tf_op jit(solution)/shard_map/ppermute | solution.py:20
  97.2 8.3 %collective-permute-start.10 = (bf16[2,256,128]{2,1,0:T(8,128)(2,1)S(1)}, bf16[2,256,128]{2,1,0:T(8,128)(2,1)S(1)}, u32[]{:S(2)}, u32[]{:S(2)}) collective-permute-start(bf16[2,256,128]{2,1,0:T(8,128)(2,1)S(1)} %get-tuple-element.12), channel_id=1, source_target_pairs={{8,0},{12,4},{16,8},{20,12},{24,16},{28,20},{32,24},{36,28},{40,32... | collective-permute-start | bytes 393224 | tf_op jit(solution)/shard_map/ppermute | solution.py:20
  99.1 10.3 %collective-permute-start.11 = (bf16[2,256,128]{2,1,0:T(8,128)(2,1)S(1)}, bf16[2,256,128]{2,1,0:T(8,128)(2,1)S(1)}, u32[]{:S(2)}, u32[]{:S(2)}) collective-permute-start(bf16[2,256,128]{2,1,0:T(8,128)(2,1)S(1)} %get-tuple-element.11), channel_id=1, source_target_pairs={{4,0},{8,4},{12,8},{16,12},{20,16},{24,20},{28,24},{32,28},{36,32}... | collective-permute-start | bytes 393224 | tf_op jit(solution)/shard_map/ppermute | solution.py:20
  101.0 15.1 %collective-permute-start.8 = (bf16[2,256,128]{2,1,0:T(8,128)(2,1)S(1)}, bf16[2,256,128]{2,1,0:T(8,128)(2,1)S(1)}, u32[]{:S(2)}, u32[]{:S(2)}) collective-permute-start(bf16[2,256,128]{2,1,0:T(8,128)(2,1)S(1)} %get-tuple-element.10), channel_id=1, source_target_pairs={{16,0},{20,4},{24,8},{28,12},{32,16},{36,20},{40,24},{44,28},{48,3... | collective-permute-start | bytes 393224 | tf_op jit(solution)/shard_map/ppermute | solution.py:20
  103.0 20.1 %collective-permute-start.9 = (bf16[2,256,128]{2,1,0:T(8,128)(2,1)S(1)}, bf16[2,256,128]{2,1,0:T(8,128)(2,1)S(1)}, u32[]{:S(2)}, u32[]{:S(2)}) collective-permute-start(bf16[2,256,128]{2,1,0:T(8,128)(2,1)S(1)} %get-tuple-element.13), channel_id=1, source_target_pairs={{12,0},{16,4},{20,8},{24,12},{28,16},{32,20},{36,24},{40,28},{44,3... | collective-permute-start | bytes 393224 | tf_op jit(solution)/shard_map/ppermute | solution.py:20
  123.1 5.9 %copy-start = (bf16[256,1024]{1,0:T(8,128)(2,1)S(1)}, bf16[256,1024]{1,0:T(8,128)(2,1)}, u32[]{:S(2)}) copy-start(bf16[256,1024]{1,0:T(8,128)(2,1)} %get-tuple-element.6) | copy-start | bytes 1572868
  123.1 5.9 %copy-start.1 = (bf16[256,1024]{1,0:T(8,128)(2,1)S(1)}, bf16[256,1024]{1,0:T(8,128)(2,1)}, u32[]{:S(2)}) copy-start(bf16[256,1024]{1,0:T(8,128)(2,1)} %get-tuple-element.8) | copy-start | bytes 1572868
  124.0 12.6 %all-to-all-start.1 = ((bf16[2,16,16,256]{3,2,0,1:T(8,128)(2,1)}), bf16[2,16,16,256]{3,2,0,1:T(8,128)(2,1)S(1)}, u32[]{:S(2)}, u32[]{:S(2)}) async-start(bf16[2,16,16,256]{3,2,0,1:T(8,128)(2,1)} %copy.22), calls=%async_computation.1 | async-start | bytes 524288 | tf_op jit(solution)/shard_map/all_to_all | solution.py:104

commit v10 on v9

--- a/solution.py
+++ b/solution.py
@@ -20,11 +20,11 @@
     return lax.ppermute(value, axis, pairs)
 
 
-def attn_kernel(bias_ref, q_ref, g_ref, k_ref, v_ref, *rest, scale, hd, per_step):
+def attn_kernel(bias_ref, q_ref, g_ref, kt_ref, vt_ref, *rest, scale, hd, per_step):
     dq_ref, dkv_ref = rest[-2:]
     gi = pl.program_id(1)
-    k = k_ref[...]
-    v = v_ref[...]
+    kt = kt_ref[...]
+    vt = vt_ref[...]
     bias = bias_ref[...]
     nt = (((1,), (1,)), ((), ()))
     tn = (((0,), (0,)), ((), ()))
@@ -34,16 +34,16 @@
         cols = slice(part * hd, (part + 1) * hd)
         q = q_ref[:, cols]
         do = g_ref[:, cols]
-        s = lax.dot_general(q, k, nt, preferred_element_type=jnp.float32) * scale + bias
+        s = jnp.dot(q, kt, preferred_element_type=jnp.float32) * scale + bias
         m = jnp.max(s, axis=1, keepdims=True)
         w = jnp.exp(s - m)
         p = w * (1.0 / jnp.sum(w, axis=1, keepdims=True))
         pb = p.astype(jnp.bfloat16)
-        o = jnp.dot(pb, v, preferred_element_type=jnp.float32)
+        o = lax.dot_general(vt, pb, nt, preferred_element_type=jnp.float32).T
         delta = jnp.sum(do.astype(jnp.float32) * o, axis=1, keepdims=True)
-        dp = lax.dot_general(do, v, nt, preferred_element_type=jnp.float32)
+        dp = jnp.dot(do, vt, preferred_element_type=jnp.float32)
         dsb = (p * (dp - delta)).astype(jnp.bfloat16)
-        dq = jnp.dot(dsb, k, preferred_element_type=jnp.float32) * scale
+        dq = lax.dot_general(kt, dsb, nt, preferred_element_type=jnp.float32).T * scale
         dq_ref[:, cols] = dq.astype(dq_ref.dtype)
         dk_part = lax.dot_general(q, dsb, tn, preferred_element_type=jnp.float32) * scale
         dv_part = lax.dot_general(do, pb, tn, preferred_element_type=jnp.float32)
@@ -63,7 +63,7 @@
 
 def attention_grads(bias, q, g, ext, group, hd, scale, per_step, head0, heads, after=()):
     rows, _ = q.shape
-    _, ext_rows, _ = ext.shape
+    _, _, ext_rows = ext.shape
     steps = group // per_step
     width = per_step * hd
     flops = 6 * 2 * rows * ext_rows * hd * heads * group
@@ -74,8 +74,8 @@
             pl.BlockSpec((rows, ext_rows), lambda h, i: (0, 0)),
             pl.BlockSpec((rows, width), lambda h, i: (0, (head0 + h) * steps + i)),
             pl.BlockSpec((rows, width), lambda h, i: (0, (head0 + h) * steps + i)),
-            pl.BlockSpec((None, ext_rows, hd), lambda h, i: (0, 0, head0 + h)),
-            pl.BlockSpec((None, ext_rows, hd), lambda h, i: (1, 0, head0 + h)),
+            pl.BlockSpec((None, hd, ext_rows), lambda h, i: (0, head0 + h, 0)),
+            pl.BlockSpec((None, hd, ext_rows), lambda h, i: (1, head0 + h, 0)),
         ]
         + [pl.BlockSpec(memory_space=pl.ANY) for _ in after],
         out_specs=[
@@ -128,9 +128,10 @@
         & (position * tok_rows - WINDOW + key_ids >= 0)
     )
     bias = jnp.where(allowed, 0.0, -jnp.inf).astype(jnp.float32)
+    extended = jnp.swapaxes(extended, 1, 2)
     query_rows = queries.reshape(tok_rows, -1)
     grad_rows = upstream.reshape(tok_rows, -1)
-    local_heads = extended.shape[2] // head_size
+    local_heads = extended.shape[1] // head_size
     d_query_parts = []
     own_parts = []
     sent = []

time: 151 us -> 156 us (1.033)
  Pallas kernels: 29.2 us -> 34.4 us
    pallas_call x2, Pallas kernels: 29.2 us -> 34.4 us  [attention_grads(): pl.pallas_call(functools.partial(attn_kernel, scale=scale, hd=hd, per_ste...]
  transfers between devices with their start and end apart: 14 -> 14, of which waited for: 9 -> 9; matrix products, arithmetic and copies ran while one was open for 3% -> 3% of each run, Pallas kernels for 10% -> 11%
where the time goes in v10:
time: 156 us
  waiting for transfers between devices  51.1 us (33%)
  starting transfers between devices  43.2 us (28%)
  Pallas kernels  34.4 us (22%)
  blocking collectives  12.5 us (8%)
  local copies, waits for them, and re-layouts  9.38 us (6%)
  other arithmetic  4.01 us (3%)
    ppermute x12, waiting for transfers between devices, shifted(): return lax.ppermute(value, axis, pairs)  38.5 us
    ppermute x12, starting transfers between devices, shifted(): return lax.ppermute(value, axis, pairs)  34.9 us
    pallas_call x2, Pallas kernels, attention_grads(): pl.pallas_call(functools.partial(attn_kernel, scale=scale, hd=hd, per_ste...  34.4 us
    all_gather x1, blocking collectives, body(): lax.all_gather(chunk.reshape(kinds, rows, -1).astype(jnp.bfloat16), 'sect...  12.5 us
    all_to_all x1, waiting for transfers between devices, scatter_layers(): lax.all_to_all(pieces.astype(jnp.bfloat16), ('section', 'tp'), split_axis...  6.59 us
    all_to_all x1, waiting for transfers between devices, body(): lax.all_to_all(shared_kv, 'tp', split_axis=2, concat_axis=1, tiled=True)  5.94 us
    all_to_all x1, starting transfers between devices, scatter_layers(): lax.all_to_all(pieces.astype(jnp.bfloat16), ('section', 'tp'), split_axis...  4.96 us
    unnamed x19, local copies, waits for them, and re-layouts  3.84 us
  transfers between devices with their start and end apart: 14, of which 9 were waited for; matrix products, arithmetic and copies ran while one was open for 3% of the time, Pallas kernels for 11%

profile of v10, /device:TPU:80, one launch (start us, length us, event | category | flops | bytes accessed | tf_op | source)
XLA Modules:
  0.0 155.6 jit_solution(18250088506289311083)
XLA Ops:
  3.0 3.4 %all-to-all-start = ((bf16[4,2,16384]{2,1,0:T(2,128)(2,1)}), bf16[4,2,16384]{2,1,0:T(2,128)(2,1)S(1)}, u32[]{:S(2)}, u32[]{:S(2)}) async-start(bf16[4,2,16384]{2,1,0:T(2,128)(2,1)} %reshape.36), calls=%async_computation | async-start | bytes 524288 | tf_op jit(solution)/shard_map/all_to_all | solution.py:113
  6.4 5.9 %all-to-all-done = bf16[4,2,16384]{2,1,0:T(2,128)(2,1)S(1)} async-done(((bf16[4,2,16384]{2,1,0:T(2,128)(2,1)}), bf16[4,2,16384]{2,1,0:T(2,128)(2,1)S(1)}, u32[]{:S(2)}, u32[]{:S(2)}) %all-to-all-start) | async-done | bytes 262176 | tf_op jit(solution)/shard_map/all_to_all | solution.py:113
  13.4 6.4 %collective-permute-start = (bf16[2,256,256]{1,2,0:T(8,128)(2,1)S(1)}, bf16[2,256,256]{1,2,0:T(8,128)(2,1)S(1)}, u32[]{:S(2)}, u32[]{:S(2)}) collective-permute-start(bf16[2,256,256]{1,2,0:T(8,128)(2,1)S(1)} %copy.29), channel_id=1, source_target_pairs={{0,16},{4,20},{8,24},{12,28},{16,32},{20,36},{24,40},{28,44},{32,4... | collective-permute-start | bytes 786440 | tf_op jit(solution)/shard_map/ppermute | solution.py:20
  19.8 3.2 %collective-permute-start.1 = (bf16[2,256,256]{1,2,0:T(8,128)(2,1)S(1)}, bf16[2,256,256]{1,2,0:T(8,128)(2,1)S(1)}, u32[]{:S(2)}, u32[]{:S(2)}) collective-permute-start(bf16[2,256,256]{1,2,0:T(8,128)(2,1)S(1)} %copy.29), channel_id=1, source_target_pairs={{0,12},{4,16},{8,20},{12,24},{16,28},{20,32},{24,36},{28,40},{32,4... | collective-permute-start | bytes 786440 | tf_op jit(solution)/shard_map/ppermute | solution.py:20
  22.9 2.9 %collective-permute-start.2 = (bf16[2,256,256]{1,2,0:T(8,128)(2,1)S(1)}, bf16[2,256,256]{1,2,0:T(8,128)(2,1)S(1)}, u32[]{:S(2)}, u32[]{:S(2)}) collective-permute-start(bf16[2,256,256]{1,2,0:T(8,128)(2,1)S(1)} %copy.29), channel_id=1, source_target_pairs={{0,8},{4,12},{8,16},{12,20},{16,24},{20,28},{24,32},{28,36},{32,40... | collective-permute-start | bytes 786440 | tf_op jit(solution)/shard_map/ppermute | solution.py:20
  27.5 5.1 %collective-permute-start.3 = (bf16[2,256,256]{1,2,0:T(8,128)(2,1)S(1)}, bf16[2,256,256]{1,2,0:T(8,128)(2,1)S(1)}, u32[]{:S(2)}, u32[]{:S(2)}) collective-permute-start(bf16[2,256,256]{1,2,0:T(8,128)(2,1)S(1)} %copy.29), channel_id=1, source_target_pairs={{0,4},{4,8},{8,12},{12,16},{16,20},{20,24},{24,28},{28,32},{32,36}... | collective-permute-start | bytes 786440 | tf_op jit(solution)/shard_map/ppermute | solution.py:20
  32.6 10.6 %collective-permute-done.1 = bf16[2,256,256]{1,2,0:T(8,128)(2,1)S(1)} collective-permute-done((bf16[2,256,256]{1,2,0:T(8,128)(2,1)S(1)}, bf16[2,256,256]{1,2,0:T(8,128)(2,1)S(1)}, u32[]{:S(2)}, u32[]{:S(2)}) %collective-permute-start.1) | collective-permute-done | bytes 262176 | tf_op jit(solution)/shard_map/ppermute | solution.py:20
  43.2 5.6 %collective-permute-done.2 = bf16[2,256,256]{1,2,0:T(8,128)(2,1)S(1)} collective-permute-done((bf16[2,256,256]{1,2,0:T(8,128)(2,1)S(1)}, bf16[2,256,256]{1,2,0:T(8,128)(2,1)S(1)}, u32[]{:S(2)}, u32[]{:S(2)}) %collective-permute-start.2) | collective-permute-done | bytes 262176 | tf_op jit(solution)/shard_map/ppermute | solution.py:20
  48.8 4.2 %collective-permute-done.3 = bf16[2,256,256]{1,2,0:T(8,128)(2,1)S(1)} collective-permute-done((bf16[2,256,256]{1,2,0:T(8,128)(2,1)S(1)}, bf16[2,256,256]{1,2,0:T(8,128)(2,1)S(1)}, u32[]{:S(2)}, u32[]{:S(2)}) %collective-permute-start.3) | collective-permute-done | bytes 262176 | tf_op jit(solution)/shard_map/ppermute | solution.py:20
  54.2 17.2 %shard_map.50 = (bf16[256,1024]{1,0:T(8,128)(2,1)}, f32[2,128,1280]{2,1,0:T(8,128)}) custom-call(f32[256,1280]{1,0:T(8,128)} %fusion.2.bias_ref, bf16[256,2048]{1,0:T(8,128)(2,1)} %bitcast.40, bf16[256,2048]{1,0:T(8,128)(2,1)} %bitcast.42, bf16[2,256,1280]{2,1,0:T(8,128)(2,1)} %bitcast.36, bf16[2,256,1280]{2,1,0:T(8,128)(2,1)} %bitcast.37), custom_call_target="tpu_custom_call" | custom-call | flops 4026531840 | bytes 4849664 | tf_op jit(solution)/shard_map/pallas_call | solution.py:70
  75.7 1.9 %collective-permute-start.5 = (bf16[2,256,128]{2,1,0:T(8,128)(2,1)S(1)}, bf16[2,256,128]{2,1,0:T(8,128)(2,1)S(1)}, u32[]{:S(2)}, u32[]{:S(2)}) collective-permute-start(bf16[2,256,128]{2,1,0:T(8,128)(2,1)S(1)} %get-tuple-element.16.rest_1_), channel_id=1, source_target_pairs={{12,0},{16,4},{20,8},{24,12},{28,16},{32,20},{36,24},{40,28},{44,3... | collective-permute-start | bytes 393224 | tf_op jit(solution)/shard_map/ppermute | solution.py:20
  77.7 1.9 %collective-permute-start.6 = (bf16[2,256,128]{2,1,0:T(8,128)(2,1)S(1)}, bf16[2,256,128]{2,1,0:T(8,128)(2,1)S(1)}, u32[]{:S(2)}, u32[]{:S(2)}) collective-permute-start(bf16[2,256,128]{2,1,0:T(8,128)(2,1)S(1)} %get-tuple-element.15.rest_2_), channel_id=1, source_target_pairs={{8,0},{12,4},{16,8},{20,12},{24,16},{28,20},{32,24},{36,28},{40,32... | collective-permute-start | bytes 393224 | tf_op jit(solution)/shard_map/ppermute | solution.py:20
  79.6 3.9 %collective-permute-start.7 = (bf16[2,256,128]{2,1,0:T(8,128)(2,1)S(1)}, bf16[2,256,128]{2,1,0:T(8,128)(2,1)S(1)}, u32[]{:S(2)}, u32[]{:S(2)}) collective-permute-start(bf16[2,256,128]{2,1,0:T(8,128)(2,1)S(1)} %get-tuple-element.14.rest_3_), channel_id=1, source_target_pairs={{4,0},{8,4},{12,8},{16,12},{20,16},{24,20},{28,24},{32,28},{36,32}... | collective-permute-start | bytes 393224 | tf_op jit(solution)/shard_map/ppermute | solution.py:20
  83.5 17.2 %shard_map.51 = (bf16[256,1024]{1,0:T(8,128)(2,1)}, f32[2,128,1280]{2,1,0:T(8,128)}) custom-call(f32[256,1280]{1,0:T(8,128)} %fusion.2.bias_ref, bf16[256,2048]{1,0:T(8,128)(2,1)} %bitcast.41, bf16[256,2048]{1,0:T(8,128)(2,1)} %bitcast.43, bf16[2,256,1280]{2,1,0:T(8,128)(2,1)} %bitcast.38, bf16[2,256,1280]{2,1,0:T(8,128)(2,1)} %bitcast.39, ...), custom_call_target="tpu_custom_call" | custom-call | flops 4026531840 | bytes 4849664 | tf_op jit(solution)/shard_map/pallas_call | solution.py:70
  102.6 1.9 %collective-permute-start.10 = (bf16[2,256,128]{2,1,0:T(8,128)(2,1)S(1)}, bf16[2,256,128]{2,1,0:T(8,128)(2,1)S(1)}, u32[]{:S(2)}, u32[]{:S(2)}) collective-permute-start(bf16[2,256,128]{2,1,0:T(8,128)(2,1)S(1)} %get-tuple-element.12), channel_id=1, source_target_pairs={{8,0},{12,4},{16,8},{20,12},{24,16},{28,20},{32,24},{36,28},{40,32... | collective-permute-start | bytes 393224 | tf_op jit(solution)/shard_map/ppermute | solution.py:20
  104.5 1.9 %collective-permute-start.11 = (bf16[2,256,128]{2,1,0:T(8,128)(2,1)S(1)}, bf16[2,256,128]{2,1,0:T(8,128)(2,1)S(1)}, u32[]{:S(2)}, u32[]{:S(2)}) collective-permute-start(bf16[2,256,128]{2,1,0:T(8,128)(2,1)S(1)} %get-tuple-element.11), channel_id=1, source_target_pairs={{4,0},{8,4},{12,8},{16,12},{20,16},{24,20},{28,24},{32,28},{36,32}... | collective-permute-start | bytes 393224 | tf_op jit(solution)/shard_map/ppermute | solution.py:20
  106.4 1.9 %collective-permute-start.8 = (bf16[2,256,128]{2,1,0:T(8,128)(2,1)S(1)}, bf16[2,256,128]{2,1,0:T(8,128)(2,1)S(1)}, u32[]{:S(2)}, u32[]{:S(2)}) collective-permute-start(bf16[2,256,128]{2,1,0:T(8,128)(2,1)S(1)} %get-tuple-element.10), channel_id=1, source_target_pairs={{16,0},{20,4},{24,8},{28,12},{32,16},{36,20},{40,24},{44,28},{48,3... | collective-permute-start | bytes 393224 | tf_op jit(solution)/shard_map/ppermute | solution.py:20
  108.4 1.9 %collective-permute-start.9 = (bf16[2,256,128]{2,1,0:T(8,128)(2,1)S(1)}, bf16[2,256,128]{2,1,0:T(8,128)(2,1)S(1)}, u32[]{:S(2)}, u32[]{:S(2)}) collective-permute-start(bf16[2,256,128]{2,1,0:T(8,128)(2,1)S(1)} %get-tuple-element.13), channel_id=1, source_target_pairs={{12,0},{16,4},{20,8},{24,12},{28,16},{32,20},{36,24},{40,28},{44,3... | collective-permute-start | bytes 393224 | tf_op jit(solution)/shard_map/ppermute | solution.py:20
  110.9 3.9 %collective-permute-done.11 = bf16[2,256,128]{2,1,0:T(8,128)(2,1)S(1)} collective-permute-done((bf16[2,256,128]{2,1,0:T(8,128)(2,1)S(1)}, bf16[2,256,128]{2,1,0:T(8,128)(2,1)S(1)}, u32[]{:S(2)}, u32[]{:S(2)}) %collective-permute-start.11) | collective-permute-done | bytes 131104 | tf_op jit(solution)/shard_map/ppermute | solution.py:20
  114.8 6.8 %collective-permute-done.8 = bf16[2,256,128]{2,1,0:T(8,128)(2,1)S(1)} collective-permute-done((bf16[2,256,128]{2,1,0:T(8,128)(2,1)S(1)}, bf16[2,256,128]{2,1,0:T(8,128)(2,1)S(1)}, u32[]{:S(2)}, u32[]{:S(2)}) %collective-permute-start.8) | collective-permute-done | bytes 131104 | tf_op jit(solution)/shard_map/ppermute | solution.py:20
  121.6 7.0 %collective-permute-done.9 = bf16[2,256,128]{2,1,0:T(8,128)(2,1)S(1)} collective-permute-done((bf16[2,256,128]{2,1,0:T(8,128)(2,1)S(1)}, bf16[2,256,128]{2,1,0:T(8,128)(2,1)S(1)}, u32[]{:S(2)}, u32[]{:S(2)}) %collective-permute-start.9) | collective-permute-done | bytes 131104 | tf_op jit(solution)/shard_map/ppermute | solution.py:20
  129.4 5.0 %all-to-all-start.1 = ((bf16[2,16,16,256]{3,2,0,1:T(8,128)(2,1)}), bf16[2,16,16,256]{3,2,0,1:T(8,128)(2,1)S(1)}, u32[]{:S(2)}, u32[]{:S(2)}) async-start(bf16[2,16,16,256]{3,2,0,1:T(8,128)(2,1)} %copy.37), calls=%async_computation.1 | async-start | bytes 524288 | tf_op jit(solution)/shard_map/all_to_all | solution.py:104
  135.5 6.6 %all-to-all-done.1 = bf16[2,16,16,256]{3,2,0,1:T(8,128)(2,1)S(1)} async-done(((bf16[2,16,16,256]{3,2,0,1:T(8,128)(2,1)}), bf16[2,16,16,256]{3,2,0,1:T(8,128)(2,1)S(1)}, u32[]{:S(2)}, u32[]{:S(2)}) %all-to-all-start.1) | async-done | bytes 262176 | tf_op jit(solution)/shard_map/all_to_all | solution.py:104
  142.2 12.5 %all_gather.3 = bf16[2,64,1024]{2,1,0:T(8,128)(2,1)S(1)} all-gather(bf16[2,16,1024]{2,1,0:T(8,128)(2,1)S(1)} %bitcast.35), channel_id=1, replica_groups=mesh['section'=4,'seq'=16,'tp'=4] {'section'}, dimensions={1}, use_global_device_ids=true | all-gather | bytes 327680 | tf_op jit(solution)/shard_map/all_gather | solution.py:156
  (50 shorter events, 15.8 us)
Async XLA Ops:
  3.0 9.4 %all-to-all-start = ((bf16[4,2,16384]{2,1,0:T(2,128)(2,1)}), bf16[4,2,16384]{2,1,0:T(2,128)(2,1)S(1)}, u32[]{:S(2)}, u32[]{:S(2)}) async-start(bf16[4,2,16384]{2,1,0:T(2,128)(2,1)} %reshape.36), calls=%async_computation | async-start | bytes 524288 | tf_op jit(solution)/shard_map/all_to_all | solution.py:113
  13.4 19.2 %collective-permute-start = (bf16[2,256,256]{1,2,0:T(8,128)(2,1)S(1)}, bf16[2,256,256]{1,2,0:T(8,128)(2,1)S(1)}, u32[]{:S(2)}, u32[]{:S(2)}) collective-permute-start(bf16[2,256,256]{1,2,0:T(8,128)(2,1)S(1)} %copy.29), channel_id=1, source_target_pairs={{0,16},{4,20},{8,24},{12,28},{16,32},{20,36},{24,40},{28,44},{32,4... | collective-permute-start | bytes 786440 | tf_op jit(solution)/shard_map/ppermute | solution.py:20
  19.8 23.4 %collective-permute-start.1 = (bf16[2,256,256]{1,2,0:T(8,128)(2,1)S(1)}, bf16[2,256,256]{1,2,0:T(8,128)(2,1)S(1)}, u32[]{:S(2)}, u32[]{:S(2)}) collective-permute-start(bf16[2,256,256]{1,2,0:T(8,128)(2,1)S(1)} %copy.29), channel_id=1, source_target_pairs={{0,12},{4,16},{8,20},{12,24},{16,28},{20,32},{24,36},{28,40},{32,4... | collective-permute-start | bytes 786440 | tf_op jit(solution)/shard_map/ppermute | solution.py:20
  22.9 25.9 %collective-permute-start.2 = (bf16[2,256,256]{1,2,0:T(8,128)(2,1)S(1)}, bf16[2,256,256]{1,2,0:T(8,128)(2,1)S(1)}, u32[]{:S(2)}, u32[]{:S(2)}) collective-permute-start(bf16[2,256,256]{1,2,0:T(8,128)(2,1)S(1)} %copy.29), channel_id=1, source_target_pairs={{0,8},{4,12},{8,16},{12,20},{16,24},{20,28},{24,32},{28,36},{32,40... | collective-permute-start | bytes 786440 | tf_op jit(solution)/shard_map/ppermute | solution.py:20
  27.5 25.6 %collective-permute-start.3 = (bf16[2,256,256]{1,2,0:T(8,128)(2,1)S(1)}, bf16[2,256,256]{1,2,0:T(8,128)(2,1)S(1)}, u32[]{:S(2)}, u32[]{:S(2)}) collective-permute-start(bf16[2,256,256]{1,2,0:T(8,128)(2,1)S(1)} %copy.29), channel_id=1, source_target_pairs={{0,4},{4,8},{8,12},{12,16},{16,20},{20,24},{24,28},{28,32},{32,36}... | collective-permute-start | bytes 786440 | tf_op jit(solution)/shard_map/ppermute | solution.py:20
  53.1 1.1 copy-start.5
  73.8 9.7 %copy-start.2 = (bf16[2,256,128]{2,1,0:T(8,128)(2,1)}, bf16[2,256,128]{2,1,0:T(8,128)(2,1)S(1)}, u32[]{:S(2)}) copy-start(bf16[2,256,128]{2,1,0:T(8,128)(2,1)S(1)} %get-tuple-element.14.rest_3_) | copy-start | bytes 393220
  73.8 9.7 %copy-start.3 = (bf16[2,256,128]{2,1,0:T(8,128)(2,1)}, bf16[2,256,128]{2,1,0:T(8,128)(2,1)S(1)}, u32[]{:S(2)}) copy-start(bf16[2,256,128]{2,1,0:T(8,128)(2,1)S(1)} %get-tuple-element.15.rest_2_) | copy-start | bytes 393220
  73.8 9.7 %copy-start.4 = (bf16[2,256,128]{2,1,0:T(8,128)(2,1)}, bf16[2,256,128]{2,1,0:T(8,128)(2,1)S(1)}, u32[]{:S(2)}) copy-start(bf16[2,256,128]{2,1,0:T(8,128)(2,1)S(1)} %get-tuple-element.16.rest_1_) | copy-start | bytes 393220
  73.8 30.7 %collective-permute-start.4 = (bf16[2,256,128]{2,1,0:T(8,128)(2,1)}, bf16[2,256,128]{2,1,0:T(8,128)(2,1)S(1)}, u32[]{:S(2)}, u32[]{:S(2)}) collective-permute-start(bf16[2,256,128]{2,1,0:T(8,128)(2,1)} %get-tuple-element.17.rest_0_), channel_id=1, source_target_pairs={{16,0},{20,4},{24,8},{28,12},{32,16},{36,20},{40,24},{44,28},{48,3... | collective-permute-start | bytes 393224 | tf_op jit(solution)/shard_map/ppermute | solution.py:20
  75.7 30.7 %collective-permute-start.5 = (bf16[2,256,128]{2,1,0:T(8,128)(2,1)S(1)}, bf16[2,256,128]{2,1,0:T(8,128)(2,1)S(1)}, u32[]{:S(2)}, u32[]{:S(2)}) collective-permute-start(bf16[2,256,128]{2,1,0:T(8,128)(2,1)S(1)} %get-tuple-element.16.rest_1_), channel_id=1, source_target_pairs={{12,0},{16,4},{20,8},{24,12},{28,16},{32,20},{36,24},{40,28},{44,3... | collective-permute-start | bytes 393224 | tf_op jit(solution)/shard_map/ppermute | solution.py:20
  77.7 30.7 %collective-permute-start.6 = (bf16[2,256,128]{2,1,0:T(8,128)(2,1)S(1)}, bf16[2,256,128]{2,1,0:T(8,128)(2,1)S(1)}, u32[]{:S(2)}, u32[]{:S(2)}) collective-permute-start(bf16[2,256,128]{2,1,0:T(8,128)(2,1)S(1)} %get-tuple-element.15.rest_2_), channel_id=1, source_target_pairs={{8,0},{12,4},{16,8},{20,12},{24,16},{28,20},{32,24},{36,28},{40,32... | collective-permute-start | bytes 393224 | tf_op jit(solution)/shard_map/ppermute | solution.py:20
  79.6 30.7 %collective-permute-start.7 = (bf16[2,256,128]{2,1,0:T(8,128)(2,1)S(1)}, bf16[2,256,128]{2,1,0:T(8,128)(2,1)S(1)}, u32[]{:S(2)}, u32[]{:S(2)}) collective-permute-start(bf16[2,256,128]{2,1,0:T(8,128)(2,1)S(1)} %get-tuple-element.14.rest_3_), channel_id=1, source_target_pairs={{4,0},{8,4},{12,8},{16,12},{20,16},{24,20},{28,24},{32,28},{36,32}... | collective-permute-start | bytes 393224 | tf_op jit(solution)/shard_map/ppermute | solution.py:20
  102.6 8.3 %collective-permute-start.10 = (bf16[2,256,128]{2,1,0:T(8,128)(2,1)S(1)}, bf16[2,256,128]{2,1,0:T(8,128)(2,1)S(1)}, u32[]{:S(2)}, u32[]{:S(2)}) collective-permute-start(bf16[2,256,128]{2,1,0:T(8,128)(2,1)S(1)} %get-tuple-element.12), channel_id=1, source_target_pairs={{8,0},{12,4},{16,8},{20,12},{24,16},{28,20},{32,24},{36,28},{40,32... | collective-permute-start | bytes 393224 | tf_op jit(solution)/shard_map/ppermute | solution.py:20
  104.5 10.3 %collective-permute-start.11 = (bf16[2,256,128]{2,1,0:T(8,128)(2,1)S(1)}, bf16[2,256,128]{2,1,0:T(8,128)(2,1)S(1)}, u32[]{:S(2)}, u32[]{:S(2)}) collective-permute-start(bf16[2,256,128]{2,1,0:T(8,128)(2,1)S(1)} %get-tuple-element.11), channel_id=1, source_target_pairs={{4,0},{8,4},{12,8},{16,12},{20,16},{24,20},{28,24},{32,28},{36,32}... | collective-permute-start | bytes 393224 | tf_op jit(solution)/shard_map/ppermute | solution.py:20
  106.4 15.2 %collective-permute-start.8 = (bf16[2,256,128]{2,1,0:T(8,128)(2,1)S(1)}, bf16[2,256,128]{2,1,0:T(8,128)(2,1)S(1)}, u32[]{:S(2)}, u32[]{:S(2)}) collective-permute-start(bf16[2,256,128]{2,1,0:T(8,128)(2,1)S(1)} %get-tuple-element.10), channel_id=1, source_target_pairs={{16,0},{20,4},{24,8},{28,12},{32,16},{36,20},{40,24},{44,28},{48,3... | collective-permute-start | bytes 393224 | tf_op jit(solution)/shard_map/ppermute | solution.py:20
  108.4 20.2 %collective-permute-start.9 = (bf16[2,256,128]{2,1,0:T(8,128)(2,1)S(1)}, bf16[2,256,128]{2,1,0:T(8,128)(2,1)S(1)}, u32[]{:S(2)}, u32[]{:S(2)}) collective-permute-start(bf16[2,256,128]{2,1,0:T(8,128)(2,1)S(1)} %get-tuple-element.13), channel_id=1, source_target_pairs={{12,0},{16,4},{20,8},{24,12},{28,16},{32,20},{36,24},{40,28},{44,3... | collective-permute-start | bytes 393224 | tf_op jit(solution)/shard_map/ppermute | solution.py:20
  128.5 5.9 %copy-start = (bf16[256,1024]{1,0:T(8,128)(2,1)S(1)}, bf16[256,1024]{1,0:T(8,128)(2,1)}, u32[]{:S(2)}) copy-start(bf16[256,1024]{1,0:T(8,128)(2,1)} %get-tuple-element.6) | copy-start | bytes 1572868
  128.5 5.9 %copy-start.1 = (bf16[256,1024]{1,0:T(8,128)(2,1)S(1)}, bf16[256,1024]{1,0:T(8,128)(2,1)}, u32[]{:S(2)}) copy-start(bf16[256,1024]{1,0:T(8,128)(2,1)} %get-tuple-element.8) | copy-start | bytes 1572868
  129.4 12.6 %all-to-all-start.1 = ((bf16[2,16,16,256]{3,2,0,1:T(8,128)(2,1)}), bf16[2,16,16,256]{3,2,0,1:T(8,128)(2,1)S(1)}, u32[]{:S(2)}, u32[]{:S(2)}) async-start(bf16[2,16,16,256]{3,2,0,1:T(8,128)(2,1)} %copy.37), calls=%async_computation.1 | async-start | bytes 524288 | tf_op jit(solution)/shard_map/all_to_all | solution.py:104

commit v11 on v9

--- a/solution.py
+++ b/solution.py
@@ -20,11 +20,13 @@
     return lax.ppermute(value, axis, pairs)
 
 
-def attn_kernel(bias_ref, q_ref, g_ref, k_ref, v_ref, *rest, scale, hd, per_step):
+def attn_kernel(bias_ref, q_ref, g_ref, k_ref, v_ref, kt_ref, vt_ref, *rest, scale, hd, per_step):
     dq_ref, dkv_ref = rest[-2:]
     gi = pl.program_id(1)
     k = k_ref[...]
     v = v_ref[...]
+    kt = kt_ref[...]
+    vt = vt_ref[...]
     bias = bias_ref[...]
     nt = (((1,), (1,)), ((), ()))
     tn = (((0,), (0,)), ((), ()))
@@ -34,14 +36,14 @@
         cols = slice(part * hd, (part + 1) * hd)
         q = q_ref[:, cols]
         do = g_ref[:, cols]
-        s = lax.dot_general(q, k, nt, preferred_element_type=jnp.float32) * scale + bias
+        s = jnp.dot(q, kt, preferred_element_type=jnp.float32) * scale + bias
         m = jnp.max(s, axis=1, keepdims=True)
         w = jnp.exp(s - m)
         p = w * (1.0 / jnp.sum(w, axis=1, keepdims=True))
         pb = p.astype(jnp.bfloat16)
         o = jnp.dot(pb, v, preferred_element_type=jnp.float32)
         delta = jnp.sum(do.astype(jnp.float32) * o, axis=1, keepdims=True)
-        dp = lax.dot_general(do, v, nt, preferred_element_type=jnp.float32)
+        dp = jnp.dot(do, vt, preferred_element_type=jnp.float32)
         dsb = (p * (dp - delta)).astype(jnp.bfloat16)
         dq = jnp.dot(dsb, k, preferred_element_type=jnp.float32) * scale
         dq_ref[:, cols] = dq.astype(dq_ref.dtype)
@@ -61,7 +63,7 @@
         dkv_ref[1] += dv
 
 
-def attention_grads(bias, q, g, ext, group, hd, scale, per_step, head0, heads, after=()):
+def attention_grads(bias, q, g, ext, ext_t, group, hd, scale, per_step, head0, heads, after=()):
     rows, _ = q.shape
     _, ext_rows, _ = ext.shape
     steps = group // per_step
@@ -76,6 +78,8 @@
             pl.BlockSpec((rows, width), lambda h, i: (0, (head0 + h) * steps + i)),
             pl.BlockSpec((None, ext_rows, hd), lambda h, i: (0, 0, head0 + h)),
             pl.BlockSpec((None, ext_rows, hd), lambda h, i: (1, 0, head0 + h)),
+            pl.BlockSpec((None, hd, ext_rows), lambda h, i: (0, head0 + h, 0)),
+            pl.BlockSpec((None, hd, ext_rows), lambda h, i: (1, head0 + h, 0)),
         ]
         + [pl.BlockSpec(memory_space=pl.ANY) for _ in after],
         out_specs=[
@@ -92,7 +96,7 @@
             transcendentals=rows * ext_rows * heads * group,
             bytes_accessed=(3 * rows * group * 2 + ext_rows * 2 * 6) * hd * heads + bias.size * 4,
         ),
-    )(bias, q, g, ext, ext, *after)
+    )(bias, q, g, ext, ext, ext_t, ext_t, *after)
 
 
 def scatter_layers(own_rows):
@@ -128,6 +132,7 @@
         & (position * tok_rows - WINDOW + key_ids >= 0)
     )
     bias = jnp.where(allowed, 0.0, -jnp.inf).astype(jnp.float32)
+    extended_t = jnp.swapaxes(extended, 1, 2)
     query_rows = queries.reshape(tok_rows, -1)
     grad_rows = upstream.reshape(tok_rows, -1)
     local_heads = extended.shape[2] // head_size
@@ -136,7 +141,7 @@
     sent = []
     for kv_head in range(local_heads):
         d_query_part, grad_ext = attention_grads(
-            bias, query_rows, grad_rows, extended, group_size, head_size, score_scale, 2, kv_head, 1, sent
+            bias, query_rows, grad_rows, extended, extended_t, group_size, head_size, score_scale, 2, kv_head, 1, sent
         )
         grad_ext = jnp.swapaxes(grad_ext, 1, 2)
         d_query_parts.append(d_query_part)

time: 151 us -> 152 us (level)
  no operation moved by 1% of the time
where the time goes in v11:
time: 152 us; the launch traced here: 151 us
  waiting for transfers between devices  51 us (34%)
  starting transfers between devices  43.3 us (28%)
  Pallas kernels  29.5 us (19%)
  blocking collectives  12.5 us (8%)
  local copies, waits for them, and re-layouts  9.83 us (6%)
  other arithmetic  4.01 us (3%)
    ppermute x12, waiting for transfers between devices, shifted(): return lax.ppermute(value, axis, pairs)  38.5 us
    ppermute x12, starting transfers between devices, shifted(): return lax.ppermute(value, axis, pairs)  34.9 us
    pallas_call x2, Pallas kernels, attention_grads(): pl.pallas_call(functools.partial(attn_kernel, scale=scale, hd=hd, per_ste...  29.5 us
    all_gather x1, blocking collectives, body(): lax.all_gather(chunk.reshape(kinds, rows, -1).astype(jnp.bfloat16), 'sect...  12.5 us
    all_to_all x1, waiting for transfers between devices, scatter_layers(): lax.all_to_all(pieces.astype(jnp.bfloat16), ('section', 'tp'), split_axis...  6.59 us
    all_to_all x1, waiting for transfers between devices, body(): lax.all_to_all(shared_kv, 'tp', split_axis=2, concat_axis=1, tiled=True)  5.94 us
    all_to_all x1, starting transfers between devices, scatter_layers(): lax.all_to_all(pieces.astype(jnp.bfloat16), ('section', 'tp'), split_axis...  4.98 us
    pallas_call x2, local copies, waits for them, and re-layouts, attention_grads(): pl.pallas_call(functools.partial(attn_kernel, scale=scale, hd=hd, per_ste...  3.41 us
  transfers between devices with their start and end apart: 14, of which 9 were waited for; matrix products, arithmetic and copies ran while one was open for 3% of the time, Pallas kernels for 10%

profile of v11, /device:TPU:80, one launch (start us, length us, event | category | flops | bytes accessed | tf_op | source)
XLA Modules:
  0.0 151.2 jit_solution(16622638713229278784)
XLA Ops:
  3.0 3.4 %all-to-all-start = ((bf16[4,2,16384]{2,1,0:T(2,128)(2,1)}), bf16[4,2,16384]{2,1,0:T(2,128)(2,1)S(1)}, u32[]{:S(2)}, u32[]{:S(2)}) async-start(bf16[4,2,16384]{2,1,0:T(2,128)(2,1)} %reshape.36), calls=%async_computation | async-start | bytes 524288 | tf_op jit(solution)/shard_map/all_to_all | solution.py:117
  6.4 5.9 %all-to-all-done = bf16[4,2,16384]{2,1,0:T(2,128)(2,1)S(1)} async-done(((bf16[4,2,16384]{2,1,0:T(2,128)(2,1)}), bf16[4,2,16384]{2,1,0:T(2,128)(2,1)S(1)}, u32[]{:S(2)}, u32[]{:S(2)}) %all-to-all-start) | async-done | bytes 262176 | tf_op jit(solution)/shard_map/all_to_all | solution.py:117
  13.4 6.4 %collective-permute-start = (bf16[2,256,256]{1,2,0:T(8,128)(2,1)S(1)}, bf16[2,256,256]{1,2,0:T(8,128)(2,1)S(1)}, u32[]{:S(2)}, u32[]{:S(2)}) collective-permute-start(bf16[2,256,256]{1,2,0:T(8,128)(2,1)S(1)} %copy.41), channel_id=1, source_target_pairs={{0,16},{4,20},{8,24},{12,28},{16,32},{20,36},{24,40},{28,44},{32,4... | collective-permute-start | bytes 786440 | tf_op jit(solution)/shard_map/ppermute | solution.py:20
  19.8 3.2 %collective-permute-start.1 = (bf16[2,256,256]{1,2,0:T(8,128)(2,1)S(1)}, bf16[2,256,256]{1,2,0:T(8,128)(2,1)S(1)}, u32[]{:S(2)}, u32[]{:S(2)}) collective-permute-start(bf16[2,256,256]{1,2,0:T(8,128)(2,1)S(1)} %copy.41), channel_id=1, source_target_pairs={{0,12},{4,16},{8,20},{12,24},{16,28},{20,32},{24,36},{28,40},{32,4... | collective-permute-start | bytes 786440 | tf_op jit(solution)/shard_map/ppermute | solution.py:20
  22.9 2.9 %collective-permute-start.2 = (bf16[2,256,256]{1,2,0:T(8,128)(2,1)S(1)}, bf16[2,256,256]{1,2,0:T(8,128)(2,1)S(1)}, u32[]{:S(2)}, u32[]{:S(2)}) collective-permute-start(bf16[2,256,256]{1,2,0:T(8,128)(2,1)S(1)} %copy.41), channel_id=1, source_target_pairs={{0,8},{4,12},{8,16},{12,20},{16,24},{20,28},{24,32},{28,36},{32,40... | collective-permute-start | bytes 786440 | tf_op jit(solution)/shard_map/ppermute | solution.py:20
  27.5 5.1 %collective-permute-start.3 = (bf16[2,256,256]{1,2,0:T(8,128)(2,1)S(1)}, bf16[2,256,256]{1,2,0:T(8,128)(2,1)S(1)}, u32[]{:S(2)}, u32[]{:S(2)}) collective-permute-start(bf16[2,256,256]{1,2,0:T(8,128)(2,1)S(1)} %copy.41), channel_id=1, source_target_pairs={{0,4},{4,8},{8,12},{12,16},{16,20},{20,24},{24,28},{28,32},{32,36}... | collective-permute-start | bytes 786440 | tf_op jit(solution)/shard_map/ppermute | solution.py:20
  32.6 10.6 %collective-permute-done.1 = bf16[2,256,256]{1,2,0:T(8,128)(2,1)S(1)} collective-permute-done((bf16[2,256,256]{1,2,0:T(8,128)(2,1)S(1)}, bf16[2,256,256]{1,2,0:T(8,128)(2,1)S(1)}, u32[]{:S(2)}, u32[]{:S(2)}) %collective-permute-start.1) | collective-permute-done | bytes 262176 | tf_op jit(solution)/shard_map/ppermute | solution.py:20
  43.2 5.6 %collective-permute-done.2 = bf16[2,256,256]{1,2,0:T(8,128)(2,1)S(1)} collective-permute-done((bf16[2,256,256]{1,2,0:T(8,128)(2,1)S(1)}, bf16[2,256,256]{1,2,0:T(8,128)(2,1)S(1)}, u32[]{:S(2)}, u32[]{:S(2)}) %collective-permute-start.2) | collective-permute-done | bytes 262176 | tf_op jit(solution)/shard_map/ppermute | solution.py:20
  48.8 4.2 %collective-permute-done.3 = bf16[2,256,256]{1,2,0:T(8,128)(2,1)S(1)} collective-permute-done((bf16[2,256,256]{1,2,0:T(8,128)(2,1)S(1)}, bf16[2,256,256]{1,2,0:T(8,128)(2,1)S(1)}, u32[]{:S(2)}, u32[]{:S(2)}) %collective-permute-start.3) | collective-permute-done | bytes 262176 | tf_op jit(solution)/shard_map/ppermute | solution.py:20
  54.6 14.8 %shard_map.50 = (bf16[256,1024]{1,0:T(8,128)(2,1)}, f32[2,128,1280]{2,1,0:T(8,128)}) custom-call(f32[256,1280]{1,0:T(8,128)} %fusion.2.bias_ref, bf16[256,2048]{1,0:T(8,128)(2,1)} %bitcast.40, bf16[256,2048]{1,0:T(8,128)(2,1)} %bitcast.42, bf16[2,1280,256]{2,1,0:T(8,128)(2,1)} %copy.46.k_ref.v_ref, bf16[2,1280,256]{2,1,0:T(8,128)(2,1)} %copy.46.k_ref.v_ref, ...), custom_call_target="tpu_custom_call" | custom-call | flops 4026531840 | bytes 4849664 | tf_op jit(solution)/shard_map/pallas_call | solution.py:72
  73.8 1.9 %collective-permute-start.5 = (bf16[2,256,128]{2,1,0:T(8,128)(2,1)S(1)}, bf16[2,256,128]{2,1,0:T(8,128)(2,1)S(1)}, u32[]{:S(2)}, u32[]{:S(2)}) collective-permute-start(bf16[2,256,128]{2,1,0:T(8,128)(2,1)S(1)} %get-tuple-element.16.rest_1_), channel_id=1, source_target_pairs={{12,0},{16,4},{20,8},{24,12},{28,16},{32,20},{36,24},{40,28},{44,3... | collective-permute-start | bytes 393224 | tf_op jit(solution)/shard_map/ppermute | solution.py:20
  75.7 1.9 %collective-permute-start.6 = (bf16[2,256,128]{2,1,0:T(8,128)(2,1)S(1)}, bf16[2,256,128]{2,1,0:T(8,128)(2,1)S(1)}, u32[]{:S(2)}, u32[]{:S(2)}) collective-permute-start(bf16[2,256,128]{2,1,0:T(8,128)(2,1)S(1)} %get-tuple-element.15.rest_2_), channel_id=1, source_target_pairs={{8,0},{12,4},{16,8},{20,12},{24,16},{28,20},{32,24},{36,28},{40,32... | collective-permute-start | bytes 393224 | tf_op jit(solution)/shard_map/ppermute | solution.py:20
  77.6 3.9 %collective-permute-start.7 = (bf16[2,256,128]{2,1,0:T(8,128)(2,1)S(1)}, bf16[2,256,128]{2,1,0:T(8,128)(2,1)S(1)}, u32[]{:S(2)}, u32[]{:S(2)}) collective-permute-start(bf16[2,256,128]{2,1,0:T(8,128)(2,1)S(1)} %get-tuple-element.14.rest_3_), channel_id=1, source_target_pairs={{4,0},{8,4},{12,8},{16,12},{20,16},{24,20},{28,24},{32,28},{36,32}... | collective-permute-start | bytes 393224 | tf_op jit(solution)/shard_map/ppermute | solution.py:20
  81.5 14.8 %shard_map.51 = (bf16[256,1024]{1,0:T(8,128)(2,1)}, f32[2,128,1280]{2,1,0:T(8,128)}) custom-call(f32[256,1280]{1,0:T(8,128)} %fusion.2.bias_ref, bf16[256,2048]{1,0:T(8,128)(2,1)} %bitcast.41, bf16[256,2048]{1,0:T(8,128)(2,1)} %bitcast.43, bf16[2,1280,256]{2,1,0:T(8,128)(2,1)} %copy.46.k_ref.v_ref, bf16[2,1280,256]{2,1,0:T(8,128)(2,1)} %copy.46.k_ref.v_ref, ...), custom_call_target="tpu_custom_call" | custom-call | flops 4026531840 | bytes 4849664 | tf_op jit(solution)/shard_map/pallas_call | solution.py:72
  98.2 1.9 %collective-permute-start.10 = (bf16[2,256,128]{2,1,0:T(8,128)(2,1)S(1)}, bf16[2,256,128]{2,1,0:T(8,128)(2,1)S(1)}, u32[]{:S(2)}, u32[]{:S(2)}) collective-permute-start(bf16[2,256,128]{2,1,0:T(8,128)(2,1)S(1)} %get-tuple-element.12), channel_id=1, source_target_pairs={{8,0},{12,4},{16,8},{20,12},{24,16},{28,20},{32,24},{36,28},{40,32... | collective-permute-start | bytes 393224 | tf_op jit(solution)/shard_map/ppermute | solution.py:20
  100.1 1.9 %collective-permute-start.11 = (bf16[2,256,128]{2,1,0:T(8,128)(2,1)S(1)}, bf16[2,256,128]{2,1,0:T(8,128)(2,1)S(1)}, u32[]{:S(2)}, u32[]{:S(2)}) collective-permute-start(bf16[2,256,128]{2,1,0:T(8,128)(2,1)S(1)} %get-tuple-element.11), channel_id=1, source_target_pairs={{4,0},{8,4},{12,8},{16,12},{20,16},{24,20},{28,24},{32,28},{36,32}... | collective-permute-start | bytes 393224 | tf_op jit(solution)/shard_map/ppermute | solution.py:20
  102.1 1.9 %collective-permute-start.8 = (bf16[2,256,128]{2,1,0:T(8,128)(2,1)S(1)}, bf16[2,256,128]{2,1,0:T(8,128)(2,1)S(1)}, u32[]{:S(2)}, u32[]{:S(2)}) collective-permute-start(bf16[2,256,128]{2,1,0:T(8,128)(2,1)S(1)} %get-tuple-element.10), channel_id=1, source_target_pairs={{16,0},{20,4},{24,8},{28,12},{32,16},{36,20},{40,24},{44,28},{48,3... | collective-permute-start | bytes 393224 | tf_op jit(solution)/shard_map/ppermute | solution.py:20
  104.0 1.9 %collective-permute-start.9 = (bf16[2,256,128]{2,1,0:T(8,128)(2,1)S(1)}, bf16[2,256,128]{2,1,0:T(8,128)(2,1)S(1)}, u32[]{:S(2)}, u32[]{:S(2)}) collective-permute-start(bf16[2,256,128]{2,1,0:T(8,128)(2,1)S(1)} %get-tuple-element.13), channel_id=1, source_target_pairs={{12,0},{16,4},{20,8},{24,12},{28,16},{32,20},{36,24},{40,28},{44,3... | collective-permute-start | bytes 393224 | tf_op jit(solution)/shard_map/ppermute | solution.py:20
  106.5 3.9 %collective-permute-done.11 = bf16[2,256,128]{2,1,0:T(8,128)(2,1)S(1)} collective-permute-done((bf16[2,256,128]{2,1,0:T(8,128)(2,1)S(1)}, bf16[2,256,128]{2,1,0:T(8,128)(2,1)S(1)}, u32[]{:S(2)}, u32[]{:S(2)}) %collective-permute-start.11) | collective-permute-done | bytes 131104 | tf_op jit(solution)/shard_map/ppermute | solution.py:20
  110.4 6.8 %collective-permute-done.8 = bf16[2,256,128]{2,1,0:T(8,128)(2,1)S(1)} collective-permute-done((bf16[2,256,128]{2,1,0:T(8,128)(2,1)S(1)}, bf16[2,256,128]{2,1,0:T(8,128)(2,1)S(1)}, u32[]{:S(2)}, u32[]{:S(2)}) %collective-permute-start.8) | collective-permute-done | bytes 131104 | tf_op jit(solution)/shard_map/ppermute | solution.py:20
  117.2 6.9 %collective-permute-done.9 = bf16[2,256,128]{2,1,0:T(8,128)(2,1)S(1)} collective-permute-done((bf16[2,256,128]{2,1,0:T(8,128)(2,1)S(1)}, bf16[2,256,128]{2,1,0:T(8,128)(2,1)S(1)}, u32[]{:S(2)}, u32[]{:S(2)}) %collective-permute-start.9) | collective-permute-done | bytes 131104 | tf_op jit(solution)/shard_map/ppermute | solution.py:20
  125.1 5.0 %all-to-all-start.1 = ((bf16[2,16,16,256]{3,2,0,1:T(8,128)(2,1)}), bf16[2,16,16,256]{3,2,0,1:T(8,128)(2,1)S(1)}, u32[]{:S(2)}, u32[]{:S(2)}) async-start(bf16[2,16,16,256]{3,2,0,1:T(8,128)(2,1)} %copy.53), calls=%async_computation.1 | async-start | bytes 524288 | tf_op jit(solution)/shard_map/all_to_all | solution.py:108
  131.1 6.6 %all-to-all-done.1 = bf16[2,16,16,256]{3,2,0,1:T(8,128)(2,1)S(1)} async-done(((bf16[2,16,16,256]{3,2,0,1:T(8,128)(2,1)}), bf16[2,16,16,256]{3,2,0,1:T(8,128)(2,1)S(1)}, u32[]{:S(2)}, u32[]{:S(2)}) %all-to-all-start.1) | async-done | bytes 262176 | tf_op jit(solution)/shard_map/all_to_all | solution.py:108
  137.9 12.5 %all_gather.3 = bf16[2,64,1024]{2,1,0:T(8,128)(2,1)S(1)} all-gather(bf16[2,16,1024]{2,1,0:T(8,128)(2,1)S(1)} %bitcast.39), channel_id=1, replica_groups=mesh['section'=4,'seq'=16,'tp'=4] {'section'}, dimensions={1}, use_global_device_ids=true | all-gather | bytes 327680 | tf_op jit(solution)/shard_map/all_gather | solution.py:160
  (51 shorter events, 16.3 us)
Async XLA Ops:
  3.0 9.4 %all-to-all-start = ((bf16[4,2,16384]{2,1,0:T(2,128)(2,1)}), bf16[4,2,16384]{2,1,0:T(2,128)(2,1)S(1)}, u32[]{:S(2)}, u32[]{:S(2)}) async-start(bf16[4,2,16384]{2,1,0:T(2,128)(2,1)} %reshape.36), calls=%async_computation | async-start | bytes 524288 | tf_op jit(solution)/shard_map/all_to_all | solution.py:117
  13.4 19.2 %collective-permute-start = (bf16[2,256,256]{1,2,0:T(8,128)(2,1)S(1)}, bf16[2,256,256]{1,2,0:T(8,128)(2,1)S(1)}, u32[]{:S(2)}, u32[]{:S(2)}) collective-permute-start(bf16[2,256,256]{1,2,0:T(8,128)(2,1)S(1)} %copy.41), channel_id=1, source_target_pairs={{0,16},{4,20},{8,24},{12,28},{16,32},{20,36},{24,40},{28,44},{32,4... | collective-permute-start | bytes 786440 | tf_op jit(solution)/shard_map/ppermute | solution.py:20
  19.8 23.4 %collective-permute-start.1 = (bf16[2,256,256]{1,2,0:T(8,128)(2,1)S(1)}, bf16[2,256,256]{1,2,0:T(8,128)(2,1)S(1)}, u32[]{:S(2)}, u32[]{:S(2)}) collective-permute-start(bf16[2,256,256]{1,2,0:T(8,128)(2,1)S(1)} %copy.41), channel_id=1, source_target_pairs={{0,12},{4,16},{8,20},{12,24},{16,28},{20,32},{24,36},{28,40},{32,4... | collective-permute-start | bytes 786440 | tf_op jit(solution)/shard_map/ppermute | solution.py:20
  22.9 25.9 %collective-permute-start.2 = (bf16[2,256,256]{1,2,0:T(8,128)(2,1)S(1)}, bf16[2,256,256]{1,2,0:T(8,128)(2,1)S(1)}, u32[]{:S(2)}, u32[]{:S(2)}) collective-permute-start(bf16[2,256,256]{1,2,0:T(8,128)(2,1)S(1)} %copy.41), channel_id=1, source_target_pairs={{0,8},{4,12},{8,16},{12,20},{16,24},{20,28},{24,32},{28,36},{32,40... | collective-permute-start | bytes 786440 | tf_op jit(solution)/shard_map/ppermute | solution.py:20
  27.5 25.6 %collective-permute-start.3 = (bf16[2,256,256]{1,2,0:T(8,128)(2,1)S(1)}, bf16[2,256,256]{1,2,0:T(8,128)(2,1)S(1)}, u32[]{:S(2)}, u32[]{:S(2)}) collective-permute-start(bf16[2,256,256]{1,2,0:T(8,128)(2,1)S(1)} %copy.41), channel_id=1, source_target_pairs={{0,4},{4,8},{8,12},{12,16},{16,20},{20,24},{24,28},{28,32},{32,36}... | collective-permute-start | bytes 786440 | tf_op jit(solution)/shard_map/ppermute | solution.py:20
  53.1 1.5 copy-start
  71.9 9.7 %copy-start.3 = (bf16[2,256,128]{2,1,0:T(8,128)(2,1)}, bf16[2,256,128]{2,1,0:T(8,128)(2,1)S(1)}, u32[]{:S(2)}) copy-start(bf16[2,256,128]{2,1,0:T(8,128)(2,1)S(1)} %get-tuple-element.14.rest_3_) | copy-start | bytes 393220
  71.9 9.7 %copy-start.4 = (bf16[2,256,128]{2,1,0:T(8,128)(2,1)}, bf16[2,256,128]{2,1,0:T(8,128)(2,1)S(1)}, u32[]{:S(2)}) copy-start(bf16[2,256,128]{2,1,0:T(8,128)(2,1)S(1)} %get-tuple-element.15.rest_2_) | copy-start | bytes 393220
  71.9 9.7 %copy-start.5 = (bf16[2,256,128]{2,1,0:T(8,128)(2,1)}, bf16[2,256,128]{2,1,0:T(8,128)(2,1)S(1)}, u32[]{:S(2)}) copy-start(bf16[2,256,128]{2,1,0:T(8,128)(2,1)S(1)} %get-tuple-element.16.rest_1_) | copy-start | bytes 393220
  71.9 28.3 %collective-permute-start.4 = (bf16[2,256,128]{2,1,0:T(8,128)(2,1)}, bf16[2,256,128]{2,1,0:T(8,128)(2,1)S(1)}, u32[]{:S(2)}, u32[]{:S(2)}) collective-permute-start(bf16[2,256,128]{2,1,0:T(8,128)(2,1)} %get-tuple-element.17.rest_0_), channel_id=1, source_target_pairs={{16,0},{20,4},{24,8},{28,12},{32,16},{36,20},{40,24},{44,28},{48,3... | collective-permute-start | bytes 393224 | tf_op jit(solution)/shard_map/ppermute | solution.py:20
  73.8 28.3 %collective-permute-start.5 = (bf16[2,256,128]{2,1,0:T(8,128)(2,1)S(1)}, bf16[2,256,128]{2,1,0:T(8,128)(2,1)S(1)}, u32[]{:S(2)}, u32[]{:S(2)}) collective-permute-start(bf16[2,256,128]{2,1,0:T(8,128)(2,1)S(1)} %get-tuple-element.16.rest_1_), channel_id=1, source_target_pairs={{12,0},{16,4},{20,8},{24,12},{28,16},{32,20},{36,24},{40,28},{44,3... | collective-permute-start | bytes 393224 | tf_op jit(solution)/shard_map/ppermute | solution.py:20
  75.7 28.3 %collective-permute-start.6 = (bf16[2,256,128]{2,1,0:T(8,128)(2,1)S(1)}, bf16[2,256,128]{2,1,0:T(8,128)(2,1)S(1)}, u32[]{:S(2)}, u32[]{:S(2)}) collective-permute-start(bf16[2,256,128]{2,1,0:T(8,128)(2,1)S(1)} %get-tuple-element.15.rest_2_), channel_id=1, source_target_pairs={{8,0},{12,4},{16,8},{20,12},{24,16},{28,20},{32,24},{36,28},{40,32... | collective-permute-start | bytes 393224 | tf_op jit(solution)/shard_map/ppermute | solution.py:20
  77.6 28.3 %collective-permute-start.7 = (bf16[2,256,128]{2,1,0:T(8,128)(2,1)S(1)}, bf16[2,256,128]{2,1,0:T(8,128)(2,1)S(1)}, u32[]{:S(2)}, u32[]{:S(2)}) collective-permute-start(bf16[2,256,128]{2,1,0:T(8,128)(2,1)S(1)} %get-tuple-element.14.rest_3_), channel_id=1, source_target_pairs={{4,0},{8,4},{12,8},{16,12},{20,16},{24,20},{28,24},{32,28},{36,32}... | collective-permute-start | bytes 393224 | tf_op jit(solution)/shard_map/ppermute | solution.py:20
  98.2 8.3 %collective-permute-start.10 = (bf16[2,256,128]{2,1,0:T(8,128)(2,1)S(1)}, bf16[2,256,128]{2,1,0:T(8,128)(2,1)S(1)}, u32[]{:S(2)}, u32[]{:S(2)}) collective-permute-start(bf16[2,256,128]{2,1,0:T(8,128)(2,1)S(1)} %get-tuple-element.12), channel_id=1, source_target_pairs={{8,0},{12,4},{16,8},{20,12},{24,16},{28,20},{32,24},{36,28},{40,32... | collective-permute-start | bytes 393224 | tf_op jit(solution)/shard_map/ppermute | solution.py:20
  100.1 10.3 %collective-permute-start.11 = (bf16[2,256,128]{2,1,0:T(8,128)(2,1)S(1)}, bf16[2,256,128]{2,1,0:T(8,128)(2,1)S(1)}, u32[]{:S(2)}, u32[]{:S(2)}) collective-permute-start(bf16[2,256,128]{2,1,0:T(8,128)(2,1)S(1)} %get-tuple-element.11), channel_id=1, source_target_pairs={{4,0},{8,4},{12,8},{16,12},{20,16},{24,20},{28,24},{32,28},{36,32}... | collective-permute-start | bytes 393224 | tf_op jit(solution)/shard_map/ppermute | solution.py:20
  102.1 15.2 %collective-permute-start.8 = (bf16[2,256,128]{2,1,0:T(8,128)(2,1)S(1)}, bf16[2,256,128]{2,1,0:T(8,128)(2,1)S(1)}, u32[]{:S(2)}, u32[]{:S(2)}) collective-permute-start(bf16[2,256,128]{2,1,0:T(8,128)(2,1)S(1)} %get-tuple-element.10), channel_id=1, source_target_pairs={{16,0},{20,4},{24,8},{28,12},{32,16},{36,20},{40,24},{44,28},{48,3... | collective-permute-start | bytes 393224 | tf_op jit(solution)/shard_map/ppermute | solution.py:20
  104.0 20.2 %collective-permute-start.9 = (bf16[2,256,128]{2,1,0:T(8,128)(2,1)S(1)}, bf16[2,256,128]{2,1,0:T(8,128)(2,1)S(1)}, u32[]{:S(2)}, u32[]{:S(2)}) collective-permute-start(bf16[2,256,128]{2,1,0:T(8,128)(2,1)S(1)} %get-tuple-element.13), channel_id=1, source_target_pairs={{12,0},{16,4},{20,8},{24,12},{28,16},{32,20},{36,24},{40,28},{44,3... | collective-permute-start | bytes 393224 | tf_op jit(solution)/shard_map/ppermute | solution.py:20
  124.2 5.9 %copy-start.1 = (bf16[256,1024]{1,0:T(8,128)(2,1)S(1)}, bf16[256,1024]{1,0:T(8,128)(2,1)}, u32[]{:S(2)}) copy-start(bf16[256,1024]{1,0:T(8,128)(2,1)} %get-tuple-element.6) | copy-start | bytes 1572868
  124.2 5.9 %copy-start.2 = (bf16[256,1024]{1,0:T(8,128)(2,1)S(1)}, bf16[256,1024]{1,0:T(8,128)(2,1)}, u32[]{:S(2)}) copy-start(bf16[256,1024]{1,0:T(8,128)(2,1)} %get-tuple-element.8) | copy-start | bytes 1572868
  125.1 12.7 %all-to-all-start.1 = ((bf16[2,16,16,256]{3,2,0,1:T(8,128)(2,1)}), bf16[2,16,16,256]{3,2,0,1:T(8,128)(2,1)S(1)}, u32[]{:S(2)}, u32[]{:S(2)}) async-start(bf16[2,16,16,256]{3,2,0,1:T(8,128)(2,1)} %copy.53), calls=%async_computation.1 | async-start | bytes 524288 | tf_op jit(solution)/shard_map/all_to_all | solution.py:108

commit v12 on v9

--- a/solution.py
+++ b/solution.py
@@ -20,8 +20,8 @@
     return lax.ppermute(value, axis, pairs)
 
 
-def attn_kernel(bias_ref, q_ref, g_ref, k_ref, v_ref, *rest, scale, hd, per_step):
-    dq_ref, dkv_ref = rest[-2:]
+def attn_kernel(bias_ref, q_ref, g_ref, k_ref, v_ref, *rest, scale, hd, per_step, sent_cols):
+    dq_ref, dkv_ref, send_ref = rest[-3:]
     gi = pl.program_id(1)
     k = k_ref[...]
     v = v_ref[...]
@@ -60,15 +60,20 @@
         dkv_ref[0] += dk
         dkv_ref[1] += dv
 
+    @pl.when(gi == pl.num_programs(1) - 1)
+    def _():
+        send_ref[0] = dkv_ref[0, :, :sent_cols].astype(send_ref.dtype)
+        send_ref[1] = dkv_ref[1, :, :sent_cols].astype(send_ref.dtype)
 
-def attention_grads(bias, q, g, ext, group, hd, scale, per_step, head0, heads, after=()):
+
+def attention_grads(bias, q, g, ext, group, hd, scale, per_step, head0, heads, sent_cols, after=()):
     rows, _ = q.shape
     _, ext_rows, _ = ext.shape
     steps = group // per_step
     width = per_step * hd
     flops = 6 * 2 * rows * ext_rows * hd * heads * group
     return pl.pallas_call(
-        functools.partial(attn_kernel, scale=scale, hd=hd, per_step=per_step),
+        functools.partial(attn_kernel, scale=scale, hd=hd, per_step=per_step, sent_cols=sent_cols),
         grid=(heads, steps),
         in_specs=[
             pl.BlockSpec((rows, ext_rows), lambda h, i: (0, 0)),
@@ -81,10 +86,12 @@
         out_specs=[
             pl.BlockSpec((rows, width), lambda h, i: (0, h * steps + i)),
             pl.BlockSpec((2, hd, ext_rows), lambda h, i: (0, h, 0)),
+            pl.BlockSpec((2, hd, sent_cols), lambda h, i: (0, h, 0)),
         ],
         out_shape=[
             jax.ShapeDtypeStruct((rows, heads * group * hd), jnp.bfloat16),
             jax.ShapeDtypeStruct((2, heads * hd, ext_rows), jnp.float32),
+            jax.ShapeDtypeStruct((2, heads * hd, sent_cols), jnp.bfloat16),
         ],
         compiler_params=pltpu.CompilerParams(dimension_semantics=("arbitrary", "arbitrary")),
         cost_estimate=pl.CostEstimate(
@@ -135,21 +142,21 @@
     own_parts = []
     sent = []
     for kv_head in range(local_heads):
-        d_query_part, grad_ext = attention_grads(
-            bias, query_rows, grad_rows, extended, group_size, head_size, score_scale, 2, kv_head, 1, sent
+        d_query_part, grad_t, sent_t = attention_grads(
+            bias, query_rows, grad_rows, extended, group_size, head_size, score_scale, 2, kv_head, 1,
+            span_blocks * tok_rows, sent,
         )
-        grad_ext = jnp.swapaxes(grad_ext, 1, 2)
         d_query_parts.append(d_query_part)
         sent = [
-            grad_ext[:, offset * tok_rows : (offset + 1) * tok_rows, :].astype(jnp.bfloat16)
+            sent_t[:, :, offset * tok_rows : (offset + 1) * tok_rows]
             for offset in range(span_blocks)
         ]
-        own_rows = grad_ext[:, span_blocks * tok_rows :, :]
+        own_t = grad_t[:, :, span_blocks * tok_rows :]
         for offset in range(span_blocks):
-            own_rows = own_rows + shifted(sent[offset], "seq", offset - span_blocks).astype(jnp.float32)
-        own_parts.append(own_rows)
+            own_t = own_t + shifted(sent[offset], "seq", offset - span_blocks).astype(jnp.float32)
+        own_parts.append(own_t)
     d_queries = jnp.concatenate(d_query_parts, axis=1).reshape(queries.shape)
-    own_rows = jnp.concatenate(own_parts, axis=2)
+    own_rows = jnp.swapaxes(jnp.concatenate(own_parts, axis=1), 1, 2)
     chunk = scatter_layers(own_rows)
     kinds, rows, tp_peers, cols = chunk.shape
     d_shared_kv = lax.all_gather(

time: 151 us -> 151 us (level)
  other arithmetic: 4.01 us -> 5.71 us
  local copies, waits for them, and re-layouts: 9.15 us -> 7.46 us
    pallas_call x2 -> x0, local copies, waits for them, and re-layouts: 3.41 us -> none  [attention_grads(): pl.pallas_call(functools.partial(attn_kernel, scale=scale, hd=hd, per_ste...]
    another operation x4 -> x2, other arithmetic: 0.35 us -> 2.07 us
    slice x2, local copies, waits for them, and re-layouts: 0.71 us -> 2.27 us  [body(): sent_t[:, :, offset * tok_rows:(offset + 1) * tok_rows]]
    unnamed x19 -> x21, local copies, waits for them, and re-layouts: 3.84 us -> 3.89 us
  transfers between devices with their start and end apart: 14 -> 14, of which waited for: 9 -> 8; matrix products, arithmetic and copies ran while one was open for 3% -> 3% of each run, Pallas kernels for 10% -> 10%
where the time goes in v12:
time: 151 us; the launch traced here: 150 us
  waiting for transfers between devices  50.1 us (33%)
  starting transfers between devices  43.3 us (29%)
  Pallas kernels  29.6 us (20%)
  blocking collectives  12.5 us (8%)
  local copies, waits for them, and re-layouts  7.46 us (5%)
  other arithmetic  5.71 us (4%)
    ppermute x12, waiting for transfers between devices, shifted(): return lax.ppermute(value, axis, pairs)  37.6 us
    ppermute x12, starting transfers between devices, shifted(): return lax.ppermute(value, axis, pairs)  34.9 us
    pallas_call x2, Pallas kernels, attention_grads(): pl.pallas_call(functools.partial(attn_kernel, scale=scale, hd=hd, per_ste...  29.6 us
    all_gather x1, blocking collectives, body(): lax.all_gather(chunk.reshape(kinds, rows, -1).astype(jnp.bfloat16), 'sect...  12.5 us
    all_to_all x1, waiting for transfers between devices, scatter_layers(): lax.all_to_all(pieces.astype(jnp.bfloat16), ('section', 'tp'), split_axis...  6.59 us
    all_to_all x1, waiting for transfers between devices, body(): lax.all_to_all(shared_kv, 'tp', split_axis=2, concat_axis=1, tiled=True)  5.94 us
    all_to_all x1, starting transfers between devices, scatter_layers(): lax.all_to_all(pieces.astype(jnp.bfloat16), ('section', 'tp'), split_axis...  4.98 us
    unnamed x21, local copies, waits for them, and re-layouts  3.89 us
  transfers between devices with their start and end apart: 14, of which 8 were waited for; matrix products, arithmetic and copies ran while one was open for 3% of the time, Pallas kernels for 10%

profile of v12, /device:TPU:80, one launch (start us, length us, event | category | flops | bytes accessed | tf_op | source)
XLA Modules:
  0.0 149.7 jit_solution(17944942611612604976)
XLA Ops:
  3.0 3.4 %all-to-all-start = ((bf16[4,2,16384]{2,1,0:T(2,128)(2,1)}), bf16[4,2,16384]{2,1,0:T(2,128)(2,1)S(1)}, u32[]{:S(2)}, u32[]{:S(2)}) async-start(bf16[4,2,16384]{2,1,0:T(2,128)(2,1)} %reshape.36), calls=%async_computation | async-start | bytes 524288 | tf_op jit(solution)/shard_map/all_to_all | solution.py:120
  6.4 5.9 %all-to-all-done = bf16[4,2,16384]{2,1,0:T(2,128)(2,1)S(1)} async-done(((bf16[4,2,16384]{2,1,0:T(2,128)(2,1)}), bf16[4,2,16384]{2,1,0:T(2,128)(2,1)S(1)}, u32[]{:S(2)}, u32[]{:S(2)}) %all-to-all-start) | async-done | bytes 262176 | tf_op jit(solution)/shard_map/all_to_all | solution.py:120
  13.1 6.4 %collective-permute-start = (bf16[2,256,256]{2,1,0:T(8,128)(2,1)S(1)}, bf16[2,256,256]{2,1,0:T(8,128)(2,1)S(1)}, u32[]{:S(2)}, u32[]{:S(2)}) collective-permute-start(bf16[2,256,256]{2,1,0:T(8,128)(2,1)S(1)} %bitcast.26), channel_id=1, source_target_pairs={{0,16},{4,20},{8,24},{12,28},{16,32},{20,36},{24,40},{28,44},{32,4... | collective-permute-start | bytes 786440 | tf_op jit(solution)/shard_map/ppermute | solution.py:20
  19.5 3.2 %collective-permute-start.1 = (bf16[2,256,256]{2,1,0:T(8,128)(2,1)S(1)}, bf16[2,256,256]{2,1,0:T(8,128)(2,1)S(1)}, u32[]{:S(2)}, u32[]{:S(2)}) collective-permute-start(bf16[2,256,256]{2,1,0:T(8,128)(2,1)S(1)} %bitcast.27), channel_id=1, source_target_pairs={{0,12},{4,16},{8,20},{12,24},{16,28},{20,32},{24,36},{28,40},{32,4... | collective-permute-start | bytes 786440 | tf_op jit(solution)/shard_map/ppermute | solution.py:20
  22.7 2.9 %collective-permute-start.2 = (bf16[2,256,256]{2,1,0:T(8,128)(2,1)S(1)}, bf16[2,256,256]{2,1,0:T(8,128)(2,1)S(1)}, u32[]{:S(2)}, u32[]{:S(2)}) collective-permute-start(bf16[2,256,256]{2,1,0:T(8,128)(2,1)S(1)} %bitcast.28), channel_id=1, source_target_pairs={{0,8},{4,12},{8,16},{12,20},{16,24},{20,28},{24,32},{28,36},{32,40... | collective-permute-start | bytes 786440 | tf_op jit(solution)/shard_map/ppermute | solution.py:20
  27.3 5.1 %collective-permute-start.3 = (bf16[2,256,256]{2,1,0:T(8,128)(2,1)S(1)}, bf16[2,256,256]{2,1,0:T(8,128)(2,1)S(1)}, u32[]{:S(2)}, u32[]{:S(2)}) collective-permute-start(bf16[2,256,256]{2,1,0:T(8,128)(2,1)S(1)} %bitcast.29), channel_id=1, source_target_pairs={{0,4},{4,8},{8,12},{12,16},{16,20},{20,24},{24,28},{28,32},{32,36}... | collective-permute-start | bytes 786440 | tf_op jit(solution)/shard_map/ppermute | solution.py:20
  32.4 10.6 %collective-permute-done.1 = bf16[2,256,256]{2,1,0:T(8,128)(2,1)S(1)} collective-permute-done((bf16[2,256,256]{2,1,0:T(8,128)(2,1)S(1)}, bf16[2,256,256]{2,1,0:T(8,128)(2,1)S(1)}, u32[]{:S(2)}, u32[]{:S(2)}) %collective-permute-start.1) | collective-permute-done | bytes 262176 | tf_op jit(solution)/shard_map/ppermute | solution.py:20
  43.0 5.6 %collective-permute-done.2 = bf16[2,256,256]{2,1,0:T(8,128)(2,1)S(1)} collective-permute-done((bf16[2,256,256]{2,1,0:T(8,128)(2,1)S(1)}, bf16[2,256,256]{2,1,0:T(8,128)(2,1)S(1)}, u32[]{:S(2)}, u32[]{:S(2)}) %collective-permute-start.2) | collective-permute-done | bytes 262176 | tf_op jit(solution)/shard_map/ppermute | solution.py:20
  48.6 4.2 %collective-permute-done.3 = bf16[2,256,256]{2,1,0:T(8,128)(2,1)S(1)} collective-permute-done((bf16[2,256,256]{2,1,0:T(8,128)(2,1)S(1)}, bf16[2,256,256]{2,1,0:T(8,128)(2,1)S(1)}, u32[]{:S(2)}, u32[]{:S(2)}) %collective-permute-start.3) | collective-permute-done | bytes 262176 | tf_op jit(solution)/shard_map/ppermute | solution.py:20
  53.9 14.8 %shard_map.50 = (bf16[256,1024]{1,0:T(8,128)(2,1)}, f32[2,128,1280]{2,1,0:T(8,128)}, bf16[2,128,1024]{2,1,0:T(8,128)(2,1)}) custom-call(f32[256,1280]{1,0:T(8,128)} %fusion.2.bias_ref, bf16[256,2048]{1,0:T(8,128)(2,1)} %bitcast.35, bf16[256,2048]{1,0:T(8,128)(2,1)} %bitcast.37, bf16[2,1280,256]{2,1,0:T(8,128)(2,1)} %copy-done.6, bf16[2,1280,256]{2,1,0:T(8,128)(2,1)} %copy-done.6), custom_call_target="tpu_custom_call" | custom-call | flops 4026531840 | bytes 4849664 | tf_op jit(solution)/shard_map/pallas_call | solution.py:75
  69.9 1.9 %collective-permute-start.4 = (bf16[2,128,256]{2,1,0:T(8,128)(2,1)S(1)}, bf16[2,128,256]{2,1,0:T(8,128)(2,1)S(1)}, u32[]{:S(2)}, u32[]{:S(2)}) collective-permute-start(bf16[2,128,256]{2,1,0:T(8,128)(2,1)S(1)} %get-tuple-element.21.rest_0_), channel_id=1, source_target_pairs={{16,0},{20,4},{24,8},{28,12},{32,16},{36,20},{40,24},{44,28},{48,3... | collective-permute-start | bytes 393224 | tf_op jit(solution)/shard_map/ppermute | solution.py:20
  71.8 1.9 %collective-permute-start.5 = (bf16[2,128,256]{2,1,0:T(8,128)(2,1)S(1)}, bf16[2,128,256]{2,1,0:T(8,128)(2,1)S(1)}, u32[]{:S(2)}, u32[]{:S(2)}) collective-permute-start(bf16[2,128,256]{2,1,0:T(8,128)(2,1)S(1)} %get-tuple-element.20.rest_1_), channel_id=1, source_target_pairs={{12,0},{16,4},{20,8},{24,12},{28,16},{32,20},{36,24},{40,28},{44,3... | collective-permute-start | bytes 393224 | tf_op jit(solution)/shard_map/ppermute | solution.py:20
  73.8 1.9 %collective-permute-start.6 = (bf16[2,128,256]{2,1,0:T(8,128)(2,1)S(1)}, bf16[2,128,256]{2,1,0:T(8,128)(2,1)S(1)}, u32[]{:S(2)}, u32[]{:S(2)}) collective-permute-start(bf16[2,128,256]{2,1,0:T(8,128)(2,1)S(1)} %get-tuple-element.19.rest_2_), channel_id=1, source_target_pairs={{8,0},{12,4},{16,8},{20,12},{24,16},{28,20},{32,24},{36,28},{40,32... | collective-permute-start | bytes 393224 | tf_op jit(solution)/shard_map/ppermute | solution.py:20
  75.7 3.9 %collective-permute-start.7 = (bf16[2,128,256]{2,1,0:T(8,128)(2,1)S(1)}, bf16[2,128,256]{2,1,0:T(8,128)(2,1)S(1)}, u32[]{:S(2)}, u32[]{:S(2)}) collective-permute-start(bf16[2,128,256]{2,1,0:T(8,128)(2,1)S(1)} %get-tuple-element.18.rest_3_), channel_id=1, source_target_pairs={{4,0},{8,4},{12,8},{16,12},{20,16},{24,20},{28,24},{32,28},{36,32}... | collective-permute-start | bytes 393224 | tf_op jit(solution)/shard_map/ppermute | solution.py:20
  79.6 14.9 %shard_map.51 = (bf16[256,1024]{1,0:T(8,128)(2,1)}, f32[2,128,1280]{2,1,0:T(8,128)}, bf16[2,128,1024]{2,1,0:T(8,128)(2,1)}) custom-call(f32[256,1280]{1,0:T(8,128)} %fusion.2.bias_ref, bf16[256,2048]{1,0:T(8,128)(2,1)} %bitcast.36, bf16[256,2048]{1,0:T(8,128)(2,1)} %bitcast.38, bf16[2,1280,256]{2,1,0:T(8,128)(2,1)} %copy-done.6, ...), custom_call_target="tpu_custom_call" | custom-call | flops 4026531840 | bytes 4849664 | tf_op jit(solution)/shard_map/pallas_call | solution.py:75
  95.6 1.9 %collective-permute-start.10 = (bf16[2,128,256]{2,1,0:T(8,128)(2,1)S(1)}, bf16[2,128,256]{2,1,0:T(8,128)(2,1)S(1)}, u32[]{:S(2)}, u32[]{:S(2)}) collective-permute-start(bf16[2,128,256]{2,1,0:T(8,128)(2,1)S(1)} %get-tuple-element.16), channel_id=1, source_target_pairs={{8,0},{12,4},{16,8},{20,12},{24,16},{28,20},{32,24},{36,28},{40,32... | collective-permute-start | bytes 393224 | tf_op jit(solution)/shard_map/ppermute | solution.py:20
  97.6 1.9 %collective-permute-start.11 = (bf16[2,128,256]{2,1,0:T(8,128)(2,1)S(1)}, bf16[2,128,256]{2,1,0:T(8,128)(2,1)S(1)}, u32[]{:S(2)}, u32[]{:S(2)}) collective-permute-start(bf16[2,128,256]{2,1,0:T(8,128)(2,1)S(1)} %get-tuple-element.15), channel_id=1, source_target_pairs={{4,0},{8,4},{12,8},{16,12},{20,16},{24,20},{28,24},{32,28},{36,32}... | collective-permute-start | bytes 393224 | tf_op jit(solution)/shard_map/ppermute | solution.py:20
  99.5 1.9 %collective-permute-start.8 = (bf16[2,128,256]{2,1,0:T(8,128)(2,1)S(1)}, bf16[2,128,256]{2,1,0:T(8,128)(2,1)S(1)}, u32[]{:S(2)}, u32[]{:S(2)}) collective-permute-start(bf16[2,128,256]{2,1,0:T(8,128)(2,1)S(1)} %get-tuple-element.14), channel_id=1, source_target_pairs={{16,0},{20,4},{24,8},{28,12},{32,16},{36,20},{40,24},{44,28},{48,3... | collective-permute-start | bytes 393224 | tf_op jit(solution)/shard_map/ppermute | solution.py:20
  104.4 3.4 %collective-permute-done.11 = bf16[2,128,256]{2,1,0:T(8,128)(2,1)S(1)} collective-permute-done((bf16[2,128,256]{2,1,0:T(8,128)(2,1)S(1)}, bf16[2,128,256]{2,1,0:T(8,128)(2,1)S(1)}, u32[]{:S(2)}, u32[]{:S(2)}) %collective-permute-start.11) | collective-permute-done | bytes 131104 | tf_op jit(solution)/shard_map/ppermute | solution.py:20
  107.9 6.8 %collective-permute-done.8 = bf16[2,128,256]{2,1,0:T(8,128)(2,1)S(1)} collective-permute-done((bf16[2,128,256]{2,1,0:T(8,128)(2,1)S(1)}, bf16[2,128,256]{2,1,0:T(8,128)(2,1)S(1)}, u32[]{:S(2)}, u32[]{:S(2)}) %collective-permute-start.8) | collective-permute-done | bytes 131104 | tf_op jit(solution)/shard_map/ppermute | solution.py:20
  114.7 6.9 %collective-permute-done.9 = bf16[2,128,256]{2,1,0:T(8,128)(2,1)S(1)} collective-permute-done((bf16[2,128,256]{2,1,0:T(8,128)(2,1)S(1)}, bf16[2,128,256]{2,1,0:T(8,128)(2,1)S(1)}, u32[]{:S(2)}, u32[]{:S(2)}) %collective-permute-start.9) | collective-permute-done | bytes 131104 | tf_op jit(solution)/shard_map/ppermute | solution.py:20
  123.6 5.0 %all-to-all-start.1 = ((bf16[2,16,16,256]{3,2,0,1:T(8,128)(2,1)}), bf16[2,16,16,256]{3,2,0,1:T(8,128)(2,1)S(1)}, u32[]{:S(2)}, u32[]{:S(2)}) async-start(bf16[2,16,16,256]{3,2,0,1:T(8,128)(2,1)} %copy.17), calls=%async_computation.1 | async-start | bytes 524288 | tf_op jit(solution)/shard_map/all_to_all | solution.py:111
  129.6 6.6 %all-to-all-done.1 = bf16[2,16,16,256]{3,2,0,1:T(8,128)(2,1)S(1)} async-done(((bf16[2,16,16,256]{3,2,0,1:T(8,128)(2,1)}), bf16[2,16,16,256]{3,2,0,1:T(8,128)(2,1)S(1)}, u32[]{:S(2)}, u32[]{:S(2)}) %all-to-all-start.1) | async-done | bytes 262176 | tf_op jit(solution)/shard_map/all_to_all | solution.py:111
  136.4 12.5 %all_gather.3 = bf16[2,64,1024]{2,1,0:T(8,128)(2,1)S(1)} all-gather(bf16[2,16,1024]{2,1,0:T(8,128)(2,1)S(1)} %bitcast.34), channel_id=1, replica_groups=mesh['section'=4,'seq'=16,'tp'=4] {'section'}, dimensions={1}, use_global_device_ids=true | all-gather | bytes 327680 | tf_op jit(solution)/shard_map/all_gather | solution.py:162
  (47 shorter events, 15.1 us)
Async XLA Ops:
  3.0 9.4 %all-to-all-start = ((bf16[4,2,16384]{2,1,0:T(2,128)(2,1)}), bf16[4,2,16384]{2,1,0:T(2,128)(2,1)S(1)}, u32[]{:S(2)}, u32[]{:S(2)}) async-start(bf16[4,2,16384]{2,1,0:T(2,128)(2,1)} %reshape.36), calls=%async_computation | async-start | bytes 524288 | tf_op jit(solution)/shard_map/all_to_all | solution.py:120
  13.1 19.2 %collective-permute-start = (bf16[2,256,256]{2,1,0:T(8,128)(2,1)S(1)}, bf16[2,256,256]{2,1,0:T(8,128)(2,1)S(1)}, u32[]{:S(2)}, u32[]{:S(2)}) collective-permute-start(bf16[2,256,256]{2,1,0:T(8,128)(2,1)S(1)} %bitcast.26), channel_id=1, source_target_pairs={{0,16},{4,20},{8,24},{12,28},{16,32},{20,36},{24,40},{28,44},{32,4... | collective-permute-start | bytes 786440 | tf_op jit(solution)/shard_map/ppermute | solution.py:20
  19.5 23.4 %collective-permute-start.1 = (bf16[2,256,256]{2,1,0:T(8,128)(2,1)S(1)}, bf16[2,256,256]{2,1,0:T(8,128)(2,1)S(1)}, u32[]{:S(2)}, u32[]{:S(2)}) collective-permute-start(bf16[2,256,256]{2,1,0:T(8,128)(2,1)S(1)} %bitcast.27), channel_id=1, source_target_pairs={{0,12},{4,16},{8,20},{12,24},{16,28},{20,32},{24,36},{28,40},{32,4... | collective-permute-start | bytes 786440 | tf_op jit(solution)/shard_map/ppermute | solution.py:20
  22.7 25.9 %collective-permute-start.2 = (bf16[2,256,256]{2,1,0:T(8,128)(2,1)S(1)}, bf16[2,256,256]{2,1,0:T(8,128)(2,1)S(1)}, u32[]{:S(2)}, u32[]{:S(2)}) collective-permute-start(bf16[2,256,256]{2,1,0:T(8,128)(2,1)S(1)} %bitcast.28), channel_id=1, source_target_pairs={{0,8},{4,12},{8,16},{12,20},{16,24},{20,28},{24,32},{28,36},{32,40... | collective-permute-start | bytes 786440 | tf_op jit(solution)/shard_map/ppermute | solution.py:20
  27.3 25.6 %collective-permute-start.3 = (bf16[2,256,256]{2,1,0:T(8,128)(2,1)S(1)}, bf16[2,256,256]{2,1,0:T(8,128)(2,1)S(1)}, u32[]{:S(2)}, u32[]{:S(2)}) collective-permute-start(bf16[2,256,256]{2,1,0:T(8,128)(2,1)S(1)} %bitcast.29), channel_id=1, source_target_pairs={{0,4},{4,8},{8,12},{12,16},{16,20},{20,24},{24,28},{28,32},{32,36}... | collective-permute-start | bytes 786440 | tf_op jit(solution)/shard_map/ppermute | solution.py:20
  52.9 1.1 copy-start.6
  69.9 9.7 %copy-start.2 = (bf16[2,128,256]{2,1,0:T(8,128)(2,1)}, bf16[2,128,256]{2,1,0:T(8,128)(2,1)S(1)}, u32[]{:S(2)}) copy-start(bf16[2,128,256]{2,1,0:T(8,128)(2,1)S(1)} %get-tuple-element.18.rest_3_) | copy-start | bytes 393220
  69.9 9.7 %copy-start.3 = (bf16[2,128,256]{2,1,0:T(8,128)(2,1)}, bf16[2,128,256]{2,1,0:T(8,128)(2,1)S(1)}, u32[]{:S(2)}) copy-start(bf16[2,128,256]{2,1,0:T(8,128)(2,1)S(1)} %get-tuple-element.19.rest_2_) | copy-start | bytes 393220
  69.9 9.7 %copy-start.4 = (bf16[2,128,256]{2,1,0:T(8,128)(2,1)}, bf16[2,128,256]{2,1,0:T(8,128)(2,1)S(1)}, u32[]{:S(2)}) copy-start(bf16[2,128,256]{2,1,0:T(8,128)(2,1)S(1)} %get-tuple-element.20.rest_1_) | copy-start | bytes 393220
  69.9 9.7 %copy-start.5 = (bf16[2,128,256]{2,1,0:T(8,128)(2,1)}, bf16[2,128,256]{2,1,0:T(8,128)(2,1)S(1)}, u32[]{:S(2)}) copy-start(bf16[2,128,256]{2,1,0:T(8,128)(2,1)S(1)} %get-tuple-element.21.rest_0_) | copy-start | bytes 393220
  69.9 27.6 %collective-permute-start.4 = (bf16[2,128,256]{2,1,0:T(8,128)(2,1)S(1)}, bf16[2,128,256]{2,1,0:T(8,128)(2,1)S(1)}, u32[]{:S(2)}, u32[]{:S(2)}) collective-permute-start(bf16[2,128,256]{2,1,0:T(8,128)(2,1)S(1)} %get-tuple-element.21.rest_0_), channel_id=1, source_target_pairs={{16,0},{20,4},{24,8},{28,12},{32,16},{36,20},{40,24},{44,28},{48,3... | collective-permute-start | bytes 393224 | tf_op jit(solution)/shard_map/ppermute | solution.py:20
  71.8 27.7 %collective-permute-start.5 = (bf16[2,128,256]{2,1,0:T(8,128)(2,1)S(1)}, bf16[2,128,256]{2,1,0:T(8,128)(2,1)S(1)}, u32[]{:S(2)}, u32[]{:S(2)}) collective-permute-start(bf16[2,128,256]{2,1,0:T(8,128)(2,1)S(1)} %get-tuple-element.20.rest_1_), channel_id=1, source_target_pairs={{12,0},{16,4},{20,8},{24,12},{28,16},{32,20},{36,24},{40,28},{44,3... | collective-permute-start | bytes 393224 | tf_op jit(solution)/shard_map/ppermute | solution.py:20
  73.8 27.7 %collective-permute-start.6 = (bf16[2,128,256]{2,1,0:T(8,128)(2,1)S(1)}, bf16[2,128,256]{2,1,0:T(8,128)(2,1)S(1)}, u32[]{:S(2)}, u32[]{:S(2)}) collective-permute-start(bf16[2,128,256]{2,1,0:T(8,128)(2,1)S(1)} %get-tuple-element.19.rest_2_), channel_id=1, source_target_pairs={{8,0},{12,4},{16,8},{20,12},{24,16},{28,20},{32,24},{36,28},{40,32... | collective-permute-start | bytes 393224 | tf_op jit(solution)/shard_map/ppermute | solution.py:20
  75.7 27.7 %collective-permute-start.7 = (bf16[2,128,256]{2,1,0:T(8,128)(2,1)S(1)}, bf16[2,128,256]{2,1,0:T(8,128)(2,1)S(1)}, u32[]{:S(2)}, u32[]{:S(2)}) collective-permute-start(bf16[2,128,256]{2,1,0:T(8,128)(2,1)S(1)} %get-tuple-element.18.rest_3_), channel_id=1, source_target_pairs={{4,0},{8,4},{12,8},{16,12},{20,16},{24,20},{28,24},{32,28},{36,32}... | collective-permute-start | bytes 393224 | tf_op jit(solution)/shard_map/ppermute | solution.py:20
  95.6 8.8 %collective-permute-start.10 = (bf16[2,128,256]{2,1,0:T(8,128)(2,1)S(1)}, bf16[2,128,256]{2,1,0:T(8,128)(2,1)S(1)}, u32[]{:S(2)}, u32[]{:S(2)}) collective-permute-start(bf16[2,128,256]{2,1,0:T(8,128)(2,1)S(1)} %get-tuple-element.16), channel_id=1, source_target_pairs={{8,0},{12,4},{16,8},{20,12},{24,16},{28,20},{32,24},{36,28},{40,32... | collective-permute-start | bytes 393224 | tf_op jit(solution)/shard_map/ppermute | solution.py:20
  97.6 10.3 %collective-permute-start.11 = (bf16[2,128,256]{2,1,0:T(8,128)(2,1)S(1)}, bf16[2,128,256]{2,1,0:T(8,128)(2,1)S(1)}, u32[]{:S(2)}, u32[]{:S(2)}) collective-permute-start(bf16[2,128,256]{2,1,0:T(8,128)(2,1)S(1)} %get-tuple-element.15), channel_id=1, source_target_pairs={{4,0},{8,4},{12,8},{16,12},{20,16},{24,20},{28,24},{32,28},{36,32}... | collective-permute-start | bytes 393224 | tf_op jit(solution)/shard_map/ppermute | solution.py:20
  99.5 15.1 %collective-permute-start.8 = (bf16[2,128,256]{2,1,0:T(8,128)(2,1)S(1)}, bf16[2,128,256]{2,1,0:T(8,128)(2,1)S(1)}, u32[]{:S(2)}, u32[]{:S(2)}) collective-permute-start(bf16[2,128,256]{2,1,0:T(8,128)(2,1)S(1)} %get-tuple-element.14), channel_id=1, source_target_pairs={{16,0},{20,4},{24,8},{28,12},{32,16},{36,20},{40,24},{44,28},{48,3... | collective-permute-start | bytes 393224 | tf_op jit(solution)/shard_map/ppermute | solution.py:20
  101.5 20.1 %collective-permute-start.9 = (bf16[2,128,256]{2,1,0:T(8,128)(2,1)S(1)}, bf16[2,128,256]{2,1,0:T(8,128)(2,1)S(1)}, u32[]{:S(2)}, u32[]{:S(2)}) collective-permute-start(bf16[2,128,256]{2,1,0:T(8,128)(2,1)S(1)} %get-tuple-element.17), channel_id=1, source_target_pairs={{12,0},{16,4},{20,8},{24,12},{28,16},{32,20},{36,24},{40,28},{44,3... | collective-permute-start | bytes 393224 | tf_op jit(solution)/shard_map/ppermute | solution.py:20
  122.6 5.9 %copy-start = (bf16[256,1024]{1,0:T(8,128)(2,1)S(1)}, bf16[256,1024]{1,0:T(8,128)(2,1)}, u32[]{:S(2)}) copy-start(bf16[256,1024]{1,0:T(8,128)(2,1)} %get-tuple-element.8) | copy-start | bytes 1572868
  122.7 5.9 %copy-start.1 = (bf16[256,1024]{1,0:T(8,128)(2,1)S(1)}, bf16[256,1024]{1,0:T(8,128)(2,1)}, u32[]{:S(2)}) copy-start(bf16[256,1024]{1,0:T(8,128)(2,1)} %get-tuple-element.10) | copy-start | bytes 1572868
  123.6 12.6 %all-to-all-start.1 = ((bf16[2,16,16,256]{3,2,0,1:T(8,128)(2,1)}), bf16[2,16,16,256]{3,2,0,1:T(8,128)(2,1)S(1)}, u32[]{:S(2)}, u32[]{:S(2)}) async-start(bf16[2,16,16,256]{3,2,0,1:T(8,128)(2,1)} %copy.17), calls=%async_computation.1 | async-start | bytes 524288 | tf_op jit(solution)/shard_map/all_to_all | solution.py:111

commit v13 on v12

--- a/solution.py
+++ b/solution.py
@@ -117,14 +117,15 @@
 
 
 def body(queries, upstream, shared_kv):
-    local_kv = lax.all_to_all(shared_kv, "tp", split_axis=2, concat_axis=1, tiled=True)
-    tok_rows = local_kv.shape[1]
+    span_blocks = WINDOW // (shared_kv.shape[1] * lax.axis_size("tp"))
+    earlier = [shifted(shared_kv, "seq", span_blocks - offset) for offset in range(span_blocks)]
+    blocks = jnp.stack(earlier + [shared_kv], axis=1)
+    blocks = lax.all_to_all(blocks, "tp", split_axis=3, concat_axis=2, tiled=True)
+    kinds, _, tok_rows, kv_cols = blocks.shape
+    extended = blocks.reshape(kinds, (span_blocks + 1) * tok_rows, kv_cols)
     head_size = HD
     group_size = QH // KVH
-    span_blocks = WINDOW // tok_rows
     score_scale = 1.0 / math.sqrt(head_size)
-    earlier = [shifted(local_kv, "seq", span_blocks - offset) for offset in range(span_blocks)]
-    extended = jnp.concatenate(earlier + [local_kv], axis=1)
     ext_rows = extended.shape[1]
     position = lax.axis_index("seq")
     row_ids = lax.broadcasted_iota(jnp.int32, (tok_rows, ext_rows), 0)

time: 151 us -> 206 us (1.36)
  waiting for transfers between devices: 50.1 us -> 94.2 us
  local copies, waits for them, and re-layouts: 7.46 us -> 18 us
    ppermute x12, waiting for transfers between devices: 37.6 us -> 71.9 us  [shifted(): return lax.ppermute(value, axis, pairs)]
    all_to_all x1, waiting for transfers between devices: 5.94 us -> 15.7 us  [body(): lax.all_to_all(blocks, 'tp', split_axis=3, concat_axis=2, tiled=True)]
    unnamed x21 -> x19, local copies, waits for them, and re-layouts: 3.89 us -> 10.3 us
    all_to_all x1, local copies, waits for them, and re-layouts: 0.39 us -> 3.84 us  [body(): lax.all_to_all(blocks, 'tp', split_axis=3, concat_axis=2, tiled=True)]
  transfers between devices with their start and end apart: 14 -> 14, of which waited for: 8 -> 9; matrix products, arithmetic and copies ran while one was open for 3% -> 3% of each run, Pallas kernels for 10% -> 7%
where the time goes in v13:
time: 206 us; the launch traced here: 205 us
  waiting for transfers between devices  94.2 us (46%)
  starting transfers between devices  44.3 us (22%)
  Pallas kernels  29.7 us (14%)
  local copies, waits for them, and re-layouts  18 us (9%)
  blocking collectives  12.5 us (6%)
  other arithmetic  5.78 us (3%)
    ppermute x12, waiting for transfers between devices, shifted(): return lax.ppermute(value, axis, pairs)  71.9 us
    ppermute x12, starting transfers between devices, shifted(): return lax.ppermute(value, axis, pairs)  35.1 us
    pallas_call x2, Pallas kernels, attention_grads(): pl.pallas_call(functools.partial(attn_kernel, scale=scale, hd=hd, per_ste...  29.7 us
    all_to_all x1, waiting for transfers between devices, body(): lax.all_to_all(blocks, 'tp', split_axis=3, concat_axis=2, tiled=True)  15.7 us
    all_gather x1, blocking collectives, body(): lax.all_gather(chunk.reshape(kinds, rows, -1).astype(jnp.bfloat16), 'sect...  12.5 us
    unnamed x19, local copies, waits for them, and re-layouts  10.3 us
    all_to_all x1, waiting for transfers between devices, scatter_layers(): lax.all_to_all(pieces.astype(jnp.bfloat16), ('section', 'tp'), split_axis...  6.59 us
    all_to_all x1, starting transfers between devices, scatter_layers(): lax.all_to_all(pieces.astype(jnp.bfloat16), ('section', 'tp'), split_axis...  4.88 us
  transfers between devices with their start and end apart: 14, of which 9 were waited for; matrix products, arithmetic and copies ran while one was open for 3% of the time, Pallas kernels for 7%

profile of v13, /device:TPU:80, one launch (start us, length us, event | category | flops | bytes accessed | tf_op | source)
XLA Modules:
  0.0 205.4 jit_solution(7161411183352979881)
XLA Ops:
  1.9 6.4 %collective-permute-start = (bf16[2,64,1024]{1,0,2:T(2,128)(2,1)S(1)}, bf16[2,64,1024]{1,0,2:T(2,128)(2,1)S(1)}, u32[]{:S(2)}, u32[]{:S(2)}) collective-permute-start(bf16[2,64,1024]{1,0,2:T(2,128)(2,1)S(1)} %copy.13), channel_id=1, source_target_pairs={{0,16},{4,20},{8,24},{12,28},{16,32},{20,36},{24,40},{28,44},{32,4... | collective-permute-start | bytes 786440 | tf_op jit(solution)/shard_map/ppermute | solution.py:20
  8.3 3.2 %collective-permute-start.1 = (bf16[2,64,1024]{1,0,2:T(2,128)(2,1)S(1)}, bf16[2,64,1024]{1,0,2:T(2,128)(2,1)S(1)}, u32[]{:S(2)}, u32[]{:S(2)}) collective-permute-start(bf16[2,64,1024]{1,0,2:T(2,128)(2,1)S(1)} %copy.13), channel_id=1, source_target_pairs={{0,12},{4,16},{8,20},{12,24},{16,28},{20,32},{24,36},{28,40},{32,4... | collective-permute-start | bytes 786440 | tf_op jit(solution)/shard_map/ppermute | solution.py:20
  11.5 2.9 %collective-permute-start.2 = (bf16[2,64,1024]{1,0,2:T(2,128)(2,1)S(1)}, bf16[2,64,1024]{1,0,2:T(2,128)(2,1)S(1)}, u32[]{:S(2)}, u32[]{:S(2)}) collective-permute-start(bf16[2,64,1024]{1,0,2:T(2,128)(2,1)S(1)} %copy.13), channel_id=1, source_target_pairs={{0,8},{4,12},{8,16},{12,20},{16,24},{20,28},{24,32},{28,36},{32,40... | collective-permute-start | bytes 786440 | tf_op jit(solution)/shard_map/ppermute | solution.py:20
  14.4 5.1 %collective-permute-start.3 = (bf16[2,64,1024]{1,0,2:T(2,128)(2,1)S(1)}, bf16[2,64,1024]{1,0,2:T(2,128)(2,1)S(1)}, u32[]{:S(2)}, u32[]{:S(2)}) collective-permute-start(bf16[2,64,1024]{1,0,2:T(2,128)(2,1)S(1)} %copy.13), channel_id=1, source_target_pairs={{0,4},{4,8},{8,12},{12,16},{16,20},{20,24},{24,28},{28,32},{32,36}... | collective-permute-start | bytes 786440 | tf_op jit(solution)/shard_map/ppermute | solution.py:20
  21.0 33.2 %collective-permute-done.1 = bf16[2,64,1024]{1,0,2:T(2,128)(2,1)S(1)} collective-permute-done((bf16[2,64,1024]{1,0,2:T(2,128)(2,1)S(1)}, bf16[2,64,1024]{1,0,2:T(2,128)(2,1)S(1)}, u32[]{:S(2)}, u32[]{:S(2)}) %collective-permute-start.1) | collective-permute-done | bytes 262176 | tf_op jit(solution)/shard_map/ppermute | solution.py:20
  54.9 10.5 %collective-permute-done.2 = bf16[2,64,1024]{1,0,2:T(2,128)(2,1)S(1)} collective-permute-done((bf16[2,64,1024]{1,0,2:T(2,128)(2,1)S(1)}, bf16[2,64,1024]{1,0,2:T(2,128)(2,1)S(1)}, u32[]{:S(2)}, u32[]{:S(2)}) %collective-permute-start.2) | collective-permute-done | bytes 262176 | tf_op jit(solution)/shard_map/ppermute | solution.py:20
  66.2 9.4 %collective-permute-done.3 = bf16[2,64,1024]{1,0,2:T(2,128)(2,1)S(1)} collective-permute-done((bf16[2,64,1024]{1,0,2:T(2,128)(2,1)S(1)}, bf16[2,64,1024]{1,0,2:T(2,128)(2,1)S(1)}, u32[]{:S(2)}, u32[]{:S(2)}) %collective-permute-start.3) | collective-permute-done | bytes 262176 | tf_op jit(solution)/shard_map/ppermute | solution.py:20
  77.0 3.0 %reshape.41 = bf16[4,2,81920]{2,1,0:T(2,128)(2,1)} reshape(bf16[1024,5,2,64]{3,2,1,0:T(2,128)(2,1)S(1)} %bitcast.35) | data formatting | bytes 2621440
  80.1 4.3 %all-to-all-start = ((bf16[4,2,81920]{2,1,0:T(2,128)(2,1)}), bf16[4,2,81920]{2,1,0:T(2,128)(2,1)}, u32[]{:S(2)}, u32[]{:S(2)}) async-start(bf16[4,2,81920]{2,1,0:T(2,128)(2,1)} %reshape.41), calls=%async_computation | async-start | bytes 2621440 | tf_op jit(solution)/shard_map/all_to_all | solution.py:123
  86.0 15.7 %all-to-all-done = bf16[4,2,81920]{2,1,0:T(2,128)(2,1)} async-done(((bf16[4,2,81920]{2,1,0:T(2,128)(2,1)}), bf16[4,2,81920]{2,1,0:T(2,128)(2,1)}, u32[]{:S(2)}, u32[]{:S(2)}) %all-to-all-start) | async-done | bytes 1310752 | tf_op jit(solution)/shard_map/all_to_all | solution.py:123
  101.7 3.4 %reshape.42 = bf16[1024,5,2,64]{3,2,1,0:T(2,128)(2,1)S(1)} reshape(bf16[4,2,81920]{2,1,0:T(2,128)(2,1)} %all-to-all-done) | data formatting | bytes 2621440
  105.1 3.8 %copy.18 = bf16[2,5,64,4,256]{4,2,3,1,0:T(8,128)(2,1)} copy(bf16[2,5,64,4,256]{2,0,1,4,3:T(2,128)(2,1)S(1)} %bitcast.34) | data formatting | bytes 2621440 | tf_op jit(solution)/shard_map/all_to_all | solution.py:123
  108.9 14.8 %shard_map.50 = (bf16[256,1024]{1,0:T(8,128)(2,1)}, f32[2,128,1280]{2,1,0:T(8,128)}, bf16[2,128,1024]{2,1,0:T(8,128)(2,1)}) custom-call(f32[256,1280]{1,0:T(8,128)} %fusion.2.bias_ref, bf16[256,2048]{1,0:T(8,128)(2,1)} %bitcast.44, bf16[256,2048]{1,0:T(8,128)(2,1)} %bitcast.46, bf16[2,1280,256]{2,1,0:T(8,128)(2,1)} %bitcast.36, bf16[2,1280,256]{2,1,0:T(8,128)(2,1)} %bitcast.37), custom_call_target="tpu_custom_call" | custom-call | flops 4026531840 | bytes 4849664 | tf_op jit(solution)/shard_map/pallas_call | solution.py:75
  124.9 1.9 collective-permute-start.4
  130.7 4.1 %collective-permute-start.7 = (bf16[2,128,256]{2,1,0:T(8,128)(2,1)S(1)}, bf16[2,128,256]{2,1,0:T(8,128)(2,1)S(1)}, u32[]{:S(2)}, u32[]{:S(2)}) collective-permute-start(bf16[2,128,256]{2,1,0:T(8,128)(2,1)S(1)} %get-tuple-element.18.rest_3_), channel_id=1, source_target_pairs={{4,0},{8,4},{12,8},{16,12},{20,16},{24,20},{28,24},{32,28},{36,32}... | collective-permute-start | bytes 393224 | tf_op jit(solution)/shard_map/ppermute | solution.py:20
  134.8 14.9 %shard_map.51 = (bf16[256,1024]{1,0:T(8,128)(2,1)}, f32[2,128,1280]{2,1,0:T(8,128)}, bf16[2,128,1024]{2,1,0:T(8,128)(2,1)}) custom-call(f32[256,1280]{1,0:T(8,128)} %fusion.2.bias_ref, bf16[256,2048]{1,0:T(8,128)(2,1)} %bitcast.45, bf16[256,2048]{1,0:T(8,128)(2,1)} %bitcast.47, bf16[2,1280,256]{2,1,0:T(8,128)(2,1)} %bitcast.38, ...), custom_call_target="tpu_custom_call" | custom-call | flops 4026531840 | bytes 4849664 | tf_op jit(solution)/shard_map/pallas_call | solution.py:75
  152.8 1.9 collective-permute-start.11
  154.7 1.9 collective-permute-start.8
  159.7 3.5 %collective-permute-done.11 = bf16[2,128,256]{2,1,0:T(8,128)(2,1)S(1)} collective-permute-done((bf16[2,128,256]{2,1,0:T(8,128)(2,1)S(1)}, bf16[2,128,256]{2,1,0:T(8,128)(2,1)S(1)}, u32[]{:S(2)}, u32[]{:S(2)}) %collective-permute-start.11) | collective-permute-done | bytes 131104 | tf_op jit(solution)/shard_map/ppermute | solution.py:20
  163.2 7.0 %collective-permute-done.8 = bf16[2,128,256]{2,1,0:T(8,128)(2,1)S(1)} collective-permute-done((bf16[2,128,256]{2,1,0:T(8,128)(2,1)S(1)}, bf16[2,128,256]{2,1,0:T(8,128)(2,1)S(1)}, u32[]{:S(2)}, u32[]{:S(2)}) %collective-permute-start.8) | collective-permute-done | bytes 131104 | tf_op jit(solution)/shard_map/ppermute | solution.py:20
  170.2 7.2 %collective-permute-done.9 = bf16[2,128,256]{2,1,0:T(8,128)(2,1)S(1)} collective-permute-done((bf16[2,128,256]{2,1,0:T(8,128)(2,1)S(1)}, bf16[2,128,256]{2,1,0:T(8,128)(2,1)S(1)}, u32[]{:S(2)}, u32[]{:S(2)}) %collective-permute-start.9) | collective-permute-done | bytes 131104 | tf_op jit(solution)/shard_map/ppermute | solution.py:20
  179.3 4.9 %all-to-all-start.1 = ((bf16[2,16,16,256]{3,2,0,1:T(8,128)(2,1)}), bf16[2,16,16,256]{3,2,0,1:T(8,128)(2,1)S(1)}, u32[]{:S(2)}, u32[]{:S(2)}) async-start(bf16[2,16,16,256]{3,2,0,1:T(8,128)(2,1)} %copy.21), calls=%async_computation.1 | async-start | bytes 524288 | tf_op jit(solution)/shard_map/all_to_all | solution.py:111
  185.3 6.6 %all-to-all-done.1 = bf16[2,16,16,256]{3,2,0,1:T(8,128)(2,1)S(1)} async-done(((bf16[2,16,16,256]{3,2,0,1:T(8,128)(2,1)}), bf16[2,16,16,256]{3,2,0,1:T(8,128)(2,1)S(1)}, u32[]{:S(2)}, u32[]{:S(2)}) %all-to-all-start.1) | async-done | bytes 262176 | tf_op jit(solution)/shard_map/all_to_all | solution.py:111
  192.0 12.5 %all_gather.3 = bf16[2,64,1024]{2,1,0:T(8,128)(2,1)S(1)} all-gather(bf16[2,16,1024]{2,1,0:T(8,128)(2,1)S(1)} %bitcast.43), channel_id=1, replica_groups=mesh['section'=4,'seq'=16,'tp'=4] {'section'}, dimensions={1}, use_global_device_ids=true | all-gather | bytes 327680 | tf_op jit(solution)/shard_map/all_gather | solution.py:163
  (45 shorter events, 22.3 us)
Async XLA Ops:
  1.9 18.7 %collective-permute-start = (bf16[2,64,1024]{1,0,2:T(2,128)(2,1)S(1)}, bf16[2,64,1024]{1,0,2:T(2,128)(2,1)S(1)}, u32[]{:S(2)}, u32[]{:S(2)}) collective-permute-start(bf16[2,64,1024]{1,0,2:T(2,128)(2,1)S(1)} %copy.13), channel_id=1, source_target_pairs={{0,16},{4,20},{8,24},{12,28},{16,32},{20,36},{24,40},{28,44},{32,4... | collective-permute-start | bytes 786440 | tf_op jit(solution)/shard_map/ppermute | solution.py:20
  8.3 45.9 %collective-permute-start.1 = (bf16[2,64,1024]{1,0,2:T(2,128)(2,1)S(1)}, bf16[2,64,1024]{1,0,2:T(2,128)(2,1)S(1)}, u32[]{:S(2)}, u32[]{:S(2)}) collective-permute-start(bf16[2,64,1024]{1,0,2:T(2,128)(2,1)S(1)} %copy.13), channel_id=1, source_target_pairs={{0,12},{4,16},{8,20},{12,24},{16,28},{20,32},{24,36},{28,40},{32,4... | collective-permute-start | bytes 786440 | tf_op jit(solution)/shard_map/ppermute | solution.py:20
  11.5 54.0 %collective-permute-start.2 = (bf16[2,64,1024]{1,0,2:T(2,128)(2,1)S(1)}, bf16[2,64,1024]{1,0,2:T(2,128)(2,1)S(1)}, u32[]{:S(2)}, u32[]{:S(2)}) collective-permute-start(bf16[2,64,1024]{1,0,2:T(2,128)(2,1)S(1)} %copy.13), channel_id=1, source_target_pairs={{0,8},{4,12},{8,16},{12,20},{16,24},{20,28},{24,32},{28,36},{32,40... | collective-permute-start | bytes 786440 | tf_op jit(solution)/shard_map/ppermute | solution.py:20
  14.4 61.2 %collective-permute-start.3 = (bf16[2,64,1024]{1,0,2:T(2,128)(2,1)S(1)}, bf16[2,64,1024]{1,0,2:T(2,128)(2,1)S(1)}, u32[]{:S(2)}, u32[]{:S(2)}) collective-permute-start(bf16[2,64,1024]{1,0,2:T(2,128)(2,1)S(1)} %copy.13), channel_id=1, source_target_pairs={{0,4},{4,8},{8,12},{12,16},{16,20},{20,24},{24,28},{28,32},{32,36}... | collective-permute-start | bytes 786440 | tf_op jit(solution)/shard_map/ppermute | solution.py:20
  80.1 21.6 %all-to-all-start = ((bf16[4,2,81920]{2,1,0:T(2,128)(2,1)}), bf16[4,2,81920]{2,1,0:T(2,128)(2,1)}, u32[]{:S(2)}, u32[]{:S(2)}) async-start(bf16[4,2,81920]{2,1,0:T(2,128)(2,1)} %reshape.41), calls=%async_computation | async-start | bytes 2621440 | tf_op jit(solution)/shard_map/all_to_all | solution.py:123
  124.9 9.9 %copy-start.2 = (bf16[2,128,256]{2,1,0:T(8,128)(2,1)}, bf16[2,128,256]{2,1,0:T(8,128)(2,1)S(1)}, u32[]{:S(2)}) copy-start(bf16[2,128,256]{2,1,0:T(8,128)(2,1)S(1)} %get-tuple-element.18.rest_3_) | copy-start | bytes 393220
  124.9 9.9 %copy-start.3 = (bf16[2,128,256]{2,1,0:T(8,128)(2,1)}, bf16[2,128,256]{2,1,0:T(8,128)(2,1)S(1)}, u32[]{:S(2)}) copy-start(bf16[2,128,256]{2,1,0:T(8,128)(2,1)S(1)} %get-tuple-element.19.rest_2_) | copy-start | bytes 393220
  124.9 9.9 %copy-start.4 = (bf16[2,128,256]{2,1,0:T(8,128)(2,1)}, bf16[2,128,256]{2,1,0:T(8,128)(2,1)S(1)}, u32[]{:S(2)}) copy-start(bf16[2,128,256]{2,1,0:T(8,128)(2,1)S(1)} %get-tuple-element.20.rest_1_) | copy-start | bytes 393220
  124.9 9.9 %copy-start.5 = (bf16[2,128,256]{2,1,0:T(8,128)(2,1)}, bf16[2,128,256]{2,1,0:T(8,128)(2,1)S(1)}, u32[]{:S(2)}) copy-start(bf16[2,128,256]{2,1,0:T(8,128)(2,1)S(1)} %get-tuple-element.21.rest_0_) | copy-start | bytes 393220
  124.9 27.9 %collective-permute-start.4 = (bf16[2,128,256]{2,1,0:T(8,128)(2,1)S(1)}, bf16[2,128,256]{2,1,0:T(8,128)(2,1)S(1)}, u32[]{:S(2)}, u32[]{:S(2)}) collective-permute-start(bf16[2,128,256]{2,1,0:T(8,128)(2,1)S(1)} %get-tuple-element.21.rest_0_), channel_id=1, source_target_pairs={{16,0},{20,4},{24,8},{28,12},{32,16},{36,20},{40,24},{44,28},{48,3... | collective-permute-start | bytes 393224 | tf_op jit(solution)/shard_map/ppermute | solution.py:20
  126.8 27.9 %collective-permute-start.5 = (bf16[2,128,256]{2,1,0:T(8,128)(2,1)S(1)}, bf16[2,128,256]{2,1,0:T(8,128)(2,1)S(1)}, u32[]{:S(2)}, u32[]{:S(2)}) collective-permute-start(bf16[2,128,256]{2,1,0:T(8,128)(2,1)S(1)} %get-tuple-element.20.rest_1_), channel_id=1, source_target_pairs={{12,0},{16,4},{20,8},{24,12},{28,16},{32,20},{36,24},{40,28},{44,3... | collective-permute-start | bytes 393224 | tf_op jit(solution)/shard_map/ppermute | solution.py:20
  128.8 27.9 %collective-permute-start.6 = (bf16[2,128,256]{2,1,0:T(8,128)(2,1)S(1)}, bf16[2,128,256]{2,1,0:T(8,128)(2,1)S(1)}, u32[]{:S(2)}, u32[]{:S(2)}) collective-permute-start(bf16[2,128,256]{2,1,0:T(8,128)(2,1)S(1)} %get-tuple-element.19.rest_2_), channel_id=1, source_target_pairs={{8,0},{12,4},{16,8},{20,12},{24,16},{28,20},{32,24},{36,28},{40,32... | collective-permute-start | bytes 393224 | tf_op jit(solution)/shard_map/ppermute | solution.py:20
  130.7 27.9 %collective-permute-start.7 = (bf16[2,128,256]{2,1,0:T(8,128)(2,1)S(1)}, bf16[2,128,256]{2,1,0:T(8,128)(2,1)S(1)}, u32[]{:S(2)}, u32[]{:S(2)}) collective-permute-start(bf16[2,128,256]{2,1,0:T(8,128)(2,1)S(1)} %get-tuple-element.18.rest_3_), channel_id=1, source_target_pairs={{4,0},{8,4},{12,8},{16,12},{20,16},{24,20},{28,24},{32,28},{36,32}... | collective-permute-start | bytes 393224 | tf_op jit(solution)/shard_map/ppermute | solution.py:20
  150.8 8.9 %collective-permute-start.10 = (bf16[2,128,256]{2,1,0:T(8,128)(2,1)S(1)}, bf16[2,128,256]{2,1,0:T(8,128)(2,1)S(1)}, u32[]{:S(2)}, u32[]{:S(2)}) collective-permute-start(bf16[2,128,256]{2,1,0:T(8,128)(2,1)S(1)} %get-tuple-element.16), channel_id=1, source_target_pairs={{8,0},{12,4},{16,8},{20,12},{24,16},{28,20},{32,24},{36,28},{40,32... | collective-permute-start | bytes 393224 | tf_op jit(solution)/shard_map/ppermute | solution.py:20
  152.8 10.4 %collective-permute-start.11 = (bf16[2,128,256]{2,1,0:T(8,128)(2,1)S(1)}, bf16[2,128,256]{2,1,0:T(8,128)(2,1)S(1)}, u32[]{:S(2)}, u32[]{:S(2)}) collective-permute-start(bf16[2,128,256]{2,1,0:T(8,128)(2,1)S(1)} %get-tuple-element.15), channel_id=1, source_target_pairs={{4,0},{8,4},{12,8},{16,12},{20,16},{24,20},{28,24},{32,28},{36,32}... | collective-permute-start | bytes 393224 | tf_op jit(solution)/shard_map/ppermute | solution.py:20
  154.7 15.5 %collective-permute-start.8 = (bf16[2,128,256]{2,1,0:T(8,128)(2,1)S(1)}, bf16[2,128,256]{2,1,0:T(8,128)(2,1)S(1)}, u32[]{:S(2)}, u32[]{:S(2)}) collective-permute-start(bf16[2,128,256]{2,1,0:T(8,128)(2,1)S(1)} %get-tuple-element.14), channel_id=1, source_target_pairs={{16,0},{20,4},{24,8},{28,12},{32,16},{36,20},{40,24},{44,28},{48,3... | collective-permute-start | bytes 393224 | tf_op jit(solution)/shard_map/ppermute | solution.py:20
  156.7 20.7 %collective-permute-start.9 = (bf16[2,128,256]{2,1,0:T(8,128)(2,1)S(1)}, bf16[2,128,256]{2,1,0:T(8,128)(2,1)S(1)}, u32[]{:S(2)}, u32[]{:S(2)}) collective-permute-start(bf16[2,128,256]{2,1,0:T(8,128)(2,1)S(1)} %get-tuple-element.17), channel_id=1, source_target_pairs={{12,0},{16,4},{20,8},{24,12},{28,16},{32,20},{36,24},{40,28},{44,3... | collective-permute-start | bytes 393224 | tf_op jit(solution)/shard_map/ppermute | solution.py:20
  158.6 25.6 %copy-start = (bf16[256,1024]{1,0:T(8,128)(2,1)S(1)}, bf16[256,1024]{1,0:T(8,128)(2,1)}, u32[]{:S(2)}) copy-start(bf16[256,1024]{1,0:T(8,128)(2,1)} %get-tuple-element.8) | copy-start | bytes 1572868
  158.6 25.6 %copy-start.1 = (bf16[256,1024]{1,0:T(8,128)(2,1)S(1)}, bf16[256,1024]{1,0:T(8,128)(2,1)}, u32[]{:S(2)}) copy-start(bf16[256,1024]{1,0:T(8,128)(2,1)} %get-tuple-element.10) | copy-start | bytes 1572868
  179.3 12.6 %all-to-all-start.1 = ((bf16[2,16,16,256]{3,2,0,1:T(8,128)(2,1)}), bf16[2,16,16,256]{3,2,0,1:T(8,128)(2,1)S(1)}, u32[]{:S(2)}, u32[]{:S(2)}) async-start(bf16[2,16,16,256]{3,2,0,1:T(8,128)(2,1)} %copy.21), calls=%async_computation.1 | async-start | bytes 524288 | tf_op jit(solution)/shard_map/all_to_all | solution.py:111

commit v14 on v12

--- a/solution.py
+++ b/solution.py
@@ -138,25 +138,16 @@
     query_rows = queries.reshape(tok_rows, -1)
     grad_rows = upstream.reshape(tok_rows, -1)
     local_heads = extended.shape[2] // head_size
-    d_query_parts = []
-    own_parts = []
-    sent = []
-    for kv_head in range(local_heads):
-        d_query_part, grad_t, sent_t = attention_grads(
-            bias, query_rows, grad_rows, extended, group_size, head_size, score_scale, 2, kv_head, 1,
-            span_blocks * tok_rows, sent,
-        )
-        d_query_parts.append(d_query_part)
-        sent = [
-            sent_t[:, :, offset * tok_rows : (offset + 1) * tok_rows]
-            for offset in range(span_blocks)
-        ]
-        own_t = grad_t[:, :, span_blocks * tok_rows :]
-        for offset in range(span_blocks):
-            own_t = own_t + shifted(sent[offset], "seq", offset - span_blocks).astype(jnp.float32)
-        own_parts.append(own_t)
-    d_queries = jnp.concatenate(d_query_parts, axis=1).reshape(queries.shape)
-    own_rows = jnp.swapaxes(jnp.concatenate(own_parts, axis=1), 1, 2)
+    d_query_rows, grad_t, sent_t = attention_grads(
+        bias, query_rows, grad_rows, extended, group_size, head_size, score_scale, 2, 0, local_heads,
+        span_blocks * tok_rows,
+    )
+    d_queries = d_query_rows.reshape(queries.shape)
+    own_t = grad_t[:, :, span_blocks * tok_rows :]
+    for offset in range(span_blocks):
+        piece = sent_t[:, :, offset * tok_rows : (offset + 1) * tok_rows]
+        own_t = own_t + shifted(piece, "seq", offset - span_blocks).astype(jnp.float32)
+    own_rows = jnp.swapaxes(own_t, 1, 2)
     chunk = scatter_layers(own_rows)
     kinds, rows, tp_peers, cols = chunk.shape
     d_shared_kv = lax.all_gather(

time: 151 us -> 151 us (level)
  blocking collectives: 12.5 us -> 24.4 us
  starting transfers between devices: 43.3 us -> 32.2 us
  waiting for transfers between devices: 50.1 us -> 56.4 us
  Pallas kernels: 29.6 us -> 27.1 us
  other arithmetic: 5.71 us -> 3.75 us
  local copies, waits for them, and re-layouts: 7.46 us -> 5.69 us
    ppermute x12 -> x8, waiting for transfers between devices: 37.6 us -> 50.4 us  [shifted(): return lax.ppermute(value, axis, pairs)]
    all_to_all x0 -> x1, blocking collectives: none -> 11.9 us  [scatter_layers(): lax.all_to_all(pieces.astype(jnp.bfloat16), ('section', 'tp'), split_axis...]
    all_to_all x1 -> x0, waiting for transfers between devices: 6.59 us -> none  [scatter_layers(): lax.all_to_all(pieces.astype(jnp.bfloat16), ('section', 'tp'), split_axis...]
    ppermute x12 -> x8, starting transfers between devices: 34.9 us -> 28.8 us  [shifted(): return lax.ppermute(value, axis, pairs)]
    all_to_all x1 -> x0, starting transfers between devices: 4.98 us -> none  [scatter_layers(): lax.all_to_all(pieces.astype(jnp.bfloat16), ('section', 'tp'), split_axis...]
    pallas_call x2 -> x1, Pallas kernels: 29.6 us -> 27.1 us  [attention_grads(): pl.pallas_call(functools.partial(attn_kernel, scale=scale, hd=hd, per_ste...]
    another operation x2 -> x0, other arithmetic: 2.07 us -> none
    unnamed x21 -> x9, local copies, waits for them, and re-layouts: 3.89 us -> 3.82 us
  transfers between devices with their start and end apart: 14 -> 9, of which waited for: 8 -> 6; matrix products, arithmetic and copies ran while one was open for 3% -> 1% of each run, Pallas kernels for 10% -> 0%
where the time goes in v14:
time: 151 us; the launch traced here: 150 us
  waiting for transfers between devices  56.4 us (37%)
  starting transfers between devices  32.2 us (21%)
  Pallas kernels  27.1 us (18%)
  blocking collectives  24.4 us (16%)
  local copies, waits for them, and re-layouts  5.69 us (4%)
  other arithmetic  3.75 us (2%)
    ppermute x8, waiting for transfers between devices, shifted(): return lax.ppermute(value, axis, pairs)  50.4 us
    ppermute x8, starting transfers between devices, shifted(): return lax.ppermute(value, axis, pairs)  28.8 us
    pallas_call x1, Pallas kernels, attention_grads(): pl.pallas_call(functools.partial(attn_kernel, scale=scale, hd=hd, per_ste...  27.1 us
    all_gather x1, blocking collectives, body(): lax.all_gather(chunk.reshape(kinds, rows, -1).astype(jnp.bfloat16), 'sect...  12.5 us
    all_to_all x1, blocking collectives, scatter_layers(): lax.all_to_all(pieces.astype(jnp.bfloat16), ('section', 'tp'), split_axis...  11.9 us
    all_to_all x1, waiting for transfers between devices, body(): lax.all_to_all(shared_kv, 'tp', split_axis=2, concat_axis=1, tiled=True)  5.94 us
    unnamed x9, local copies, waits for them, and re-layouts  3.82 us
    all_to_all x1, starting transfers between devices, body(): lax.all_to_all(shared_kv, 'tp', split_axis=2, concat_axis=1, tiled=True)  3.41 us
  transfers between devices with their start and end apart: 9, of which 6 were waited for; matrix products, arithmetic and copies ran while one was open for 1% of the time, Pallas kernels for 0%

profile of v14, /device:TPU:80, one launch (start us, length us, event | category | flops | bytes accessed | tf_op | source)
XLA Modules:
  0.0 150.3 jit_solution(9276468482004358328)
XLA Ops:
  0.6 1.3 copy.13
  1.9 1.1 reshape.36
  3.0 3.4 %all-to-all-start = ((bf16[4,2,16384]{2,1,0:T(2,128)(2,1)}), bf16[4,2,16384]{2,1,0:T(2,128)(2,1)S(1)}, u32[]{:S(2)}, u32[]{:S(2)}) async-start(bf16[4,2,16384]{2,1,0:T(2,128)(2,1)} %reshape.36), calls=%async_computation | async-start | bytes 524288 | tf_op jit(solution)/shard_map/all_to_all | solution.py:120
  6.4 5.9 %all-to-all-done = bf16[4,2,16384]{2,1,0:T(2,128)(2,1)S(1)} async-done(((bf16[4,2,16384]{2,1,0:T(2,128)(2,1)}), bf16[4,2,16384]{2,1,0:T(2,128)(2,1)S(1)}, u32[]{:S(2)}, u32[]{:S(2)}) %all-to-all-start) | async-done | bytes 262176 | tf_op jit(solution)/shard_map/all_to_all | solution.py:120
  13.1 3.8 %collective-permute-start.2 = (bf16[2,256,256]{2,1,0:T(8,128)(2,1)S(1)}, bf16[2,256,256]{2,1,0:T(8,128)(2,1)S(1)}, u32[]{:S(2)}, u32[]{:S(2)}) collective-permute-start(bf16[2,256,256]{2,1,0:T(8,128)(2,1)S(1)} %bitcast.25), channel_id=1, source_target_pairs={{0,8},{4,12},{8,16},{12,20},{16,24},{20,28},{24,32},{28,36},{32,40... | collective-permute-start | bytes 786440 | tf_op jit(solution)/shard_map/ppermute | solution.py:20
  17.0 5.3 %collective-permute-start.1 = (bf16[2,256,256]{2,1,0:T(8,128)(2,1)S(1)}, bf16[2,256,256]{2,1,0:T(8,128)(2,1)S(1)}, u32[]{:S(2)}, u32[]{:S(2)}) collective-permute-start(bf16[2,256,256]{2,1,0:T(8,128)(2,1)S(1)} %bitcast.26), channel_id=1, source_target_pairs={{0,12},{4,16},{8,20},{12,24},{16,28},{20,32},{24,36},{28,40},{32,4... | collective-permute-start | bytes 786440 | tf_op jit(solution)/shard_map/ppermute | solution.py:20
  22.2 3.4 %collective-permute-start = (bf16[2,256,256]{2,1,0:T(8,128)(2,1)S(1)}, bf16[2,256,256]{2,1,0:T(8,128)(2,1)S(1)}, u32[]{:S(2)}, u32[]{:S(2)}) collective-permute-start(bf16[2,256,256]{2,1,0:T(8,128)(2,1)S(1)} %bitcast.27), channel_id=1, source_target_pairs={{0,16},{4,20},{8,24},{12,28},{16,32},{20,36},{24,40},{28,44},{32,4... | collective-permute-start | bytes 786440 | tf_op jit(solution)/shard_map/ppermute | solution.py:20
  25.6 1.6 %fusion.2.bias_ref = f32[256,1280]{1,0:T(8,128)} fusion(s32[256]{0:T(256)S(1)} %get-tuple-element.12, s32[256]{0:T(256)S(1)} %get-tuple-element.13, pred[1280]{0:T(1024)(128)(4,1)S(1)} %add_compare_fusion), kind=kLoop, calls=%fused_computation.4 | loop fusion | flops 1638400 | bytes 1314048 | tf_op jit(solution)/shard_map/jit(_where)/select_n | solution.py:137
  27.2 5.1 %collective-permute-start.3 = (bf16[2,256,256]{2,1,0:T(8,128)(2,1)S(1)}, bf16[2,256,256]{2,1,0:T(8,128)(2,1)S(1)}, u32[]{:S(2)}, u32[]{:S(2)}) collective-permute-start(bf16[2,256,256]{2,1,0:T(8,128)(2,1)S(1)} %bitcast.28), channel_id=1, source_target_pairs={{0,4},{4,8},{8,12},{12,16},{16,20},{20,24},{24,28},{28,32},{32,36}... | collective-permute-start | bytes 786440 | tf_op jit(solution)/shard_map/ppermute | solution.py:20
  32.3 13.4 %collective-permute-done = bf16[2,256,256]{2,1,0:T(8,128)(2,1)S(1)} collective-permute-done((bf16[2,256,256]{2,1,0:T(8,128)(2,1)S(1)}, bf16[2,256,256]{2,1,0:T(8,128)(2,1)S(1)}, u32[]{:S(2)}, u32[]{:S(2)}) %collective-permute-start) | collective-permute-done | bytes 262176 | tf_op jit(solution)/shard_map/ppermute | solution.py:20
  45.8 4.5 %collective-permute-done.3 = bf16[2,256,256]{2,1,0:T(8,128)(2,1)S(1)} collective-permute-done((bf16[2,256,256]{2,1,0:T(8,128)(2,1)S(1)}, bf16[2,256,256]{2,1,0:T(8,128)(2,1)S(1)}, u32[]{:S(2)}, u32[]{:S(2)}) %collective-permute-start.3) | collective-permute-done | bytes 262176 | tf_op jit(solution)/shard_map/ppermute | solution.py:20
  50.4 1.0 copy-done
  51.4 27.1 %shard_map.50 = (bf16[256,2048]{1,0:T(8,128)(2,1)}, f32[2,256,1280]{2,1,0:T(8,128)}, bf16[2,256,1024]{2,1,0:T(8,128)(2,1)}) custom-call(f32[256,1280]{1,0:T(8,128)} %fusion.2.bias_ref, bf16[256,2048]{1,0:T(8,128)(2,1)} %bitcast.34, bf16[256,2048]{1,0:T(8,128)(2,1)} %bitcast.35, bf16[2,1280,256]{2,1,0:T(8,128)(2,1)} %copy-done, bf16[2,1280,256]{2,1,0:T(8,128)(2,1)} %copy-done), custom_call_target="tpu_custom_call" | custom-call | flops 8053063680 | bytes 8388608 | tf_op jit(solution)/shard_map/pallas_call | solution.py:75
  78.6 1.3 fusion.6
  79.8 1.9 %collective-permute-start.4 = (bf16[2,256,256]{2,1,0:T(8,128)(2,1)S(1)}, bf16[2,256,256]{2,1,0:T(8,128)(2,1)S(1)}, u32[]{:S(2)}, u32[]{:S(2)}) collective-permute-start(bf16[2,256,256]{2,1,0:T(8,128)(2,1)S(1)} %get-tuple-element.8), channel_id=1, source_target_pairs={{16,0},{20,4},{24,8},{28,12},{32,16},{36,20},{40,24},{44,28},{48,3... | collective-permute-start | bytes 786440 | tf_op jit(solution)/shard_map/ppermute | solution.py:20
  81.8 5.4 %collective-permute-start.7 = (bf16[2,256,256]{2,1,0:T(8,128)(2,1)S(1)}, bf16[2,256,256]{2,1,0:T(8,128)(2,1)S(1)}, u32[]{:S(2)}, u32[]{:S(2)}) collective-permute-start(bf16[2,256,256]{2,1,0:T(8,128)(2,1)S(1)} %get-tuple-element.9), channel_id=1, source_target_pairs={{4,0},{8,4},{12,8},{16,12},{20,16},{24,20},{28,24},{32,28},{36,32}... | collective-permute-start | bytes 786440 | tf_op jit(solution)/shard_map/ppermute | solution.py:20
  87.2 1.9 %collective-permute-start.6 = (bf16[2,256,256]{2,1,0:T(8,128)(2,1)S(1)}, bf16[2,256,256]{2,1,0:T(8,128)(2,1)S(1)}, u32[]{:S(2)}, u32[]{:S(2)}) collective-permute-start(bf16[2,256,256]{2,1,0:T(8,128)(2,1)S(1)} %get-tuple-element.10), channel_id=1, source_target_pairs={{8,0},{12,4},{16,8},{20,12},{24,16},{28,20},{32,24},{36,28},{40,32... | collective-permute-start | bytes 786440 | tf_op jit(solution)/shard_map/ppermute | solution.py:20
  89.1 1.9 %collective-permute-start.5 = (bf16[2,256,256]{2,1,0:T(8,128)(2,1)S(1)}, bf16[2,256,256]{2,1,0:T(8,128)(2,1)S(1)}, u32[]{:S(2)}, u32[]{:S(2)}) collective-permute-start(bf16[2,256,256]{2,1,0:T(8,128)(2,1)S(1)} %get-tuple-element.11), channel_id=1, source_target_pairs={{12,0},{16,4},{20,8},{24,12},{28,16},{32,20},{36,24},{40,28},{44,3... | collective-permute-start | bytes 786440 | tf_op jit(solution)/shard_map/ppermute | solution.py:20
  91.1 7.6 %collective-permute-done.4 = bf16[2,256,256]{2,1,0:T(8,128)(2,1)S(1)} collective-permute-done((bf16[2,256,256]{2,1,0:T(8,128)(2,1)S(1)}, bf16[2,256,256]{2,1,0:T(8,128)(2,1)S(1)}, u32[]{:S(2)}, u32[]{:S(2)}) %collective-permute-start.4) | collective-permute-done | bytes 262176 | tf_op jit(solution)/shard_map/ppermute | solution.py:20
  98.6 6.4 %collective-permute-done.7 = bf16[2,256,256]{2,1,0:T(8,128)(2,1)S(1)} collective-permute-done((bf16[2,256,256]{2,1,0:T(8,128)(2,1)S(1)}, bf16[2,256,256]{2,1,0:T(8,128)(2,1)S(1)}, u32[]{:S(2)}, u32[]{:S(2)}) %collective-permute-start.7) | collective-permute-done | bytes 262176 | tf_op jit(solution)/shard_map/ppermute | solution.py:20
  105.0 18.6 %collective-permute-done.5 = bf16[2,256,256]{2,1,0:T(8,128)(2,1)S(1)} collective-permute-done((bf16[2,256,256]{2,1,0:T(8,128)(2,1)S(1)}, bf16[2,256,256]{2,1,0:T(8,128)(2,1)S(1)}, u32[]{:S(2)}, u32[]{:S(2)}) %collective-permute-start.5) | collective-permute-done | bytes 262176 | tf_op jit(solution)/shard_map/ppermute | solution.py:20
  123.6 1.2 fusion.3
  125.0 11.9 %all_to_all.23 = bf16[2,16,16,256]{3,2,0,1:T(8,128)(2,1)S(1)} all-to-all(bf16[2,16,16,256]{3,2,0,1:T(8,128)(2,1)S(1)} %copy.17), channel_id=1, replica_groups=mesh['section'=4,'seq'=16,'tp'=4] {'section','tp'}, dimensions={1} | all-to-all | bytes 524288 | tf_op jit(solution)/shard_map/all_to_all | solution.py:111
  137.0 12.5 %all_gather.3 = bf16[2,64,1024]{2,1,0:T(8,128)(2,1)S(1)} all-gather(bf16[2,16,1024]{2,1,0:T(8,128)(2,1)S(1)} %bitcast.33), channel_id=1, replica_groups=mesh['section'=4,'seq'=16,'tp'=4] {'section'}, dimensions={1}, use_global_device_ids=true | all-gather | bytes 327680 | tf_op jit(solution)/shard_map/all_gather | solution.py:153
  (21 shorter events, 2.0 us)
Async XLA Ops:
  3.0 9.4 %all-to-all-start = ((bf16[4,2,16384]{2,1,0:T(2,128)(2,1)}), bf16[4,2,16384]{2,1,0:T(2,128)(2,1)S(1)}, u32[]{:S(2)}, u32[]{:S(2)}) async-start(bf16[4,2,16384]{2,1,0:T(2,128)(2,1)} %reshape.36), calls=%async_computation | async-start | bytes 524288 | tf_op jit(solution)/shard_map/all_to_all | solution.py:120
  13.1 32.6 %collective-permute-start.2 = (bf16[2,256,256]{2,1,0:T(8,128)(2,1)S(1)}, bf16[2,256,256]{2,1,0:T(8,128)(2,1)S(1)}, u32[]{:S(2)}, u32[]{:S(2)}) collective-permute-start(bf16[2,256,256]{2,1,0:T(8,128)(2,1)S(1)} %bitcast.25), channel_id=1, source_target_pairs={{0,8},{4,12},{8,16},{12,20},{16,24},{20,28},{24,32},{28,36},{32,40... | collective-permute-start | bytes 786440 | tf_op jit(solution)/shard_map/ppermute | solution.py:20
  17.0 28.8 %collective-permute-start.1 = (bf16[2,256,256]{2,1,0:T(8,128)(2,1)S(1)}, bf16[2,256,256]{2,1,0:T(8,128)(2,1)S(1)}, u32[]{:S(2)}, u32[]{:S(2)}) collective-permute-start(bf16[2,256,256]{2,1,0:T(8,128)(2,1)S(1)} %bitcast.26), channel_id=1, source_target_pairs={{0,12},{4,16},{8,20},{12,24},{16,28},{20,32},{24,36},{28,40},{32,4... | collective-permute-start | bytes 786440 | tf_op jit(solution)/shard_map/ppermute | solution.py:20
  22.2 23.5 %collective-permute-start = (bf16[2,256,256]{2,1,0:T(8,128)(2,1)S(1)}, bf16[2,256,256]{2,1,0:T(8,128)(2,1)S(1)}, u32[]{:S(2)}, u32[]{:S(2)}) collective-permute-start(bf16[2,256,256]{2,1,0:T(8,128)(2,1)S(1)} %bitcast.27), channel_id=1, source_target_pairs={{0,16},{4,20},{8,24},{12,28},{16,32},{20,36},{24,40},{28,44},{32,4... | collective-permute-start | bytes 786440 | tf_op jit(solution)/shard_map/ppermute | solution.py:20
  27.2 23.1 %collective-permute-start.3 = (bf16[2,256,256]{2,1,0:T(8,128)(2,1)S(1)}, bf16[2,256,256]{2,1,0:T(8,128)(2,1)S(1)}, u32[]{:S(2)}, u32[]{:S(2)}) collective-permute-start(bf16[2,256,256]{2,1,0:T(8,128)(2,1)S(1)} %bitcast.28), channel_id=1, source_target_pairs={{0,4},{4,8},{8,12},{12,16},{16,20},{20,24},{24,28},{28,32},{32,36}... | collective-permute-start | bytes 786440 | tf_op jit(solution)/shard_map/ppermute | solution.py:20
  50.4 1.1 copy-start
  79.8 18.8 %collective-permute-start.4 = (bf16[2,256,256]{2,1,0:T(8,128)(2,1)S(1)}, bf16[2,256,256]{2,1,0:T(8,128)(2,1)S(1)}, u32[]{:S(2)}, u32[]{:S(2)}) collective-permute-start(bf16[2,256,256]{2,1,0:T(8,128)(2,1)S(1)} %get-tuple-element.8), channel_id=1, source_target_pairs={{16,0},{20,4},{24,8},{28,12},{32,16},{36,20},{40,24},{44,28},{48,3... | collective-permute-start | bytes 786440 | tf_op jit(solution)/shard_map/ppermute | solution.py:20
  81.8 23.3 %collective-permute-start.7 = (bf16[2,256,256]{2,1,0:T(8,128)(2,1)S(1)}, bf16[2,256,256]{2,1,0:T(8,128)(2,1)S(1)}, u32[]{:S(2)}, u32[]{:S(2)}) collective-permute-start(bf16[2,256,256]{2,1,0:T(8,128)(2,1)S(1)} %get-tuple-element.9), channel_id=1, source_target_pairs={{4,0},{8,4},{12,8},{16,12},{20,16},{24,20},{28,24},{32,28},{36,32}... | collective-permute-start | bytes 786440 | tf_op jit(solution)/shard_map/ppermute | solution.py:20
  87.2 17.8 %collective-permute-start.6 = (bf16[2,256,256]{2,1,0:T(8,128)(2,1)S(1)}, bf16[2,256,256]{2,1,0:T(8,128)(2,1)S(1)}, u32[]{:S(2)}, u32[]{:S(2)}) collective-permute-start(bf16[2,256,256]{2,1,0:T(8,128)(2,1)S(1)} %get-tuple-element.10), channel_id=1, source_target_pairs={{8,0},{12,4},{16,8},{20,12},{24,16},{28,20},{32,24},{36,28},{40,32... | collective-permute-start | bytes 786440 | tf_op jit(solution)/shard_map/ppermute | solution.py:20
  89.1 34.4 %collective-permute-start.5 = (bf16[2,256,256]{2,1,0:T(8,128)(2,1)S(1)}, bf16[2,256,256]{2,1,0:T(8,128)(2,1)S(1)}, u32[]{:S(2)}, u32[]{:S(2)}) collective-permute-start(bf16[2,256,256]{2,1,0:T(8,128)(2,1)S(1)} %get-tuple-element.11), channel_id=1, source_target_pairs={{12,0},{16,4},{20,8},{24,12},{28,16},{32,20},{36,24},{40,28},{44,3... | collective-permute-start | bytes 786440 | tf_op jit(solution)/shard_map/ppermute | solution.py:20

commit v15 on v14

--- a/solution.py
+++ b/solution.py
@@ -102,18 +102,19 @@
     )(bias, q, g, ext, ext, *after)
 
 
-def scatter_layers(own_rows):
+def sum_layers(own_rows):
     sections = lax.axis_size("section")
     peers = lax.axis_size("tp")
     kinds, rows, cols = own_rows.shape
-    pieces = own_rows.reshape(kinds, peers, sections, rows // (peers * sections), cols)
-    pieces = jnp.swapaxes(pieces, 1, 2).reshape(kinds, sections * peers, rows // (peers * sections), cols)
-    pieces = lax.all_to_all(pieces.astype(jnp.bfloat16), ("section", "tp"), split_axis=1, concat_axis=1)
-    pieces = pieces.astype(jnp.float32).reshape(kinds, sections, peers, rows // (peers * sections), cols)
-    chunk = pieces[:, 0]
+    per = rows // peers
+    pieces = own_rows.astype(jnp.bfloat16).reshape(kinds, 1, peers, per, cols)
+    pieces = jnp.broadcast_to(pieces, (kinds, sections, peers, per, cols)).reshape(kinds, sections * peers, per, cols)
+    pieces = lax.all_to_all(pieces, ("section", "tp"), split_axis=1, concat_axis=1)
+    pieces = pieces.astype(jnp.float32).reshape(kinds, sections, peers, per, cols)
+    total = pieces[:, 0]
     for other in range(1, sections):
-        chunk = chunk + pieces[:, other]
-    return jnp.swapaxes(chunk, 1, 2)
+        total = total + pieces[:, other]
+    return jnp.swapaxes(total, 1, 2).reshape(kinds, per, peers * cols)
 
 
 def body(queries, upstream, shared_kv):
@@ -148,11 +149,7 @@
         piece = sent_t[:, :, offset * tok_rows : (offset + 1) * tok_rows]
         own_t = own_t + shifted(piece, "seq", offset - span_blocks).astype(jnp.float32)
     own_rows = jnp.swapaxes(own_t, 1, 2)
-    chunk = scatter_layers(own_rows)
-    kinds, rows, tp_peers, cols = chunk.shape
-    d_shared_kv = lax.all_gather(
-        chunk.reshape(kinds, rows, -1).astype(jnp.bfloat16), "section", axis=1, tiled=True
-    ).astype(jnp.float32)
+    d_shared_kv = sum_layers(own_rows)
     return (d_queries, d_shared_kv)
 
 

time: 151 us -> 152 us (level)
  the two profiles are of different devices: /device:TPU:80 before, /device:TPU:16 now
where the time goes in v15:
time: 152 us
  waiting for transfers between devices  64.3 us (42%)
  starting transfers between devices  28.6 us (19%)
  Pallas kernels  27.1 us (18%)
  blocking collectives  21 us (14%)
  local copies, waits for them, and re-layouts  6.71 us (4%)
  other arithmetic  3.22 us (2%)
    ppermute x8, waiting for transfers between devices, shifted(): return lax.ppermute(value, axis, pairs)  58.3 us
    pallas_call x1, Pallas kernels, attention_grads(): pl.pallas_call(functools.partial(attn_kernel, scale=scale, hd=hd, per_ste...  27.1 us
    ppermute x8, starting transfers between devices, shifted(): return lax.ppermute(value, axis, pairs)  25.2 us
    all_to_all x1, blocking collectives, sum_layers(): lax.all_to_all(pieces, ('section', 'tp'), split_axis=1, concat_axis=1)  21 us
    all_to_all x1, waiting for transfers between devices, body(): lax.all_to_all(shared_kv, 'tp', split_axis=2, concat_axis=1, tiled=True)  5.94 us
    unnamed x9, local copies, waits for them, and re-layouts  3.83 us
    all_to_all x1, starting transfers between devices, body(): lax.all_to_all(shared_kv, 'tp', split_axis=2, concat_axis=1, tiled=True)  3.41 us
  transfers between devices with their start and end apart: 9, of which 5 were waited for; matrix products, arithmetic and copies ran while one was open for 1% of the time, Pallas kernels for 0%

profile of v15, /device:TPU:16, one launch (start us, length us, event | category | flops | bytes accessed | tf_op | source)
XLA Modules:
  0.0 151.8 jit_solution(96643177822904323)
XLA Ops:
  0.6 1.3 copy.12
  1.9 1.1 reshape.39
  3.0 3.4 %all-to-all-start = ((bf16[4,2,16384]{2,1,0:T(2,128)(2,1)}), bf16[4,2,16384]{2,1,0:T(2,128)(2,1)S(1)}, u32[]{:S(2)}, u32[]{:S(2)}) async-start(bf16[4,2,16384]{2,1,0:T(2,128)(2,1)} %reshape.39), calls=%async_computation | async-start | bytes 524288 | tf_op jit(solution)/shard_map/all_to_all | solution.py:121
  6.4 5.9 %all-to-all-done = bf16[4,2,16384]{2,1,0:T(2,128)(2,1)S(1)} async-done(((bf16[4,2,16384]{2,1,0:T(2,128)(2,1)}), bf16[4,2,16384]{2,1,0:T(2,128)(2,1)S(1)}, u32[]{:S(2)}, u32[]{:S(2)}) %all-to-all-start) | async-done | bytes 262176 | tf_op jit(solution)/shard_map/all_to_all | solution.py:121
  12.4 0.3 reshape.40
  12.7 0.4 copy.13
  13.1 3.8 %collective-permute-start.2 = (bf16[2,256,256]{2,1,0:T(8,128)(2,1)S(1)}, bf16[2,256,256]{2,1,0:T(8,128)(2,1)S(1)}, u32[]{:S(2)}, u32[]{:S(2)}) collective-permute-start(bf16[2,256,256]{2,1,0:T(8,128)(2,1)S(1)} %bitcast.25), channel_id=1, source_target_pairs={{0,8},{4,12},{8,16},{12,20},{16,24},{20,28},{24,32},{28,36},{32,40... | collective-permute-start | bytes 786440 | tf_op jit(solution)/shard_map/ppermute | solution.py:20
  17.0 5.0 %collective-permute-start.1 = (bf16[2,256,256]{2,1,0:T(8,128)(2,1)S(1)}, bf16[2,256,256]{2,1,0:T(8,128)(2,1)S(1)}, u32[]{:S(2)}, u32[]{:S(2)}) collective-permute-start(bf16[2,256,256]{2,1,0:T(8,128)(2,1)S(1)} %bitcast.26), channel_id=1, source_target_pairs={{0,12},{4,16},{8,20},{12,24},{16,28},{20,32},{24,36},{28,40},{32,4... | collective-permute-start | bytes 786440 | tf_op jit(solution)/shard_map/ppermute | solution.py:20
  21.9 5.5 %collective-permute-start = (bf16[2,256,256]{2,1,0:T(8,128)(2,1)S(1)}, bf16[2,256,256]{2,1,0:T(8,128)(2,1)S(1)}, u32[]{:S(2)}, u32[]{:S(2)}) collective-permute-start(bf16[2,256,256]{2,1,0:T(8,128)(2,1)S(1)} %bitcast.27), channel_id=1, source_target_pairs={{0,16},{4,20},{8,24},{12,28},{16,32},{20,36},{24,40},{28,44},{32,4... | collective-permute-start | bytes 786440 | tf_op jit(solution)/shard_map/ppermute | solution.py:20
  27.4 1.6 %fusion.2.bias_ref = f32[256,1280]{1,0:T(8,128)} fusion(s32[256]{0:T(256)S(1)} %get-tuple-element.12, s32[256]{0:T(256)S(1)} %get-tuple-element.13, pred[1280]{0:T(1024)(128)(4,1)S(1)} %add_compare_fusion), kind=kLoop, calls=%fused_computation.4 | loop fusion | flops 1638400 | bytes 1314048 | tf_op jit(solution)/shard_map/jit(_where)/select_n | solution.py:138
  29.1 5.1 %collective-permute-start.3 = (bf16[2,256,256]{2,1,0:T(8,128)(2,1)S(1)}, bf16[2,256,256]{2,1,0:T(8,128)(2,1)S(1)}, u32[]{:S(2)}, u32[]{:S(2)}) collective-permute-start(bf16[2,256,256]{2,1,0:T(8,128)(2,1)S(1)} %bitcast.28), channel_id=1, source_target_pairs={{0,4},{4,8},{8,12},{12,16},{16,20},{20,24},{24,28},{28,32},{32,36}... | collective-permute-start | bytes 786440 | tf_op jit(solution)/shard_map/ppermute | solution.py:20
  34.3 5.1 %collective-permute-done.3 = bf16[2,256,256]{2,1,0:T(8,128)(2,1)S(1)} collective-permute-done((bf16[2,256,256]{2,1,0:T(8,128)(2,1)S(1)}, bf16[2,256,256]{2,1,0:T(8,128)(2,1)S(1)}, u32[]{:S(2)}, u32[]{:S(2)}) %collective-permute-start.3) | collective-permute-done | bytes 262176 | tf_op jit(solution)/shard_map/ppermute | solution.py:20
  39.4 1.0 copy-done
  40.5 27.1 %shard_map.50 = (bf16[256,2048]{1,0:T(8,128)(2,1)}, f32[2,256,1280]{2,1,0:T(8,128)}, bf16[2,256,1024]{2,1,0:T(8,128)(2,1)}) custom-call(f32[256,1280]{1,0:T(8,128)} %fusion.2.bias_ref, bf16[256,2048]{1,0:T(8,128)(2,1)} %bitcast.32, bf16[256,2048]{1,0:T(8,128)(2,1)} %bitcast.33, bf16[2,1280,256]{2,1,0:T(8,128)(2,1)} %copy-done, bf16[2,1280,256]{2,1,0:T(8,128)(2,1)} %copy-done), custom_call_target="tpu_custom_call" | custom-call | flops 8053063680 | bytes 8388608 | tf_op jit(solution)/shard_map/pallas_call | solution.py:75
  67.6 1.3 fusion.5
  68.8 1.3 collective-permute-start.4
  70.1 1.9 %collective-permute-start.7 = (bf16[2,256,256]{2,1,0:T(8,128)(2,1)S(1)}, bf16[2,256,256]{2,1,0:T(8,128)(2,1)S(1)}, u32[]{:S(2)}, u32[]{:S(2)}) collective-permute-start(bf16[2,256,256]{2,1,0:T(8,128)(2,1)S(1)} %get-tuple-element.9), channel_id=1, source_target_pairs={{4,0},{8,4},{12,8},{16,12},{20,16},{24,20},{28,24},{32,28},{36,32}... | collective-permute-start | bytes 786440 | tf_op jit(solution)/shard_map/ppermute | solution.py:20
  72.1 1.3 collective-permute-start.6
  73.4 1.3 collective-permute-start.5
  74.7 22.7 %collective-permute-done.4 = bf16[2,256,256]{2,1,0:T(8,128)(2,1)S(1)} collective-permute-done((bf16[2,256,256]{2,1,0:T(8,128)(2,1)S(1)}, bf16[2,256,256]{2,1,0:T(8,128)(2,1)S(1)}, u32[]{:S(2)}, u32[]{:S(2)}) %collective-permute-start.4) | collective-permute-done | bytes 262176 | tf_op jit(solution)/shard_map/ppermute | solution.py:20
  97.4 30.5 %collective-permute-done.5 = bf16[2,256,256]{2,1,0:T(8,128)(2,1)S(1)} collective-permute-done((bf16[2,256,256]{2,1,0:T(8,128)(2,1)S(1)}, bf16[2,256,256]{2,1,0:T(8,128)(2,1)S(1)}, u32[]{:S(2)}, u32[]{:S(2)}) %collective-permute-start.5) | collective-permute-done | bytes 262176 | tf_op jit(solution)/shard_map/ppermute | solution.py:20
  127.9 1.2 fusion.4
  129.4 21.0 %all_to_all.23 = bf16[2,16,64,256]{3,2,0,1:T(8,128)(2,1)S(1)} all-to-all(bf16[2,16,64,256]{3,2,0,1:T(8,128)(2,1)S(1)} %bitcast.22), channel_id=1, replica_groups=mesh['section'=4,'seq'=16,'tp'=4] {'section','tp'}, dimensions={1} | all-to-all | bytes 2097152 | tf_op jit(solution)/shard_map/all_to_all | solution.py:112
  151.0 0.9 copy.18
  (19 shorter events, 1.0 us)
Async XLA Ops:
  3.0 9.4 %all-to-all-start = ((bf16[4,2,16384]{2,1,0:T(2,128)(2,1)}), bf16[4,2,16384]{2,1,0:T(2,128)(2,1)S(1)}, u32[]{:S(2)}, u32[]{:S(2)}) async-start(bf16[4,2,16384]{2,1,0:T(2,128)(2,1)} %reshape.39), calls=%async_computation | async-start | bytes 524288 | tf_op jit(solution)/shard_map/all_to_all | solution.py:121
  13.1 21.1 %collective-permute-start.2 = (bf16[2,256,256]{2,1,0:T(8,128)(2,1)S(1)}, bf16[2,256,256]{2,1,0:T(8,128)(2,1)S(1)}, u32[]{:S(2)}, u32[]{:S(2)}) collective-permute-start(bf16[2,256,256]{2,1,0:T(8,128)(2,1)S(1)} %bitcast.25), channel_id=1, source_target_pairs={{0,8},{4,12},{8,16},{12,20},{16,24},{20,28},{24,32},{28,36},{32,40... | collective-permute-start | bytes 786440 | tf_op jit(solution)/shard_map/ppermute | solution.py:20
  17.0 17.2 %collective-permute-start.1 = (bf16[2,256,256]{2,1,0:T(8,128)(2,1)S(1)}, bf16[2,256,256]{2,1,0:T(8,128)(2,1)S(1)}, u32[]{:S(2)}, u32[]{:S(2)}) collective-permute-start(bf16[2,256,256]{2,1,0:T(8,128)(2,1)S(1)} %bitcast.26), channel_id=1, source_target_pairs={{0,12},{4,16},{8,20},{12,24},{16,28},{20,32},{24,36},{28,40},{32,4... | collective-permute-start | bytes 786440 | tf_op jit(solution)/shard_map/ppermute | solution.py:20
  21.9 12.2 %collective-permute-start = (bf16[2,256,256]{2,1,0:T(8,128)(2,1)S(1)}, bf16[2,256,256]{2,1,0:T(8,128)(2,1)S(1)}, u32[]{:S(2)}, u32[]{:S(2)}) collective-permute-start(bf16[2,256,256]{2,1,0:T(8,128)(2,1)S(1)} %bitcast.27), channel_id=1, source_target_pairs={{0,16},{4,20},{8,24},{12,28},{16,32},{20,36},{24,40},{28,44},{32,4... | collective-permute-start | bytes 786440 | tf_op jit(solution)/shard_map/ppermute | solution.py:20
  29.1 10.3 %collective-permute-start.3 = (bf16[2,256,256]{2,1,0:T(8,128)(2,1)S(1)}, bf16[2,256,256]{2,1,0:T(8,128)(2,1)S(1)}, u32[]{:S(2)}, u32[]{:S(2)}) collective-permute-start(bf16[2,256,256]{2,1,0:T(8,128)(2,1)S(1)} %bitcast.28), channel_id=1, source_target_pairs={{0,4},{4,8},{8,12},{12,16},{16,20},{20,24},{24,28},{28,32},{32,36}... | collective-permute-start | bytes 786440 | tf_op jit(solution)/shard_map/ppermute | solution.py:20
  39.4 1.1 copy-start
  68.8 28.5 %collective-permute-start.4 = (bf16[2,256,256]{2,1,0:T(8,128)(2,1)S(1)}, bf16[2,256,256]{2,1,0:T(8,128)(2,1)S(1)}, u32[]{:S(2)}, u32[]{:S(2)}) collective-permute-start(bf16[2,256,256]{2,1,0:T(8,128)(2,1)S(1)} %get-tuple-element.8), channel_id=1, source_target_pairs={{16,0},{20,4},{24,8},{28,12},{32,16},{36,20},{40,24},{44,28},{48,3... | collective-permute-start | bytes 786440 | tf_op jit(solution)/shard_map/ppermute | solution.py:20
  70.1 27.2 %collective-permute-start.7 = (bf16[2,256,256]{2,1,0:T(8,128)(2,1)S(1)}, bf16[2,256,256]{2,1,0:T(8,128)(2,1)S(1)}, u32[]{:S(2)}, u32[]{:S(2)}) collective-permute-start(bf16[2,256,256]{2,1,0:T(8,128)(2,1)S(1)} %get-tuple-element.9), channel_id=1, source_target_pairs={{4,0},{8,4},{12,8},{16,12},{20,16},{24,20},{28,24},{32,28},{36,32}... | collective-permute-start | bytes 786440 | tf_op jit(solution)/shard_map/ppermute | solution.py:20
  72.1 25.4 %collective-permute-start.6 = (bf16[2,256,256]{2,1,0:T(8,128)(2,1)S(1)}, bf16[2,256,256]{2,1,0:T(8,128)(2,1)S(1)}, u32[]{:S(2)}, u32[]{:S(2)}) collective-permute-start(bf16[2,256,256]{2,1,0:T(8,128)(2,1)S(1)} %get-tuple-element.10), channel_id=1, source_target_pairs={{8,0},{12,4},{16,8},{20,12},{24,16},{28,20},{32,24},{36,28},{40,32... | collective-permute-start | bytes 786440 | tf_op jit(solution)/shard_map/ppermute | solution.py:20
  73.4 54.6 %collective-permute-start.5 = (bf16[2,256,256]{2,1,0:T(8,128)(2,1)S(1)}, bf16[2,256,256]{2,1,0:T(8,128)(2,1)S(1)}, u32[]{:S(2)}, u32[]{:S(2)}) collective-permute-start(bf16[2,256,256]{2,1,0:T(8,128)(2,1)S(1)} %get-tuple-element.11), channel_id=1, source_target_pairs={{12,0},{16,4},{20,8},{24,12},{28,16},{32,20},{36,24},{40,28},{44,3... | collective-permute-start | bytes 786440 | tf_op jit(solution)/shard_map/ppermute | solution.py:20

commit v16 on v14

--- a/solution.py
+++ b/solution.py
@@ -139,7 +139,7 @@
     grad_rows = upstream.reshape(tok_rows, -1)
     local_heads = extended.shape[2] // head_size
     d_query_rows, grad_t, sent_t = attention_grads(
-        bias, query_rows, grad_rows, extended, group_size, head_size, score_scale, 2, 0, local_heads,
+        bias, query_rows, grad_rows, extended, group_size, head_size, score_scale, 4, 0, local_heads,
         span_blocks * tok_rows,
     )
     d_queries = d_query_rows.reshape(queries.shape)

time: 151 us -> 149 us (0.987)
  Pallas kernels: 27.1 us -> 25.3 us
    pallas_call x1, Pallas kernels: 27.1 us -> 25.3 us  [attention_grads(): pl.pallas_call(functools.partial(attn_kernel, scale=scale, hd=hd, per_ste...]
where the time goes in v16:
time: 149 us
  waiting for transfers between devices  56.4 us (38%)
  starting transfers between devices  32.2 us (22%)
  Pallas kernels  25.3 us (17%)
  blocking collectives  24.4 us (16%)
  local copies, waits for them, and re-layouts  5.69 us (4%)
  other arithmetic  3.75 us (3%)
    ppermute x8, waiting for transfers between devices, shifted(): return lax.ppermute(value, axis, pairs)  50.4 us
    ppermute x8, starting transfers between devices, shifted(): return lax.ppermute(value, axis, pairs)  28.7 us
    pallas_call x1, Pallas kernels, attention_grads(): pl.pallas_call(functools.partial(attn_kernel, scale=scale, hd=hd, per_ste...  25.3 us
    all_gather x1, blocking collectives, body(): lax.all_gather(chunk.reshape(kinds, rows, -1).astype(jnp.bfloat16), 'sect...  12.5 us
    all_to_all x1, blocking collectives, scatter_layers(): lax.all_to_all(pieces.astype(jnp.bfloat16), ('section', 'tp'), split_axis...  11.9 us
    all_to_all x1, waiting for transfers between devices, body(): lax.all_to_all(shared_kv, 'tp', split_axis=2, concat_axis=1, tiled=True)  5.94 us
    unnamed x9, local copies, waits for them, and re-layouts  3.82 us
    all_to_all x1, starting transfers between devices, body(): lax.all_to_all(shared_kv, 'tp', split_axis=2, concat_axis=1, tiled=True)  3.41 us
  transfers between devices with their start and end apart: 9, of which 6 were waited for; matrix products, arithmetic and copies ran while one was open for 1% of the time, Pallas kernels for 0%

profile of v16, /device:TPU:80, one launch (start us, length us, event | category | flops | bytes accessed | tf_op | source)
XLA Modules:
  0.0 148.6 jit_solution(7389716670793694495)
XLA Ops:
  0.6 1.3 copy.13
  1.9 1.1 reshape.36
  3.0 3.4 %all-to-all-start = ((bf16[4,2,16384]{2,1,0:T(2,128)(2,1)}), bf16[4,2,16384]{2,1,0:T(2,128)(2,1)S(1)}, u32[]{:S(2)}, u32[]{:S(2)}) async-start(bf16[4,2,16384]{2,1,0:T(2,128)(2,1)} %reshape.36), calls=%async_computation | async-start | bytes 524288 | tf_op jit(solution)/shard_map/all_to_all | solution.py:120
  6.4 5.9 %all-to-all-done = bf16[4,2,16384]{2,1,0:T(2,128)(2,1)S(1)} async-done(((bf16[4,2,16384]{2,1,0:T(2,128)(2,1)}), bf16[4,2,16384]{2,1,0:T(2,128)(2,1)S(1)}, u32[]{:S(2)}, u32[]{:S(2)}) %all-to-all-start) | async-done | bytes 262176 | tf_op jit(solution)/shard_map/all_to_all | solution.py:120
  13.1 3.8 %collective-permute-start.2 = (bf16[2,256,256]{2,1,0:T(8,128)(2,1)S(1)}, bf16[2,256,256]{2,1,0:T(8,128)(2,1)S(1)}, u32[]{:S(2)}, u32[]{:S(2)}) collective-permute-start(bf16[2,256,256]{2,1,0:T(8,128)(2,1)S(1)} %bitcast.25), channel_id=1, source_target_pairs={{0,8},{4,12},{8,16},{12,20},{16,24},{20,28},{24,32},{28,36},{32,40... | collective-permute-start | bytes 786440 | tf_op jit(solution)/shard_map/ppermute | solution.py:20
  17.0 5.3 %collective-permute-start.1 = (bf16[2,256,256]{2,1,0:T(8,128)(2,1)S(1)}, bf16[2,256,256]{2,1,0:T(8,128)(2,1)S(1)}, u32[]{:S(2)}, u32[]{:S(2)}) collective-permute-start(bf16[2,256,256]{2,1,0:T(8,128)(2,1)S(1)} %bitcast.26), channel_id=1, source_target_pairs={{0,12},{4,16},{8,20},{12,24},{16,28},{20,32},{24,36},{28,40},{32,4... | collective-permute-start | bytes 786440 | tf_op jit(solution)/shard_map/ppermute | solution.py:20
  22.2 3.4 %collective-permute-start = (bf16[2,256,256]{2,1,0:T(8,128)(2,1)S(1)}, bf16[2,256,256]{2,1,0:T(8,128)(2,1)S(1)}, u32[]{:S(2)}, u32[]{:S(2)}) collective-permute-start(bf16[2,256,256]{2,1,0:T(8,128)(2,1)S(1)} %bitcast.27), channel_id=1, source_target_pairs={{0,16},{4,20},{8,24},{12,28},{16,32},{20,36},{24,40},{28,44},{32,4... | collective-permute-start | bytes 786440 | tf_op jit(solution)/shard_map/ppermute | solution.py:20
  25.6 1.6 %fusion.2.bias_ref = f32[256,1280]{1,0:T(8,128)} fusion(s32[256]{0:T(256)S(1)} %get-tuple-element.12, s32[256]{0:T(256)S(1)} %get-tuple-element.13, pred[1280]{0:T(1024)(128)(4,1)S(1)} %add_compare_fusion), kind=kLoop, calls=%fused_computation.4 | loop fusion | flops 1638400 | bytes 1314048 | tf_op jit(solution)/shard_map/jit(_where)/select_n | solution.py:137
  27.2 5.1 %collective-permute-start.3 = (bf16[2,256,256]{2,1,0:T(8,128)(2,1)S(1)}, bf16[2,256,256]{2,1,0:T(8,128)(2,1)S(1)}, u32[]{:S(2)}, u32[]{:S(2)}) collective-permute-start(bf16[2,256,256]{2,1,0:T(8,128)(2,1)S(1)} %bitcast.28), channel_id=1, source_target_pairs={{0,4},{4,8},{8,12},{12,16},{16,20},{20,24},{24,28},{28,32},{32,36}... | collective-permute-start | bytes 786440 | tf_op jit(solution)/shard_map/ppermute | solution.py:20
  32.3 13.4 %collective-permute-done = bf16[2,256,256]{2,1,0:T(8,128)(2,1)S(1)} collective-permute-done((bf16[2,256,256]{2,1,0:T(8,128)(2,1)S(1)}, bf16[2,256,256]{2,1,0:T(8,128)(2,1)S(1)}, u32[]{:S(2)}, u32[]{:S(2)}) %collective-permute-start) | collective-permute-done | bytes 262176 | tf_op jit(solution)/shard_map/ppermute | solution.py:20
  45.8 4.5 %collective-permute-done.3 = bf16[2,256,256]{2,1,0:T(8,128)(2,1)S(1)} collective-permute-done((bf16[2,256,256]{2,1,0:T(8,128)(2,1)S(1)}, bf16[2,256,256]{2,1,0:T(8,128)(2,1)S(1)}, u32[]{:S(2)}, u32[]{:S(2)}) %collective-permute-start.3) | collective-permute-done | bytes 262176 | tf_op jit(solution)/shard_map/ppermute | solution.py:20
  50.4 1.0 copy-done
  51.4 25.3 %shard_map.50 = (bf16[256,2048]{1,0:T(8,128)(2,1)}, f32[2,256,1280]{2,1,0:T(8,128)}, bf16[2,256,1024]{2,1,0:T(8,128)(2,1)}) custom-call(f32[256,1280]{1,0:T(8,128)} %fusion.2.bias_ref, bf16[256,2048]{1,0:T(8,128)(2,1)} %bitcast.34, bf16[256,2048]{1,0:T(8,128)(2,1)} %bitcast.35, bf16[2,1280,256]{2,1,0:T(8,128)(2,1)} %copy-done, bf16[2,1280,256]{2,1,0:T(8,128)(2,1)} %copy-done), custom_call_target="tpu_custom_call" | custom-call | flops 8053063680 | bytes 8388608 | tf_op jit(solution)/shard_map/pallas_call | solution.py:75
  76.8 1.3 fusion.6
  78.0 1.9 %collective-permute-start.4 = (bf16[2,256,256]{2,1,0:T(8,128)(2,1)S(1)}, bf16[2,256,256]{2,1,0:T(8,128)(2,1)S(1)}, u32[]{:S(2)}, u32[]{:S(2)}) collective-permute-start(bf16[2,256,256]{2,1,0:T(8,128)(2,1)S(1)} %get-tuple-element.8), channel_id=1, source_target_pairs={{16,0},{20,4},{24,8},{28,12},{32,16},{36,20},{40,24},{44,28},{48,3... | collective-permute-start | bytes 786440 | tf_op jit(solution)/shard_map/ppermute | solution.py:20
  80.0 5.4 %collective-permute-start.7 = (bf16[2,256,256]{2,1,0:T(8,128)(2,1)S(1)}, bf16[2,256,256]{2,1,0:T(8,128)(2,1)S(1)}, u32[]{:S(2)}, u32[]{:S(2)}) collective-permute-start(bf16[2,256,256]{2,1,0:T(8,128)(2,1)S(1)} %get-tuple-element.9), channel_id=1, source_target_pairs={{4,0},{8,4},{12,8},{16,12},{20,16},{24,20},{28,24},{32,28},{36,32}... | collective-permute-start | bytes 786440 | tf_op jit(solution)/shard_map/ppermute | solution.py:20
  85.4 1.9 %collective-permute-start.6 = (bf16[2,256,256]{2,1,0:T(8,128)(2,1)S(1)}, bf16[2,256,256]{2,1,0:T(8,128)(2,1)S(1)}, u32[]{:S(2)}, u32[]{:S(2)}) collective-permute-start(bf16[2,256,256]{2,1,0:T(8,128)(2,1)S(1)} %get-tuple-element.10), channel_id=1, source_target_pairs={{8,0},{12,4},{16,8},{20,12},{24,16},{28,20},{32,24},{36,28},{40,32... | collective-permute-start | bytes 786440 | tf_op jit(solution)/shard_map/ppermute | solution.py:20
  87.3 1.9 %collective-permute-start.5 = (bf16[2,256,256]{2,1,0:T(8,128)(2,1)S(1)}, bf16[2,256,256]{2,1,0:T(8,128)(2,1)S(1)}, u32[]{:S(2)}, u32[]{:S(2)}) collective-permute-start(bf16[2,256,256]{2,1,0:T(8,128)(2,1)S(1)} %get-tuple-element.11), channel_id=1, source_target_pairs={{12,0},{16,4},{20,8},{24,12},{28,16},{32,20},{36,24},{40,28},{44,3... | collective-permute-start | bytes 786440 | tf_op jit(solution)/shard_map/ppermute | solution.py:20
  89.3 7.5 %collective-permute-done.4 = bf16[2,256,256]{2,1,0:T(8,128)(2,1)S(1)} collective-permute-done((bf16[2,256,256]{2,1,0:T(8,128)(2,1)S(1)}, bf16[2,256,256]{2,1,0:T(8,128)(2,1)S(1)}, u32[]{:S(2)}, u32[]{:S(2)}) %collective-permute-start.4) | collective-permute-done | bytes 262176 | tf_op jit(solution)/shard_map/ppermute | solution.py:20
  96.7 6.5 %collective-permute-done.7 = bf16[2,256,256]{2,1,0:T(8,128)(2,1)S(1)} collective-permute-done((bf16[2,256,256]{2,1,0:T(8,128)(2,1)S(1)}, bf16[2,256,256]{2,1,0:T(8,128)(2,1)S(1)}, u32[]{:S(2)}, u32[]{:S(2)}) %collective-permute-start.7) | collective-permute-done | bytes 262176 | tf_op jit(solution)/shard_map/ppermute | solution.py:20
  103.2 18.6 %collective-permute-done.5 = bf16[2,256,256]{2,1,0:T(8,128)(2,1)S(1)} collective-permute-done((bf16[2,256,256]{2,1,0:T(8,128)(2,1)S(1)}, bf16[2,256,256]{2,1,0:T(8,128)(2,1)S(1)}, u32[]{:S(2)}, u32[]{:S(2)}) %collective-permute-start.5) | collective-permute-done | bytes 262176 | tf_op jit(solution)/shard_map/ppermute | solution.py:20
  121.8 1.2 fusion.3
  123.2 11.9 %all_to_all.23 = bf16[2,16,16,256]{3,2,0,1:T(8,128)(2,1)S(1)} all-to-all(bf16[2,16,16,256]{3,2,0,1:T(8,128)(2,1)S(1)} %copy.17), channel_id=1, replica_groups=mesh['section'=4,'seq'=16,'tp'=4] {'section','tp'}, dimensions={1} | all-to-all | bytes 524288 | tf_op jit(solution)/shard_map/all_to_all | solution.py:111
  135.2 12.5 %all_gather.3 = bf16[2,64,1024]{2,1,0:T(8,128)(2,1)S(1)} all-gather(bf16[2,16,1024]{2,1,0:T(8,128)(2,1)S(1)} %bitcast.33), channel_id=1, replica_groups=mesh['section'=4,'seq'=16,'tp'=4] {'section'}, dimensions={1}, use_global_device_ids=true | all-gather | bytes 327680 | tf_op jit(solution)/shard_map/all_gather | solution.py:153
  (21 shorter events, 2.0 us)
Async XLA Ops:
  3.0 9.4 %all-to-all-start = ((bf16[4,2,16384]{2,1,0:T(2,128)(2,1)}), bf16[4,2,16384]{2,1,0:T(2,128)(2,1)S(1)}, u32[]{:S(2)}, u32[]{:S(2)}) async-start(bf16[4,2,16384]{2,1,0:T(2,128)(2,1)} %reshape.36), calls=%async_computation | async-start | bytes 524288 | tf_op jit(solution)/shard_map/all_to_all | solution.py:120
  13.1 32.6 %collective-permute-start.2 = (bf16[2,256,256]{2,1,0:T(8,128)(2,1)S(1)}, bf16[2,256,256]{2,1,0:T(8,128)(2,1)S(1)}, u32[]{:S(2)}, u32[]{:S(2)}) collective-permute-start(bf16[2,256,256]{2,1,0:T(8,128)(2,1)S(1)} %bitcast.25), channel_id=1, source_target_pairs={{0,8},{4,12},{8,16},{12,20},{16,24},{20,28},{24,32},{28,36},{32,40... | collective-permute-start | bytes 786440 | tf_op jit(solution)/shard_map/ppermute | solution.py:20
  17.0 28.8 %collective-permute-start.1 = (bf16[2,256,256]{2,1,0:T(8,128)(2,1)S(1)}, bf16[2,256,256]{2,1,0:T(8,128)(2,1)S(1)}, u32[]{:S(2)}, u32[]{:S(2)}) collective-permute-start(bf16[2,256,256]{2,1,0:T(8,128)(2,1)S(1)} %bitcast.26), channel_id=1, source_target_pairs={{0,12},{4,16},{8,20},{12,24},{16,28},{20,32},{24,36},{28,40},{32,4... | collective-permute-start | bytes 786440 | tf_op jit(solution)/shard_map/ppermute | solution.py:20
  22.2 23.5 %collective-permute-start = (bf16[2,256,256]{2,1,0:T(8,128)(2,1)S(1)}, bf16[2,256,256]{2,1,0:T(8,128)(2,1)S(1)}, u32[]{:S(2)}, u32[]{:S(2)}) collective-permute-start(bf16[2,256,256]{2,1,0:T(8,128)(2,1)S(1)} %bitcast.27), channel_id=1, source_target_pairs={{0,16},{4,20},{8,24},{12,28},{16,32},{20,36},{24,40},{28,44},{32,4... | collective-permute-start | bytes 786440 | tf_op jit(solution)/shard_map/ppermute | solution.py:20
  27.2 23.1 %collective-permute-start.3 = (bf16[2,256,256]{2,1,0:T(8,128)(2,1)S(1)}, bf16[2,256,256]{2,1,0:T(8,128)(2,1)S(1)}, u32[]{:S(2)}, u32[]{:S(2)}) collective-permute-start(bf16[2,256,256]{2,1,0:T(8,128)(2,1)S(1)} %bitcast.28), channel_id=1, source_target_pairs={{0,4},{4,8},{8,12},{12,16},{16,20},{20,24},{24,28},{28,32},{32,36}... | collective-permute-start | bytes 786440 | tf_op jit(solution)/shard_map/ppermute | solution.py:20
  50.4 1.1 copy-start
  78.0 18.7 %collective-permute-start.4 = (bf16[2,256,256]{2,1,0:T(8,128)(2,1)S(1)}, bf16[2,256,256]{2,1,0:T(8,128)(2,1)S(1)}, u32[]{:S(2)}, u32[]{:S(2)}) collective-permute-start(bf16[2,256,256]{2,1,0:T(8,128)(2,1)S(1)} %get-tuple-element.8), channel_id=1, source_target_pairs={{16,0},{20,4},{24,8},{28,12},{32,16},{36,20},{40,24},{44,28},{48,3... | collective-permute-start | bytes 786440 | tf_op jit(solution)/shard_map/ppermute | solution.py:20
  80.0 23.3 %collective-permute-start.7 = (bf16[2,256,256]{2,1,0:T(8,128)(2,1)S(1)}, bf16[2,256,256]{2,1,0:T(8,128)(2,1)S(1)}, u32[]{:S(2)}, u32[]{:S(2)}) collective-permute-start(bf16[2,256,256]{2,1,0:T(8,128)(2,1)S(1)} %get-tuple-element.9), channel_id=1, source_target_pairs={{4,0},{8,4},{12,8},{16,12},{20,16},{24,20},{28,24},{32,28},{36,32}... | collective-permute-start | bytes 786440 | tf_op jit(solution)/shard_map/ppermute | solution.py:20
  85.4 17.8 %collective-permute-start.6 = (bf16[2,256,256]{2,1,0:T(8,128)(2,1)S(1)}, bf16[2,256,256]{2,1,0:T(8,128)(2,1)S(1)}, u32[]{:S(2)}, u32[]{:S(2)}) collective-permute-start(bf16[2,256,256]{2,1,0:T(8,128)(2,1)S(1)} %get-tuple-element.10), channel_id=1, source_target_pairs={{8,0},{12,4},{16,8},{20,12},{24,16},{28,20},{32,24},{36,28},{40,32... | collective-permute-start | bytes 786440 | tf_op jit(solution)/shard_map/ppermute | solution.py:20
  87.3 34.5 %collective-permute-start.5 = (bf16[2,256,256]{2,1,0:T(8,128)(2,1)S(1)}, bf16[2,256,256]{2,1,0:T(8,128)(2,1)S(1)}, u32[]{:S(2)}, u32[]{:S(2)}) collective-permute-start(bf16[2,256,256]{2,1,0:T(8,128)(2,1)S(1)} %get-tuple-element.11), channel_id=1, source_target_pairs={{12,0},{16,4},{20,8},{24,12},{28,16},{32,20},{36,24},{40,28},{44,3... | collective-permute-start | bytes 786440 | tf_op jit(solution)/shard_map/ppermute | solution.py:20

commit v17 on v16

--- a/solution.py
+++ b/solution.py
@@ -139,7 +139,7 @@
     grad_rows = upstream.reshape(tok_rows, -1)
     local_heads = extended.shape[2] // head_size
     d_query_rows, grad_t, sent_t = attention_grads(
-        bias, query_rows, grad_rows, extended, group_size, head_size, score_scale, 4, 0, local_heads,
+        bias, query_rows, grad_rows, extended, group_size, head_size, score_scale, group_size, 0, local_heads,
         span_blocks * tok_rows,
     )
     d_queries = d_query_rows.reshape(queries.shape)

time: 149 us -> 148 us (level)
  no operation moved by 1% of the time
where the time goes in v17:
time: 148 us
  waiting for transfers between devices  56.4 us (38%)
  starting transfers between devices  32.2 us (22%)
  Pallas kernels  24.4 us (16%)
  blocking collectives  24.4 us (16%)
  local copies, waits for them, and re-layouts  5.69 us (4%)
  other arithmetic  3.75 us (3%)
    ppermute x8, waiting for transfers between devices, shifted(): return lax.ppermute(value, axis, pairs)  50.5 us
    ppermute x8, starting transfers between devices, shifted(): return lax.ppermute(value, axis, pairs)  28.8 us
    pallas_call x1, Pallas kernels, attention_grads(): pl.pallas_call(functools.partial(attn_kernel, scale=scale, hd=hd, per_ste...  24.4 us
    all_gather x1, blocking collectives, body(): lax.all_gather(chunk.reshape(kinds, rows, -1).astype(jnp.bfloat16), 'sect...  12.5 us
    all_to_all x1, blocking collectives, scatter_layers(): lax.all_to_all(pieces.astype(jnp.bfloat16), ('section', 'tp'), split_axis...  11.8 us
    all_to_all x1, waiting for transfers between devices, body(): lax.all_to_all(shared_kv, 'tp', split_axis=2, concat_axis=1, tiled=True)  5.94 us
    unnamed x9, local copies, waits for them, and re-layouts  3.82 us
    all_to_all x1, starting transfers between devices, body(): lax.all_to_all(shared_kv, 'tp', split_axis=2, concat_axis=1, tiled=True)  3.41 us
  transfers between devices with their start and end apart: 9, of which 6 were waited for; matrix products, arithmetic and copies ran while one was open for 1% of the time, Pallas kernels for 0%

profile of v17, /device:TPU:80, one launch (start us, length us, event | category | flops | bytes accessed | tf_op | source)
XLA Modules:
  0.0 147.6 jit_solution(452984753011224596)
XLA Ops:
  0.6 1.3 copy.13
  1.9 1.1 reshape.36
  3.0 3.4 %all-to-all-start = ((bf16[4,2,16384]{2,1,0:T(2,128)(2,1)}), bf16[4,2,16384]{2,1,0:T(2,128)(2,1)S(1)}, u32[]{:S(2)}, u32[]{:S(2)}) async-start(bf16[4,2,16384]{2,1,0:T(2,128)(2,1)} %reshape.36), calls=%async_computation | async-start | bytes 524288 | tf_op jit(solution)/shard_map/all_to_all | solution.py:120
  6.4 5.9 %all-to-all-done = bf16[4,2,16384]{2,1,0:T(2,128)(2,1)S(1)} async-done(((bf16[4,2,16384]{2,1,0:T(2,128)(2,1)}), bf16[4,2,16384]{2,1,0:T(2,128)(2,1)S(1)}, u32[]{:S(2)}, u32[]{:S(2)}) %all-to-all-start) | async-done | bytes 262176 | tf_op jit(solution)/shard_map/all_to_all | solution.py:120
  13.1 3.8 %collective-permute-start.2 = (bf16[2,256,256]{2,1,0:T(8,128)(2,1)S(1)}, bf16[2,256,256]{2,1,0:T(8,128)(2,1)S(1)}, u32[]{:S(2)}, u32[]{:S(2)}) collective-permute-start(bf16[2,256,256]{2,1,0:T(8,128)(2,1)S(1)} %bitcast.25), channel_id=1, source_target_pairs={{0,8},{4,12},{8,16},{12,20},{16,24},{20,28},{24,32},{28,36},{32,40... | collective-permute-start | bytes 786440 | tf_op jit(solution)/shard_map/ppermute | solution.py:20
  17.0 5.3 %collective-permute-start.1 = (bf16[2,256,256]{2,1,0:T(8,128)(2,1)S(1)}, bf16[2,256,256]{2,1,0:T(8,128)(2,1)S(1)}, u32[]{:S(2)}, u32[]{:S(2)}) collective-permute-start(bf16[2,256,256]{2,1,0:T(8,128)(2,1)S(1)} %bitcast.26), channel_id=1, source_target_pairs={{0,12},{4,16},{8,20},{12,24},{16,28},{20,32},{24,36},{28,40},{32,4... | collective-permute-start | bytes 786440 | tf_op jit(solution)/shard_map/ppermute | solution.py:20
  22.2 3.4 %collective-permute-start = (bf16[2,256,256]{2,1,0:T(8,128)(2,1)S(1)}, bf16[2,256,256]{2,1,0:T(8,128)(2,1)S(1)}, u32[]{:S(2)}, u32[]{:S(2)}) collective-permute-start(bf16[2,256,256]{2,1,0:T(8,128)(2,1)S(1)} %bitcast.27), channel_id=1, source_target_pairs={{0,16},{4,20},{8,24},{12,28},{16,32},{20,36},{24,40},{28,44},{32,4... | collective-permute-start | bytes 786440 | tf_op jit(solution)/shard_map/ppermute | solution.py:20
  25.6 1.6 %fusion.2.bias_ref = f32[256,1280]{1,0:T(8,128)} fusion(s32[256]{0:T(256)S(1)} %get-tuple-element.12, s32[256]{0:T(256)S(1)} %get-tuple-element.13, pred[1280]{0:T(1024)(128)(4,1)S(1)} %add_compare_fusion), kind=kLoop, calls=%fused_computation.4 | loop fusion | flops 1638400 | bytes 1314048 | tf_op jit(solution)/shard_map/jit(_where)/select_n | solution.py:137
  27.2 5.1 %collective-permute-start.3 = (bf16[2,256,256]{2,1,0:T(8,128)(2,1)S(1)}, bf16[2,256,256]{2,1,0:T(8,128)(2,1)S(1)}, u32[]{:S(2)}, u32[]{:S(2)}) collective-permute-start(bf16[2,256,256]{2,1,0:T(8,128)(2,1)S(1)} %bitcast.28), channel_id=1, source_target_pairs={{0,4},{4,8},{8,12},{12,16},{16,20},{20,24},{24,28},{28,32},{32,36}... | collective-permute-start | bytes 786440 | tf_op jit(solution)/shard_map/ppermute | solution.py:20
  32.3 13.4 %collective-permute-done = bf16[2,256,256]{2,1,0:T(8,128)(2,1)S(1)} collective-permute-done((bf16[2,256,256]{2,1,0:T(8,128)(2,1)S(1)}, bf16[2,256,256]{2,1,0:T(8,128)(2,1)S(1)}, u32[]{:S(2)}, u32[]{:S(2)}) %collective-permute-start) | collective-permute-done | bytes 262176 | tf_op jit(solution)/shard_map/ppermute | solution.py:20
  45.8 4.5 %collective-permute-done.3 = bf16[2,256,256]{2,1,0:T(8,128)(2,1)S(1)} collective-permute-done((bf16[2,256,256]{2,1,0:T(8,128)(2,1)S(1)}, bf16[2,256,256]{2,1,0:T(8,128)(2,1)S(1)}, u32[]{:S(2)}, u32[]{:S(2)}) %collective-permute-start.3) | collective-permute-done | bytes 262176 | tf_op jit(solution)/shard_map/ppermute | solution.py:20
  50.4 1.0 copy-done
  51.4 24.4 %shard_map.50 = (bf16[256,2048]{1,0:T(8,128)(2,1)}, f32[2,256,1280]{2,1,0:T(8,128)}, bf16[2,256,1024]{2,1,0:T(8,128)(2,1)}) custom-call(f32[256,1280]{1,0:T(8,128)} %fusion.2.bias_ref, bf16[256,2048]{1,0:T(8,128)(2,1)} %bitcast.34, bf16[256,2048]{1,0:T(8,128)(2,1)} %bitcast.35, bf16[2,1280,256]{2,1,0:T(8,128)(2,1)} %copy-done, bf16[2,1280,256]{2,1,0:T(8,128)(2,1)} %copy-done), custom_call_target="tpu_custom_call" | custom-call | flops 8053063680 | bytes 8388608 | tf_op jit(solution)/shard_map/pallas_call | solution.py:75
  75.9 1.3 fusion.6
  77.1 1.9 %collective-permute-start.4 = (bf16[2,256,256]{2,1,0:T(8,128)(2,1)S(1)}, bf16[2,256,256]{2,1,0:T(8,128)(2,1)S(1)}, u32[]{:S(2)}, u32[]{:S(2)}) collective-permute-start(bf16[2,256,256]{2,1,0:T(8,128)(2,1)S(1)} %get-tuple-element.8), channel_id=1, source_target_pairs={{16,0},{20,4},{24,8},{28,12},{32,16},{36,20},{40,24},{44,28},{48,3... | collective-permute-start | bytes 786440 | tf_op jit(solution)/shard_map/ppermute | solution.py:20
  79.1 5.4 %collective-permute-start.7 = (bf16[2,256,256]{2,1,0:T(8,128)(2,1)S(1)}, bf16[2,256,256]{2,1,0:T(8,128)(2,1)S(1)}, u32[]{:S(2)}, u32[]{:S(2)}) collective-permute-start(bf16[2,256,256]{2,1,0:T(8,128)(2,1)S(1)} %get-tuple-element.9), channel_id=1, source_target_pairs={{4,0},{8,4},{12,8},{16,12},{20,16},{24,20},{28,24},{32,28},{36,32}... | collective-permute-start | bytes 786440 | tf_op jit(solution)/shard_map/ppermute | solution.py:20
  84.5 1.9 %collective-permute-start.6 = (bf16[2,256,256]{2,1,0:T(8,128)(2,1)S(1)}, bf16[2,256,256]{2,1,0:T(8,128)(2,1)S(1)}, u32[]{:S(2)}, u32[]{:S(2)}) collective-permute-start(bf16[2,256,256]{2,1,0:T(8,128)(2,1)S(1)} %get-tuple-element.10), channel_id=1, source_target_pairs={{8,0},{12,4},{16,8},{20,12},{24,16},{28,20},{32,24},{36,28},{40,32... | collective-permute-start | bytes 786440 | tf_op jit(solution)/shard_map/ppermute | solution.py:20
  86.4 1.9 %collective-permute-start.5 = (bf16[2,256,256]{2,1,0:T(8,128)(2,1)S(1)}, bf16[2,256,256]{2,1,0:T(8,128)(2,1)S(1)}, u32[]{:S(2)}, u32[]{:S(2)}) collective-permute-start(bf16[2,256,256]{2,1,0:T(8,128)(2,1)S(1)} %get-tuple-element.11), channel_id=1, source_target_pairs={{12,0},{16,4},{20,8},{24,12},{28,16},{32,20},{36,24},{40,28},{44,3... | collective-permute-start | bytes 786440 | tf_op jit(solution)/shard_map/ppermute | solution.py:20
  88.4 7.6 %collective-permute-done.4 = bf16[2,256,256]{2,1,0:T(8,128)(2,1)S(1)} collective-permute-done((bf16[2,256,256]{2,1,0:T(8,128)(2,1)S(1)}, bf16[2,256,256]{2,1,0:T(8,128)(2,1)S(1)}, u32[]{:S(2)}, u32[]{:S(2)}) %collective-permute-start.4) | collective-permute-done | bytes 262176 | tf_op jit(solution)/shard_map/ppermute | solution.py:20
  95.9 6.4 %collective-permute-done.7 = bf16[2,256,256]{2,1,0:T(8,128)(2,1)S(1)} collective-permute-done((bf16[2,256,256]{2,1,0:T(8,128)(2,1)S(1)}, bf16[2,256,256]{2,1,0:T(8,128)(2,1)S(1)}, u32[]{:S(2)}, u32[]{:S(2)}) %collective-permute-start.7) | collective-permute-done | bytes 262176 | tf_op jit(solution)/shard_map/ppermute | solution.py:20
  102.3 18.6 %collective-permute-done.5 = bf16[2,256,256]{2,1,0:T(8,128)(2,1)S(1)} collective-permute-done((bf16[2,256,256]{2,1,0:T(8,128)(2,1)S(1)}, bf16[2,256,256]{2,1,0:T(8,128)(2,1)S(1)}, u32[]{:S(2)}, u32[]{:S(2)}) %collective-permute-start.5) | collective-permute-done | bytes 262176 | tf_op jit(solution)/shard_map/ppermute | solution.py:20
  120.9 1.2 fusion.3
  122.3 11.8 %all_to_all.23 = bf16[2,16,16,256]{3,2,0,1:T(8,128)(2,1)S(1)} all-to-all(bf16[2,16,16,256]{3,2,0,1:T(8,128)(2,1)S(1)} %copy.17), channel_id=1, replica_groups=mesh['section'=4,'seq'=16,'tp'=4] {'section','tp'}, dimensions={1} | all-to-all | bytes 524288 | tf_op jit(solution)/shard_map/all_to_all | solution.py:111
  134.3 12.5 %all_gather.3 = bf16[2,64,1024]{2,1,0:T(8,128)(2,1)S(1)} all-gather(bf16[2,16,1024]{2,1,0:T(8,128)(2,1)S(1)} %bitcast.33), channel_id=1, replica_groups=mesh['section'=4,'seq'=16,'tp'=4] {'section'}, dimensions={1}, use_global_device_ids=true | all-gather | bytes 327680 | tf_op jit(solution)/shard_map/all_gather | solution.py:153
  (21 shorter events, 2.0 us)
Async XLA Ops:
  3.0 9.4 %all-to-all-start = ((bf16[4,2,16384]{2,1,0:T(2,128)(2,1)}), bf16[4,2,16384]{2,1,0:T(2,128)(2,1)S(1)}, u32[]{:S(2)}, u32[]{:S(2)}) async-start(bf16[4,2,16384]{2,1,0:T(2,128)(2,1)} %reshape.36), calls=%async_computation | async-start | bytes 524288 | tf_op jit(solution)/shard_map/all_to_all | solution.py:120
  13.1 32.6 %collective-permute-start.2 = (bf16[2,256,256]{2,1,0:T(8,128)(2,1)S(1)}, bf16[2,256,256]{2,1,0:T(8,128)(2,1)S(1)}, u32[]{:S(2)}, u32[]{:S(2)}) collective-permute-start(bf16[2,256,256]{2,1,0:T(8,128)(2,1)S(1)} %bitcast.25), channel_id=1, source_target_pairs={{0,8},{4,12},{8,16},{12,20},{16,24},{20,28},{24,32},{28,36},{32,40... | collective-permute-start | bytes 786440 | tf_op jit(solution)/shard_map/ppermute | solution.py:20
  17.0 28.8 %collective-permute-start.1 = (bf16[2,256,256]{2,1,0:T(8,128)(2,1)S(1)}, bf16[2,256,256]{2,1,0:T(8,128)(2,1)S(1)}, u32[]{:S(2)}, u32[]{:S(2)}) collective-permute-start(bf16[2,256,256]{2,1,0:T(8,128)(2,1)S(1)} %bitcast.26), channel_id=1, source_target_pairs={{0,12},{4,16},{8,20},{12,24},{16,28},{20,32},{24,36},{28,40},{32,4... | collective-permute-start | bytes 786440 | tf_op jit(solution)/shard_map/ppermute | solution.py:20
  22.2 23.5 %collective-permute-start = (bf16[2,256,256]{2,1,0:T(8,128)(2,1)S(1)}, bf16[2,256,256]{2,1,0:T(8,128)(2,1)S(1)}, u32[]{:S(2)}, u32[]{:S(2)}) collective-permute-start(bf16[2,256,256]{2,1,0:T(8,128)(2,1)S(1)} %bitcast.27), channel_id=1, source_target_pairs={{0,16},{4,20},{8,24},{12,28},{16,32},{20,36},{24,40},{28,44},{32,4... | collective-permute-start | bytes 786440 | tf_op jit(solution)/shard_map/ppermute | solution.py:20
  27.2 23.1 %collective-permute-start.3 = (bf16[2,256,256]{2,1,0:T(8,128)(2,1)S(1)}, bf16[2,256,256]{2,1,0:T(8,128)(2,1)S(1)}, u32[]{:S(2)}, u32[]{:S(2)}) collective-permute-start(bf16[2,256,256]{2,1,0:T(8,128)(2,1)S(1)} %bitcast.28), channel_id=1, source_target_pairs={{0,4},{4,8},{8,12},{12,16},{16,20},{20,24},{24,28},{28,32},{32,36}... | collective-permute-start | bytes 786440 | tf_op jit(solution)/shard_map/ppermute | solution.py:20
  50.4 1.1 copy-start
  77.1 18.8 %collective-permute-start.4 = (bf16[2,256,256]{2,1,0:T(8,128)(2,1)S(1)}, bf16[2,256,256]{2,1,0:T(8,128)(2,1)S(1)}, u32[]{:S(2)}, u32[]{:S(2)}) collective-permute-start(bf16[2,256,256]{2,1,0:T(8,128)(2,1)S(1)} %get-tuple-element.8), channel_id=1, source_target_pairs={{16,0},{20,4},{24,8},{28,12},{32,16},{36,20},{40,24},{44,28},{48,3... | collective-permute-start | bytes 786440 | tf_op jit(solution)/shard_map/ppermute | solution.py:20
  79.1 23.3 %collective-permute-start.7 = (bf16[2,256,256]{2,1,0:T(8,128)(2,1)S(1)}, bf16[2,256,256]{2,1,0:T(8,128)(2,1)S(1)}, u32[]{:S(2)}, u32[]{:S(2)}) collective-permute-start(bf16[2,256,256]{2,1,0:T(8,128)(2,1)S(1)} %get-tuple-element.9), channel_id=1, source_target_pairs={{4,0},{8,4},{12,8},{16,12},{20,16},{24,20},{28,24},{32,28},{36,32}... | collective-permute-start | bytes 786440 | tf_op jit(solution)/shard_map/ppermute | solution.py:20
  84.5 17.8 %collective-permute-start.6 = (bf16[2,256,256]{2,1,0:T(8,128)(2,1)S(1)}, bf16[2,256,256]{2,1,0:T(8,128)(2,1)S(1)}, u32[]{:S(2)}, u32[]{:S(2)}) collective-permute-start(bf16[2,256,256]{2,1,0:T(8,128)(2,1)S(1)} %get-tuple-element.10), channel_id=1, source_target_pairs={{8,0},{12,4},{16,8},{20,12},{24,16},{28,20},{32,24},{36,28},{40,32... | collective-permute-start | bytes 786440 | tf_op jit(solution)/shard_map/ppermute | solution.py:20
  86.4 34.5 %collective-permute-start.5 = (bf16[2,256,256]{2,1,0:T(8,128)(2,1)S(1)}, bf16[2,256,256]{2,1,0:T(8,128)(2,1)S(1)}, u32[]{:S(2)}, u32[]{:S(2)}) collective-permute-start(bf16[2,256,256]{2,1,0:T(8,128)(2,1)S(1)} %get-tuple-element.11), channel_id=1, source_target_pairs={{12,0},{16,4},{20,8},{24,12},{28,16},{32,20},{36,24},{40,28},{44,3... | collective-permute-start | bytes 786440 | tf_op jit(solution)/shard_map/ppermute | solution.py:20

commit v18 on v17

--- a/solution.py
+++ b/solution.py
@@ -21,8 +21,7 @@
 
 
 def attn_kernel(bias_ref, q_ref, g_ref, k_ref, v_ref, *rest, scale, hd, per_step, sent_cols):
-    dq_ref, dkv_ref, send_ref = rest[-3:]
-    gi = pl.program_id(1)
+    dq_ref, own_ref, send_ref = rest[-3:]
     k = k_ref[...]
     v = v_ref[...]
     bias = bias_ref[...]
@@ -50,26 +49,17 @@
         dk = dk_part if dk is None else dk + dk_part
         dv = dv_part if dv is None else dv + dv_part
 
-    @pl.when(gi == 0)
-    def _():
-        dkv_ref[0] = dk
-        dkv_ref[1] = dv
-
-    @pl.when(gi > 0)
-    def _():
-        dkv_ref[0] += dk
-        dkv_ref[1] += dv
-
-    @pl.when(gi == pl.num_programs(1) - 1)
-    def _():
-        send_ref[0] = dkv_ref[0, :, :sent_cols].astype(send_ref.dtype)
-        send_ref[1] = dkv_ref[1, :, :sent_cols].astype(send_ref.dtype)
+    own_ref[0] = dk[:, sent_cols:]
+    own_ref[1] = dv[:, sent_cols:]
+    send_ref[0] = dk[:, :sent_cols].astype(send_ref.dtype)
+    send_ref[1] = dv[:, :sent_cols].astype(send_ref.dtype)
 
 
 def attention_grads(bias, q, g, ext, group, hd, scale, per_step, head0, heads, sent_cols, after=()):
     rows, _ = q.shape
     _, ext_rows, _ = ext.shape
     steps = group // per_step
+    assert steps == 1
     width = per_step * hd
     flops = 6 * 2 * rows * ext_rows * hd * heads * group
     return pl.pallas_call(
@@ -85,12 +75,12 @@
         + [pl.BlockSpec(memory_space=pl.ANY) for _ in after],
         out_specs=[
             pl.BlockSpec((rows, width), lambda h, i: (0, h * steps + i)),
-            pl.BlockSpec((2, hd, ext_rows), lambda h, i: (0, h, 0)),
+            pl.BlockSpec((2, hd, ext_rows - sent_cols), lambda h, i: (0, h, 0)),
             pl.BlockSpec((2, hd, sent_cols), lambda h, i: (0, h, 0)),
         ],
         out_shape=[
             jax.ShapeDtypeStruct((rows, heads * group * hd), jnp.bfloat16),
-            jax.ShapeDtypeStruct((2, heads * hd, ext_rows), jnp.float32),
+            jax.ShapeDtypeStruct((2, heads * hd, ext_rows - sent_cols), jnp.float32),
             jax.ShapeDtypeStruct((2, heads * hd, sent_cols), jnp.bfloat16),
         ],
         compiler_params=pltpu.CompilerParams(dimension_semantics=("arbitrary", "arbitrary")),
@@ -143,7 +133,7 @@
         span_blocks * tok_rows,
     )
     d_queries = d_query_rows.reshape(queries.shape)
-    own_t = grad_t[:, :, span_blocks * tok_rows :]
+    own_t = grad_t
     for offset in range(span_blocks):
         piece = sent_t[:, :, offset * tok_rows : (offset + 1) * tok_rows]
         own_t = own_t + shifted(piece, "seq", offset - span_blocks).astype(jnp.float32)

time: 148 us -> 147 us (level)
    unnamed x9 -> x11, local copies, waits for them, and re-layouts: 3.82 us -> 3.84 us
where the time goes in v18:
time: 147 us; the launch traced here: 146 us
  waiting for transfers between devices  56.4 us (38%)
  starting transfers between devices  32.2 us (22%)
  blocking collectives  24.4 us (17%)
  Pallas kernels  24 us (16%)
  local copies, waits for them, and re-layouts  5.76 us (4%)
  other arithmetic  2.72 us (2%)
    ppermute x8, waiting for transfers between devices, shifted(): return lax.ppermute(value, axis, pairs)  50.4 us
    ppermute x8, starting transfers between devices, shifted(): return lax.ppermute(value, axis, pairs)  28.8 us
    pallas_call x1, Pallas kernels, attention_grads(): pl.pallas_call(functools.partial(attn_kernel, scale=scale, hd=hd, per_ste...  24 us
    all_gather x1, blocking collectives, body(): lax.all_gather(chunk.reshape(kinds, rows, -1).astype(jnp.bfloat16), 'sect...  12.5 us
    all_to_all x1, blocking collectives, scatter_layers(): lax.all_to_all(pieces.astype(jnp.bfloat16), ('section', 'tp'), split_axis...  11.9 us
    all_to_all x1, waiting for transfers between devices, body(): lax.all_to_all(shared_kv, 'tp', split_axis=2, concat_axis=1, tiled=True)  5.94 us
    unnamed x11, local copies, waits for them, and re-layouts  3.84 us
    all_to_all x1, starting transfers between devices, body(): lax.all_to_all(shared_kv, 'tp', split_axis=2, concat_axis=1, tiled=True)  3.41 us
  transfers between devices with their start and end apart: 9, of which 6 were waited for; matrix products, arithmetic and copies ran while one was open for 1% of the time, Pallas kernels for 0%

profile of v18, /device:TPU:80, one launch (start us, length us, event | category | flops | bytes accessed | tf_op | source)
XLA Modules:
  0.0 146.3 jit_solution(13304060944142382735)
XLA Ops:
  0.6 1.3 copy.13
  1.9 1.1 reshape.36
  3.0 3.4 %all-to-all-start = ((bf16[4,2,16384]{2,1,0:T(2,128)(2,1)}), bf16[4,2,16384]{2,1,0:T(2,128)(2,1)S(1)}, u32[]{:S(2)}, u32[]{:S(2)}) async-start(bf16[4,2,16384]{2,1,0:T(2,128)(2,1)} %reshape.36), calls=%async_computation | async-start | bytes 524288 | tf_op jit(solution)/shard_map/all_to_all | solution.py:110
  6.4 5.9 %all-to-all-done = bf16[4,2,16384]{2,1,0:T(2,128)(2,1)S(1)} async-done(((bf16[4,2,16384]{2,1,0:T(2,128)(2,1)}), bf16[4,2,16384]{2,1,0:T(2,128)(2,1)S(1)}, u32[]{:S(2)}, u32[]{:S(2)}) %all-to-all-start) | async-done | bytes 262176 | tf_op jit(solution)/shard_map/all_to_all | solution.py:110
  13.1 3.8 %collective-permute-start.2 = (bf16[2,256,256]{2,1,0:T(8,128)(2,1)S(1)}, bf16[2,256,256]{2,1,0:T(8,128)(2,1)S(1)}, u32[]{:S(2)}, u32[]{:S(2)}) collective-permute-start(bf16[2,256,256]{2,1,0:T(8,128)(2,1)S(1)} %bitcast.25), channel_id=1, source_target_pairs={{0,8},{4,12},{8,16},{12,20},{16,24},{20,28},{24,32},{28,36},{32,40... | collective-permute-start | bytes 786440 | tf_op jit(solution)/shard_map/ppermute | solution.py:20
  17.0 5.3 %collective-permute-start.1 = (bf16[2,256,256]{2,1,0:T(8,128)(2,1)S(1)}, bf16[2,256,256]{2,1,0:T(8,128)(2,1)S(1)}, u32[]{:S(2)}, u32[]{:S(2)}) collective-permute-start(bf16[2,256,256]{2,1,0:T(8,128)(2,1)S(1)} %bitcast.26), channel_id=1, source_target_pairs={{0,12},{4,16},{8,20},{12,24},{16,28},{20,32},{24,36},{28,40},{32,4... | collective-permute-start | bytes 786440 | tf_op jit(solution)/shard_map/ppermute | solution.py:20
  22.2 3.4 %collective-permute-start = (bf16[2,256,256]{2,1,0:T(8,128)(2,1)S(1)}, bf16[2,256,256]{2,1,0:T(8,128)(2,1)S(1)}, u32[]{:S(2)}, u32[]{:S(2)}) collective-permute-start(bf16[2,256,256]{2,1,0:T(8,128)(2,1)S(1)} %bitcast.27), channel_id=1, source_target_pairs={{0,16},{4,20},{8,24},{12,28},{16,32},{20,36},{24,40},{28,44},{32,4... | collective-permute-start | bytes 786440 | tf_op jit(solution)/shard_map/ppermute | solution.py:20
  25.6 1.6 %fusion.2.bias_ref = f32[256,1280]{1,0:T(8,128)} fusion(s32[256]{0:T(256)S(1)} %get-tuple-element.12, s32[256]{0:T(256)S(1)} %get-tuple-element.13, pred[1280]{0:T(1024)(128)(4,1)S(1)} %add_compare_fusion), kind=kLoop, calls=%fused_computation.4 | loop fusion | flops 1638400 | bytes 1314048 | tf_op jit(solution)/shard_map/jit(_where)/select_n | solution.py:127
  27.3 5.1 %collective-permute-start.3 = (bf16[2,256,256]{2,1,0:T(8,128)(2,1)S(1)}, bf16[2,256,256]{2,1,0:T(8,128)(2,1)S(1)}, u32[]{:S(2)}, u32[]{:S(2)}) collective-permute-start(bf16[2,256,256]{2,1,0:T(8,128)(2,1)S(1)} %bitcast.28), channel_id=1, source_target_pairs={{0,4},{4,8},{8,12},{12,16},{16,20},{20,24},{24,28},{28,32},{32,36}... | collective-permute-start | bytes 786440 | tf_op jit(solution)/shard_map/ppermute | solution.py:20
  32.4 13.3 %collective-permute-done = bf16[2,256,256]{2,1,0:T(8,128)(2,1)S(1)} collective-permute-done((bf16[2,256,256]{2,1,0:T(8,128)(2,1)S(1)}, bf16[2,256,256]{2,1,0:T(8,128)(2,1)S(1)}, u32[]{:S(2)}, u32[]{:S(2)}) %collective-permute-start) | collective-permute-done | bytes 262176 | tf_op jit(solution)/shard_map/ppermute | solution.py:20
  45.8 4.5 %collective-permute-done.3 = bf16[2,256,256]{2,1,0:T(8,128)(2,1)S(1)} collective-permute-done((bf16[2,256,256]{2,1,0:T(8,128)(2,1)S(1)}, bf16[2,256,256]{2,1,0:T(8,128)(2,1)S(1)}, u32[]{:S(2)}, u32[]{:S(2)}) %collective-permute-start.3) | collective-permute-done | bytes 262176 | tf_op jit(solution)/shard_map/ppermute | solution.py:20
  50.4 1.0 copy-done.1
  51.5 24.0 %shard_map.50 = (bf16[256,2048]{1,0:T(8,128)(2,1)}, f32[2,256,256]{2,1,0:T(8,128)}, bf16[2,256,1024]{2,1,0:T(8,128)(2,1)}) custom-call(f32[256,1280]{1,0:T(8,128)} %fusion.2.bias_ref, bf16[256,2048]{1,0:T(8,128)(2,1)} %bitcast.34, bf16[256,2048]{1,0:T(8,128)(2,1)} %bitcast.35, bf16[2,1280,256]{2,1,0:T(8,128)(2,1)} %copy-done.1, bf16[2,1280,256]{2,1,0:T(8,128)(2,1)} %copy-done.1), custom_call_target="tpu_custom_call" | custom-call | flops 8053063680 | bytes 8388608 | tf_op jit(solution)/shard_map/pallas_call | solution.py:65
  75.5 1.3 fusion.6
  76.8 1.9 %collective-permute-start.4 = (bf16[2,256,256]{2,1,0:T(8,128)(2,1)S(1)}, bf16[2,256,256]{2,1,0:T(8,128)(2,1)S(1)}, u32[]{:S(2)}, u32[]{:S(2)}) collective-permute-start(bf16[2,256,256]{2,1,0:T(8,128)(2,1)S(1)} %get-tuple-element.8), channel_id=1, source_target_pairs={{16,0},{20,4},{24,8},{28,12},{32,16},{36,20},{40,24},{44,28},{48,3... | collective-permute-start | bytes 786440 | tf_op jit(solution)/shard_map/ppermute | solution.py:20
  78.8 5.4 %collective-permute-start.7 = (bf16[2,256,256]{2,1,0:T(8,128)(2,1)S(1)}, bf16[2,256,256]{2,1,0:T(8,128)(2,1)S(1)}, u32[]{:S(2)}, u32[]{:S(2)}) collective-permute-start(bf16[2,256,256]{2,1,0:T(8,128)(2,1)S(1)} %get-tuple-element.9), channel_id=1, source_target_pairs={{4,0},{8,4},{12,8},{16,12},{20,16},{24,20},{28,24},{32,28},{36,32}... | collective-permute-start | bytes 786440 | tf_op jit(solution)/shard_map/ppermute | solution.py:20
  84.2 1.9 %collective-permute-start.6 = (bf16[2,256,256]{2,1,0:T(8,128)(2,1)S(1)}, bf16[2,256,256]{2,1,0:T(8,128)(2,1)S(1)}, u32[]{:S(2)}, u32[]{:S(2)}) collective-permute-start(bf16[2,256,256]{2,1,0:T(8,128)(2,1)S(1)} %get-tuple-element.10), channel_id=1, source_target_pairs={{8,0},{12,4},{16,8},{20,12},{24,16},{28,20},{32,24},{36,28},{40,32... | collective-permute-start | bytes 786440 | tf_op jit(solution)/shard_map/ppermute | solution.py:20
  86.1 1.9 %collective-permute-start.5 = (bf16[2,256,256]{2,1,0:T(8,128)(2,1)S(1)}, bf16[2,256,256]{2,1,0:T(8,128)(2,1)S(1)}, u32[]{:S(2)}, u32[]{:S(2)}) collective-permute-start(bf16[2,256,256]{2,1,0:T(8,128)(2,1)S(1)} %get-tuple-element.11), channel_id=1, source_target_pairs={{12,0},{16,4},{20,8},{24,12},{28,16},{32,20},{36,24},{40,28},{44,3... | collective-permute-start | bytes 786440 | tf_op jit(solution)/shard_map/ppermute | solution.py:20
  88.1 7.6 %collective-permute-done.4 = bf16[2,256,256]{2,1,0:T(8,128)(2,1)S(1)} collective-permute-done((bf16[2,256,256]{2,1,0:T(8,128)(2,1)S(1)}, bf16[2,256,256]{2,1,0:T(8,128)(2,1)S(1)}, u32[]{:S(2)}, u32[]{:S(2)}) %collective-permute-start.4) | collective-permute-done | bytes 262176 | tf_op jit(solution)/shard_map/ppermute | solution.py:20
  95.6 6.4 %collective-permute-done.7 = bf16[2,256,256]{2,1,0:T(8,128)(2,1)S(1)} collective-permute-done((bf16[2,256,256]{2,1,0:T(8,128)(2,1)S(1)}, bf16[2,256,256]{2,1,0:T(8,128)(2,1)S(1)}, u32[]{:S(2)}, u32[]{:S(2)}) %collective-permute-start.7) | collective-permute-done | bytes 262176 | tf_op jit(solution)/shard_map/ppermute | solution.py:20
  102.0 18.6 %collective-permute-done.5 = bf16[2,256,256]{2,1,0:T(8,128)(2,1)S(1)} collective-permute-done((bf16[2,256,256]{2,1,0:T(8,128)(2,1)S(1)}, bf16[2,256,256]{2,1,0:T(8,128)(2,1)S(1)}, u32[]{:S(2)}, u32[]{:S(2)}) %collective-permute-start.5) | collective-permute-done | bytes 262176 | tf_op jit(solution)/shard_map/ppermute | solution.py:20
  120.9 11.9 %all_to_all.23 = bf16[2,16,16,256]{3,2,0,1:T(8,128)(2,1)S(1)} all-to-all(bf16[2,16,16,256]{3,2,0,1:T(8,128)(2,1)S(1)} %copy.17), channel_id=1, replica_groups=mesh['section'=4,'seq'=16,'tp'=4] {'section','tp'}, dimensions={1} | all-to-all | bytes 524288 | tf_op jit(solution)/shard_map/all_to_all | solution.py:101
  132.9 12.5 %all_gather.3 = bf16[2,64,1024]{2,1,0:T(8,128)(2,1)S(1)} all-gather(bf16[2,16,1024]{2,1,0:T(8,128)(2,1)S(1)} %bitcast.33), channel_id=1, replica_groups=mesh['section'=4,'seq'=16,'tp'=4] {'section'}, dimensions={1}, use_global_device_ids=true | all-gather | bytes 327680 | tf_op jit(solution)/shard_map/all_gather | solution.py:143
  145.5 0.8 convert_element_type.56
  (23 shorter events, 1.3 us)
Async XLA Ops:
  3.0 9.4 %all-to-all-start = ((bf16[4,2,16384]{2,1,0:T(2,128)(2,1)}), bf16[4,2,16384]{2,1,0:T(2,128)(2,1)S(1)}, u32[]{:S(2)}, u32[]{:S(2)}) async-start(bf16[4,2,16384]{2,1,0:T(2,128)(2,1)} %reshape.36), calls=%async_computation | async-start | bytes 524288 | tf_op jit(solution)/shard_map/all_to_all | solution.py:110
  13.1 32.6 %collective-permute-start.2 = (bf16[2,256,256]{2,1,0:T(8,128)(2,1)S(1)}, bf16[2,256,256]{2,1,0:T(8,128)(2,1)S(1)}, u32[]{:S(2)}, u32[]{:S(2)}) collective-permute-start(bf16[2,256,256]{2,1,0:T(8,128)(2,1)S(1)} %bitcast.25), channel_id=1, source_target_pairs={{0,8},{4,12},{8,16},{12,20},{16,24},{20,28},{24,32},{28,36},{32,40... | collective-permute-start | bytes 786440 | tf_op jit(solution)/shard_map/ppermute | solution.py:20
  17.0 28.8 %collective-permute-start.1 = (bf16[2,256,256]{2,1,0:T(8,128)(2,1)S(1)}, bf16[2,256,256]{2,1,0:T(8,128)(2,1)S(1)}, u32[]{:S(2)}, u32[]{:S(2)}) collective-permute-start(bf16[2,256,256]{2,1,0:T(8,128)(2,1)S(1)} %bitcast.26), channel_id=1, source_target_pairs={{0,12},{4,16},{8,20},{12,24},{16,28},{20,32},{24,36},{28,40},{32,4... | collective-permute-start | bytes 786440 | tf_op jit(solution)/shard_map/ppermute | solution.py:20
  22.2 23.5 %collective-permute-start = (bf16[2,256,256]{2,1,0:T(8,128)(2,1)S(1)}, bf16[2,256,256]{2,1,0:T(8,128)(2,1)S(1)}, u32[]{:S(2)}, u32[]{:S(2)}) collective-permute-start(bf16[2,256,256]{2,1,0:T(8,128)(2,1)S(1)} %bitcast.27), channel_id=1, source_target_pairs={{0,16},{4,20},{8,24},{12,28},{16,32},{20,36},{24,40},{28,44},{32,4... | collective-permute-start | bytes 786440 | tf_op jit(solution)/shard_map/ppermute | solution.py:20
  27.3 23.1 %collective-permute-start.3 = (bf16[2,256,256]{2,1,0:T(8,128)(2,1)S(1)}, bf16[2,256,256]{2,1,0:T(8,128)(2,1)S(1)}, u32[]{:S(2)}, u32[]{:S(2)}) collective-permute-start(bf16[2,256,256]{2,1,0:T(8,128)(2,1)S(1)} %bitcast.28), channel_id=1, source_target_pairs={{0,4},{4,8},{8,12},{12,16},{16,20},{20,24},{24,28},{28,32},{32,36}... | collective-permute-start | bytes 786440 | tf_op jit(solution)/shard_map/ppermute | solution.py:20
  50.4 1.1 copy-start.1
  75.5 45.1 %copy-start = (f32[2,256,256]{2,1,0:T(8,128)S(1)}, f32[2,256,256]{2,1,0:T(8,128)}, u32[]{:S(2)}) copy-start(f32[2,256,256]{2,1,0:T(8,128)} %get-tuple-element.6) | copy-start | bytes 1572868
  76.8 18.8 %collective-permute-start.4 = (bf16[2,256,256]{2,1,0:T(8,128)(2,1)S(1)}, bf16[2,256,256]{2,1,0:T(8,128)(2,1)S(1)}, u32[]{:S(2)}, u32[]{:S(2)}) collective-permute-start(bf16[2,256,256]{2,1,0:T(8,128)(2,1)S(1)} %get-tuple-element.8), channel_id=1, source_target_pairs={{16,0},{20,4},{24,8},{28,12},{32,16},{36,20},{40,24},{44,28},{48,3... | collective-permute-start | bytes 786440 | tf_op jit(solution)/shard_map/ppermute | solution.py:20
  78.8 23.3 %collective-permute-start.7 = (bf16[2,256,256]{2,1,0:T(8,128)(2,1)S(1)}, bf16[2,256,256]{2,1,0:T(8,128)(2,1)S(1)}, u32[]{:S(2)}, u32[]{:S(2)}) collective-permute-start(bf16[2,256,256]{2,1,0:T(8,128)(2,1)S(1)} %get-tuple-element.9), channel_id=1, source_target_pairs={{4,0},{8,4},{12,8},{16,12},{20,16},{24,20},{28,24},{32,28},{36,32}... | collective-permute-start | bytes 786440 | tf_op jit(solution)/shard_map/ppermute | solution.py:20
  84.2 17.8 %collective-permute-start.6 = (bf16[2,256,256]{2,1,0:T(8,128)(2,1)S(1)}, bf16[2,256,256]{2,1,0:T(8,128)(2,1)S(1)}, u32[]{:S(2)}, u32[]{:S(2)}) collective-permute-start(bf16[2,256,256]{2,1,0:T(8,128)(2,1)S(1)} %get-tuple-element.10), channel_id=1, source_target_pairs={{8,0},{12,4},{16,8},{20,12},{24,16},{28,20},{32,24},{36,28},{40,32... | collective-permute-start | bytes 786440 | tf_op jit(solution)/shard_map/ppermute | solution.py:20
  86.1 34.5 %collective-permute-start.5 = (bf16[2,256,256]{2,1,0:T(8,128)(2,1)S(1)}, bf16[2,256,256]{2,1,0:T(8,128)(2,1)S(1)}, u32[]{:S(2)}, u32[]{:S(2)}) collective-permute-start(bf16[2,256,256]{2,1,0:T(8,128)(2,1)S(1)} %get-tuple-element.11), channel_id=1, source_target_pairs={{12,0},{16,4},{20,8},{24,12},{28,16},{32,20},{36,24},{40,28},{44,3... | collective-permute-start | bytes 786440 | tf_op jit(solution)/shard_map/ppermute | solution.py:20

commit v19 on v18

--- a/solution.py
+++ b/solution.py
@@ -51,11 +51,14 @@
 
     own_ref[0] = dk[:, sent_cols:]
     own_ref[1] = dv[:, sent_cols:]
-    send_ref[0] = dk[:, :sent_cols].astype(send_ref.dtype)
-    send_ref[1] = dv[:, :sent_cols].astype(send_ref.dtype)
+    piece = send_ref.shape[-1]
+    for offset in range(send_ref.shape[0]):
+        lanes = slice(offset * piece, (offset + 1) * piece)
+        send_ref[offset, 0] = dk[:, lanes].astype(send_ref.dtype)
+        send_ref[offset, 1] = dv[:, lanes].astype(send_ref.dtype)
 
 
-def attention_grads(bias, q, g, ext, group, hd, scale, per_step, head0, heads, sent_cols, after=()):
+def attention_grads(bias, q, g, ext, group, hd, scale, per_step, head0, heads, sent_cols, piece, after=()):
     rows, _ = q.shape
     _, ext_rows, _ = ext.shape
     steps = group // per_step
@@ -76,12 +79,12 @@
         out_specs=[
             pl.BlockSpec((rows, width), lambda h, i: (0, h * steps + i)),
             pl.BlockSpec((2, hd, ext_rows - sent_cols), lambda h, i: (0, h, 0)),
-            pl.BlockSpec((2, hd, sent_cols), lambda h, i: (0, h, 0)),
+            pl.BlockSpec((sent_cols // piece, 2, hd, piece), lambda h, i: (0, 0, h, 0)),
         ],
         out_shape=[
             jax.ShapeDtypeStruct((rows, heads * group * hd), jnp.bfloat16),
             jax.ShapeDtypeStruct((2, heads * hd, ext_rows - sent_cols), jnp.float32),
-            jax.ShapeDtypeStruct((2, heads * hd, sent_cols), jnp.bfloat16),
+            jax.ShapeDtypeStruct((sent_cols // piece, 2, heads * hd, piece), jnp.bfloat16),
         ],
         compiler_params=pltpu.CompilerParams(dimension_semantics=("arbitrary", "arbitrary")),
         cost_estimate=pl.CostEstimate(
@@ -130,12 +133,12 @@
     local_heads = extended.shape[2] // head_size
     d_query_rows, grad_t, sent_t = attention_grads(
         bias, query_rows, grad_rows, extended, group_size, head_size, score_scale, group_size, 0, local_heads,
-        span_blocks * tok_rows,
+        span_blocks * tok_rows, tok_rows,
     )
     d_queries = d_query_rows.reshape(queries.shape)
     own_t = grad_t
     for offset in range(span_blocks):
-        piece = sent_t[:, :, offset * tok_rows : (offset + 1) * tok_rows]
+        piece = sent_t[offset]
         own_t = own_t + shifted(piece, "seq", offset - span_blocks).astype(jnp.float32)
     own_rows = jnp.swapaxes(own_t, 1, 2)
     chunk = scatter_layers(own_rows)

time: 147 us -> 147 us (level)
  no operation moved by 1% of the time
where the time goes in v19:
time: 147 us; the launch traced here: 146 us
  waiting for transfers between devices  56.4 us (38%)
  starting transfers between devices  32.2 us (22%)
  blocking collectives  24.4 us (17%)
  Pallas kernels  24 us (16%)
  local copies, waits for them, and re-layouts  5.75 us (4%)
  other arithmetic  2.72 us (2%)
    ppermute x8, waiting for transfers between devices, shifted(): return lax.ppermute(value, axis, pairs)  50.4 us
    ppermute x8, starting transfers between devices, shifted(): return lax.ppermute(value, axis, pairs)  28.8 us
    pallas_call x1, Pallas kernels, attention_grads(): pl.pallas_call(functools.partial(attn_kernel, scale=scale, hd=hd, per_ste...  24 us
    all_gather x1, blocking collectives, body(): lax.all_gather(chunk.reshape(kinds, rows, -1).astype(jnp.bfloat16), 'sect...  12.5 us
    all_to_all x1, blocking collectives, scatter_layers(): lax.all_to_all(pieces.astype(jnp.bfloat16), ('section', 'tp'), split_axis...  11.9 us
    all_to_all x1, waiting for transfers between devices, body(): lax.all_to_all(shared_kv, 'tp', split_axis=2, concat_axis=1, tiled=True)  5.94 us
    unnamed x11, local copies, waits for them, and re-layouts  3.84 us
    all_to_all x1, starting transfers between devices, body(): lax.all_to_all(shared_kv, 'tp', split_axis=2, concat_axis=1, tiled=True)  3.41 us
  transfers between devices with their start and end apart: 9, of which 6 were waited for; matrix products, arithmetic and copies ran while one was open for 1% of the time, Pallas kernels for 0%

profile of v19, /device:TPU:80, one launch (start us, length us, event | category | flops | bytes accessed | tf_op | source)
XLA Modules:
  0.0 146.3 jit_solution(81889284902432204)
XLA Ops:
  0.6 1.3 copy.13
  1.9 1.1 reshape.36
  3.0 3.4 %all-to-all-start = ((bf16[4,2,16384]{2,1,0:T(2,128)(2,1)}), bf16[4,2,16384]{2,1,0:T(2,128)(2,1)S(1)}, u32[]{:S(2)}, u32[]{:S(2)}) async-start(bf16[4,2,16384]{2,1,0:T(2,128)(2,1)} %reshape.36), calls=%async_computation | async-start | bytes 524288 | tf_op jit(solution)/shard_map/all_to_all | solution.py:113
  6.4 5.9 %all-to-all-done = bf16[4,2,16384]{2,1,0:T(2,128)(2,1)S(1)} async-done(((bf16[4,2,16384]{2,1,0:T(2,128)(2,1)}), bf16[4,2,16384]{2,1,0:T(2,128)(2,1)S(1)}, u32[]{:S(2)}, u32[]{:S(2)}) %all-to-all-start) | async-done | bytes 262176 | tf_op jit(solution)/shard_map/all_to_all | solution.py:113
  13.1 3.8 %collective-permute-start.2 = (bf16[2,256,256]{2,1,0:T(8,128)(2,1)S(1)}, bf16[2,256,256]{2,1,0:T(8,128)(2,1)S(1)}, u32[]{:S(2)}, u32[]{:S(2)}) collective-permute-start(bf16[2,256,256]{2,1,0:T(8,128)(2,1)S(1)} %bitcast.33), channel_id=1, source_target_pairs={{0,8},{4,12},{8,16},{12,20},{16,24},{20,28},{24,32},{28,36},{32,40... | collective-permute-start | bytes 786440 | tf_op jit(solution)/shard_map/ppermute | solution.py:20
  17.0 5.3 %collective-permute-start.1 = (bf16[2,256,256]{2,1,0:T(8,128)(2,1)S(1)}, bf16[2,256,256]{2,1,0:T(8,128)(2,1)S(1)}, u32[]{:S(2)}, u32[]{:S(2)}) collective-permute-start(bf16[2,256,256]{2,1,0:T(8,128)(2,1)S(1)} %bitcast.34), channel_id=1, source_target_pairs={{0,12},{4,16},{8,20},{12,24},{16,28},{20,32},{24,36},{28,40},{32,4... | collective-permute-start | bytes 786440 | tf_op jit(solution)/shard_map/ppermute | solution.py:20
  22.2 3.4 %collective-permute-start = (bf16[2,256,256]{2,1,0:T(8,128)(2,1)S(1)}, bf16[2,256,256]{2,1,0:T(8,128)(2,1)S(1)}, u32[]{:S(2)}, u32[]{:S(2)}) collective-permute-start(bf16[2,256,256]{2,1,0:T(8,128)(2,1)S(1)} %bitcast.35), channel_id=1, source_target_pairs={{0,16},{4,20},{8,24},{12,28},{16,32},{20,36},{24,40},{28,44},{32,4... | collective-permute-start | bytes 786440 | tf_op jit(solution)/shard_map/ppermute | solution.py:20
  25.6 1.6 %fusion.2.bias_ref = f32[256,1280]{1,0:T(8,128)} fusion(s32[256]{0:T(256)S(1)} %get-tuple-element.12, s32[256]{0:T(256)S(1)} %get-tuple-element.13, pred[1280]{0:T(1024)(128)(4,1)S(1)} %add_compare_fusion), kind=kLoop, calls=%fused_computation.4 | loop fusion | flops 1638400 | bytes 1314048 | tf_op jit(solution)/shard_map/jit(_where)/select_n | solution.py:130
  27.3 5.1 %collective-permute-start.3 = (bf16[2,256,256]{2,1,0:T(8,128)(2,1)S(1)}, bf16[2,256,256]{2,1,0:T(8,128)(2,1)S(1)}, u32[]{:S(2)}, u32[]{:S(2)}) collective-permute-start(bf16[2,256,256]{2,1,0:T(8,128)(2,1)S(1)} %bitcast.36), channel_id=1, source_target_pairs={{0,4},{4,8},{8,12},{12,16},{16,20},{20,24},{24,28},{28,32},{32,36}... | collective-permute-start | bytes 786440 | tf_op jit(solution)/shard_map/ppermute | solution.py:20
  32.4 13.3 %collective-permute-done = bf16[2,256,256]{2,1,0:T(8,128)(2,1)S(1)} collective-permute-done((bf16[2,256,256]{2,1,0:T(8,128)(2,1)S(1)}, bf16[2,256,256]{2,1,0:T(8,128)(2,1)S(1)}, u32[]{:S(2)}, u32[]{:S(2)}) %collective-permute-start) | collective-permute-done | bytes 262176 | tf_op jit(solution)/shard_map/ppermute | solution.py:20
  45.8 4.5 %collective-permute-done.3 = bf16[2,256,256]{2,1,0:T(8,128)(2,1)S(1)} collective-permute-done((bf16[2,256,256]{2,1,0:T(8,128)(2,1)S(1)}, bf16[2,256,256]{2,1,0:T(8,128)(2,1)S(1)}, u32[]{:S(2)}, u32[]{:S(2)}) %collective-permute-start.3) | collective-permute-done | bytes 262176 | tf_op jit(solution)/shard_map/ppermute | solution.py:20
  50.4 1.0 copy-done.1
  51.5 24.0 %shard_map.50 = (bf16[256,2048]{1,0:T(8,128)(2,1)}, f32[2,256,256]{2,1,0:T(8,128)}, bf16[4,2,256,256]{3,2,1,0:T(8,128)(2,1)}) custom-call(f32[256,1280]{1,0:T(8,128)} %fusion.2.bias_ref, bf16[256,2048]{1,0:T(8,128)(2,1)} %bitcast.42, bf16[256,2048]{1,0:T(8,128)(2,1)} %bitcast.43, bf16[2,1280,256]{2,1,0:T(8,128)(2,1)} %copy-done.1, ...), custom_call_target="tpu_custom_call" | custom-call | flops 8053063680 | bytes 8388608 | tf_op jit(solution)/shard_map/pallas_call | solution.py:68
  75.5 1.3 slice_bitcast_fusion.3
  76.8 1.9 %collective-permute-start.4 = (bf16[2,256,256]{2,1,0:T(8,128)(2,1)S(1)}, bf16[2,256,256]{2,1,0:T(8,128)(2,1)S(1)}, u32[]{:S(2)}, u32[]{:S(2)}) collective-permute-start(bf16[2,256,256]{2,1,0:T(8,128)(2,1)S(1)} %get-tuple-element.8), channel_id=1, source_target_pairs={{16,0},{20,4},{24,8},{28,12},{32,16},{36,20},{40,24},{44,28},{48,3... | collective-permute-start | bytes 786440 | tf_op jit(solution)/shard_map/ppermute | solution.py:20
  78.7 5.4 %collective-permute-start.7 = (bf16[2,256,256]{2,1,0:T(8,128)(2,1)S(1)}, bf16[2,256,256]{2,1,0:T(8,128)(2,1)S(1)}, u32[]{:S(2)}, u32[]{:S(2)}) collective-permute-start(bf16[2,256,256]{2,1,0:T(8,128)(2,1)S(1)} %get-tuple-element.9), channel_id=1, source_target_pairs={{4,0},{8,4},{12,8},{16,12},{20,16},{24,20},{28,24},{32,28},{36,32}... | collective-permute-start | bytes 786440 | tf_op jit(solution)/shard_map/ppermute | solution.py:20
  84.2 1.9 %collective-permute-start.6 = (bf16[2,256,256]{2,1,0:T(8,128)(2,1)S(1)}, bf16[2,256,256]{2,1,0:T(8,128)(2,1)S(1)}, u32[]{:S(2)}, u32[]{:S(2)}) collective-permute-start(bf16[2,256,256]{2,1,0:T(8,128)(2,1)S(1)} %get-tuple-element.10), channel_id=1, source_target_pairs={{8,0},{12,4},{16,8},{20,12},{24,16},{28,20},{32,24},{36,28},{40,32... | collective-permute-start | bytes 786440 | tf_op jit(solution)/shard_map/ppermute | solution.py:20
  86.1 1.9 %collective-permute-start.5 = (bf16[2,256,256]{2,1,0:T(8,128)(2,1)S(1)}, bf16[2,256,256]{2,1,0:T(8,128)(2,1)S(1)}, u32[]{:S(2)}, u32[]{:S(2)}) collective-permute-start(bf16[2,256,256]{2,1,0:T(8,128)(2,1)S(1)} %get-tuple-element.11), channel_id=1, source_target_pairs={{12,0},{16,4},{20,8},{24,12},{28,16},{32,20},{36,24},{40,28},{44,3... | collective-permute-start | bytes 786440 | tf_op jit(solution)/shard_map/ppermute | solution.py:20
  88.0 7.6 %collective-permute-done.4 = bf16[2,256,256]{2,1,0:T(8,128)(2,1)S(1)} collective-permute-done((bf16[2,256,256]{2,1,0:T(8,128)(2,1)S(1)}, bf16[2,256,256]{2,1,0:T(8,128)(2,1)S(1)}, u32[]{:S(2)}, u32[]{:S(2)}) %collective-permute-start.4) | collective-permute-done | bytes 262176 | tf_op jit(solution)/shard_map/ppermute | solution.py:20
  95.6 6.4 %collective-permute-done.7 = bf16[2,256,256]{2,1,0:T(8,128)(2,1)S(1)} collective-permute-done((bf16[2,256,256]{2,1,0:T(8,128)(2,1)S(1)}, bf16[2,256,256]{2,1,0:T(8,128)(2,1)S(1)}, u32[]{:S(2)}, u32[]{:S(2)}) %collective-permute-start.7) | collective-permute-done | bytes 262176 | tf_op jit(solution)/shard_map/ppermute | solution.py:20
  102.0 18.6 %collective-permute-done.5 = bf16[2,256,256]{2,1,0:T(8,128)(2,1)S(1)} collective-permute-done((bf16[2,256,256]{2,1,0:T(8,128)(2,1)S(1)}, bf16[2,256,256]{2,1,0:T(8,128)(2,1)S(1)}, u32[]{:S(2)}, u32[]{:S(2)}) %collective-permute-start.5) | collective-permute-done | bytes 262176 | tf_op jit(solution)/shard_map/ppermute | solution.py:20
  120.9 11.9 %all_to_all.23 = bf16[2,16,16,256]{3,2,0,1:T(8,128)(2,1)S(1)} all-to-all(bf16[2,16,16,256]{3,2,0,1:T(8,128)(2,1)S(1)} %copy.17), channel_id=1, replica_groups=mesh['section'=4,'seq'=16,'tp'=4] {'section','tp'}, dimensions={1} | all-to-all | bytes 524288 | tf_op jit(solution)/shard_map/all_to_all | solution.py:104
  132.9 12.5 %all_gather.3 = bf16[2,64,1024]{2,1,0:T(8,128)(2,1)S(1)} all-gather(bf16[2,16,1024]{2,1,0:T(8,128)(2,1)S(1)} %bitcast.41), channel_id=1, replica_groups=mesh['section'=4,'seq'=16,'tp'=4] {'section'}, dimensions={1}, use_global_device_ids=true | all-gather | bytes 327680 | tf_op jit(solution)/shard_map/all_gather | solution.py:146
  145.4 0.8 convert_element_type.56
  (23 shorter events, 1.3 us)
Async XLA Ops:
  3.0 9.4 %all-to-all-start = ((bf16[4,2,16384]{2,1,0:T(2,128)(2,1)}), bf16[4,2,16384]{2,1,0:T(2,128)(2,1)S(1)}, u32[]{:S(2)}, u32[]{:S(2)}) async-start(bf16[4,2,16384]{2,1,0:T(2,128)(2,1)} %reshape.36), calls=%async_computation | async-start | bytes 524288 | tf_op jit(solution)/shard_map/all_to_all | solution.py:113
  13.1 32.6 %collective-permute-start.2 = (bf16[2,256,256]{2,1,0:T(8,128)(2,1)S(1)}, bf16[2,256,256]{2,1,0:T(8,128)(2,1)S(1)}, u32[]{:S(2)}, u32[]{:S(2)}) collective-permute-start(bf16[2,256,256]{2,1,0:T(8,128)(2,1)S(1)} %bitcast.33), channel_id=1, source_target_pairs={{0,8},{4,12},{8,16},{12,20},{16,24},{20,28},{24,32},{28,36},{32,40... | collective-permute-start | bytes 786440 | tf_op jit(solution)/shard_map/ppermute | solution.py:20
  17.0 28.8 %collective-permute-start.1 = (bf16[2,256,256]{2,1,0:T(8,128)(2,1)S(1)}, bf16[2,256,256]{2,1,0:T(8,128)(2,1)S(1)}, u32[]{:S(2)}, u32[]{:S(2)}) collective-permute-start(bf16[2,256,256]{2,1,0:T(8,128)(2,1)S(1)} %bitcast.34), channel_id=1, source_target_pairs={{0,12},{4,16},{8,20},{12,24},{16,28},{20,32},{24,36},{28,40},{32,4... | collective-permute-start | bytes 786440 | tf_op jit(solution)/shard_map/ppermute | solution.py:20
  22.2 23.5 %collective-permute-start = (bf16[2,256,256]{2,1,0:T(8,128)(2,1)S(1)}, bf16[2,256,256]{2,1,0:T(8,128)(2,1)S(1)}, u32[]{:S(2)}, u32[]{:S(2)}) collective-permute-start(bf16[2,256,256]{2,1,0:T(8,128)(2,1)S(1)} %bitcast.35), channel_id=1, source_target_pairs={{0,16},{4,20},{8,24},{12,28},{16,32},{20,36},{24,40},{28,44},{32,4... | collective-permute-start | bytes 786440 | tf_op jit(solution)/shard_map/ppermute | solution.py:20
  27.3 23.1 %collective-permute-start.3 = (bf16[2,256,256]{2,1,0:T(8,128)(2,1)S(1)}, bf16[2,256,256]{2,1,0:T(8,128)(2,1)S(1)}, u32[]{:S(2)}, u32[]{:S(2)}) collective-permute-start(bf16[2,256,256]{2,1,0:T(8,128)(2,1)S(1)} %bitcast.36), channel_id=1, source_target_pairs={{0,4},{4,8},{8,12},{12,16},{16,20},{20,24},{24,28},{28,32},{32,36}... | collective-permute-start | bytes 786440 | tf_op jit(solution)/shard_map/ppermute | solution.py:20
  50.4 1.1 copy-start.1
  75.5 45.1 %copy-start = (f32[2,256,256]{2,1,0:T(8,128)S(1)}, f32[2,256,256]{2,1,0:T(8,128)}, u32[]{:S(2)}) copy-start(f32[2,256,256]{2,1,0:T(8,128)} %get-tuple-element.6) | copy-start | bytes 1572868
  76.8 18.8 %collective-permute-start.4 = (bf16[2,256,256]{2,1,0:T(8,128)(2,1)S(1)}, bf16[2,256,256]{2,1,0:T(8,128)(2,1)S(1)}, u32[]{:S(2)}, u32[]{:S(2)}) collective-permute-start(bf16[2,256,256]{2,1,0:T(8,128)(2,1)S(1)} %get-tuple-element.8), channel_id=1, source_target_pairs={{16,0},{20,4},{24,8},{28,12},{32,16},{36,20},{40,24},{44,28},{48,3... | collective-permute-start | bytes 786440 | tf_op jit(solution)/shard_map/ppermute | solution.py:20
  78.7 23.3 %collective-permute-start.7 = (bf16[2,256,256]{2,1,0:T(8,128)(2,1)S(1)}, bf16[2,256,256]{2,1,0:T(8,128)(2,1)S(1)}, u32[]{:S(2)}, u32[]{:S(2)}) collective-permute-start(bf16[2,256,256]{2,1,0:T(8,128)(2,1)S(1)} %get-tuple-element.9), channel_id=1, source_target_pairs={{4,0},{8,4},{12,8},{16,12},{20,16},{24,20},{28,24},{32,28},{36,32}... | collective-permute-start | bytes 786440 | tf_op jit(solution)/shard_map/ppermute | solution.py:20
  84.2 17.8 %collective-permute-start.6 = (bf16[2,256,256]{2,1,0:T(8,128)(2,1)S(1)}, bf16[2,256,256]{2,1,0:T(8,128)(2,1)S(1)}, u32[]{:S(2)}, u32[]{:S(2)}) collective-permute-start(bf16[2,256,256]{2,1,0:T(8,128)(2,1)S(1)} %get-tuple-element.10), channel_id=1, source_target_pairs={{8,0},{12,4},{16,8},{20,12},{24,16},{28,20},{32,24},{36,28},{40,32... | collective-permute-start | bytes 786440 | tf_op jit(solution)/shard_map/ppermute | solution.py:20
  86.1 34.5 %collective-permute-start.5 = (bf16[2,256,256]{2,1,0:T(8,128)(2,1)S(1)}, bf16[2,256,256]{2,1,0:T(8,128)(2,1)S(1)}, u32[]{:S(2)}, u32[]{:S(2)}) collective-permute-start(bf16[2,256,256]{2,1,0:T(8,128)(2,1)S(1)} %get-tuple-element.11), channel_id=1, source_target_pairs={{12,0},{16,4},{20,8},{24,12},{28,16},{32,20},{36,24},{40,28},{44,3... | collective-permute-start | bytes 786440 | tf_op jit(solution)/shard_map/ppermute | solution.py:20

commit v20 on v18

--- a/solution.py
+++ b/solution.py
@@ -20,11 +20,18 @@
     return lax.ppermute(value, axis, pairs)
 
 
-def attn_kernel(bias_ref, q_ref, g_ref, k_ref, v_ref, *rest, scale, hd, per_step, sent_cols):
+def attn_kernel(bias_ref, q_ref, g_ref, k_ref, v_ref, *rest, scale, hd, per_step, sent_cols, window):
     dq_ref, own_ref, send_ref = rest[-3:]
     k = k_ref[...]
     v = v_ref[...]
-    bias = bias_ref[...]
+    lines = lax.broadcasted_iota(jnp.int32, (q_ref.shape[0], k_ref.shape[0]), 0)
+    keys = lax.broadcasted_iota(jnp.int32, (q_ref.shape[0], k_ref.shape[0]), 1)
+    allowed = (
+        (keys >= lines + 1)
+        & (keys <= lines + window)
+        & (bias_ref[0] * q_ref.shape[0] - window + keys >= 0)
+    )
+    bias = jnp.where(allowed, 0.0, -jnp.inf).astype(jnp.float32)
     nt = (((1,), (1,)), ((), ()))
     tn = (((0,), (0,)), ((), ()))
     dk = None
@@ -63,10 +70,10 @@
     width = per_step * hd
     flops = 6 * 2 * rows * ext_rows * hd * heads * group
     return pl.pallas_call(
-        functools.partial(attn_kernel, scale=scale, hd=hd, per_step=per_step, sent_cols=sent_cols),
+        functools.partial(attn_kernel, scale=scale, hd=hd, per_step=per_step, sent_cols=sent_cols, window=WINDOW),
         grid=(heads, steps),
         in_specs=[
-            pl.BlockSpec((rows, ext_rows), lambda h, i: (0, 0)),
+            pl.BlockSpec(memory_space=pltpu.SMEM),
             pl.BlockSpec((rows, width), lambda h, i: (0, (head0 + h) * steps + i)),
             pl.BlockSpec((rows, width), lambda h, i: (0, (head0 + h) * steps + i)),
             pl.BlockSpec((None, ext_rows, hd), lambda h, i: (0, 0, head0 + h)),
@@ -87,7 +94,7 @@
         cost_estimate=pl.CostEstimate(
             flops=flops,
             transcendentals=rows * ext_rows * heads * group,
-            bytes_accessed=(3 * rows * group * 2 + ext_rows * 2 * 6) * hd * heads + bias.size * 4,
+            bytes_accessed=(3 * rows * group * 2 + ext_rows * 2 * 6) * hd * heads,
         ),
     )(bias, q, g, ext, ext, *after)
 
@@ -124,7 +131,7 @@
         & (key_ids <= row_ids + WINDOW)
         & (position * tok_rows - WINDOW + key_ids >= 0)
     )
-    bias = jnp.where(allowed, 0.0, -jnp.inf).astype(jnp.float32)
+    bias = jnp.reshape(position, (1,)).astype(jnp.int32)
     query_rows = queries.reshape(tok_rows, -1)
     grad_rows = upstream.reshape(tok_rows, -1)
     local_heads = extended.shape[2] // head_size

time: 147 us -> 146 us (level)
  blocking collectives: 24.4 us -> 33 us
  starting transfers between devices: 32.2 us -> 27.2 us
  other arithmetic: 2.72 us -> 1.08 us
  waiting for transfers between devices: 56.4 us -> 54.8 us
    all_to_all x0 -> x1, blocking collectives: none -> 8.39 us  [body(): lax.all_to_all(shared_kv, 'tp', split_axis=2, concat_axis=1, tiled=True)]
    all_to_all x1 -> x0, waiting for transfers between devices: 5.94 us -> none  [body(): lax.all_to_all(shared_kv, 'tp', split_axis=2, concat_axis=1, tiled=True)]
    ppermute x8, waiting for transfers between devices: 50.4 us -> 54.8 us  [shifted(): return lax.ppermute(value, axis, pairs)]
    all_to_all x1 -> x0, starting transfers between devices: 3.41 us -> none  [body(): lax.all_to_all(shared_kv, 'tp', split_axis=2, concat_axis=1, tiled=True)]
    select_n x1 -> x0, other arithmetic: 1.63 us -> none  [body(): bias = jnp.where(allowed, 0.0, -jnp.inf).astype(jnp.float32)]
    ppermute x8, starting transfers between devices: 28.8 us -> 27.2 us  [shifted(): return lax.ppermute(value, axis, pairs)]
  transfers between devices with their start and end apart: 9 -> 8, of which waited for: 6 -> 6; matrix products, arithmetic and copies ran while one was open for 1% -> 0% of each run, Pallas kernels for 0% -> 0%
where the time goes in v20:
time: 146 us; the launch traced here: 145 us
  waiting for transfers between devices  54.8 us (38%)
  blocking collectives  33 us (23%)
  starting transfers between devices  27.2 us (19%)
  Pallas kernels  23.2 us (16%)
  local copies, waits for them, and re-layouts  5.09 us (3%)
    ppermute x8, waiting for transfers between devices, shifted(): return lax.ppermute(value, axis, pairs)  54.8 us
    ppermute x8, starting transfers between devices, shifted(): return lax.ppermute(value, axis, pairs)  27.2 us
    pallas_call x1, Pallas kernels, attention_grads(): pl.pallas_call(functools.partial(attn_kernel, scale=scale, hd=hd, per_ste...  23.2 us
    all_gather x1, blocking collectives, body(): lax.all_gather(chunk.reshape(kinds, rows, -1).astype(jnp.bfloat16), 'sect...  12.5 us
    all_to_all x1, blocking collectives, scatter_layers(): lax.all_to_all(pieces.astype(jnp.bfloat16), ('section', 'tp'), split_axis...  12.1 us
    all_to_all x1, blocking collectives, body(): lax.all_to_all(shared_kv, 'tp', split_axis=2, concat_axis=1, tiled=True)  8.39 us
    unnamed x11, local copies, waits for them, and re-layouts  3.16 us
  transfers between devices with their start and end apart: 8, of which 6 were waited for; matrix products, arithmetic and copies ran while one was open for 0% of the time, Pallas kernels for 0%

profile of v20, /device:TPU:80, one launch (start us, length us, event | category | flops | bytes accessed | tf_op | source)
XLA Modules:
  0.0 145.2 jit_solution(13960461819324460356)
XLA Ops:
  0.6 1.3 copy.13
  1.9 0.4 reshape.40
  2.3 8.4 %all_to_all.23 = bf16[4,2,16384]{2,1,0:T(2,128)(2,1)S(1)} all-to-all(bf16[4,2,16384]{2,1,0:T(2,128)(2,1)S(1)} %reshape.40), channel_id=1, replica_groups=mesh['section'=4,'seq'=16,'tp'=4] {'tp'}, dimensions={0} | all-to-all | bytes 524288 | tf_op jit(solution)/shard_map/all_to_all | solution.py:117
  11.0 0.4 copy.14
  11.4 6.4 %collective-permute-start = (bf16[2,256,256]{2,1,0:T(8,128)(2,1)S(1)}, bf16[2,256,256]{2,1,0:T(8,128)(2,1)S(1)}, u32[]{:S(2)}, u32[]{:S(2)}) collective-permute-start(bf16[2,256,256]{2,1,0:T(8,128)(2,1)S(1)} %bitcast.26), channel_id=1, source_target_pairs={{0,16},{4,20},{8,24},{12,28},{16,32},{20,36},{24,40},{28,44},{32,4... | collective-permute-start | bytes 786440 | tf_op jit(solution)/shard_map/ppermute | solution.py:20
  17.8 3.4 %collective-permute-start.1 = (bf16[2,256,256]{2,1,0:T(8,128)(2,1)S(1)}, bf16[2,256,256]{2,1,0:T(8,128)(2,1)S(1)}, u32[]{:S(2)}, u32[]{:S(2)}) collective-permute-start(bf16[2,256,256]{2,1,0:T(8,128)(2,1)S(1)} %bitcast.27), channel_id=1, source_target_pairs={{0,12},{4,16},{8,20},{12,24},{16,28},{20,32},{24,36},{28,40},{32,4... | collective-permute-start | bytes 786440 | tf_op jit(solution)/shard_map/ppermute | solution.py:20
  21.3 2.9 %collective-permute-start.2 = (bf16[2,256,256]{2,1,0:T(8,128)(2,1)S(1)}, bf16[2,256,256]{2,1,0:T(8,128)(2,1)S(1)}, u32[]{:S(2)}, u32[]{:S(2)}) collective-permute-start(bf16[2,256,256]{2,1,0:T(8,128)(2,1)S(1)} %bitcast.28), channel_id=1, source_target_pairs={{0,8},{4,12},{8,16},{12,20},{16,24},{20,28},{24,32},{28,36},{32,40... | collective-permute-start | bytes 786440 | tf_op jit(solution)/shard_map/ppermute | solution.py:20
  24.2 4.8 %collective-permute-start.3 = (bf16[2,256,256]{2,1,0:T(8,128)(2,1)S(1)}, bf16[2,256,256]{2,1,0:T(8,128)(2,1)S(1)}, u32[]{:S(2)}, u32[]{:S(2)}) collective-permute-start(bf16[2,256,256]{2,1,0:T(8,128)(2,1)S(1)} %bitcast.29), channel_id=1, source_target_pairs={{0,4},{4,8},{8,12},{12,16},{16,20},{20,24},{24,28},{28,32},{32,36}... | collective-permute-start | bytes 786440 | tf_op jit(solution)/shard_map/ppermute | solution.py:20
  29.1 12.2 %collective-permute-done.1 = bf16[2,256,256]{2,1,0:T(8,128)(2,1)S(1)} collective-permute-done((bf16[2,256,256]{2,1,0:T(8,128)(2,1)S(1)}, bf16[2,256,256]{2,1,0:T(8,128)(2,1)S(1)}, u32[]{:S(2)}, u32[]{:S(2)}) %collective-permute-start.1) | collective-permute-done | bytes 262176 | tf_op jit(solution)/shard_map/ppermute | solution.py:20
  41.3 5.6 %collective-permute-done.2 = bf16[2,256,256]{2,1,0:T(8,128)(2,1)S(1)} collective-permute-done((bf16[2,256,256]{2,1,0:T(8,128)(2,1)S(1)}, bf16[2,256,256]{2,1,0:T(8,128)(2,1)S(1)}, u32[]{:S(2)}, u32[]{:S(2)}) %collective-permute-start.2) | collective-permute-done | bytes 262176 | tf_op jit(solution)/shard_map/ppermute | solution.py:20
  46.9 4.1 %collective-permute-done.3 = bf16[2,256,256]{2,1,0:T(8,128)(2,1)S(1)} collective-permute-done((bf16[2,256,256]{2,1,0:T(8,128)(2,1)S(1)}, bf16[2,256,256]{2,1,0:T(8,128)(2,1)S(1)}, u32[]{:S(2)}, u32[]{:S(2)}) %collective-permute-start.3) | collective-permute-done | bytes 262176 | tf_op jit(solution)/shard_map/ppermute | solution.py:20
  51.1 1.1 copy-done.1
  52.2 23.2 %shard_map.50 = (bf16[256,2048]{1,0:T(8,128)(2,1)}, f32[2,256,256]{2,1,0:T(8,128)}, bf16[2,256,1024]{2,1,0:T(8,128)(2,1)}) custom-call(s32[1]{0:T(128)} %bitcast.bias_ref, bf16[256,2048]{1,0:T(8,128)(2,1)} %bitcast.35, bf16[256,2048]{1,0:T(8,128)(2,1)} %bitcast.36, bf16[2,1280,256]{2,1,0:T(8,128)(2,1)} %copy-done.1, bf16[2,1280,256]{2,1,0:T(8,128)(2,1)} %copy-done.1), custom_call_target="tpu_custom_call" | custom-call | flops 8053063680 | bytes 7077888 | tf_op jit(solution)/shard_map/pallas_call | solution.py:72
  75.4 1.3 fusion.3
  76.7 1.9 %collective-permute-start.4 = (bf16[2,256,256]{2,1,0:T(8,128)(2,1)S(1)}, bf16[2,256,256]{2,1,0:T(8,128)(2,1)S(1)}, u32[]{:S(2)}, u32[]{:S(2)}) collective-permute-start(bf16[2,256,256]{2,1,0:T(8,128)(2,1)S(1)} %get-tuple-element.8), channel_id=1, source_target_pairs={{16,0},{20,4},{24,8},{28,12},{32,16},{36,20},{40,24},{44,28},{48,3... | collective-permute-start | bytes 786440 | tf_op jit(solution)/shard_map/ppermute | solution.py:20
  78.7 3.9 %collective-permute-start.7 = (bf16[2,256,256]{2,1,0:T(8,128)(2,1)S(1)}, bf16[2,256,256]{2,1,0:T(8,128)(2,1)S(1)}, u32[]{:S(2)}, u32[]{:S(2)}) collective-permute-start(bf16[2,256,256]{2,1,0:T(8,128)(2,1)S(1)} %get-tuple-element.9), channel_id=1, source_target_pairs={{4,0},{8,4},{12,8},{16,12},{20,16},{24,20},{28,24},{32,28},{36,32}... | collective-permute-start | bytes 786440 | tf_op jit(solution)/shard_map/ppermute | solution.py:20
  82.5 1.9 %collective-permute-start.6 = (bf16[2,256,256]{2,1,0:T(8,128)(2,1)S(1)}, bf16[2,256,256]{2,1,0:T(8,128)(2,1)S(1)}, u32[]{:S(2)}, u32[]{:S(2)}) collective-permute-start(bf16[2,256,256]{2,1,0:T(8,128)(2,1)S(1)} %get-tuple-element.10), channel_id=1, source_target_pairs={{8,0},{12,4},{16,8},{20,12},{24,16},{28,20},{32,24},{36,28},{40,32... | collective-permute-start | bytes 786440 | tf_op jit(solution)/shard_map/ppermute | solution.py:20
  84.4 1.9 %collective-permute-start.5 = (bf16[2,256,256]{2,1,0:T(8,128)(2,1)S(1)}, bf16[2,256,256]{2,1,0:T(8,128)(2,1)S(1)}, u32[]{:S(2)}, u32[]{:S(2)}) collective-permute-start(bf16[2,256,256]{2,1,0:T(8,128)(2,1)S(1)} %get-tuple-element.11), channel_id=1, source_target_pairs={{12,0},{16,4},{20,8},{24,12},{28,16},{32,20},{36,24},{40,28},{44,3... | collective-permute-start | bytes 786440 | tf_op jit(solution)/shard_map/ppermute | solution.py:20
  86.4 8.4 %collective-permute-done.4 = bf16[2,256,256]{2,1,0:T(8,128)(2,1)S(1)} collective-permute-done((bf16[2,256,256]{2,1,0:T(8,128)(2,1)S(1)}, bf16[2,256,256]{2,1,0:T(8,128)(2,1)S(1)}, u32[]{:S(2)}, u32[]{:S(2)}) %collective-permute-start.4) | collective-permute-done | bytes 262176 | tf_op jit(solution)/shard_map/ppermute | solution.py:20
  94.8 7.1 %collective-permute-done.7 = bf16[2,256,256]{2,1,0:T(8,128)(2,1)S(1)} collective-permute-done((bf16[2,256,256]{2,1,0:T(8,128)(2,1)S(1)}, bf16[2,256,256]{2,1,0:T(8,128)(2,1)S(1)}, u32[]{:S(2)}, u32[]{:S(2)}) %collective-permute-start.7) | collective-permute-done | bytes 262176 | tf_op jit(solution)/shard_map/ppermute | solution.py:20
  101.9 17.3 %collective-permute-done.5 = bf16[2,256,256]{2,1,0:T(8,128)(2,1)S(1)} collective-permute-done((bf16[2,256,256]{2,1,0:T(8,128)(2,1)S(1)}, bf16[2,256,256]{2,1,0:T(8,128)(2,1)S(1)}, u32[]{:S(2)}, u32[]{:S(2)}) %collective-permute-start.5) | collective-permute-done | bytes 262176 | tf_op jit(solution)/shard_map/ppermute | solution.py:20
  119.6 12.1 %all_to_all.24 = bf16[2,16,16,256]{3,2,0,1:T(8,128)(2,1)S(1)} all-to-all(bf16[2,16,16,256]{3,2,0,1:T(8,128)(2,1)S(1)} %copy.17), channel_id=1, replica_groups=mesh['section'=4,'seq'=16,'tp'=4] {'section','tp'}, dimensions={1} | all-to-all | bytes 524288 | tf_op jit(solution)/shard_map/all_to_all | solution.py:108
  131.8 12.5 %all_gather.3 = bf16[2,64,1024]{2,1,0:T(8,128)(2,1)S(1)} all-gather(bf16[2,16,1024]{2,1,0:T(8,128)(2,1)S(1)} %bitcast.34), channel_id=1, replica_groups=mesh['section'=4,'seq'=16,'tp'=4] {'section'}, dimensions={1}, use_global_device_ids=true | all-gather | bytes 327680 | tf_op jit(solution)/shard_map/all_gather | solution.py:150
  144.4 0.8 convert_element_type.56
  (19 shorter events, 0.9 us)
Async XLA Ops:
  11.4 17.6 %collective-permute-start = (bf16[2,256,256]{2,1,0:T(8,128)(2,1)S(1)}, bf16[2,256,256]{2,1,0:T(8,128)(2,1)S(1)}, u32[]{:S(2)}, u32[]{:S(2)}) collective-permute-start(bf16[2,256,256]{2,1,0:T(8,128)(2,1)S(1)} %bitcast.26), channel_id=1, source_target_pairs={{0,16},{4,20},{8,24},{12,28},{16,32},{20,36},{24,40},{28,44},{32,4... | collective-permute-start | bytes 786440 | tf_op jit(solution)/shard_map/ppermute | solution.py:20
  17.8 23.4 %collective-permute-start.1 = (bf16[2,256,256]{2,1,0:T(8,128)(2,1)S(1)}, bf16[2,256,256]{2,1,0:T(8,128)(2,1)S(1)}, u32[]{:S(2)}, u32[]{:S(2)}) collective-permute-start(bf16[2,256,256]{2,1,0:T(8,128)(2,1)S(1)} %bitcast.27), channel_id=1, source_target_pairs={{0,12},{4,16},{8,20},{12,24},{16,28},{20,32},{24,36},{28,40},{32,4... | collective-permute-start | bytes 786440 | tf_op jit(solution)/shard_map/ppermute | solution.py:20
  21.3 25.6 %collective-permute-start.2 = (bf16[2,256,256]{2,1,0:T(8,128)(2,1)S(1)}, bf16[2,256,256]{2,1,0:T(8,128)(2,1)S(1)}, u32[]{:S(2)}, u32[]{:S(2)}) collective-permute-start(bf16[2,256,256]{2,1,0:T(8,128)(2,1)S(1)} %bitcast.28), channel_id=1, source_target_pairs={{0,8},{4,12},{8,16},{12,20},{16,24},{20,28},{24,32},{28,36},{32,40... | collective-permute-start | bytes 786440 | tf_op jit(solution)/shard_map/ppermute | solution.py:20
  24.2 26.9 %collective-permute-start.3 = (bf16[2,256,256]{2,1,0:T(8,128)(2,1)S(1)}, bf16[2,256,256]{2,1,0:T(8,128)(2,1)S(1)}, u32[]{:S(2)}, u32[]{:S(2)}) collective-permute-start(bf16[2,256,256]{2,1,0:T(8,128)(2,1)S(1)} %bitcast.29), channel_id=1, source_target_pairs={{0,4},{4,8},{8,12},{12,16},{16,20},{20,24},{24,28},{28,32},{32,36}... | collective-permute-start | bytes 786440 | tf_op jit(solution)/shard_map/ppermute | solution.py:20
  51.1 1.1 copy-start.1
  75.4 43.8 %copy-start = (f32[2,256,256]{2,1,0:T(8,128)S(1)}, f32[2,256,256]{2,1,0:T(8,128)}, u32[]{:S(2)}) copy-start(f32[2,256,256]{2,1,0:T(8,128)} %get-tuple-element.6) | copy-start | bytes 1572868
  76.7 18.1 %collective-permute-start.4 = (bf16[2,256,256]{2,1,0:T(8,128)(2,1)S(1)}, bf16[2,256,256]{2,1,0:T(8,128)(2,1)S(1)}, u32[]{:S(2)}, u32[]{:S(2)}) collective-permute-start(bf16[2,256,256]{2,1,0:T(8,128)(2,1)S(1)} %get-tuple-element.8), channel_id=1, source_target_pairs={{16,0},{20,4},{24,8},{28,12},{32,16},{36,20},{40,24},{44,28},{48,3... | collective-permute-start | bytes 786440 | tf_op jit(solution)/shard_map/ppermute | solution.py:20
  78.7 23.2 %collective-permute-start.7 = (bf16[2,256,256]{2,1,0:T(8,128)(2,1)S(1)}, bf16[2,256,256]{2,1,0:T(8,128)(2,1)S(1)}, u32[]{:S(2)}, u32[]{:S(2)}) collective-permute-start(bf16[2,256,256]{2,1,0:T(8,128)(2,1)S(1)} %get-tuple-element.9), channel_id=1, source_target_pairs={{4,0},{8,4},{12,8},{16,12},{20,16},{24,20},{28,24},{32,28},{36,32}... | collective-permute-start | bytes 786440 | tf_op jit(solution)/shard_map/ppermute | solution.py:20
  82.5 19.4 %collective-permute-start.6 = (bf16[2,256,256]{2,1,0:T(8,128)(2,1)S(1)}, bf16[2,256,256]{2,1,0:T(8,128)(2,1)S(1)}, u32[]{:S(2)}, u32[]{:S(2)}) collective-permute-start(bf16[2,256,256]{2,1,0:T(8,128)(2,1)S(1)} %get-tuple-element.10), channel_id=1, source_target_pairs={{8,0},{12,4},{16,8},{20,12},{24,16},{28,20},{32,24},{36,28},{40,32... | collective-permute-start | bytes 786440 | tf_op jit(solution)/shard_map/ppermute | solution.py:20
  84.4 34.8 %collective-permute-start.5 = (bf16[2,256,256]{2,1,0:T(8,128)(2,1)S(1)}, bf16[2,256,256]{2,1,0:T(8,128)(2,1)S(1)}, u32[]{:S(2)}, u32[]{:S(2)}) collective-permute-start(bf16[2,256,256]{2,1,0:T(8,128)(2,1)S(1)} %get-tuple-element.11), channel_id=1, source_target_pairs={{12,0},{16,4},{20,8},{24,12},{28,16},{32,20},{36,24},{40,28},{44,3... | collective-permute-start | bytes 786440 | tf_op jit(solution)/shard_map/ppermute | solution.py:20

commit v21 on v20

--- a/solution.py
+++ b/solution.py
@@ -147,9 +147,7 @@
     own_rows = jnp.swapaxes(own_t, 1, 2)
     chunk = scatter_layers(own_rows)
     kinds, rows, tp_peers, cols = chunk.shape
-    d_shared_kv = lax.all_gather(
-        chunk.reshape(kinds, rows, -1).astype(jnp.bfloat16), "section", axis=1, tiled=True
-    ).astype(jnp.float32)
+    d_shared_kv = lax.all_gather(chunk.reshape(kinds, rows, -1), "section", axis=1, tiled=True)
     return (d_queries, d_shared_kv)
 
 

time: 146 us -> 146 us (level)
    unnamed x11 -> x12, local copies, waits for them, and re-layouts: 3.16 us -> 3.95 us
where the time goes in v21:
time: 146 us
  waiting for transfers between devices  54.8 us (38%)
  blocking collectives  33.8 us (23%)
  starting transfers between devices  27.2 us (19%)
  Pallas kernels  23.2 us (16%)
  local copies, waits for them, and re-layouts  5.89 us (4%)
    ppermute x8, waiting for transfers between devices, shifted(): return lax.ppermute(value, axis, pairs)  54.8 us
    ppermute x8, starting transfers between devices, shifted(): return lax.ppermute(value, axis, pairs)  27.2 us
    pallas_call x1, Pallas kernels, attention_grads(): pl.pallas_call(functools.partial(attn_kernel, scale=scale, hd=hd, per_ste...  23.2 us
    all_gather x1, blocking collectives, body(): lax.all_gather(chunk.reshape(kinds, rows, -1), 'section', axis=1, tiled=T...  13.3 us
    all_to_all x1, blocking collectives, scatter_layers(): lax.all_to_all(pieces.astype(jnp.bfloat16), ('section', 'tp'), split_axis...  12.1 us
    all_to_all x1, blocking collectives, body(): lax.all_to_all(shared_kv, 'tp', split_axis=2, concat_axis=1, tiled=True)  8.39 us
    unnamed x12, local copies, waits for them, and re-layouts  3.95 us
  transfers between devices with their start and end apart: 8, of which 6 were waited for; matrix products, arithmetic and copies ran while one was open for 0% of the time, Pallas kernels for 0%

profile of v21, /device:TPU:80, one launch (start us, length us, event | category | flops | bytes accessed | tf_op | source)
XLA Modules:
  0.0 146.0 jit_solution(6469738821582396219)
XLA Ops:
  0.6 1.3 copy.13
  1.9 0.4 reshape.41
  2.3 8.4 %all_to_all.23 = bf16[4,2,16384]{2,1,0:T(2,128)(2,1)S(1)} all-to-all(bf16[4,2,16384]{2,1,0:T(2,128)(2,1)S(1)} %reshape.41), channel_id=1, replica_groups=mesh['section'=4,'seq'=16,'tp'=4] {'tp'}, dimensions={0} | all-to-all | bytes 524288 | tf_op jit(solution)/shard_map/all_to_all | solution.py:117
  11.0 0.4 copy.14
  11.4 6.4 %collective-permute-start = (bf16[2,256,256]{2,1,0:T(8,128)(2,1)S(1)}, bf16[2,256,256]{2,1,0:T(8,128)(2,1)S(1)}, u32[]{:S(2)}, u32[]{:S(2)}) collective-permute-start(bf16[2,256,256]{2,1,0:T(8,128)(2,1)S(1)} %bitcast.26), channel_id=1, source_target_pairs={{0,16},{4,20},{8,24},{12,28},{16,32},{20,36},{24,40},{28,44},{32,4... | collective-permute-start | bytes 786440 | tf_op jit(solution)/shard_map/ppermute | solution.py:20
  17.8 3.4 %collective-permute-start.1 = (bf16[2,256,256]{2,1,0:T(8,128)(2,1)S(1)}, bf16[2,256,256]{2,1,0:T(8,128)(2,1)S(1)}, u32[]{:S(2)}, u32[]{:S(2)}) collective-permute-start(bf16[2,256,256]{2,1,0:T(8,128)(2,1)S(1)} %bitcast.27), channel_id=1, source_target_pairs={{0,12},{4,16},{8,20},{12,24},{16,28},{20,32},{24,36},{28,40},{32,4... | collective-permute-start | bytes 786440 | tf_op jit(solution)/shard_map/ppermute | solution.py:20
  21.3 2.9 %collective-permute-start.2 = (bf16[2,256,256]{2,1,0:T(8,128)(2,1)S(1)}, bf16[2,256,256]{2,1,0:T(8,128)(2,1)S(1)}, u32[]{:S(2)}, u32[]{:S(2)}) collective-permute-start(bf16[2,256,256]{2,1,0:T(8,128)(2,1)S(1)} %bitcast.28), channel_id=1, source_target_pairs={{0,8},{4,12},{8,16},{12,20},{16,24},{20,28},{24,32},{28,36},{32,40... | collective-permute-start | bytes 786440 | tf_op jit(solution)/shard_map/ppermute | solution.py:20
  24.2 4.8 %collective-permute-start.3 = (bf16[2,256,256]{2,1,0:T(8,128)(2,1)S(1)}, bf16[2,256,256]{2,1,0:T(8,128)(2,1)S(1)}, u32[]{:S(2)}, u32[]{:S(2)}) collective-permute-start(bf16[2,256,256]{2,1,0:T(8,128)(2,1)S(1)} %bitcast.29), channel_id=1, source_target_pairs={{0,4},{4,8},{8,12},{12,16},{16,20},{20,24},{24,28},{28,32},{32,36}... | collective-permute-start | bytes 786440 | tf_op jit(solution)/shard_map/ppermute | solution.py:20
  29.1 12.2 %collective-permute-done.1 = bf16[2,256,256]{2,1,0:T(8,128)(2,1)S(1)} collective-permute-done((bf16[2,256,256]{2,1,0:T(8,128)(2,1)S(1)}, bf16[2,256,256]{2,1,0:T(8,128)(2,1)S(1)}, u32[]{:S(2)}, u32[]{:S(2)}) %collective-permute-start.1) | collective-permute-done | bytes 262176 | tf_op jit(solution)/shard_map/ppermute | solution.py:20
  41.3 5.6 %collective-permute-done.2 = bf16[2,256,256]{2,1,0:T(8,128)(2,1)S(1)} collective-permute-done((bf16[2,256,256]{2,1,0:T(8,128)(2,1)S(1)}, bf16[2,256,256]{2,1,0:T(8,128)(2,1)S(1)}, u32[]{:S(2)}, u32[]{:S(2)}) %collective-permute-start.2) | collective-permute-done | bytes 262176 | tf_op jit(solution)/shard_map/ppermute | solution.py:20
  46.9 4.1 %collective-permute-done.3 = bf16[2,256,256]{2,1,0:T(8,128)(2,1)S(1)} collective-permute-done((bf16[2,256,256]{2,1,0:T(8,128)(2,1)S(1)}, bf16[2,256,256]{2,1,0:T(8,128)(2,1)S(1)}, u32[]{:S(2)}, u32[]{:S(2)}) %collective-permute-start.3) | collective-permute-done | bytes 262176 | tf_op jit(solution)/shard_map/ppermute | solution.py:20
  51.1 1.1 copy-done.1
  52.2 23.2 %shard_map.50 = (bf16[256,2048]{1,0:T(8,128)(2,1)}, f32[2,256,256]{2,1,0:T(8,128)}, bf16[2,256,1024]{2,1,0:T(8,128)(2,1)}) custom-call(s32[1]{0:T(128)} %bitcast.bias_ref, bf16[256,2048]{1,0:T(8,128)(2,1)} %bitcast.35, bf16[256,2048]{1,0:T(8,128)(2,1)} %bitcast.36, bf16[2,1280,256]{2,1,0:T(8,128)(2,1)} %copy-done.1, bf16[2,1280,256]{2,1,0:T(8,128)(2,1)} %copy-done.1), custom_call_target="tpu_custom_call" | custom-call | flops 8053063680 | bytes 7077888 | tf_op jit(solution)/shard_map/pallas_call | solution.py:72
  75.4 1.3 fusion.2
  76.7 1.9 %collective-permute-start.4 = (bf16[2,256,256]{2,1,0:T(8,128)(2,1)S(1)}, bf16[2,256,256]{2,1,0:T(8,128)(2,1)S(1)}, u32[]{:S(2)}, u32[]{:S(2)}) collective-permute-start(bf16[2,256,256]{2,1,0:T(8,128)(2,1)S(1)} %get-tuple-element.8), channel_id=1, source_target_pairs={{16,0},{20,4},{24,8},{28,12},{32,16},{36,20},{40,24},{44,28},{48,3... | collective-permute-start | bytes 786440 | tf_op jit(solution)/shard_map/ppermute | solution.py:20
  78.7 3.9 %collective-permute-start.7 = (bf16[2,256,256]{2,1,0:T(8,128)(2,1)S(1)}, bf16[2,256,256]{2,1,0:T(8,128)(2,1)S(1)}, u32[]{:S(2)}, u32[]{:S(2)}) collective-permute-start(bf16[2,256,256]{2,1,0:T(8,128)(2,1)S(1)} %get-tuple-element.9), channel_id=1, source_target_pairs={{4,0},{8,4},{12,8},{16,12},{20,16},{24,20},{28,24},{32,28},{36,32}... | collective-permute-start | bytes 786440 | tf_op jit(solution)/shard_map/ppermute | solution.py:20
  82.5 1.9 %collective-permute-start.6 = (bf16[2,256,256]{2,1,0:T(8,128)(2,1)S(1)}, bf16[2,256,256]{2,1,0:T(8,128)(2,1)S(1)}, u32[]{:S(2)}, u32[]{:S(2)}) collective-permute-start(bf16[2,256,256]{2,1,0:T(8,128)(2,1)S(1)} %get-tuple-element.10), channel_id=1, source_target_pairs={{8,0},{12,4},{16,8},{20,12},{24,16},{28,20},{32,24},{36,28},{40,32... | collective-permute-start | bytes 786440 | tf_op jit(solution)/shard_map/ppermute | solution.py:20
  84.4 1.9 %collective-permute-start.5 = (bf16[2,256,256]{2,1,0:T(8,128)(2,1)S(1)}, bf16[2,256,256]{2,1,0:T(8,128)(2,1)S(1)}, u32[]{:S(2)}, u32[]{:S(2)}) collective-permute-start(bf16[2,256,256]{2,1,0:T(8,128)(2,1)S(1)} %get-tuple-element.11), channel_id=1, source_target_pairs={{12,0},{16,4},{20,8},{24,12},{28,16},{32,20},{36,24},{40,28},{44,3... | collective-permute-start | bytes 786440 | tf_op jit(solution)/shard_map/ppermute | solution.py:20
  86.4 8.4 %collective-permute-done.4 = bf16[2,256,256]{2,1,0:T(8,128)(2,1)S(1)} collective-permute-done((bf16[2,256,256]{2,1,0:T(8,128)(2,1)S(1)}, bf16[2,256,256]{2,1,0:T(8,128)(2,1)S(1)}, u32[]{:S(2)}, u32[]{:S(2)}) %collective-permute-start.4) | collective-permute-done | bytes 262176 | tf_op jit(solution)/shard_map/ppermute | solution.py:20
  94.8 7.1 %collective-permute-done.7 = bf16[2,256,256]{2,1,0:T(8,128)(2,1)S(1)} collective-permute-done((bf16[2,256,256]{2,1,0:T(8,128)(2,1)S(1)}, bf16[2,256,256]{2,1,0:T(8,128)(2,1)S(1)}, u32[]{:S(2)}, u32[]{:S(2)}) %collective-permute-start.7) | collective-permute-done | bytes 262176 | tf_op jit(solution)/shard_map/ppermute | solution.py:20
  101.9 17.3 %collective-permute-done.5 = bf16[2,256,256]{2,1,0:T(8,128)(2,1)S(1)} collective-permute-done((bf16[2,256,256]{2,1,0:T(8,128)(2,1)S(1)}, bf16[2,256,256]{2,1,0:T(8,128)(2,1)S(1)}, u32[]{:S(2)}, u32[]{:S(2)}) %collective-permute-start.5) | collective-permute-done | bytes 262176 | tf_op jit(solution)/shard_map/ppermute | solution.py:20
  119.6 12.1 %all_to_all.24 = bf16[2,16,16,256]{3,2,0,1:T(8,128)(2,1)S(1)} all-to-all(bf16[2,16,16,256]{3,2,0,1:T(8,128)(2,1)S(1)} %copy.17), channel_id=1, replica_groups=mesh['section'=4,'seq'=16,'tp'=4] {'section','tp'}, dimensions={1} | all-to-all | bytes 524288 | tf_op jit(solution)/shard_map/all_to_all | solution.py:108
  131.8 13.3 %all_gather.3 = f32[2,64,1024]{2,1,0:T(8,128)S(1)} all-gather(f32[2,16,1024]{2,1,0:T(8,128)S(1)} %bitcast.34), channel_id=1, replica_groups=mesh['section'=4,'seq'=16,'tp'=4] {'section'}, dimensions={1}, use_global_device_ids=true | all-gather | bytes 655360 | tf_op jit(solution)/shard_map/all_gather | solution.py:150
  145.2 0.8 copy.26
  (19 shorter events, 0.9 us)
Async XLA Ops:
  11.4 17.6 %collective-permute-start = (bf16[2,256,256]{2,1,0:T(8,128)(2,1)S(1)}, bf16[2,256,256]{2,1,0:T(8,128)(2,1)S(1)}, u32[]{:S(2)}, u32[]{:S(2)}) collective-permute-start(bf16[2,256,256]{2,1,0:T(8,128)(2,1)S(1)} %bitcast.26), channel_id=1, source_target_pairs={{0,16},{4,20},{8,24},{12,28},{16,32},{20,36},{24,40},{28,44},{32,4... | collective-permute-start | bytes 786440 | tf_op jit(solution)/shard_map/ppermute | solution.py:20
  17.8 23.4 %collective-permute-start.1 = (bf16[2,256,256]{2,1,0:T(8,128)(2,1)S(1)}, bf16[2,256,256]{2,1,0:T(8,128)(2,1)S(1)}, u32[]{:S(2)}, u32[]{:S(2)}) collective-permute-start(bf16[2,256,256]{2,1,0:T(8,128)(2,1)S(1)} %bitcast.27), channel_id=1, source_target_pairs={{0,12},{4,16},{8,20},{12,24},{16,28},{20,32},{24,36},{28,40},{32,4... | collective-permute-start | bytes 786440 | tf_op jit(solution)/shard_map/ppermute | solution.py:20
  21.3 25.6 %collective-permute-start.2 = (bf16[2,256,256]{2,1,0:T(8,128)(2,1)S(1)}, bf16[2,256,256]{2,1,0:T(8,128)(2,1)S(1)}, u32[]{:S(2)}, u32[]{:S(2)}) collective-permute-start(bf16[2,256,256]{2,1,0:T(8,128)(2,1)S(1)} %bitcast.28), channel_id=1, source_target_pairs={{0,8},{4,12},{8,16},{12,20},{16,24},{20,28},{24,32},{28,36},{32,40... | collective-permute-start | bytes 786440 | tf_op jit(solution)/shard_map/ppermute | solution.py:20
  24.2 26.9 %collective-permute-start.3 = (bf16[2,256,256]{2,1,0:T(8,128)(2,1)S(1)}, bf16[2,256,256]{2,1,0:T(8,128)(2,1)S(1)}, u32[]{:S(2)}, u32[]{:S(2)}) collective-permute-start(bf16[2,256,256]{2,1,0:T(8,128)(2,1)S(1)} %bitcast.29), channel_id=1, source_target_pairs={{0,4},{4,8},{8,12},{12,16},{16,20},{20,24},{24,28},{28,32},{32,36}... | collective-permute-start | bytes 786440 | tf_op jit(solution)/shard_map/ppermute | solution.py:20
  51.1 1.1 copy-start.1
  75.4 43.8 %copy-start = (f32[2,256,256]{2,1,0:T(8,128)S(1)}, f32[2,256,256]{2,1,0:T(8,128)}, u32[]{:S(2)}) copy-start(f32[2,256,256]{2,1,0:T(8,128)} %get-tuple-element.6) | copy-start | bytes 1572868
  76.7 18.1 %collective-permute-start.4 = (bf16[2,256,256]{2,1,0:T(8,128)(2,1)S(1)}, bf16[2,256,256]{2,1,0:T(8,128)(2,1)S(1)}, u32[]{:S(2)}, u32[]{:S(2)}) collective-permute-start(bf16[2,256,256]{2,1,0:T(8,128)(2,1)S(1)} %get-tuple-element.8), channel_id=1, source_target_pairs={{16,0},{20,4},{24,8},{28,12},{32,16},{36,20},{40,24},{44,28},{48,3... | collective-permute-start | bytes 786440 | tf_op jit(solution)/shard_map/ppermute | solution.py:20
  78.7 23.2 %collective-permute-start.7 = (bf16[2,256,256]{2,1,0:T(8,128)(2,1)S(1)}, bf16[2,256,256]{2,1,0:T(8,128)(2,1)S(1)}, u32[]{:S(2)}, u32[]{:S(2)}) collective-permute-start(bf16[2,256,256]{2,1,0:T(8,128)(2,1)S(1)} %get-tuple-element.9), channel_id=1, source_target_pairs={{4,0},{8,4},{12,8},{16,12},{20,16},{24,20},{28,24},{32,28},{36,32}... | collective-permute-start | bytes 786440 | tf_op jit(solution)/shard_map/ppermute | solution.py:20
  82.5 19.4 %collective-permute-start.6 = (bf16[2,256,256]{2,1,0:T(8,128)(2,1)S(1)}, bf16[2,256,256]{2,1,0:T(8,128)(2,1)S(1)}, u32[]{:S(2)}, u32[]{:S(2)}) collective-permute-start(bf16[2,256,256]{2,1,0:T(8,128)(2,1)S(1)} %get-tuple-element.10), channel_id=1, source_target_pairs={{8,0},{12,4},{16,8},{20,12},{24,16},{28,20},{32,24},{36,28},{40,32... | collective-permute-start | bytes 786440 | tf_op jit(solution)/shard_map/ppermute | solution.py:20
  84.4 34.8 %collective-permute-start.5 = (bf16[2,256,256]{2,1,0:T(8,128)(2,1)S(1)}, bf16[2,256,256]{2,1,0:T(8,128)(2,1)S(1)}, u32[]{:S(2)}, u32[]{:S(2)}) collective-permute-start(bf16[2,256,256]{2,1,0:T(8,128)(2,1)S(1)} %get-tuple-element.11), channel_id=1, source_target_pairs={{12,0},{16,4},{20,8},{24,12},{28,16},{32,20},{36,24},{40,28},{44,3... | collective-permute-start | bytes 786440 | tf_op jit(solution)/shard_map/ppermute | solution.py:20

commit v22 on v20

--- a/solution.py
+++ b/solution.py
@@ -51,11 +51,12 @@
         dsb = (p * (dp - delta)).astype(jnp.bfloat16)
         dq = jnp.dot(dsb, k, preferred_element_type=jnp.float32) * scale
         dq_ref[:, cols] = dq.astype(dq_ref.dtype)
-        dk_part = lax.dot_general(q, dsb, tn, preferred_element_type=jnp.float32) * scale
+        dk_part = lax.dot_general(q, dsb, tn, preferred_element_type=jnp.float32)
         dv_part = lax.dot_general(do, pb, tn, preferred_element_type=jnp.float32)
         dk = dk_part if dk is None else dk + dk_part
         dv = dv_part if dv is None else dv + dv_part
 
+    dk = dk * scale
     own_ref[0] = dk[:, sent_cols:]
     own_ref[1] = dv[:, sent_cols:]
     send_ref[0] = dk[:, :sent_cols].astype(send_ref.dtype)

time: 146 us -> 146 us (level)
  no operation moved by 1% of the time
where the time goes in v22:
time: 146 us; the launch traced here: 145 us
  waiting for transfers between devices  54.8 us (38%)
  blocking collectives  33 us (23%)
  starting transfers between devices  27.2 us (19%)
  Pallas kernels  23 us (16%)
  local copies, waits for them, and re-layouts  5.09 us (3%)
    ppermute x8, waiting for transfers between devices, shifted(): return lax.ppermute(value, axis, pairs)  54.8 us
    ppermute x8, starting transfers between devices, shifted(): return lax.ppermute(value, axis, pairs)  27.2 us
    pallas_call x1, Pallas kernels, attention_grads(): pl.pallas_call(functools.partial(attn_kernel, scale=scale, hd=hd, per_ste...  23 us
    all_gather x1, blocking collectives, body(): lax.all_gather(chunk.reshape(kinds, rows, -1).astype(jnp.bfloat16), 'sect...  12.5 us
    all_to_all x1, blocking collectives, scatter_layers(): lax.all_to_all(pieces.astype(jnp.bfloat16), ('section', 'tp'), split_axis...  12.1 us
    all_to_all x1, blocking collectives, body(): lax.all_to_all(shared_kv, 'tp', split_axis=2, concat_axis=1, tiled=True)  8.39 us
    unnamed x11, local copies, waits for them, and re-layouts  3.16 us
  transfers between devices with their start and end apart: 8, of which 6 were waited for; matrix products, arithmetic and copies ran while one was open for 0% of the time, Pallas kernels for 0%

profile of v22, /device:TPU:80, one launch (start us, length us, event | category | flops | bytes accessed | tf_op | source)
XLA Modules:
  0.0 145.1 jit_solution(11139827415481324455)
XLA Ops:
  0.6 1.3 copy.13
  1.9 0.4 reshape.40
  2.3 8.4 %all_to_all.23 = bf16[4,2,16384]{2,1,0:T(2,128)(2,1)S(1)} all-to-all(bf16[4,2,16384]{2,1,0:T(2,128)(2,1)S(1)} %reshape.40), channel_id=1, replica_groups=mesh['section'=4,'seq'=16,'tp'=4] {'tp'}, dimensions={0} | all-to-all | bytes 524288 | tf_op jit(solution)/shard_map/all_to_all | solution.py:118
  11.0 0.4 copy.14
  11.4 6.4 %collective-permute-start = (bf16[2,256,256]{2,1,0:T(8,128)(2,1)S(1)}, bf16[2,256,256]{2,1,0:T(8,128)(2,1)S(1)}, u32[]{:S(2)}, u32[]{:S(2)}) collective-permute-start(bf16[2,256,256]{2,1,0:T(8,128)(2,1)S(1)} %bitcast.26), channel_id=1, source_target_pairs={{0,16},{4,20},{8,24},{12,28},{16,32},{20,36},{24,40},{28,44},{32,4... | collective-permute-start | bytes 786440 | tf_op jit(solution)/shard_map/ppermute | solution.py:20
  17.8 3.4 %collective-permute-start.1 = (bf16[2,256,256]{2,1,0:T(8,128)(2,1)S(1)}, bf16[2,256,256]{2,1,0:T(8,128)(2,1)S(1)}, u32[]{:S(2)}, u32[]{:S(2)}) collective-permute-start(bf16[2,256,256]{2,1,0:T(8,128)(2,1)S(1)} %bitcast.27), channel_id=1, source_target_pairs={{0,12},{4,16},{8,20},{12,24},{16,28},{20,32},{24,36},{28,40},{32,4... | collective-permute-start | bytes 786440 | tf_op jit(solution)/shard_map/ppermute | solution.py:20
  21.3 2.9 %collective-permute-start.2 = (bf16[2,256,256]{2,1,0:T(8,128)(2,1)S(1)}, bf16[2,256,256]{2,1,0:T(8,128)(2,1)S(1)}, u32[]{:S(2)}, u32[]{:S(2)}) collective-permute-start(bf16[2,256,256]{2,1,0:T(8,128)(2,1)S(1)} %bitcast.28), channel_id=1, source_target_pairs={{0,8},{4,12},{8,16},{12,20},{16,24},{20,28},{24,32},{28,36},{32,40... | collective-permute-start | bytes 786440 | tf_op jit(solution)/shard_map/ppermute | solution.py:20
  24.2 4.8 %collective-permute-start.3 = (bf16[2,256,256]{2,1,0:T(8,128)(2,1)S(1)}, bf16[2,256,256]{2,1,0:T(8,128)(2,1)S(1)}, u32[]{:S(2)}, u32[]{:S(2)}) collective-permute-start(bf16[2,256,256]{2,1,0:T(8,128)(2,1)S(1)} %bitcast.29), channel_id=1, source_target_pairs={{0,4},{4,8},{8,12},{12,16},{16,20},{20,24},{24,28},{28,32},{32,36}... | collective-permute-start | bytes 786440 | tf_op jit(solution)/shard_map/ppermute | solution.py:20
  29.1 12.2 %collective-permute-done.1 = bf16[2,256,256]{2,1,0:T(8,128)(2,1)S(1)} collective-permute-done((bf16[2,256,256]{2,1,0:T(8,128)(2,1)S(1)}, bf16[2,256,256]{2,1,0:T(8,128)(2,1)S(1)}, u32[]{:S(2)}, u32[]{:S(2)}) %collective-permute-start.1) | collective-permute-done | bytes 262176 | tf_op jit(solution)/shard_map/ppermute | solution.py:20
  41.3 5.6 %collective-permute-done.2 = bf16[2,256,256]{2,1,0:T(8,128)(2,1)S(1)} collective-permute-done((bf16[2,256,256]{2,1,0:T(8,128)(2,1)S(1)}, bf16[2,256,256]{2,1,0:T(8,128)(2,1)S(1)}, u32[]{:S(2)}, u32[]{:S(2)}) %collective-permute-start.2) | collective-permute-done | bytes 262176 | tf_op jit(solution)/shard_map/ppermute | solution.py:20
  46.9 4.1 %collective-permute-done.3 = bf16[2,256,256]{2,1,0:T(8,128)(2,1)S(1)} collective-permute-done((bf16[2,256,256]{2,1,0:T(8,128)(2,1)S(1)}, bf16[2,256,256]{2,1,0:T(8,128)(2,1)S(1)}, u32[]{:S(2)}, u32[]{:S(2)}) %collective-permute-start.3) | collective-permute-done | bytes 262176 | tf_op jit(solution)/shard_map/ppermute | solution.py:20
  51.1 1.1 copy-done.1
  52.2 23.0 %shard_map.50 = (bf16[256,2048]{1,0:T(8,128)(2,1)}, f32[2,256,256]{2,1,0:T(8,128)}, bf16[2,256,1024]{2,1,0:T(8,128)(2,1)}) custom-call(s32[1]{0:T(128)} %bitcast.bias_ref, bf16[256,2048]{1,0:T(8,128)(2,1)} %bitcast.35, bf16[256,2048]{1,0:T(8,128)(2,1)} %bitcast.36, bf16[2,1280,256]{2,1,0:T(8,128)(2,1)} %copy-done.1, bf16[2,1280,256]{2,1,0:T(8,128)(2,1)} %copy-done.1), custom_call_target="tpu_custom_call" | custom-call | flops 8053063680 | bytes 7077888 | tf_op jit(solution)/shard_map/pallas_call | solution.py:73
  75.2 1.3 fusion.3
  76.6 1.9 %collective-permute-start.4 = (bf16[2,256,256]{2,1,0:T(8,128)(2,1)S(1)}, bf16[2,256,256]{2,1,0:T(8,128)(2,1)S(1)}, u32[]{:S(2)}, u32[]{:S(2)}) collective-permute-start(bf16[2,256,256]{2,1,0:T(8,128)(2,1)S(1)} %get-tuple-element.8), channel_id=1, source_target_pairs={{16,0},{20,4},{24,8},{28,12},{32,16},{36,20},{40,24},{44,28},{48,3... | collective-permute-start | bytes 786440 | tf_op jit(solution)/shard_map/ppermute | solution.py:20
  78.5 3.9 %collective-permute-start.7 = (bf16[2,256,256]{2,1,0:T(8,128)(2,1)S(1)}, bf16[2,256,256]{2,1,0:T(8,128)(2,1)S(1)}, u32[]{:S(2)}, u32[]{:S(2)}) collective-permute-start(bf16[2,256,256]{2,1,0:T(8,128)(2,1)S(1)} %get-tuple-element.9), channel_id=1, source_target_pairs={{4,0},{8,4},{12,8},{16,12},{20,16},{24,20},{28,24},{32,28},{36,32}... | collective-permute-start | bytes 786440 | tf_op jit(solution)/shard_map/ppermute | solution.py:20
  82.4 1.9 %collective-permute-start.6 = (bf16[2,256,256]{2,1,0:T(8,128)(2,1)S(1)}, bf16[2,256,256]{2,1,0:T(8,128)(2,1)S(1)}, u32[]{:S(2)}, u32[]{:S(2)}) collective-permute-start(bf16[2,256,256]{2,1,0:T(8,128)(2,1)S(1)} %get-tuple-element.10), channel_id=1, source_target_pairs={{8,0},{12,4},{16,8},{20,12},{24,16},{28,20},{32,24},{36,28},{40,32... | collective-permute-start | bytes 786440 | tf_op jit(solution)/shard_map/ppermute | solution.py:20
  84.3 1.9 %collective-permute-start.5 = (bf16[2,256,256]{2,1,0:T(8,128)(2,1)S(1)}, bf16[2,256,256]{2,1,0:T(8,128)(2,1)S(1)}, u32[]{:S(2)}, u32[]{:S(2)}) collective-permute-start(bf16[2,256,256]{2,1,0:T(8,128)(2,1)S(1)} %get-tuple-element.11), channel_id=1, source_target_pairs={{12,0},{16,4},{20,8},{24,12},{28,16},{32,20},{36,24},{40,28},{44,3... | collective-permute-start | bytes 786440 | tf_op jit(solution)/shard_map/ppermute | solution.py:20
  86.2 8.4 %collective-permute-done.4 = bf16[2,256,256]{2,1,0:T(8,128)(2,1)S(1)} collective-permute-done((bf16[2,256,256]{2,1,0:T(8,128)(2,1)S(1)}, bf16[2,256,256]{2,1,0:T(8,128)(2,1)S(1)}, u32[]{:S(2)}, u32[]{:S(2)}) %collective-permute-start.4) | collective-permute-done | bytes 262176 | tf_op jit(solution)/shard_map/ppermute | solution.py:20
  94.6 7.1 %collective-permute-done.7 = bf16[2,256,256]{2,1,0:T(8,128)(2,1)S(1)} collective-permute-done((bf16[2,256,256]{2,1,0:T(8,128)(2,1)S(1)}, bf16[2,256,256]{2,1,0:T(8,128)(2,1)S(1)}, u32[]{:S(2)}, u32[]{:S(2)}) %collective-permute-start.7) | collective-permute-done | bytes 262176 | tf_op jit(solution)/shard_map/ppermute | solution.py:20
  101.8 17.3 %collective-permute-done.5 = bf16[2,256,256]{2,1,0:T(8,128)(2,1)S(1)} collective-permute-done((bf16[2,256,256]{2,1,0:T(8,128)(2,1)S(1)}, bf16[2,256,256]{2,1,0:T(8,128)(2,1)S(1)}, u32[]{:S(2)}, u32[]{:S(2)}) %collective-permute-start.5) | collective-permute-done | bytes 262176 | tf_op jit(solution)/shard_map/ppermute | solution.py:20
  119.4 12.1 %all_to_all.24 = bf16[2,16,16,256]{3,2,0,1:T(8,128)(2,1)S(1)} all-to-all(bf16[2,16,16,256]{3,2,0,1:T(8,128)(2,1)S(1)} %copy.17), channel_id=1, replica_groups=mesh['section'=4,'seq'=16,'tp'=4] {'section','tp'}, dimensions={1} | all-to-all | bytes 524288 | tf_op jit(solution)/shard_map/all_to_all | solution.py:109
  131.7 12.5 %all_gather.3 = bf16[2,64,1024]{2,1,0:T(8,128)(2,1)S(1)} all-gather(bf16[2,16,1024]{2,1,0:T(8,128)(2,1)S(1)} %bitcast.34), channel_id=1, replica_groups=mesh['section'=4,'seq'=16,'tp'=4] {'section'}, dimensions={1}, use_global_device_ids=true | all-gather | bytes 327680 | tf_op jit(solution)/shard_map/all_gather | solution.py:151
  144.2 0.8 convert_element_type.56
  (19 shorter events, 0.9 us)
Async XLA Ops:
  11.4 17.6 %collective-permute-start = (bf16[2,256,256]{2,1,0:T(8,128)(2,1)S(1)}, bf16[2,256,256]{2,1,0:T(8,128)(2,1)S(1)}, u32[]{:S(2)}, u32[]{:S(2)}) collective-permute-start(bf16[2,256,256]{2,1,0:T(8,128)(2,1)S(1)} %bitcast.26), channel_id=1, source_target_pairs={{0,16},{4,20},{8,24},{12,28},{16,32},{20,36},{24,40},{28,44},{32,4... | collective-permute-start | bytes 786440 | tf_op jit(solution)/shard_map/ppermute | solution.py:20
  17.8 23.4 %collective-permute-start.1 = (bf16[2,256,256]{2,1,0:T(8,128)(2,1)S(1)}, bf16[2,256,256]{2,1,0:T(8,128)(2,1)S(1)}, u32[]{:S(2)}, u32[]{:S(2)}) collective-permute-start(bf16[2,256,256]{2,1,0:T(8,128)(2,1)S(1)} %bitcast.27), channel_id=1, source_target_pairs={{0,12},{4,16},{8,20},{12,24},{16,28},{20,32},{24,36},{28,40},{32,4... | collective-permute-start | bytes 786440 | tf_op jit(solution)/shard_map/ppermute | solution.py:20
  21.3 25.6 %collective-permute-start.2 = (bf16[2,256,256]{2,1,0:T(8,128)(2,1)S(1)}, bf16[2,256,256]{2,1,0:T(8,128)(2,1)S(1)}, u32[]{:S(2)}, u32[]{:S(2)}) collective-permute-start(bf16[2,256,256]{2,1,0:T(8,128)(2,1)S(1)} %bitcast.28), channel_id=1, source_target_pairs={{0,8},{4,12},{8,16},{12,20},{16,24},{20,28},{24,32},{28,36},{32,40... | collective-permute-start | bytes 786440 | tf_op jit(solution)/shard_map/ppermute | solution.py:20
  24.2 26.9 %collective-permute-start.3 = (bf16[2,256,256]{2,1,0:T(8,128)(2,1)S(1)}, bf16[2,256,256]{2,1,0:T(8,128)(2,1)S(1)}, u32[]{:S(2)}, u32[]{:S(2)}) collective-permute-start(bf16[2,256,256]{2,1,0:T(8,128)(2,1)S(1)} %bitcast.29), channel_id=1, source_target_pairs={{0,4},{4,8},{8,12},{12,16},{16,20},{20,24},{24,28},{28,32},{32,36}... | collective-permute-start | bytes 786440 | tf_op jit(solution)/shard_map/ppermute | solution.py:20
  51.1 1.1 copy-start.1
  75.2 43.9 %copy-start = (f32[2,256,256]{2,1,0:T(8,128)S(1)}, f32[2,256,256]{2,1,0:T(8,128)}, u32[]{:S(2)}) copy-start(f32[2,256,256]{2,1,0:T(8,128)} %get-tuple-element.6) | copy-start | bytes 1572868
  76.6 18.1 %collective-permute-start.4 = (bf16[2,256,256]{2,1,0:T(8,128)(2,1)S(1)}, bf16[2,256,256]{2,1,0:T(8,128)(2,1)S(1)}, u32[]{:S(2)}, u32[]{:S(2)}) collective-permute-start(bf16[2,256,256]{2,1,0:T(8,128)(2,1)S(1)} %get-tuple-element.8), channel_id=1, source_target_pairs={{16,0},{20,4},{24,8},{28,12},{32,16},{36,20},{40,24},{44,28},{48,3... | collective-permute-start | bytes 786440 | tf_op jit(solution)/shard_map/ppermute | solution.py:20
  78.5 23.3 %collective-permute-start.7 = (bf16[2,256,256]{2,1,0:T(8,128)(2,1)S(1)}, bf16[2,256,256]{2,1,0:T(8,128)(2,1)S(1)}, u32[]{:S(2)}, u32[]{:S(2)}) collective-permute-start(bf16[2,256,256]{2,1,0:T(8,128)(2,1)S(1)} %get-tuple-element.9), channel_id=1, source_target_pairs={{4,0},{8,4},{12,8},{16,12},{20,16},{24,20},{28,24},{32,28},{36,32}... | collective-permute-start | bytes 786440 | tf_op jit(solution)/shard_map/ppermute | solution.py:20
  82.4 19.4 %collective-permute-start.6 = (bf16[2,256,256]{2,1,0:T(8,128)(2,1)S(1)}, bf16[2,256,256]{2,1,0:T(8,128)(2,1)S(1)}, u32[]{:S(2)}, u32[]{:S(2)}) collective-permute-start(bf16[2,256,256]{2,1,0:T(8,128)(2,1)S(1)} %get-tuple-element.10), channel_id=1, source_target_pairs={{8,0},{12,4},{16,8},{20,12},{24,16},{28,20},{32,24},{36,28},{40,32... | collective-permute-start | bytes 786440 | tf_op jit(solution)/shard_map/ppermute | solution.py:20
  84.3 34.8 %collective-permute-start.5 = (bf16[2,256,256]{2,1,0:T(8,128)(2,1)S(1)}, bf16[2,256,256]{2,1,0:T(8,128)(2,1)S(1)}, u32[]{:S(2)}, u32[]{:S(2)}) collective-permute-start(bf16[2,256,256]{2,1,0:T(8,128)(2,1)S(1)} %get-tuple-element.11), channel_id=1, source_target_pairs={{12,0},{16,4},{20,8},{24,12},{28,16},{32,20},{36,24},{40,28},{44,3... | collective-permute-start | bytes 786440 | tf_op jit(solution)/shard_map/ppermute | solution.py:20
